TPU v7x, 768 devices: a whole 4x8x12 slice. The times are simulated.
768 devices in a mesh: dp: 16 (over x_hi, y), tile: 48 (over z, x_lo, core).
Axes of the slice: x: 4 (x_hi: 2, x_lo: 2; x = x_hi * 2 + x_lo), y: 8, z: 12, core: 2. Of those that a mesh axis runs over, the one named last changes fastest.
Arguments:
- section_map: bfloat16 [32, 192, 32, 3072], P('dp', 'tile'), may hold values from -16 to 16
- dw_kernel: bfloat16 [7, 7, 3072], replicated, may hold values from -0.875 to 0.875
- conv_bias: float32 [3072], replicated, may hold values from -3 to 3
- ln_gain: float32 [3072], replicated, may hold values from 0.5 to 1.5
- layer_scale: float32 [3072], replicated, may hold values from 0.25 to 1
- head_gain: float32 [3072], replicated, may hold values from 0.5 to 1.5
- head_weight: bfloat16 [3072, 1024], replicated, may hold values from -0.109375 to 0.109375
- texts: bfloat16 [192, 1024], P('dp'), may hold values from -6 to 6
- positives: int32 [192], replicated, may hold values from 0 to 191, each once
- sources: int32 [192], replicated, may hold values from 0 to 31
- numerators: int32 [32], replicated, may hold values from 1 to 8
Outputs:
- grad_map: bfloat16 [32, 192, 32, 3072], P('dp', 'tile')
- text_grad: float32 [192, 1024], P('dp')
- group_sums: float32 [32], replicated
Inputs may be any that keep to these rules, and one draw needn't show every extreme that they name: `positives`: every text is the match of exactly one image.
All inputs are finite; a program needn't handle non-finite values.
Results may differ from a plain program's by a relative error of at most 0.0083.
Values may be sent and summed in bfloat16 or wider, within the bound.
No kernel may reach another device: no remote copies, remote signals or barrier semaphores. Data moves between devices by JAX's collectives and lax.ppermute only.
A program may use at most 64 MiB of HBM per device.

v0:
```python
import jax
import jax.numpy as jnp
from jax import lax
from jax.sharding import PartitionSpec as P

H = 32
W = 32
SOURCES = 32


LOGIT_SCALE = 10.0
LOGIT_BIAS = -5.0


def padded(value, sides, width):
    for axis, dim in sides:
        devices, length = (lax.axis_size(axis), value.shape[dim])
        up = [(i, (i + 1) % devices) for i in range(devices - 1)]
        down = [(j, i) for i, j in up]
        last = lax.slice_in_dim(value, length - width, length, axis=dim)
        leading = lax.slice_in_dim(value, 0, width, axis=dim)
        before = lax.ppermute(last, axis, up)
        after = lax.ppermute(leading, axis, down)
        value = jnp.concatenate([before, value, after], axis=dim)
    return value


def cell_norm(values, gain):
    center = values - jnp.mean(values, axis=-1, keepdims=True)
    spread = jnp.mean(center * center, axis=-1, keepdims=True)
    return center * lax.rsqrt(spread + 1e-06) * gain


def unit_rows(values):
    return values * lax.rsqrt(jnp.sum(values * values, axis=-1, keepdims=True) + 1e-06)


def depthwise_rows(field, kernel, row_start):
    batch_rows, row_count, width, channels = field.shape
    framed = padded(field, (("tile", 1),), 3)
    positions = jnp.arange(row_count + 6)
    top_open = row_start % H != 0
    bottom_open = (row_start + row_count) % H != 0
    keeping = ((positions >= 3) | top_open) & ((positions < row_count + 3) | bottom_open)
    framed = jnp.where(keeping[None, :, None, None], framed, jnp.zeros_like(framed))
    framed = jnp.pad(framed, ((0, 0), (0, 0), (3, 3), (0, 0)))
    summed = jnp.zeros(field.shape, jnp.float32)
    for tap_row in range(7):
        for tap_col in range(7):
            window = framed[:, tap_row : tap_row + row_count, tap_col : tap_col + width, :].astype(
                jnp.float32
            )
            summed = summed + window * kernel[tap_row, tap_col].astype(jnp.float32)
    return summed


def local(
    section_map,
    dw_kernel,
    conv_bias,
    ln_gain,
    layer_scale,
    head_gain,
    head_weight,
    texts,
    positives,
    sources,
    numerators,
):
    batch_rows, row_count, width, channels = section_map.shape
    tile_count = lax.axis_size("tile")
    img_tile = tile_count * row_count // H
    local_images = batch_rows * img_tile
    row_start = lax.axis_index("tile") * row_count
    slot_mask = (jnp.arange(img_tile) == row_start // H).astype(jnp.float32)
    conved = depthwise_rows(section_map, dw_kernel, row_start) + conv_bias
    section_out = section_map.astype(jnp.float32) + layer_scale * cell_norm(conved, ln_gain)
    partial_value = jnp.sum(section_out, axis=(1, 2)) / (H * W)
    placed = partial_value[:, None, :] * slot_mask[None, :, None]
    pooled = lax.psum(placed, "tile").reshape(local_images, channels)
    head_in = cell_norm(pooled, head_gain).astype(jnp.bfloat16)
    embed = jnp.dot(head_in, head_weight, preferred_element_type=jnp.float32)
    image_vec = unit_rows(embed).astype(jnp.bfloat16)
    text_f = texts.astype(jnp.float32)
    text_vec = unit_rows(text_f).astype(jnp.bfloat16)
    dp_base = lax.axis_index("dp") * local_images
    source_table = (sources[:, None] == jnp.arange(SOURCES)[None, :]).astype(jnp.float32)
    weights_all = (
        SOURCES
        * jnp.sum(source_table * numerators.astype(jnp.float32)[None, :], axis=1)
        / jnp.sum(numerators).astype(jnp.float32)
    )
    my_weight = lax.dynamic_slice_in_dim(weights_all, dp_base, local_images)
    my_table = lax.dynamic_slice_in_dim(source_table, dp_base, local_images)
    my_pos = lax.dynamic_slice_in_dim(positives, dp_base, local_images)
    piece = lax.all_gather(text_vec, "dp", axis=0, tiled=True)
    count = piece.shape[0]
    logits = (
        LOGIT_SCALE * jnp.dot(image_vec, piece.T, preferred_element_type=jnp.float32) + LOGIT_BIAS
    )
    labels = jnp.where(my_pos[:, None] == jnp.arange(count)[None, :], 1.0, -1.0).astype(jnp.float32)
    row_loss = jnp.sum(jax.nn.softplus(-labels * logits), axis=1)
    pair_grad = (my_weight[:, None] * -labels * jax.nn.sigmoid(-labels * logits)).astype(
        jnp.bfloat16
    )
    image_dir = LOGIT_SCALE * jnp.dot(pair_grad, piece, preferred_element_type=jnp.float32)
    block = LOGIT_SCALE * lax.dot_general(
        pair_grad, image_vec, (((0,), (0,)), ((), ())), preferred_element_type=jnp.float32
    )
    text_terms = block
    row_loss, image_dir, text_terms = (row_loss, image_dir, text_terms)
    text_dir = lax.psum_scatter(text_terms, "dp", scatter_dimension=0, tiled=True)
    group_part = jnp.sum(my_table * (my_weight * row_loss)[:, None], axis=0)
    group_sums = lax.psum(group_part, "dp")
    text_back = jax.vjp(unit_rows, text_f)[1]
    text_grad = text_back(text_dir)[0]
    embed_back = jax.vjp(unit_rows, embed)[1]
    embed_grad = embed_back(image_dir)[0].astype(jnp.bfloat16)
    head_grad = jnp.dot(embed_grad, head_weight.T, preferred_element_type=jnp.float32)
    pool_back = jax.vjp(lambda values: cell_norm(values, head_gain), pooled)[1]
    pooled_grad = pool_back(head_grad)[0]
    own_grad = jnp.sum(
        pooled_grad.reshape(batch_rows, img_tile, channels) * slot_mask[None, :, None], axis=1
    )
    norm_back = jax.vjp(lambda values: cell_norm(values, ln_gain), conved)[1]
    seeded = jnp.broadcast_to((layer_scale * own_grad)[:, None, None, :], conved.shape)
    conv_grad = norm_back(seeded)[0].astype(jnp.bfloat16)
    spread = depthwise_rows(conv_grad, dw_kernel[::-1, ::-1, :], row_start)
    grad_map = (own_grad[:, None, None, :] + spread).astype(jnp.bfloat16)
    return (grad_map, text_grad, group_sums)


def solution(mesh):
    placed = (
        P("dp", "tile", None, None),
        P(),
        P(),
        P(),
        P(),
        P(),
        P(),
        P("dp", None),
        P(),
        P(),
        P(),
    )
    return jax.shard_map(
        local,
        mesh=mesh,
        in_specs=placed,
        out_specs=(P("dp", "tile", None, None), P("dp", None), P()),
        check_vma=False,
    )
```

profile of v0, /device:TPU:6, one launch (start us, length us, event | category | flops | bytes accessed | tf_op | source)
XLA Modules:
  0.0 583.9 jit_solution(4079145896862112133)
XLA Ops:
  7.3 3.3 fusion.24
  10.6 1.9 collective-permute-start
  12.5 3.6 collective-permute-start.1
  16.9 0.6 fusion.25
  18.3 0.9 slice_convert_fusion.48
  19.1 42.9 %all-gather = bf16[16,12,1024]{2,1,0:T(8,128)(2,1)S(1)} all-gather(bf16[1,12,1024]{2,1,0:T(8,128)(2,1)S(1)} %fusion.13), channel_id=1, replica_groups=mesh['dp'=16,'tile'=48] {'dp'}, dimensions={0}, use_global_device_ids=true | all-gather | bytes 417792 | tf_op jit(solution)/shard_map/all_gather | solution.py:96
  62.2 0.6 dynamic_slice.10
  62.8 0.7 select_reduce_fusion
  64.3 2.0 maximum_select_fusion
  66.8 27.8 %fusion.22 = (f32[2,4,32]{2,1,0:T(4,128)S(1)}, f32[2,4,32,3072]{3,2,1,0:T(8,128)S(1)}) fusion(f32[3072]{0:T(1024)S(1)} %copy-done.105, f32[3072]{0:T(1024)S(1)} %bitcast.76, f32[3072]{0:T(1024)S(1)} %bitcast.78, f32[3072]{0:T(1024)S(1)} %bitcast.82, f32[3072]{0:T(1024)S(1)} %bitcast.84, bf16[2,10,32,3072]{3,2,1,0:T(8,128)(2,1)S(1)} %maximum_select_fusion, ...), kind=kLoop, calls=%fused_computation.195 | loop fusion | flops 116391680 | bytes 18703360 | tf_op jit(solution)/shard_map/reduce_sum | solution.py:29
  95.1 0.6 copy-done.103
  96.0 1.0 add_reduce_fusion
  97.0 0.8 broadcast_multiply_fusion
  97.8 1.2 multiply_divide_fusion
  99.0 304.4 %all-reduce.6.cloned.1.call-done = f32[2,6,3072]{2,1,0:T(8,128)} async-done(((f32[2,6,3072]{2,1,0:T(8,128)}), f32[2,6,3072]{2,1,0:T(8,128)}) %all-reduce.6.cloned.1.call-update) | async-done | bytes 147472 | tf_op jit(solution)/shard_map/psum | solution.py:80
  403.4 1.6 reduce_sum.167
  405.0 1.2 broadcast_multiply_fusion.4
  406.3 1.3 div.87
  407.6 1.1 multiply_reduce_fusion.3
  408.7 0.6 multiply_add_fusion.1
  409.3 1.3 add.453
  410.6 1.2 rsqrt.45
  411.8 1.6 reshape.538
  413.4 4.0 multiply_reduce_fusion.5
  417.9 0.6 fusion.20
  418.8 1.2 convolution_multiply_fusion.1
  420.1 4.6 multiply_reduce_fusion.2
  425.1 0.8 multiply_reduce_fusion.1
  426.0 0.6 copy-done.8
  426.6 0.7 broadcast_multiply_fusion.1
  427.8 0.8 fusion.2
  428.6 1.0 add_convert_fusion.1
  429.6 1.1 copy-done.2
  430.8 1.3 fusion.23
  432.1 2.1 collective-permute-start.2
  434.2 3.5 collective-permute-start.3
  437.6 49.6 %fusion = f32[16,1024]{1,0:T(8,128)S(1)} fusion(f32[192,1024]{1,0:T(8,128)S(1)} %copy-done.4), kind=kCustom, calls=%all-reduce-scatter | all-reduce-scatter fusion | flops 262145 | bytes 856064
  487.3 1.9 collective-permute-start.7
  489.3 1.3 dynamic-slice.4
  491.2 3.2 collective-permute-start.6
  494.5 1.9 collective-permute-start.5
  496.4 4.2 collective-permute-done.7
  500.6 1.9 collective-permute-start.4
  502.6 42.7 %psum.15 = f32[32]{0:T(128)} all-reduce(f32[32]{0:T(128)S(1)} %multiply_reduce_fusion.6), channel_id=1, replica_groups=mesh['dp'=16,'tile'=48] {'dp'}, use_global_device_ids=true, to_apply=%region_20.21 | all-reduce | flops 32 | bytes 256 | tf_op jit(solution)/shard_map/psum | solution.py:114
  545.4 0.6 concatenate.8
  546.1 0.7 add_add_fusion.3
  547.2 2.1 maximum_select_fusion.1
  549.7 27.3 %add_convert_fusion = bf16[2,4,32,3072]{3,2,1,0:T(8,128)(2,1)} fusion(bf16[2,10,32,3072]{3,2,1,0:T(8,128)(2,1)S(1)} %maximum_select_fusion.1, f32[2,3072]{1,0:T(2,128)S(1)} %copy-done.9, f32[3072]{0:T(1024)S(1)} %bitcast.77, f32[3072]{0:T(1024)S(1)} %bitcast.79, f32[3072]{0:T(1024)S(1)} %bitcast.83, f32[3072]{0:T(1024)S(1)} %bitcast.85, ...), kind=kLoop, calls=%fused_computation.7 | loop fusion | flops 116391936 | bytes 17141760 | tf_op jit(solution)/shard_map/convert_element_type | solution.py:129
  (279 shorter events, 4.3 us)
Async XLA Ops:
  7.2 57.2 %copy-start = (bf16[2,4,32,3072]{3,2,1,0:T(8,128)(2,1)S(1)}, bf16[2,4,32,3072]{3,2,1,0:T(8,128)(2,1)}, u32[]{:S(2)}) copy-start(bf16[2,4,32,3072]{3,2,1,0:T(8,128)(2,1)} %param.11) | copy-start | bytes 4718596
  7.2 9.6 %copy-start.6 = (bf16[12,1024]{1,0:T(8,128)(2,1)S(1)}, bf16[12,1024]{1,0:T(8,128)(2,1)}, u32[]{:S(2)}) copy-start(bf16[12,1024]{1,0:T(8,128)(2,1)} %param.18) | copy-start | bytes 73732
  7.2 9.7 %copy-start.120 = (s32[32]{0:T(128)S(1)}, s32[32]{0:T(128)}, u32[]{:S(2)}) copy-start(s32[32]{0:T(128)} %param.21) | copy-start | bytes 388
  7.2 11.1 %copy-start.5 = (bf16[7,7,3072]{2,1,0:T(8,128)(2,1)S(1)}, bf16[7,7,3072]{2,1,0:T(8,128)(2,1)}, u32[]{:S(2)}) copy-start(bf16[7,7,3072]{2,1,0:T(8,128)(2,1)} %param.12) | copy-start | bytes 903172
  7.2 54.9 %copy-start.119 = (s32[192]{0:T(256)S(1)}, s32[192]{0:T(256)}, u32[]{:S(2)}) copy-start(s32[192]{0:T(256)} %param.19) | copy-start | bytes 2308
  7.2 55.6 %copy-start.108 = (s32[192]{0:T(256)S(1)}, s32[192]{0:T(256)}, u32[]{:S(2)}) copy-start(s32[192]{0:T(256)} %param.20) | copy-start | bytes 2308
  7.2 396.2 %all-reduce.6.cloned.1.call-start = ((), (), s32[]{:S(2)}) async-start(), calls=%async_computation | async-start | bytes 393216 | tf_op jit(solution)/shard_map/psum | solution.py:80
  10.6 53.7 %collective-permute-start = (bf16[2,3,32,3072]{3,2,1,0:T(8,128)(2,1)}, bf16[2,3,32,3072]{3,2,1,0:T(8,128)(2,1)}, u32[]{:S(2)}, u32[]{:S(2)}) collective-permute-start(bf16[2,3,32,3072]{3,2,1,0:T(8,128)(2,1)} %get-tuple-element.11), channel_id=1, source_target_pairs={{0,1},{1,2},{2,3},{3,4},{4,5},{5,6},{6,7},{7,8},{8,9},{9,10},{10,1... | collective-permute-start | bytes 3538952 | tf_op jit(solution)/shard_map/ppermute | solution.py:22
  12.5 51.8 %collective-permute-start.1 = (bf16[2,3,32,3072]{3,2,1,0:T(8,128)(2,1)}, bf16[2,3,32,3072]{3,2,1,0:T(8,128)(2,1)}, u32[]{:S(2)}, u32[]{:S(2)}) collective-permute-start(bf16[2,3,32,3072]{3,2,1,0:T(8,128)(2,1)} %get-tuple-element.12), channel_id=1, source_target_pairs={{1,0},{2,1},{3,2},{4,3},{5,4},{6,5},{7,6},{8,7},{9,8},{10,9},{11,1... | collective-permute-start | bytes 3538952 | tf_op jit(solution)/shard_map/ppermute | solution.py:23
  19.1 47.2 %copy-start.33 = (f32[1,1,3072]{2,1,0:T(1,128)}, f32[1,1,3072]{2,1,0:T(1,128)S(1)}, u32[]{:S(2)}) copy-start(f32[1,1,3072]{2,1,0:T(1,128)S(1)} %get-tuple-element.13) | copy-start | bytes 36868
  62.2 4.2 copy-start.113
  63.6 2.7 copy-start.11
  63.7 2.7 copy-start.13
  63.7 2.7 copy-start.15
  63.7 2.7 copy-start.17
  63.7 2.7 copy-start.19
  63.7 2.7 copy-start.21
  63.7 2.7 copy-start.23
  63.7 2.7 copy-start.25
  63.7 2.7 copy-start.27
  63.7 2.7 copy-start.29
  63.7 2.7 copy-start.31
  63.9 2.5 copy-start.71
  63.9 2.5 copy-start.73
  63.9 2.5 copy-start.75
  64.0 2.5 copy-start.77
  64.0 2.5 copy-start.79
  413.4 4.1 copy-start.106
  413.4 4.5 copy-start.110
  413.4 6.6 %copy-start.3 = (f32[12,3072]{1,0:T(8,128)S(1)}, f32[12,3072]{1,0:T(8,128)}, u32[]{:S(2)}) copy-start(f32[12,3072]{1,0:T(8,128)} %reshape.538) | copy-start | bytes 442372
  413.4 6.6 %copy-start.102 = (f32[3072]{0:T(1024)S(1)}, f32[3072]{0:T(1024)}, u32[]{:S(2)}) copy-start(f32[3072]{0:T(1024)} %param.16) | copy-start | bytes 36868
  413.4 6.6 %copy-start.107 = (f32[12]{0:T(128)S(1)}, f32[12]{0:T(128)}, u32[]{:S(2)}) copy-start(f32[12]{0:T(128)} %div.87) | copy-start | bytes 148
  420.1 4.7 copy-start.121
  420.1 4.7 copy-start.115
  425.1 2.6 copy-start.104
  425.1 2.6 copy-start.100
  430.7 6.9 %copy-start.4 = (f32[192,1024]{1,0:T(8,128)S(1)}, f32[192,1024]{1,0:T(8,128)}, u32[]{:S(2)}) copy-start(f32[192,1024]{1,0:T(8,128)} %convolution_multiply_fusion.1) | copy-start | bytes 2359300
  430.7 58.5 %copy-start.109 = (s32[192]{0:T(256)S(1)}, s32[192]{0:T(256)}, u32[]{:S(2)}) copy-start(s32[192]{0:T(256)} %param.20) | copy-start | bytes 2308
  430.7 71.8 %copy-start.116 = (f32[12]{0:T(128)S(1)}, f32[12]{0:T(128)}, u32[]{:S(2)}) copy-start(f32[12]{0:T(128)} %get-tuple-element.3) | copy-start | bytes 148
  430.7 115.2 %copy-start.7 = (bf16[12,1024]{1,0:T(8,128)(2,1)S(1)}, bf16[12,1024]{1,0:T(8,128)(2,1)}, u32[]{:S(2)}) copy-start(bf16[12,1024]{1,0:T(8,128)(2,1)} %param.18) | copy-start | bytes 73732
  430.7 115.4 %copy-start.118 = (f32[12]{0:T(128)S(1)}, f32[12]{0:T(128)}, u32[]{:S(2)}) copy-start(f32[12]{0:T(128)} %copy-done.117) | copy-start | bytes 148
  430.8 115.4 %copy-start.112 = (f32[12]{0:T(128)S(1)}, f32[12]{0:T(128)}, u32[]{:S(2)}) copy-start(f32[12]{0:T(128)} %copy-done.111) | copy-start | bytes 148
  432.1 115.2 %collective-permute-start.2 = (bf16[2,3,32,3072]{3,2,1,0:T(8,128)(2,1)}, bf16[2,3,32,3072]{3,2,1,0:T(8,128)(2,1)S(1)}, u32[]{:S(2)}, u32[]{:S(2)}) collective-permute-start(bf16[2,3,32,3072]{3,2,1,0:T(8,128)(2,1)} %get-tuple-element.9), channel_id=1, source_target_pairs={{0,1},{1,2},{2,3},{3,4},{4,5},{5,6},{6,7},{7,8},{8,9},{9,10},{10,1... | collective-permute-start | bytes 3538952 | tf_op jit(solution)/shard_map/ppermute | solution.py:22
  434.2 113.1 %collective-permute-start.3 = (bf16[2,3,32,3072]{3,2,1,0:T(8,128)(2,1)S(1)}, bf16[2,3,32,3072]{3,2,1,0:T(8,128)(2,1)}, u32[]{:S(2)}, u32[]{:S(2)}) collective-permute-start(bf16[2,3,32,3072]{3,2,1,0:T(8,128)(2,1)S(1)} %get-tuple-element.10), channel_id=1, source_target_pairs={{1,0},{2,1},{3,2},{4,3},{5,4},{6,5},{7,6},{8,7},{9,8},{10,9},{11,1... | collective-permute-start | bytes 3538952 | tf_op jit(solution)/shard_map/ppermute | solution.py:23
  487.3 13.3 %collective-permute-start.7 = (f32[12,1024]{1,0:T(8,128)S(1)}, f32[12,1024]{1,0:T(8,128)S(1)}, u32[]{:S(2)}, u32[]{:S(2)}) collective-permute-start(f32[12,1024]{1,0:T(8,128)S(1)} %slice.732), channel_id=1, source_target_pairs={{0,192},{48,240},{96,288},{144,336},{192,384},{240,432},{288,480},... | collective-permute-start | bytes 147464
  491.2 54.1 %collective-permute-start.6 = (f32[16,1024]{1,0:T(8,128)S(1)}, f32[16,1024]{1,0:T(8,128)S(1)}, u32[]{:S(2)}, u32[]{:S(2)}) collective-permute-start(f32[16,1024]{1,0:T(8,128)S(1)} %fusion), channel_id=1, source_target_pairs={{0,144},{48,192},{96,240},{144,288},{192,336},{240,384},{288,432},... | collective-permute-start | bytes 196616
  494.5 50.9 %collective-permute-start.5 = (f32[16,1024]{1,0:T(8,128)S(1)}, f32[16,1024]{1,0:T(8,128)S(1)}, u32[]{:S(2)}, u32[]{:S(2)}) collective-permute-start(f32[16,1024]{1,0:T(8,128)S(1)} %fusion), channel_id=1, source_target_pairs={{0,96},{48,144},{96,192},{144,240},{192,288},{240,336},{288,384},{... | collective-permute-start | bytes 196616
  500.6 44.8 %collective-permute-start.4 = (f32[16,1024]{1,0:T(8,128)S(1)}, f32[16,1024]{1,0:T(8,128)S(1)}, u32[]{:S(2)}, u32[]{:S(2)}) collective-permute-start(f32[16,1024]{1,0:T(8,128)S(1)} %fusion), channel_id=1, source_target_pairs={{0,48},{48,96},{96,144},{144,192},{192,240},{240,288},{288,336},{3... | collective-permute-start | bytes 196616
  (83 other events, 196.0 us)
Sparse Core Ops, SparseCore 0:
  97.9 305.4 all-reduce.5
where the time goes:
time: 587 us; the launch traced here: 584 us
  waiting for transfers between devices  309 us (53%)
  blocking collectives  135 us (23%)
  other arithmetic  76 us (13%)
  starting transfers between devices  20.1 us (3%)
  between operations  17.4 us (3%)
  local copies, waits for them, and re-layouts  15.8 us (3%)
  matrix products  10.6 us (2%)
    psum x1, waiting for transfers between devices, local(): pooled = lax.psum(placed, 'tile').reshape(local_images, channels)  304 us
    unnamed x1, blocking collectives  49.6 us
    all_gather x1, blocking collectives, local(): piece = lax.all_gather(text_vec, 'dp', axis=0, tiled=True)  42.9 us
    psum x1, blocking collectives, local(): group_sums = lax.psum(group_part, 'dp')  42.7 us
    reduce_sum x4, other arithmetic, cell_norm(): center = values - jnp.mean(values, axis=-1, keepdims=True)  30.4 us
    convert_element_type x1, other arithmetic, local(): grad_map = (own_grad[:, None, None, :] + spread).astype(jnp.bfloat16)  27.3 us
  transfers between devices with their start and end apart: 9, of which 2 were waited for; matrix products, arithmetic and copies ran while one was open for 10% of the time, Pallas kernels for 0%

commit v1 on v0

v1 whole, which is shorter than its diff:
```python
import jax
import jax.numpy as jnp
from jax import lax
from jax.sharding import Mesh
from jax.sharding import PartitionSpec as P

H = 32
W = 32
SOURCES = 32


LOGIT_SCALE = 10.0
LOGIT_BIAS = -5.0


def halo_rows(value, width):
    devices = lax.axis_size("row")
    up = [(i, i + 1) for i in range(devices - 1)]
    down = [(j, i) for i, j in up]
    length = value.shape[1]
    last = lax.slice_in_dim(value, length - width, length, axis=1)
    leading = lax.slice_in_dim(value, 0, width, axis=1)
    before = lax.ppermute(last, "row", up)
    after = lax.ppermute(leading, "row", down)
    return jnp.concatenate([before, value, after], axis=1)


def group_sum(value):
    devices = lax.axis_size("row")
    step = 1
    while step < devices:
        pairs = [(i, i ^ step) for i in range(devices)]
        value = value + lax.ppermute(value, "row", pairs)
        step *= 2
    return value


def cell_norm(values, gain):
    center = values - jnp.mean(values, axis=-1, keepdims=True)
    spread = jnp.mean(center * center, axis=-1, keepdims=True)
    return center * lax.rsqrt(spread + 1e-06) * gain


def unit_rows(values):
    return values * lax.rsqrt(jnp.sum(values * values, axis=-1, keepdims=True) + 1e-06)


def depthwise_rows(field, kernel):
    batch_rows, row_count, width, channels = field.shape
    framed = halo_rows(field, 3)
    framed = jnp.pad(framed, ((0, 0), (0, 0), (3, 3), (0, 0)))
    summed = jnp.zeros(field.shape, jnp.float32)
    for tap_row in range(7):
        for tap_col in range(7):
            window = framed[:, tap_row : tap_row + row_count, tap_col : tap_col + width, :].astype(
                jnp.float32
            )
            summed = summed + window * kernel[tap_row, tap_col].astype(jnp.float32)
    return summed


def local(
    section_map,
    dw_kernel,
    conv_bias,
    ln_gain,
    layer_scale,
    head_gain,
    head_weight,
    texts,
    positives,
    sources,
    numerators,
):
    batch_rows, row_count, width, channels = section_map.shape
    img_count = lax.axis_size("img")
    dp_count = lax.axis_size("dp")
    dp_at = lax.axis_index("dp")
    img_at = lax.axis_index("img")
    conved = depthwise_rows(section_map, dw_kernel) + conv_bias
    section_out = section_map.astype(jnp.float32) + layer_scale * cell_norm(conved, ln_gain)
    partial_value = jnp.sum(section_out, axis=(1, 2)) / (H * W)
    pooled = group_sum(partial_value)
    head_in = cell_norm(pooled, head_gain).astype(jnp.bfloat16)
    embed = jnp.dot(head_in, head_weight, preferred_element_type=jnp.float32)
    image_vec = unit_rows(embed).astype(jnp.bfloat16)
    text_f = texts.astype(jnp.float32)
    text_vec = unit_rows(text_f).astype(jnp.bfloat16)
    text_count = texts.shape[0]
    share = text_count // img_count
    text_share = lax.dynamic_slice_in_dim(text_vec, img_at * share, share)
    payload = jnp.concatenate([image_vec, text_share], axis=0)
    gathered = lax.all_gather(payload, "img", axis=0)
    gathered = lax.all_gather(gathered, "dp", axis=0)
    image_all = jnp.transpose(gathered[:, :, :batch_rows, :], (0, 2, 1, 3)).reshape(
        dp_count * batch_rows * img_count, -1
    )
    text_all = gathered[:, :, batch_rows:, :].reshape(dp_count * text_count, -1)
    count = text_all.shape[0]
    logits = (
        LOGIT_SCALE * jnp.dot(image_all, text_all.T, preferred_element_type=jnp.float32)
        + LOGIT_BIAS
    )
    labels = jnp.where(positives[:, None] == jnp.arange(count)[None, :], 1.0, -1.0).astype(
        jnp.float32
    )
    source_table = (sources[:, None] == jnp.arange(SOURCES)[None, :]).astype(jnp.float32)
    weights = (
        SOURCES
        * numerators[sources].astype(jnp.float32)
        / jnp.sum(numerators).astype(jnp.float32)
    )
    row_loss = jnp.sum(jax.nn.softplus(-labels * logits), axis=1)
    group_sums = jnp.sum(source_table * (weights * row_loss)[:, None], axis=0)
    pair_grad = (weights[:, None] * -labels * jax.nn.sigmoid(-labels * logits)).astype(
        jnp.bfloat16
    )
    own_rows = (dp_at * batch_rows + jnp.arange(batch_rows)) * img_count + img_at
    own_pair = jnp.take(pair_grad, own_rows, axis=0)
    image_dir = LOGIT_SCALE * jnp.dot(own_pair, text_all, preferred_element_type=jnp.float32)
    text_pair = lax.dynamic_slice_in_dim(pair_grad, dp_at * text_count, text_count, axis=1)
    text_dir = LOGIT_SCALE * lax.dot_general(
        text_pair, image_all, (((0,), (0,)), ((), ())), preferred_element_type=jnp.float32
    )
    text_back = jax.vjp(unit_rows, text_f)[1]
    text_grad = text_back(text_dir)[0]
    embed_back = jax.vjp(unit_rows, embed)[1]
    embed_grad = embed_back(image_dir)[0].astype(jnp.bfloat16)
    head_grad = jnp.dot(embed_grad, head_weight.T, preferred_element_type=jnp.float32)
    pool_back = jax.vjp(lambda values: cell_norm(values, head_gain), pooled)[1]
    own_grad = pool_back(head_grad)[0]
    norm_back = jax.vjp(lambda values: cell_norm(values, ln_gain), conved)[1]
    seeded = jnp.broadcast_to((layer_scale * own_grad)[:, None, None, :], conved.shape)
    conv_grad = norm_back(seeded)[0].astype(jnp.bfloat16)
    spread = depthwise_rows(conv_grad, dw_kernel[::-1, ::-1, :])
    grad_map = (own_grad[:, None, None, :] + spread).astype(jnp.bfloat16)
    return (grad_map, text_grad, group_sums)


def solution(mesh):
    dp_count, tile_count = mesh.devices.shape

    def run(section_map, *rest):
        rows_each = section_map.shape[1] // tile_count
        per_image = H // rows_each
        assert per_image & (per_image - 1) == 0
        split = Mesh(
            mesh.devices.reshape(dp_count, tile_count // per_image, per_image),
            ("dp", "img", "row"),
        )
        tiled = ("img", "row")
        placed = (
            P("dp", tiled, None, None),
            P(),
            P(),
            P(),
            P(),
            P(),
            P(),
            P("dp", None),
            P(),
            P(),
            P(),
        )
        return jax.shard_map(
            local,
            mesh=split,
            in_specs=placed,
            out_specs=(P("dp", tiled, None, None), P("dp", None), P()),
            check_vma=False,
        )(section_map, *rest)

    return run
```

time: 587 us -> 273 us (0.47)
  waiting for transfers between devices: 309 us -> 46.5 us
  blocking collectives: 135 us -> 74.8 us
  other arithmetic: 76 us -> 95 us
  between operations: 17.4 us -> 3.17 us
    psum x1 -> x0, waiting for transfers between devices: 304 us -> none  [local(): pooled = lax.psum(placed, 'tile').reshape(local_images, channels)]
    unnamed x1 -> x0, blocking collectives: 49.6 us -> none
    ppermute x4 -> x7, waiting for transfers between devices: 0.01 us -> 46.5 us  [the longest x2 41.5 us: halo_rows(): before = lax.ppermute(last, 'row', up)]
    psum x1 -> x0, blocking collectives: 42.7 us -> none  [local(): group_sums = lax.psum(group_part, 'dp')]
    all_gather x1 -> x2, blocking collectives: 42.9 us -> 74.8 us  [the longest x1 44.8 us: local(): gathered = lax.all_gather(gathered, 'dp', axis=0)]
    mul x3 -> x1, other arithmetic: 1.37 us -> 21.1 us  [local(): group_sums = jnp.sum(source_table * (weights * row_loss)[:, None], axis=0)]
    unnamed x4 -> x0, starting transfers between devices: 8.99 us -> none
    ppermute x4 -> x7, starting transfers between devices: 11.1 us -> 18.1 us  [the longest x2 7.28 us: halo_rows(): after = lax.ppermute(leading, 'row', down)]
  transfers between devices with their start and end apart: 9 -> 7, of which waited for: 2 -> 5; matrix products, arithmetic and copies ran while one was open for 10% -> 4% of each run, Pallas kernels for 0% -> 0%
where the time goes in v1:
time: 273 us; the launch traced here: 270 us
  other arithmetic  95 us (35%)
  blocking collectives  74.8 us (27%)
  waiting for transfers between devices  46.5 us (17%)
  local copies, waits for them, and re-layouts  20.3 us (7%)
  starting transfers between devices  18.1 us (7%)
  matrix products  12.2 us (4%)
  between operations  3.17 us (1%)
    all_gather x1, blocking collectives, local(): gathered = lax.all_gather(gathered, 'dp', axis=0)  44.8 us
    ppermute x2, waiting for transfers between devices, halo_rows(): before = lax.ppermute(last, 'row', up)  41.5 us
    all_gather x1, blocking collectives, local(): gathered = lax.all_gather(payload, 'img', axis=0)  30 us
    reduce_sum x4, other arithmetic, cell_norm(): center = values - jnp.mean(values, axis=-1, keepdims=True)  28.7 us
    convert_element_type x1, other arithmetic, local(): grad_map = (own_grad[:, None, None, :] + spread).astype(jnp.bfloat16)  25.6 us
    mul x1, other arithmetic, local(): group_sums = jnp.sum(source_table * (weights * row_loss)[:, None], axis=0)  21.1 us
    ppermute x2, starting transfers between devices, halo_rows(): after = lax.ppermute(leading, 'row', down)  7.28 us
    ppermute x3, starting transfers between devices, group_sum(): value = value + lax.ppermute(value, 'row', pairs)  6.97 us
  transfers between devices with their start and end apart: 7, of which 5 were waited for; matrix products, arithmetic and copies ran while one was open for 4% of the time, Pallas kernels for 0%

profile of v1, /device:TPU:6, one launch (start us, length us, event | category | flops | bytes accessed | tf_op | source)
XLA Modules:
  0.0 270.1 jit_solution(744760124403164039)
XLA Ops:
  0.7 3.3 %fusion.64 = (bf16[2,3,32,3072]{3,2,1,0:T(8,128)(2,1)}, bf16[2,3,32,3072]{3,2,1,0:T(8,128)(2,1)}) fusion(bf16[2,4,32,3072]{3,2,1,0:T(8,128)(2,1)} %param.11), kind=kLoop, calls=%fused_computation.216 | loop fusion | bytes 4718592 | tf_op jit(solution)/shard_map/slice | solution.py:21
  4.0 1.9 collective-permute-start
  5.9 3.6 %collective-permute-start.1 = (bf16[2,3,32,3072]{3,2,1,0:T(8,128)(2,1)}, bf16[2,3,32,3072]{3,2,1,0:T(8,128)(2,1)}, u32[]{:S(2)}, u32[]{:S(2)}) collective-permute-start(bf16[2,3,32,3072]{3,2,1,0:T(8,128)(2,1)} %get-tuple-element.18), channel_id=1, source_target_pairs={{1,0},{2,1},{3,2},{4,3},{5,4},{6,5},{7,6},{9,8},{10,9},{11,10},{12... | collective-permute-start | bytes 3538952 | tf_op jit(solution)/shard_map/ppermute | solution.py:24
  10.1 0.7 fusion.66
  10.9 0.8 slice_convert_fusion.47
  11.8 0.7 fusion.67
  12.5 0.7 multiply_reduce_fusion.2
  13.1 1.1 add_rsqrt_fusion
  14.3 20.1 %collective-permute-done = bf16[2,3,32,3072]{3,2,1,0:T(8,128)(2,1)S(1)} collective-permute-done((bf16[2,3,32,3072]{3,2,1,0:T(8,128)(2,1)}, bf16[2,3,32,3072]{3,2,1,0:T(8,128)(2,1)S(1)}, u32[]{:S(2)}, u32[]{:S(2)}) %collective-permute-start) | collective-permute-done | bytes 1179680 | tf_op jit(solution)/shard_map/ppermute | solution.py:23
  34.8 3.4 %select_maximum_fusion.2 = bf16[2,10,38,3072]{3,2,1,0:T(8,128)(2,1)S(1)} fusion(bf16[2,3,32,3072]{3,2,1,0:T(8,128)(2,1)} %collective-permute-done.1, bf16[2,4,32,3072]{3,2,1,0:T(8,128)(2,1)S(1)} %copy-done, bf16[2,3,32,3072]{3,2,1,0:T(8,128)(2,1)S(1)} %collective-permute-done), kind=kLoop, calls=%fused_computation.6 | loop fusion | flops 28016640 | bytes 8601600 | tf_op jit(solution)/shard_map/concatenate | solution.py:25
  38.3 1.5 constant_dynamic-update-slice_fusion.2
  40.2 27.6 %fusion.61 = (f32[2,4,32]{2,1,0:T(4,128)S(1)}, f32[2,4,32,3072]{3,2,1,0:T(8,128)S(1)}) fusion(f32[3072]{0:T(1024)S(1)} %copy-done.97, f32[3072]{0:T(1024)S(1)} %bitcast.115, bf16[2,10,38,3072]{3,2,1,0:T(8,128)(2,1)S(1)} %select_maximum_fusion.2, f32[3072]{0:T(1024)S(1)} %bitcast.117, f32[3072]{0:T(1024)S(1)} %bitcast.121, f32[3072]{0:T(1024)S(1)} %bitcast.123, ...), kind=kLoop, calls=%fused_computation.214 | loop fusion | flops 116391680 | bytes 80831488 | tf_op jit(solution)/shard_map/reduce_sum | solution.py:39
  68.5 1.0 fusion.27
  69.5 1.9 collective-permute-start.2
  71.4 1.1 collective-permute-done.2
  72.6 1.9 collective-permute-start.3
  75.1 3.2 %collective-permute-done.3 = f32[2,3072]{1,0:T(2,128)S(1)} collective-permute-done((f32[2,3072]{1,0:T(2,128)S(1)}, f32[2,3072]{1,0:T(2,128)S(1)}, u32[]{:S(2)}, u32[]{:S(2)}) %collective-permute-start.3) | collective-permute-done | bytes 24608 | tf_op jit(solution)/shard_map/ppermute | solution.py:33
  78.3 3.1 %collective-permute-start.4 = (f32[2,3072]{1,0:T(2,128)S(1)}, f32[2,3072]{1,0:T(2,128)S(1)}, u32[]{:S(2)}, u32[]{:S(2)}) collective-permute-start(f32[2,3072]{1,0:T(2,128)S(1)} %add.502), channel_id=1, source_target_pairs={{0,4},{1,5},{2,6},{3,7},{4,0},{5,1},{6,2},{7,3},{8,12},{9,13},{10,... | collective-permute-start | bytes 73736 | tf_op jit(solution)/shard_map/ppermute | solution.py:33
  82.0 0.6 reduce_sum.140
  83.4 0.7 collective-permute-done.4
  85.0 3.9 %multiply_reduce_fusion.6 = (f32[2]{0:T(128)S(1)}, f32[2,1024]{1,0:T(2,128)S(1)}) fusion(bf16[3072,1024]{1,0:T(8,128)(2,1)} %param.17, f32[2]{0:T(128)S(1)} %fusion.54, f32[3072]{0:T(1024)S(1)} %copy-done.92, f32[2,3072]{1,0:T(2,128)S(1)} %get-tuple-element.10, f32[2]{0:T(128)S(1)} %broadcast_multiply_fusion.5), kind=kOutput, calls=%fused_computation.147 | convolution fusion | flops 12611582 | bytes 6336536 | tf_op jit(solution)/shard_map/dot_general | solution.py:85
  89.5 30.0 %all-gather.2 = bf16[6,4,1024]{2,1,0:T(4,128)(2,1)S(1)} all-gather(bf16[1,4,1024]{2,1,0:T(4,128)(2,1)S(1)} %maximum_bitcast_fusion), channel_id=2, replica_groups=mesh['dp'=16,'img'=6,'row'=8] {'img'}, dimensions={0}, use_global_device_ids=true | all-gather | bytes 57344 | tf_op jit(solution)/shard_map/all_gather | solution.py:93
  119.5 44.8 %all-gather.1 = bf16[96,4,1024]{2,1,0:T(4,128)(2,1)S(1)} all-gather(bf16[6,4,1024]{2,1,0:T(4,128)(2,1)S(1)} %all-gather.2), channel_id=3, replica_groups=mesh['dp'=16,'img'=6,'row'=8] {'dp'}, dimensions={0}, use_global_device_ids=true | all-gather | bytes 835584 | tf_op jit(solution)/shard_map/all_gather | solution.py:94
  164.3 1.3 fusion.65
  165.6 0.9 copy.23
  166.5 1.2 reshape.524
  167.7 1.9 reshape.525
  169.6 1.4 fusion.37
  171.0 21.1 %fusion.57 = (f32[192]{0:T(256)}, f32[192]{0:T(256)S(1)}) fusion(f32[192]{0:T(256)S(1)} %get-tuple-element.108, f32[]{:T(128)S(6)} %convert_element_type.925, s32[]{:T(128)} %bitcast.31, s32[]{:T(128)} %bitcast.30, s32[]{:T(128)} %bitcast.29, s32[]{:T(128)} %bitcast.28, s32[]{:T(128)} %bitcast.27, s32[]{:T(128)} %bitcast.26, s32[]{:T(128)} %bitcast.25, ...), kind=kLoop, calls=%fused_computation.211 | loop fusion | flops 13248 | bytes 3204 | tf_op jit(solution)/shard_map/mul | solution.py:114
  192.1 1.4 multiply_convert_fusion
  193.5 1.6 copy.20
  195.1 2.1 gather_fusion
  197.3 1.3 multiply_reduce_fusion.5
  199.3 4.6 %multiply_reduce_fusion.3 = (f32[2]{0:T(128)S(1)}, f32[2,3072]{1,0:T(2,128)S(1)}) fusion(f32[2,3072]{1,0:T(2,128)} %copy-done.5, f32[2]{0:T(128)} %copy-done.98, f32[3072]{0:T(1024)} %param.16, bf16[3072,1024]{1,0:T(8,128)(2,1)} %param.17, f32[2,1024]{1,0:T(2,128)} %copy-done.89, f32[2,1024]{1,0:T(2,128)S(1)} %get-tuple-element.111, ...), kind=kOutput, calls=%fused_computation.76 | convolution fusion | flops 12617726 | bytes 6369312 | tf_op jit(solution)/shard_map/dot_general | solution.py:129
  204.2 0.7 broadcast_multiply_fusion
  205.4 0.8 fusion.30
  206.2 1.0 add_convert_fusion.1
  207.2 1.1 copy-done.2
  208.3 1.7 fusion.63
  210.0 1.9 collective-permute-start.5
  211.9 3.6 %collective-permute-start.6 = (bf16[2,3,32,3072]{3,2,1,0:T(8,128)(2,1)}, bf16[2,3,32,3072]{3,2,1,0:T(8,128)(2,1)S(1)}, u32[]{:S(2)}, u32[]{:S(2)}) collective-permute-start(bf16[2,3,32,3072]{3,2,1,0:T(8,128)(2,1)} %get-tuple-element.14), channel_id=1, source_target_pairs={{1,0},{2,1},{3,2},{4,3},{5,4},{6,5},{7,6},{9,8},{10,9},{11,10},{12... | collective-permute-start | bytes 3538952 | tf_op jit(solution)/shard_map/ppermute | solution.py:24
  215.6 0.6 select_reduce_fusion
  216.2 1.0 multiply_reduce_fusion.1
  217.2 0.6 broadcast_multiply_fusion.3
  217.9 0.7 add_add_fusion.1
  219.0 21.4 %collective-permute-done.5 = bf16[2,3,32,3072]{3,2,1,0:T(8,128)(2,1)S(1)} collective-permute-done((bf16[2,3,32,3072]{3,2,1,0:T(8,128)(2,1)}, bf16[2,3,32,3072]{3,2,1,0:T(8,128)(2,1)S(1)}, u32[]{:S(2)}, u32[]{:S(2)}) %collective-permute-start.5) | collective-permute-done | bytes 1179680 | tf_op jit(solution)/shard_map/ppermute | solution.py:23
  240.4 3.5 %select_maximum_fusion = bf16[2,10,38,3072]{3,2,1,0:T(8,128)(2,1)S(1)} fusion(bf16[2,3,32,3072]{3,2,1,0:T(8,128)(2,1)S(1)} %collective-permute-done.6, bf16[2,4,32,3072]{3,2,1,0:T(8,128)(2,1)} %copy-done.2, bf16[2,3,32,3072]{3,2,1,0:T(8,128)(2,1)S(1)} %collective-permute-done.5), kind=kLoop, calls=%fused_computation.4 | loop fusion | flops 28016640 | bytes 8601600 | tf_op jit(solution)/shard_map/concatenate | solution.py:25
  244.3 25.6 %add_convert_fusion = bf16[2,4,32,3072]{3,2,1,0:T(8,128)(2,1)} fusion(bf16[2,4,32,3072]{3,2,1,0:T(8,128)(2,1)S(1)} %copy-done.3, bf16[2,3,32,3072]{3,2,1,0:T(8,128)(2,1)S(1)} %collective-permute-done.6, bf16[2,3,32,3072]{3,2,1,0:T(8,128)(2,1)S(1)} %collective-permute-done.5, bf16[2,10,38,3072]{3,2,1,0:T(8,128)(2,1)S(1)} %select_maximum_fusion, ...), kind=kLoop, calls=%fused_computation.46 | loop fusion | flops 121110528 | bytes 72192000 | tf_op jit(solution)/shard_map/convert_element_type | solution.py:136
  (246 shorter events, 5.9 us)
Async XLA Ops:
  0.6 33.8 %copy-start = (bf16[2,4,32,3072]{3,2,1,0:T(8,128)(2,1)S(1)}, bf16[2,4,32,3072]{3,2,1,0:T(8,128)(2,1)}, u32[]{:S(2)}) copy-start(bf16[2,4,32,3072]{3,2,1,0:T(8,128)(2,1)} %param.11) | copy-start | bytes 4718596
  4.0 30.4 %collective-permute-start = (bf16[2,3,32,3072]{3,2,1,0:T(8,128)(2,1)}, bf16[2,3,32,3072]{3,2,1,0:T(8,128)(2,1)S(1)}, u32[]{:S(2)}, u32[]{:S(2)}) collective-permute-start(bf16[2,3,32,3072]{3,2,1,0:T(8,128)(2,1)} %get-tuple-element.17), channel_id=1, source_target_pairs={{0,1},{1,2},{2,3},{3,4},{4,5},{5,6},{6,7},{8,9},{9,10},{10,11},{11... | collective-permute-start | bytes 3538952 | tf_op jit(solution)/shard_map/ppermute | solution.py:23
  5.9 28.9 %collective-permute-start.1 = (bf16[2,3,32,3072]{3,2,1,0:T(8,128)(2,1)}, bf16[2,3,32,3072]{3,2,1,0:T(8,128)(2,1)}, u32[]{:S(2)}, u32[]{:S(2)}) collective-permute-start(bf16[2,3,32,3072]{3,2,1,0:T(8,128)(2,1)} %get-tuple-element.18), channel_id=1, source_target_pairs={{1,0},{2,1},{3,2},{4,3},{5,4},{6,5},{7,6},{9,8},{10,9},{11,10},{12... | collective-permute-start | bytes 3538952 | tf_op jit(solution)/shard_map/ppermute | solution.py:24
  9.7 30.0 %copy-start.33 = (f32[1,1,3072]{2,1,0:T(1,128)}, f32[1,1,3072]{2,1,0:T(1,128)S(1)}, u32[]{:S(2)}) copy-start(f32[1,1,3072]{2,1,0:T(1,128)S(1)} %get-tuple-element.21) | copy-start | bytes 36868
  9.7 30.0 %copy-start.35 = (f32[1,1,3072]{2,1,0:T(1,128)}, f32[1,1,3072]{2,1,0:T(1,128)S(1)}, u32[]{:S(2)}) copy-start(f32[1,1,3072]{2,1,0:T(1,128)S(1)} %get-tuple-element.22) | copy-start | bytes 36868
  9.8 30.0 %copy-start.37 = (f32[1,1,3072]{2,1,0:T(1,128)}, f32[1,1,3072]{2,1,0:T(1,128)S(1)}, u32[]{:S(2)}) copy-start(f32[1,1,3072]{2,1,0:T(1,128)S(1)} %get-tuple-element.23) | copy-start | bytes 36868
  9.8 30.0 %copy-start.39 = (f32[1,1,3072]{2,1,0:T(1,128)}, f32[1,1,3072]{2,1,0:T(1,128)S(1)}, u32[]{:S(2)}) copy-start(f32[1,1,3072]{2,1,0:T(1,128)S(1)} %get-tuple-element.24) | copy-start | bytes 36868
  9.8 30.0 %copy-start.41 = (f32[1,1,3072]{2,1,0:T(1,128)}, f32[1,1,3072]{2,1,0:T(1,128)S(1)}, u32[]{:S(2)}) copy-start(f32[1,1,3072]{2,1,0:T(1,128)S(1)} %get-tuple-element.25) | copy-start | bytes 36868
  9.8 30.0 %copy-start.43 = (f32[1,1,3072]{2,1,0:T(1,128)}, f32[1,1,3072]{2,1,0:T(1,128)S(1)}, u32[]{:S(2)}) copy-start(f32[1,1,3072]{2,1,0:T(1,128)S(1)} %get-tuple-element.26) | copy-start | bytes 36868
  9.8 30.0 %copy-start.45 = (f32[1,1,3072]{2,1,0:T(1,128)}, f32[1,1,3072]{2,1,0:T(1,128)S(1)}, u32[]{:S(2)}) copy-start(f32[1,1,3072]{2,1,0:T(1,128)S(1)} %get-tuple-element.27) | copy-start | bytes 36868
  9.8 30.0 %copy-start.47 = (f32[1,1,3072]{2,1,0:T(1,128)}, f32[1,1,3072]{2,1,0:T(1,128)S(1)}, u32[]{:S(2)}) copy-start(f32[1,1,3072]{2,1,0:T(1,128)S(1)} %get-tuple-element.28) | copy-start | bytes 36868
  9.8 30.0 %copy-start.49 = (f32[1,1,3072]{2,1,0:T(1,128)}, f32[1,1,3072]{2,1,0:T(1,128)S(1)}, u32[]{:S(2)}) copy-start(f32[1,1,3072]{2,1,0:T(1,128)S(1)} %get-tuple-element.29) | copy-start | bytes 36868
  9.8 30.0 %copy-start.51 = (f32[1,1,3072]{2,1,0:T(1,128)}, f32[1,1,3072]{2,1,0:T(1,128)S(1)}, u32[]{:S(2)}) copy-start(f32[1,1,3072]{2,1,0:T(1,128)S(1)} %get-tuple-element.30) | copy-start | bytes 36868
  9.8 30.0 %copy-start.53 = (f32[1,1,3072]{2,1,0:T(1,128)}, f32[1,1,3072]{2,1,0:T(1,128)S(1)}, u32[]{:S(2)}) copy-start(f32[1,1,3072]{2,1,0:T(1,128)S(1)} %get-tuple-element.31) | copy-start | bytes 36868
  9.8 30.0 %copy-start.55 = (f32[1,1,3072]{2,1,0:T(1,128)}, f32[1,1,3072]{2,1,0:T(1,128)S(1)}, u32[]{:S(2)}) copy-start(f32[1,1,3072]{2,1,0:T(1,128)S(1)} %get-tuple-element.32) | copy-start | bytes 36868
  9.9 30.0 %copy-start.57 = (f32[1,1,3072]{2,1,0:T(1,128)}, f32[1,1,3072]{2,1,0:T(1,128)S(1)}, u32[]{:S(2)}) copy-start(f32[1,1,3072]{2,1,0:T(1,128)S(1)} %get-tuple-element.33) | copy-start | bytes 36868
  9.9 30.0 %copy-start.59 = (f32[1,1,3072]{2,1,0:T(1,128)}, f32[1,1,3072]{2,1,0:T(1,128)S(1)}, u32[]{:S(2)}) copy-start(f32[1,1,3072]{2,1,0:T(1,128)S(1)} %get-tuple-element.34) | copy-start | bytes 36868
  9.9 30.0 %copy-start.61 = (f32[1,1,3072]{2,1,0:T(1,128)}, f32[1,1,3072]{2,1,0:T(1,128)S(1)}, u32[]{:S(2)}) copy-start(f32[1,1,3072]{2,1,0:T(1,128)S(1)} %get-tuple-element.35) | copy-start | bytes 36868
  9.9 30.0 %copy-start.63 = (f32[1,1,3072]{2,1,0:T(1,128)}, f32[1,1,3072]{2,1,0:T(1,128)S(1)}, u32[]{:S(2)}) copy-start(f32[1,1,3072]{2,1,0:T(1,128)S(1)} %get-tuple-element.36) | copy-start | bytes 36868
  9.9 30.0 %copy-start.65 = (f32[1,1,3072]{2,1,0:T(1,128)}, f32[1,1,3072]{2,1,0:T(1,128)S(1)}, u32[]{:S(2)}) copy-start(f32[1,1,3072]{2,1,0:T(1,128)S(1)} %get-tuple-element.37) | copy-start | bytes 36868
  9.9 30.0 %copy-start.67 = (f32[1,1,3072]{2,1,0:T(1,128)}, f32[1,1,3072]{2,1,0:T(1,128)S(1)}, u32[]{:S(2)}) copy-start(f32[1,1,3072]{2,1,0:T(1,128)S(1)} %get-tuple-element.38) | copy-start | bytes 36868
  9.9 30.0 %copy-start.69 = (f32[1,1,3072]{2,1,0:T(1,128)}, f32[1,1,3072]{2,1,0:T(1,128)S(1)}, u32[]{:S(2)}) copy-start(f32[1,1,3072]{2,1,0:T(1,128)S(1)} %get-tuple-element.39) | copy-start | bytes 36868
  10.0 29.9 %copy-start.11 = (f32[1,1,3072]{2,1,0:T(1,128)}, f32[1,1,3072]{2,1,0:T(1,128)S(1)}, u32[]{:S(2)}) copy-start(f32[1,1,3072]{2,1,0:T(1,128)S(1)} %get-tuple-element.59) | copy-start | bytes 36868
  10.0 29.9 %copy-start.13 = (f32[1,1,3072]{2,1,0:T(1,128)}, f32[1,1,3072]{2,1,0:T(1,128)S(1)}, u32[]{:S(2)}) copy-start(f32[1,1,3072]{2,1,0:T(1,128)S(1)} %get-tuple-element.60) | copy-start | bytes 36868
  10.1 29.9 %copy-start.15 = (f32[1,1,3072]{2,1,0:T(1,128)}, f32[1,1,3072]{2,1,0:T(1,128)S(1)}, u32[]{:S(2)}) copy-start(f32[1,1,3072]{2,1,0:T(1,128)S(1)} %get-tuple-element.61) | copy-start | bytes 36868
  10.1 29.9 %copy-start.17 = (f32[1,1,3072]{2,1,0:T(1,128)}, f32[1,1,3072]{2,1,0:T(1,128)S(1)}, u32[]{:S(2)}) copy-start(f32[1,1,3072]{2,1,0:T(1,128)S(1)} %get-tuple-element.62) | copy-start | bytes 36868
  10.1 29.9 %copy-start.19 = (f32[1,1,3072]{2,1,0:T(1,128)}, f32[1,1,3072]{2,1,0:T(1,128)S(1)}, u32[]{:S(2)}) copy-start(f32[1,1,3072]{2,1,0:T(1,128)S(1)} %get-tuple-element.63) | copy-start | bytes 36868
  10.1 29.9 %copy-start.21 = (f32[1,1,3072]{2,1,0:T(1,128)}, f32[1,1,3072]{2,1,0:T(1,128)S(1)}, u32[]{:S(2)}) copy-start(f32[1,1,3072]{2,1,0:T(1,128)S(1)} %get-tuple-element.64) | copy-start | bytes 36868
  10.1 29.9 %copy-start.23 = (f32[1,1,3072]{2,1,0:T(1,128)}, f32[1,1,3072]{2,1,0:T(1,128)S(1)}, u32[]{:S(2)}) copy-start(f32[1,1,3072]{2,1,0:T(1,128)S(1)} %get-tuple-element.65) | copy-start | bytes 36868
  10.1 29.9 %copy-start.25 = (f32[1,1,3072]{2,1,0:T(1,128)}, f32[1,1,3072]{2,1,0:T(1,128)S(1)}, u32[]{:S(2)}) copy-start(f32[1,1,3072]{2,1,0:T(1,128)S(1)} %get-tuple-element.66) | copy-start | bytes 36868
  10.1 29.9 %copy-start.27 = (f32[1,1,3072]{2,1,0:T(1,128)}, f32[1,1,3072]{2,1,0:T(1,128)S(1)}, u32[]{:S(2)}) copy-start(f32[1,1,3072]{2,1,0:T(1,128)S(1)} %get-tuple-element.67) | copy-start | bytes 36868
  10.1 29.9 %copy-start.29 = (f32[1,1,3072]{2,1,0:T(1,128)}, f32[1,1,3072]{2,1,0:T(1,128)S(1)}, u32[]{:S(2)}) copy-start(f32[1,1,3072]{2,1,0:T(1,128)S(1)} %get-tuple-element.68) | copy-start | bytes 36868
  10.1 29.9 %copy-start.31 = (f32[1,1,3072]{2,1,0:T(1,128)}, f32[1,1,3072]{2,1,0:T(1,128)S(1)}, u32[]{:S(2)}) copy-start(f32[1,1,3072]{2,1,0:T(1,128)S(1)} %get-tuple-element.69) | copy-start | bytes 36868
  11.7 28.4 %copy-start.71 = (f32[1,1,3072]{2,1,0:T(1,128)}, f32[1,1,3072]{2,1,0:T(1,128)S(1)}, u32[]{:S(2)}) copy-start(f32[1,1,3072]{2,1,0:T(1,128)S(1)} %get-tuple-element.40) | copy-start | bytes 36868
  11.7 28.4 %copy-start.73 = (f32[1,1,3072]{2,1,0:T(1,128)}, f32[1,1,3072]{2,1,0:T(1,128)S(1)}, u32[]{:S(2)}) copy-start(f32[1,1,3072]{2,1,0:T(1,128)S(1)} %get-tuple-element.41) | copy-start | bytes 36868
  11.7 28.4 %copy-start.75 = (f32[1,1,3072]{2,1,0:T(1,128)}, f32[1,1,3072]{2,1,0:T(1,128)S(1)}, u32[]{:S(2)}) copy-start(f32[1,1,3072]{2,1,0:T(1,128)S(1)} %get-tuple-element.42) | copy-start | bytes 36868
  11.7 28.4 %copy-start.77 = (f32[1,1,3072]{2,1,0:T(1,128)}, f32[1,1,3072]{2,1,0:T(1,128)S(1)}, u32[]{:S(2)}) copy-start(f32[1,1,3072]{2,1,0:T(1,128)S(1)} %get-tuple-element.43) | copy-start | bytes 36868
  11.7 28.4 %copy-start.79 = (f32[1,1,3072]{2,1,0:T(1,128)}, f32[1,1,3072]{2,1,0:T(1,128)S(1)}, u32[]{:S(2)}) copy-start(f32[1,1,3072]{2,1,0:T(1,128)S(1)} %get-tuple-element.44) | copy-start | bytes 36868
  11.7 28.4 %copy-start.81 = (f32[1,1,3072]{2,1,0:T(1,128)}, f32[1,1,3072]{2,1,0:T(1,128)S(1)}, u32[]{:S(2)}) copy-start(f32[1,1,3072]{2,1,0:T(1,128)S(1)} %get-tuple-element.45) | copy-start | bytes 36868
  11.7 28.4 %copy-start.83 = (f32[1,1,3072]{2,1,0:T(1,128)}, f32[1,1,3072]{2,1,0:T(1,128)S(1)}, u32[]{:S(2)}) copy-start(f32[1,1,3072]{2,1,0:T(1,128)S(1)} %get-tuple-element.46) | copy-start | bytes 36868
  11.7 28.4 %copy-start.85 = (f32[1,1,3072]{2,1,0:T(1,128)}, f32[1,1,3072]{2,1,0:T(1,128)S(1)}, u32[]{:S(2)}) copy-start(f32[1,1,3072]{2,1,0:T(1,128)S(1)} %get-tuple-element.47) | copy-start | bytes 36868
  11.7 28.4 %copy-start.87 = (f32[1,1,3072]{2,1,0:T(1,128)}, f32[1,1,3072]{2,1,0:T(1,128)S(1)}, u32[]{:S(2)}) copy-start(f32[1,1,3072]{2,1,0:T(1,128)S(1)} %get-tuple-element.48) | copy-start | bytes 36868
  69.5 3.1 %collective-permute-start.2 = (f32[2,3072]{1,0:T(2,128)S(1)}, f32[2,3072]{1,0:T(2,128)S(1)}, u32[]{:S(2)}, u32[]{:S(2)}) collective-permute-start(f32[2,3072]{1,0:T(2,128)S(1)} %broadcast_multiply_fusion.1), channel_id=1, source_target_pairs={{0,1},{1,0},{2,3},{3,2},{4,5},{5,4},{6,7},{7,6},{8,9},{9,8},{10,11... | collective-permute-start | bytes 73736 | tf_op jit(solution)/shard_map/ppermute | solution.py:33
  72.6 5.7 %collective-permute-start.3 = (f32[2,3072]{1,0:T(2,128)S(1)}, f32[2,3072]{1,0:T(2,128)S(1)}, u32[]{:S(2)}, u32[]{:S(2)}) collective-permute-start(f32[2,3072]{1,0:T(2,128)S(1)} %fusion.56), channel_id=1, source_target_pairs={{0,2},{1,3},{2,0},{3,1},{4,6},{5,7},{6,4},{7,5},{8,10},{9,11},{10,... | collective-permute-start | bytes 73736 | tf_op jit(solution)/shard_map/ppermute | solution.py:33
  78.3 5.7 %collective-permute-start.4 = (f32[2,3072]{1,0:T(2,128)S(1)}, f32[2,3072]{1,0:T(2,128)S(1)}, u32[]{:S(2)}, u32[]{:S(2)}) collective-permute-start(f32[2,3072]{1,0:T(2,128)S(1)} %add.502), channel_id=1, source_target_pairs={{0,4},{1,5},{2,6},{3,7},{4,0},{5,1},{6,2},{7,3},{8,12},{9,13},{10,... | collective-permute-start | bytes 73736 | tf_op jit(solution)/shard_map/ppermute | solution.py:33
  88.9 77.6 %copy-start.89 = (f32[2,1024]{1,0:T(2,128)}, f32[2,1024]{1,0:T(2,128)S(1)}, u32[]{:S(2)}) copy-start(f32[2,1024]{1,0:T(2,128)S(1)} %get-tuple-element.107) | copy-start | bytes 24580
  210.0 30.4 %collective-permute-start.5 = (bf16[2,3,32,3072]{3,2,1,0:T(8,128)(2,1)}, bf16[2,3,32,3072]{3,2,1,0:T(8,128)(2,1)S(1)}, u32[]{:S(2)}, u32[]{:S(2)}) collective-permute-start(bf16[2,3,32,3072]{3,2,1,0:T(8,128)(2,1)} %get-tuple-element.13), channel_id=1, source_target_pairs={{0,1},{1,2},{2,3},{3,4},{4,5},{5,6},{6,7},{8,9},{9,10},{10,11},{11... | collective-permute-start | bytes 3538952 | tf_op jit(solution)/shard_map/ppermute | solution.py:23
  211.9 28.4 %collective-permute-start.6 = (bf16[2,3,32,3072]{3,2,1,0:T(8,128)(2,1)}, bf16[2,3,32,3072]{3,2,1,0:T(8,128)(2,1)S(1)}, u32[]{:S(2)}, u32[]{:S(2)}) collective-permute-start(bf16[2,3,32,3072]{3,2,1,0:T(8,128)(2,1)} %get-tuple-element.14), channel_id=1, source_target_pairs={{1,0},{2,1},{3,2},{4,3},{5,4},{6,5},{7,6},{9,8},{10,9},{11,10},{12... | collective-permute-start | bytes 3538952 | tf_op jit(solution)/shard_map/ppermute | solution.py:24
  (67 other events, 1163.0 us)

commit v2 on v1

--- a/solution.py
+++ b/solution.py
@@ -33,6 +33,36 @@
         value = value + lax.ppermute(value, "row", pairs)
         step *= 2
     return value
+
+
+def gather_stages(value, axis, radices):
+    place = 1
+    devices = lax.axis_size(axis)
+    at = lax.axis_index(axis)
+    for radix in radices:
+        digit = (at // place) % radix
+        got = [value]
+        for shift in range(1, radix):
+            pairs = []
+            for src in range(devices):
+                d = (src // place) % radix
+                pairs.append((src, src + ((d + shift) % radix - d) * place))
+            got.append(lax.ppermute(value, axis, pairs))
+        stacked = jnp.stack(got)
+        order = (digit - jnp.arange(radix)) % radix
+        value = jnp.take(stacked, order, axis=0)
+        place *= radix
+    return value.reshape((devices,) + value.shape[len(radices) :])
+
+
+def radix_split(count):
+    parts = []
+    for radix in (4, 3, 2):
+        while count % radix == 0 and count > 1:
+            parts.append(radix)
+            count //= radix
+    assert count == 1
+    return parts
 
 
 def cell_norm(values, gain):
@@ -90,8 +120,8 @@
     share = text_count // img_count
     text_share = lax.dynamic_slice_in_dim(text_vec, img_at * share, share)
     payload = jnp.concatenate([image_vec, text_share], axis=0)
-    gathered = lax.all_gather(payload, "img", axis=0)
-    gathered = lax.all_gather(gathered, "dp", axis=0)
+    gathered = gather_stages(payload, "img", radix_split(img_count))
+    gathered = gather_stages(gathered, "dp", radix_split(dp_count))
     image_all = jnp.transpose(gathered[:, :, :batch_rows, :], (0, 2, 1, 3)).reshape(
         dp_count * batch_rows * img_count, -1
     )
@@ -110,7 +140,7 @@
         * numerators[sources].astype(jnp.float32)
         / jnp.sum(numerators).astype(jnp.float32)
     )
-    row_loss = jnp.sum(jax.nn.softplus(-labels * logits), axis=1)
+    row_loss = lax.optimization_barrier(jnp.sum(jax.nn.softplus(-labels * logits), axis=1))
     group_sums = jnp.sum(source_table * (weights * row_loss)[:, None], axis=0)
     pair_grad = (weights[:, None] * -labels * jax.nn.sigmoid(-labels * logits)).astype(
         jnp.bfloat16

time: 273 us -> 276 us (1.011)
  the two profiles are of different devices: /device:TPU:6 before, /device:TPU:10 now
where the time goes in v2:
time: 276 us; the launch traced here: 274 us
  other arithmetic  104 us (38%)
  starting transfers between devices  69.9 us (25%)
  waiting for transfers between devices  58.2 us (21%)
  local copies, waits for them, and re-layouts  26.8 us (10%)
  matrix products  12.2 us (4%)
  between operations  3.44 us (1%)
    ppermute x9, starting transfers between devices, gather_stages(): got.append(lax.ppermute(value, axis, pairs))  52.2 us
    ppermute x2, waiting for transfers between devices, halo_rows(): before = lax.ppermute(last, 'row', up)  39 us
    reduce_sum x4, other arithmetic, cell_norm(): center = values - jnp.mean(values, axis=-1, keepdims=True)  28.7 us
    convert_element_type x1, other arithmetic, local(): grad_map = (own_grad[:, None, None, :] + spread).astype(jnp.bfloat16)  25.6 us
    mul x1, other arithmetic, local(): group_sums = jnp.sum(source_table * (weights * row_loss)[:, None], axis=0)  21.3 us
    ppermute x9, waiting for transfers between devices, gather_stages(): got.append(lax.ppermute(value, axis, pairs))  13.1 us
    ppermute x2, starting transfers between devices, halo_rows(): after = lax.ppermute(leading, 'row', down)  7.28 us
    concatenate x2, other arithmetic, halo_rows(): return jnp.concatenate([before, value, after], axis=1)  6.92 us
  transfers between devices with their start and end apart: 16, of which 8 were waited for; matrix products, arithmetic and copies ran while one was open for 5% of the time, Pallas kernels for 0%

profile of v2, /device:TPU:10, one launch (start us, length us, event | category | flops | bytes accessed | tf_op | source)
XLA Modules:
  0.0 274.2 jit_solution(6181400042565668718)
XLA Ops:
  0.7 3.3 %fusion.75 = (bf16[2,3,32,3072]{3,2,1,0:T(8,128)(2,1)}, bf16[2,3,32,3072]{3,2,1,0:T(8,128)(2,1)}) fusion(bf16[2,4,32,3072]{3,2,1,0:T(8,128)(2,1)} %param.11), kind=kLoop, calls=%fused_computation.278 | loop fusion | bytes 4718592 | tf_op jit(solution)/shard_map/slice | solution.py:21
  4.0 1.9 collective-permute-start
  5.9 3.6 %collective-permute-start.1 = (bf16[2,3,32,3072]{3,2,1,0:T(8,128)(2,1)}, bf16[2,3,32,3072]{3,2,1,0:T(8,128)(2,1)}, u32[]{:S(2)}, u32[]{:S(2)}) collective-permute-start(bf16[2,3,32,3072]{3,2,1,0:T(8,128)(2,1)} %get-tuple-element.18), channel_id=1, source_target_pairs={{1,0},{2,1},{3,2},{4,3},{5,4},{6,5},{7,6},{9,8},{10,9},{11,10},{12... | collective-permute-start | bytes 3538952 | tf_op jit(solution)/shard_map/ppermute | solution.py:24
  15.7 1.1 add_rsqrt_fusion
  16.8 17.6 %collective-permute-done = bf16[2,3,32,3072]{3,2,1,0:T(8,128)(2,1)S(1)} collective-permute-done((bf16[2,3,32,3072]{3,2,1,0:T(8,128)(2,1)}, bf16[2,3,32,3072]{3,2,1,0:T(8,128)(2,1)S(1)}, u32[]{:S(2)}, u32[]{:S(2)}) %collective-permute-start) | collective-permute-done | bytes 1179680 | tf_op jit(solution)/shard_map/ppermute | solution.py:23
  34.9 3.4 %select_maximum_fusion.2 = bf16[2,10,38,3072]{3,2,1,0:T(8,128)(2,1)S(1)} fusion(bf16[2,3,32,3072]{3,2,1,0:T(8,128)(2,1)} %collective-permute-done.1, bf16[2,4,32,3072]{3,2,1,0:T(8,128)(2,1)S(1)} %copy-done, bf16[2,3,32,3072]{3,2,1,0:T(8,128)(2,1)S(1)} %collective-permute-done), kind=kLoop, calls=%fused_computation.10 | loop fusion | flops 28016640 | bytes 8601600 | tf_op jit(solution)/shard_map/concatenate | solution.py:25
  38.3 1.5 constant_dynamic-update-slice_fusion.2
  40.2 27.6 %fusion.72 = (f32[2,4,32]{2,1,0:T(4,128)S(1)}, f32[2,4,32,3072]{3,2,1,0:T(8,128)S(1)}) fusion(f32[3072]{0:T(1024)S(1)} %copy-done.97, f32[3072]{0:T(1024)S(1)} %bitcast.143, bf16[2,10,38,3072]{3,2,1,0:T(8,128)(2,1)S(1)} %select_maximum_fusion.2, f32[3072]{0:T(1024)S(1)} %bitcast.145, f32[3072]{0:T(1024)S(1)} %bitcast.149, f32[3072]{0:T(1024)S(1)} %bitcast.151, ...), kind=kLoop, calls=%fused_computation.276 | loop fusion | flops 116391680 | bytes 80831488 | tf_op jit(solution)/shard_map/reduce_sum | solution.py:69
  69.5 1.9 collective-permute-start.2
  72.6 1.9 collective-permute-start.3
  75.1 3.2 %collective-permute-done.3 = f32[2,3072]{1,0:T(2,128)S(1)} collective-permute-done((f32[2,3072]{1,0:T(2,128)S(1)}, f32[2,3072]{1,0:T(2,128)S(1)}, u32[]{:S(2)}, u32[]{:S(2)}) %collective-permute-start.3) | collective-permute-done | bytes 24608 | tf_op jit(solution)/shard_map/ppermute | solution.py:33
  78.3 2.8 %collective-permute-start.4 = (f32[2,3072]{1,0:T(2,128)S(1)}, f32[2,3072]{1,0:T(2,128)S(1)}, u32[]{:S(2)}, u32[]{:S(2)}) collective-permute-start(f32[2,3072]{1,0:T(2,128)S(1)} %add.657), channel_id=1, source_target_pairs={{0,4},{1,5},{2,6},{3,7},{4,0},{5,1},{6,2},{7,3},{8,12},{9,13},{10,... | collective-permute-start | bytes 73736 | tf_op jit(solution)/shard_map/ppermute | solution.py:33
  81.8 2.3 collective-permute-done.4
  85.0 3.9 %multiply_reduce_fusion.6 = (f32[2]{0:T(128)S(1)}, f32[2,1024]{1,0:T(2,128)S(1)}) fusion(bf16[3072,1024]{1,0:T(8,128)(2,1)} %param.17, f32[2]{0:T(128)S(1)} %fusion.64, f32[3072]{0:T(1024)S(1)} %copy-done.92, f32[2,3072]{1,0:T(2,128)S(1)} %get-tuple-element.10, f32[2]{0:T(128)S(1)} %broadcast_multiply_fusion.5), kind=kOutput, calls=%fused_computation.162 | convolution fusion | flops 12611582 | bytes 6336536 | tf_op jit(solution)/shard_map/dot_general | solution.py:115
  89.6 6.1 %collective-permute-start.5 = (bf16[4,1024]{1,0:T(4,128)(2,1)S(1)}, bf16[4,1024]{1,0:T(4,128)(2,1)S(1)}, u32[]{:S(2)}, u32[]{:S(2)}) collective-permute-start(bf16[4,1024]{1,0:T(4,128)(2,1)S(1)} %get-tuple-element.71), channel_id=1, source_target_pairs={{0,8},{8,16},{16,0},{24,32},{32,40},{40,24},{1,9},{9,17},{17,1},{2... | collective-permute-start | bytes 24584 | tf_op jit(solution)/shard_map/ppermute | solution.py:50
  95.7 6.7 %collective-permute-start.6 = (bf16[4,1024]{1,0:T(4,128)(2,1)S(1)}, bf16[4,1024]{1,0:T(4,128)(2,1)S(1)}, u32[]{:S(2)}, u32[]{:S(2)}) collective-permute-start(bf16[4,1024]{1,0:T(4,128)(2,1)S(1)} %get-tuple-element.71), channel_id=1, source_target_pairs={{0,16},{8,0},{16,8},{24,40},{32,24},{40,32},{1,17},{9,1},{17,9},{2... | collective-permute-start | bytes 24584 | tf_op jit(solution)/shard_map/ppermute | solution.py:50
  105.5 12.6 %collective-permute-start.7 = (bf16[3,4,1024]{2,1,0:T(4,128)(2,1)S(1)}, bf16[3,4,1024]{2,1,0:T(4,128)(2,1)S(1)}, u32[]{:S(2)}, u32[]{:S(2)}) collective-permute-start(bf16[3,4,1024]{2,1,0:T(4,128)(2,1)S(1)} %broadcast_select_fusion.1), channel_id=1, source_target_pairs={{0,24},{8,32},{16,40},{24,0},{32,8},{40,16},{1,25},{9,33},{17,41},... | collective-permute-start | bytes 73736 | tf_op jit(solution)/shard_map/ppermute | solution.py:50
  118.2 1.7 collective-permute-done.7
  120.7 3.5 %collective-permute-start.8 = (bf16[6,4,1024]{2,1,0:T(4,128)(2,1)S(1)}, bf16[6,4,1024]{2,1,0:T(4,128)(2,1)S(1)}, u32[]{:S(2)}, u32[]{:S(2)}) collective-permute-start(bf16[6,4,1024]{2,1,0:T(4,128)(2,1)S(1)} %bitcast_select_fusion.2), channel_id=1, source_target_pairs={{0,48},{48,96},{96,144},{144,0},{192,240},{240,288},{288,336},{336... | collective-permute-start | bytes 147464 | tf_op jit(solution)/shard_map/ppermute | solution.py:50
  124.2 3.1 %collective-permute-start.9 = (bf16[6,4,1024]{2,1,0:T(4,128)(2,1)S(1)}, bf16[6,4,1024]{2,1,0:T(4,128)(2,1)S(1)}, u32[]{:S(2)}, u32[]{:S(2)}) collective-permute-start(bf16[6,4,1024]{2,1,0:T(4,128)(2,1)S(1)} %bitcast_select_fusion.2), channel_id=1, source_target_pairs={{0,96},{48,144},{96,0},{144,48},{192,288},{240,336},{288,192},{336... | collective-permute-start | bytes 147464 | tf_op jit(solution)/shard_map/ppermute | solution.py:50
  127.4 3.7 %collective-permute-start.10 = (bf16[6,4,1024]{2,1,0:T(4,128)(2,1)S(1)}, bf16[6,4,1024]{2,1,0:T(4,128)(2,1)S(1)}, u32[]{:S(2)}, u32[]{:S(2)}) collective-permute-start(bf16[6,4,1024]{2,1,0:T(4,128)(2,1)S(1)} %bitcast_select_fusion.2), channel_id=1, source_target_pairs={{0,144},{48,0},{96,48},{144,96},{192,336},{240,192},{288,240},{336... | collective-permute-start | bytes 147464 | tf_op jit(solution)/shard_map/ppermute | solution.py:50
  131.2 2.1 collective-permute-done.10
  135.2 7.7 %collective-permute-start.11 = (bf16[4,6,4,1024]{3,2,1,0:T(4,128)(2,1)S(1)}, bf16[4,6,4,1024]{3,2,1,0:T(4,128)(2,1)S(1)}, u32[]{:S(2)}, u32[]{:S(2)}) collective-permute-start(bf16[4,6,4,1024]{3,2,1,0:T(4,128)(2,1)S(1)} %broadcast_select_fusion), channel_id=1, source_target_pairs={{0,192},{48,240},{96,288},{144,336},{192,384},{240,432},{288,480},... | collective-permute-start | bytes 589832 | tf_op jit(solution)/shard_map/ppermute | solution.py:50
  143.0 4.0 %collective-permute-start.12 = (bf16[4,6,4,1024]{3,2,1,0:T(4,128)(2,1)S(1)}, bf16[4,6,4,1024]{3,2,1,0:T(4,128)(2,1)S(1)}, u32[]{:S(2)}, u32[]{:S(2)}) collective-permute-start(bf16[4,6,4,1024]{3,2,1,0:T(4,128)(2,1)S(1)} %broadcast_select_fusion), channel_id=1, source_target_pairs={{0,384},{48,432},{96,480},{144,528},{192,576},{240,624},{288,672},... | collective-permute-start | bytes 589832 | tf_op jit(solution)/shard_map/ppermute | solution.py:50
  147.0 4.6 %collective-permute-start.13 = (bf16[4,6,4,1024]{3,2,1,0:T(4,128)(2,1)S(1)}, bf16[4,6,4,1024]{3,2,1,0:T(4,128)(2,1)S(1)}, u32[]{:S(2)}, u32[]{:S(2)}) collective-permute-start(bf16[4,6,4,1024]{3,2,1,0:T(4,128)(2,1)S(1)} %broadcast_select_fusion), channel_id=1, source_target_pairs={{0,576},{48,624},{96,672},{144,720},{192,0},{240,48},{288,96},{336... | collective-permute-start | bytes 589832 | tf_op jit(solution)/shard_map/ppermute | solution.py:50
  152.4 9.3 %collective-permute-done.13 = bf16[4,6,4,1024]{3,2,1,0:T(4,128)(2,1)S(1)} collective-permute-done((bf16[4,6,4,1024]{3,2,1,0:T(4,128)(2,1)S(1)}, bf16[4,6,4,1024]{3,2,1,0:T(4,128)(2,1)S(1)}, u32[]{:S(2)}, u32[]{:S(2)}) %collective-permute-start.13) | collective-permute-done | bytes 196640 | tf_op jit(solution)/shard_map/ppermute | solution.py:50
  161.7 1.6 pad_maximum_fusion.2
  163.3 3.3 %gather_fusion.3 = bf16[4,4,6,4,1024]{4,3,2,1,0:T(4,128)(2,1)} fusion(bf16[4,4,6,4,1024]{4,3,2,1,0:T(4,128)(2,1)} %pad_maximum_fusion.2, s32[1024]{0:T(1024)} %pad_clamp_fusion.1), kind=kCustom, calls=%fused_computation.3 | custom fusion | bytes 1572880 | tf_op jit(solution)/shard_map/jit(_take)/gather | solution.py:53
  166.6 1.6 bitcast_select_fusion
  168.2 1.3 slice_bitcast_fusion
  170.4 1.2 reshape.752
  171.5 1.9 reshape.753
  173.4 1.4 fusion.37
  174.9 21.3 %fusion.68 = (f32[192]{0:T(256)}, f32[192]{0:T(256)S(1)}) fusion(f32[192]{0:T(256)S(1)} %get-tuple-element.110, f32[]{:T(128)S(6)} %convert_element_type.922, s32[]{:T(128)} %bitcast.31, s32[]{:T(128)} %bitcast.30, s32[]{:T(128)} %bitcast.29, s32[]{:T(128)} %bitcast.28, s32[]{:T(128)} %bitcast.27, s32[]{:T(128)} %bitcast.26, s32[]{:T(128)} %bitcast.25, ...), kind=kLoop, calls=%fused_computation.273 | loop fusion | flops 13248 | bytes 3204 | tf_op jit(solution)/shard_map/mul | solution.py:144
  196.1 1.4 multiply_convert_fusion
  197.5 1.6 copy.20
  199.2 2.2 gather_fusion.4
  201.3 1.3 multiply_reduce_fusion.5
  203.4 4.6 %multiply_reduce_fusion.3 = (f32[2]{0:T(128)S(1)}, f32[2,3072]{1,0:T(2,128)S(1)}) fusion(f32[2,3072]{1,0:T(2,128)} %copy-done.5, f32[2]{0:T(128)} %copy-done.98, f32[3072]{0:T(1024)} %param.16, bf16[3072,1024]{1,0:T(8,128)(2,1)} %param.17, f32[2,1024]{1,0:T(2,128)} %copy-done.89, f32[2,1024]{1,0:T(2,128)S(1)} %get-tuple-element.113, ...), kind=kOutput, calls=%fused_computation.90 | convolution fusion | flops 12617726 | bytes 6369312 | tf_op jit(solution)/shard_map/dot_general | solution.py:159
  210.3 1.0 add_convert_fusion.1
  211.3 1.1 copy-done.2
  212.5 1.7 fusion.74
  214.2 1.9 collective-permute-start.14
  216.1 3.6 %collective-permute-start.15 = (bf16[2,3,32,3072]{3,2,1,0:T(8,128)(2,1)}, bf16[2,3,32,3072]{3,2,1,0:T(8,128)(2,1)S(1)}, u32[]{:S(2)}, u32[]{:S(2)}) collective-permute-start(bf16[2,3,32,3072]{3,2,1,0:T(8,128)(2,1)} %get-tuple-element.14), channel_id=1, source_target_pairs={{1,0},{2,1},{3,2},{4,3},{5,4},{6,5},{7,6},{9,8},{10,9},{11,10},{12... | collective-permute-start | bytes 3538952 | tf_op jit(solution)/shard_map/ppermute | solution.py:24
  220.4 1.0 multiply_reduce_fusion.1
  223.1 21.4 %collective-permute-done.14 = bf16[2,3,32,3072]{3,2,1,0:T(8,128)(2,1)S(1)} collective-permute-done((bf16[2,3,32,3072]{3,2,1,0:T(8,128)(2,1)}, bf16[2,3,32,3072]{3,2,1,0:T(8,128)(2,1)S(1)}, u32[]{:S(2)}, u32[]{:S(2)}) %collective-permute-start.14) | collective-permute-done | bytes 1179680 | tf_op jit(solution)/shard_map/ppermute | solution.py:23
  244.5 3.5 %select_maximum_fusion = bf16[2,10,38,3072]{3,2,1,0:T(8,128)(2,1)S(1)} fusion(bf16[2,3,32,3072]{3,2,1,0:T(8,128)(2,1)S(1)} %collective-permute-done.15, bf16[2,4,32,3072]{3,2,1,0:T(8,128)(2,1)} %copy-done.2, bf16[2,3,32,3072]{3,2,1,0:T(8,128)(2,1)S(1)} %collective-permute-done.14), kind=kLoop, calls=%fused_computation.8 | loop fusion | flops 28016640 | bytes 8601600 | tf_op jit(solution)/shard_map/concatenate | solution.py:25
  248.4 25.6 %add_convert_fusion = bf16[2,4,32,3072]{3,2,1,0:T(8,128)(2,1)} fusion(bf16[2,4,32,3072]{3,2,1,0:T(8,128)(2,1)S(1)} %copy-done.3, bf16[2,3,32,3072]{3,2,1,0:T(8,128)(2,1)S(1)} %collective-permute-done.15, bf16[2,3,32,3072]{3,2,1,0:T(8,128)(2,1)S(1)} %collective-permute-done.14, bf16[2,10,38,3072]{3,2,1,0:T(8,128)(2,1)S(1)} %select_maximum_fusion, ...), kind=kLoop, calls=%fused_computation.50 | loop fusion | flops 121110528 | bytes 72192000 | tf_op jit(solution)/shard_map/convert_element_type | solution.py:166
  (293 shorter events, 23.8 us)
Async XLA Ops:
  0.6 33.8 %copy-start = (bf16[2,4,32,3072]{3,2,1,0:T(8,128)(2,1)S(1)}, bf16[2,4,32,3072]{3,2,1,0:T(8,128)(2,1)}, u32[]{:S(2)}) copy-start(bf16[2,4,32,3072]{3,2,1,0:T(8,128)(2,1)} %param.11) | copy-start | bytes 4718596
  4.0 30.4 %collective-permute-start = (bf16[2,3,32,3072]{3,2,1,0:T(8,128)(2,1)}, bf16[2,3,32,3072]{3,2,1,0:T(8,128)(2,1)S(1)}, u32[]{:S(2)}, u32[]{:S(2)}) collective-permute-start(bf16[2,3,32,3072]{3,2,1,0:T(8,128)(2,1)} %get-tuple-element.17), channel_id=1, source_target_pairs={{0,1},{1,2},{2,3},{3,4},{4,5},{5,6},{6,7},{8,9},{9,10},{10,11},{11... | collective-permute-start | bytes 3538952 | tf_op jit(solution)/shard_map/ppermute | solution.py:23
  5.9 28.9 %collective-permute-start.1 = (bf16[2,3,32,3072]{3,2,1,0:T(8,128)(2,1)}, bf16[2,3,32,3072]{3,2,1,0:T(8,128)(2,1)}, u32[]{:S(2)}, u32[]{:S(2)}) collective-permute-start(bf16[2,3,32,3072]{3,2,1,0:T(8,128)(2,1)} %get-tuple-element.18), channel_id=1, source_target_pairs={{1,0},{2,1},{3,2},{4,3},{5,4},{6,5},{7,6},{9,8},{10,9},{11,10},{12... | collective-permute-start | bytes 3538952 | tf_op jit(solution)/shard_map/ppermute | solution.py:24
  9.8 30.0 %copy-start.33 = (f32[1,1,3072]{2,1,0:T(1,128)}, f32[1,1,3072]{2,1,0:T(1,128)S(1)}, u32[]{:S(2)}) copy-start(f32[1,1,3072]{2,1,0:T(1,128)S(1)} %get-tuple-element.21) | copy-start | bytes 36868
  9.8 30.0 %copy-start.35 = (f32[1,1,3072]{2,1,0:T(1,128)}, f32[1,1,3072]{2,1,0:T(1,128)S(1)}, u32[]{:S(2)}) copy-start(f32[1,1,3072]{2,1,0:T(1,128)S(1)} %get-tuple-element.22) | copy-start | bytes 36868
  9.8 30.0 %copy-start.37 = (f32[1,1,3072]{2,1,0:T(1,128)}, f32[1,1,3072]{2,1,0:T(1,128)S(1)}, u32[]{:S(2)}) copy-start(f32[1,1,3072]{2,1,0:T(1,128)S(1)} %get-tuple-element.23) | copy-start | bytes 36868
  9.8 30.0 %copy-start.39 = (f32[1,1,3072]{2,1,0:T(1,128)}, f32[1,1,3072]{2,1,0:T(1,128)S(1)}, u32[]{:S(2)}) copy-start(f32[1,1,3072]{2,1,0:T(1,128)S(1)} %get-tuple-element.24) | copy-start | bytes 36868
  9.8 30.0 %copy-start.41 = (f32[1,1,3072]{2,1,0:T(1,128)}, f32[1,1,3072]{2,1,0:T(1,128)S(1)}, u32[]{:S(2)}) copy-start(f32[1,1,3072]{2,1,0:T(1,128)S(1)} %get-tuple-element.25) | copy-start | bytes 36868
  9.8 30.0 %copy-start.43 = (f32[1,1,3072]{2,1,0:T(1,128)}, f32[1,1,3072]{2,1,0:T(1,128)S(1)}, u32[]{:S(2)}) copy-start(f32[1,1,3072]{2,1,0:T(1,128)S(1)} %get-tuple-element.26) | copy-start | bytes 36868
  9.8 30.0 %copy-start.45 = (f32[1,1,3072]{2,1,0:T(1,128)}, f32[1,1,3072]{2,1,0:T(1,128)S(1)}, u32[]{:S(2)}) copy-start(f32[1,1,3072]{2,1,0:T(1,128)S(1)} %get-tuple-element.27) | copy-start | bytes 36868
  9.8 30.0 %copy-start.47 = (f32[1,1,3072]{2,1,0:T(1,128)}, f32[1,1,3072]{2,1,0:T(1,128)S(1)}, u32[]{:S(2)}) copy-start(f32[1,1,3072]{2,1,0:T(1,128)S(1)} %get-tuple-element.28) | copy-start | bytes 36868
  9.8 30.0 %copy-start.49 = (f32[1,1,3072]{2,1,0:T(1,128)}, f32[1,1,3072]{2,1,0:T(1,128)S(1)}, u32[]{:S(2)}) copy-start(f32[1,1,3072]{2,1,0:T(1,128)S(1)} %get-tuple-element.29) | copy-start | bytes 36868
  9.8 30.0 %copy-start.51 = (f32[1,1,3072]{2,1,0:T(1,128)}, f32[1,1,3072]{2,1,0:T(1,128)S(1)}, u32[]{:S(2)}) copy-start(f32[1,1,3072]{2,1,0:T(1,128)S(1)} %get-tuple-element.30) | copy-start | bytes 36868
  9.9 30.0 %copy-start.53 = (f32[1,1,3072]{2,1,0:T(1,128)}, f32[1,1,3072]{2,1,0:T(1,128)S(1)}, u32[]{:S(2)}) copy-start(f32[1,1,3072]{2,1,0:T(1,128)S(1)} %get-tuple-element.31) | copy-start | bytes 36868
  9.9 30.0 %copy-start.55 = (f32[1,1,3072]{2,1,0:T(1,128)}, f32[1,1,3072]{2,1,0:T(1,128)S(1)}, u32[]{:S(2)}) copy-start(f32[1,1,3072]{2,1,0:T(1,128)S(1)} %get-tuple-element.32) | copy-start | bytes 36868
  9.9 30.0 %copy-start.57 = (f32[1,1,3072]{2,1,0:T(1,128)}, f32[1,1,3072]{2,1,0:T(1,128)S(1)}, u32[]{:S(2)}) copy-start(f32[1,1,3072]{2,1,0:T(1,128)S(1)} %get-tuple-element.33) | copy-start | bytes 36868
  9.9 30.0 %copy-start.59 = (f32[1,1,3072]{2,1,0:T(1,128)}, f32[1,1,3072]{2,1,0:T(1,128)S(1)}, u32[]{:S(2)}) copy-start(f32[1,1,3072]{2,1,0:T(1,128)S(1)} %get-tuple-element.34) | copy-start | bytes 36868
  9.9 30.0 %copy-start.61 = (f32[1,1,3072]{2,1,0:T(1,128)}, f32[1,1,3072]{2,1,0:T(1,128)S(1)}, u32[]{:S(2)}) copy-start(f32[1,1,3072]{2,1,0:T(1,128)S(1)} %get-tuple-element.35) | copy-start | bytes 36868
  9.9 30.0 %copy-start.63 = (f32[1,1,3072]{2,1,0:T(1,128)}, f32[1,1,3072]{2,1,0:T(1,128)S(1)}, u32[]{:S(2)}) copy-start(f32[1,1,3072]{2,1,0:T(1,128)S(1)} %get-tuple-element.36) | copy-start | bytes 36868
  9.9 30.0 %copy-start.65 = (f32[1,1,3072]{2,1,0:T(1,128)}, f32[1,1,3072]{2,1,0:T(1,128)S(1)}, u32[]{:S(2)}) copy-start(f32[1,1,3072]{2,1,0:T(1,128)S(1)} %get-tuple-element.37) | copy-start | bytes 36868
  9.9 30.0 %copy-start.67 = (f32[1,1,3072]{2,1,0:T(1,128)}, f32[1,1,3072]{2,1,0:T(1,128)S(1)}, u32[]{:S(2)}) copy-start(f32[1,1,3072]{2,1,0:T(1,128)S(1)} %get-tuple-element.38) | copy-start | bytes 36868
  9.9 30.0 %copy-start.69 = (f32[1,1,3072]{2,1,0:T(1,128)}, f32[1,1,3072]{2,1,0:T(1,128)S(1)}, u32[]{:S(2)}) copy-start(f32[1,1,3072]{2,1,0:T(1,128)S(1)} %get-tuple-element.39) | copy-start | bytes 36868
  10.1 29.9 %copy-start.11 = (f32[1,1,3072]{2,1,0:T(1,128)}, f32[1,1,3072]{2,1,0:T(1,128)S(1)}, u32[]{:S(2)}) copy-start(f32[1,1,3072]{2,1,0:T(1,128)S(1)} %get-tuple-element.59) | copy-start | bytes 36868
  10.1 29.9 %copy-start.13 = (f32[1,1,3072]{2,1,0:T(1,128)}, f32[1,1,3072]{2,1,0:T(1,128)S(1)}, u32[]{:S(2)}) copy-start(f32[1,1,3072]{2,1,0:T(1,128)S(1)} %get-tuple-element.60) | copy-start | bytes 36868
  10.1 29.9 %copy-start.15 = (f32[1,1,3072]{2,1,0:T(1,128)}, f32[1,1,3072]{2,1,0:T(1,128)S(1)}, u32[]{:S(2)}) copy-start(f32[1,1,3072]{2,1,0:T(1,128)S(1)} %get-tuple-element.61) | copy-start | bytes 36868
  10.1 29.9 %copy-start.17 = (f32[1,1,3072]{2,1,0:T(1,128)}, f32[1,1,3072]{2,1,0:T(1,128)S(1)}, u32[]{:S(2)}) copy-start(f32[1,1,3072]{2,1,0:T(1,128)S(1)} %get-tuple-element.62) | copy-start | bytes 36868
  10.1 29.9 %copy-start.19 = (f32[1,1,3072]{2,1,0:T(1,128)}, f32[1,1,3072]{2,1,0:T(1,128)S(1)}, u32[]{:S(2)}) copy-start(f32[1,1,3072]{2,1,0:T(1,128)S(1)} %get-tuple-element.63) | copy-start | bytes 36868
  10.1 29.9 %copy-start.21 = (f32[1,1,3072]{2,1,0:T(1,128)}, f32[1,1,3072]{2,1,0:T(1,128)S(1)}, u32[]{:S(2)}) copy-start(f32[1,1,3072]{2,1,0:T(1,128)S(1)} %get-tuple-element.64) | copy-start | bytes 36868
  10.1 29.9 %copy-start.23 = (f32[1,1,3072]{2,1,0:T(1,128)}, f32[1,1,3072]{2,1,0:T(1,128)S(1)}, u32[]{:S(2)}) copy-start(f32[1,1,3072]{2,1,0:T(1,128)S(1)} %get-tuple-element.65) | copy-start | bytes 36868
  10.1 29.9 %copy-start.25 = (f32[1,1,3072]{2,1,0:T(1,128)}, f32[1,1,3072]{2,1,0:T(1,128)S(1)}, u32[]{:S(2)}) copy-start(f32[1,1,3072]{2,1,0:T(1,128)S(1)} %get-tuple-element.66) | copy-start | bytes 36868
  10.1 29.9 %copy-start.27 = (f32[1,1,3072]{2,1,0:T(1,128)}, f32[1,1,3072]{2,1,0:T(1,128)S(1)}, u32[]{:S(2)}) copy-start(f32[1,1,3072]{2,1,0:T(1,128)S(1)} %get-tuple-element.67) | copy-start | bytes 36868
  10.1 29.9 %copy-start.29 = (f32[1,1,3072]{2,1,0:T(1,128)}, f32[1,1,3072]{2,1,0:T(1,128)S(1)}, u32[]{:S(2)}) copy-start(f32[1,1,3072]{2,1,0:T(1,128)S(1)} %get-tuple-element.68) | copy-start | bytes 36868
  10.2 29.9 %copy-start.31 = (f32[1,1,3072]{2,1,0:T(1,128)}, f32[1,1,3072]{2,1,0:T(1,128)S(1)}, u32[]{:S(2)}) copy-start(f32[1,1,3072]{2,1,0:T(1,128)S(1)} %get-tuple-element.69) | copy-start | bytes 36868
  69.5 3.1 %collective-permute-start.2 = (f32[2,3072]{1,0:T(2,128)S(1)}, f32[2,3072]{1,0:T(2,128)S(1)}, u32[]{:S(2)}, u32[]{:S(2)}) collective-permute-start(f32[2,3072]{1,0:T(2,128)S(1)} %broadcast_multiply_fusion.1), channel_id=1, source_target_pairs={{0,1},{1,0},{2,3},{3,2},{4,5},{5,4},{6,7},{7,6},{8,9},{9,8},{10,11... | collective-permute-start | bytes 73736 | tf_op jit(solution)/shard_map/ppermute | solution.py:33
  72.6 5.7 %collective-permute-start.3 = (f32[2,3072]{1,0:T(2,128)S(1)}, f32[2,3072]{1,0:T(2,128)S(1)}, u32[]{:S(2)}, u32[]{:S(2)}) collective-permute-start(f32[2,3072]{1,0:T(2,128)S(1)} %fusion.67), channel_id=1, source_target_pairs={{0,2},{1,3},{2,0},{3,1},{4,6},{5,7},{6,4},{7,5},{8,10},{9,11},{10,... | collective-permute-start | bytes 73736 | tf_op jit(solution)/shard_map/ppermute | solution.py:33
  78.3 5.7 %collective-permute-start.4 = (f32[2,3072]{1,0:T(2,128)S(1)}, f32[2,3072]{1,0:T(2,128)S(1)}, u32[]{:S(2)}, u32[]{:S(2)}) collective-permute-start(f32[2,3072]{1,0:T(2,128)S(1)} %add.657), channel_id=1, source_target_pairs={{0,4},{1,5},{2,6},{3,7},{4,0},{5,1},{6,2},{7,3},{8,12},{9,13},{10,... | collective-permute-start | bytes 73736 | tf_op jit(solution)/shard_map/ppermute | solution.py:33
  89.6 15.1 %collective-permute-start.5 = (bf16[4,1024]{1,0:T(4,128)(2,1)S(1)}, bf16[4,1024]{1,0:T(4,128)(2,1)S(1)}, u32[]{:S(2)}, u32[]{:S(2)}) collective-permute-start(bf16[4,1024]{1,0:T(4,128)(2,1)S(1)} %get-tuple-element.71), channel_id=1, source_target_pairs={{0,8},{8,16},{16,0},{24,32},{32,40},{40,24},{1,9},{9,17},{17,1},{2... | collective-permute-start | bytes 24584 | tf_op jit(solution)/shard_map/ppermute | solution.py:50
  95.7 9.0 %collective-permute-start.6 = (bf16[4,1024]{1,0:T(4,128)(2,1)S(1)}, bf16[4,1024]{1,0:T(4,128)(2,1)S(1)}, u32[]{:S(2)}, u32[]{:S(2)}) collective-permute-start(bf16[4,1024]{1,0:T(4,128)(2,1)S(1)} %get-tuple-element.71), channel_id=1, source_target_pairs={{0,16},{8,0},{16,8},{24,40},{32,24},{40,32},{1,17},{9,1},{17,9},{2... | collective-permute-start | bytes 24584 | tf_op jit(solution)/shard_map/ppermute | solution.py:50
  105.5 14.4 %collective-permute-start.7 = (bf16[3,4,1024]{2,1,0:T(4,128)(2,1)S(1)}, bf16[3,4,1024]{2,1,0:T(4,128)(2,1)S(1)}, u32[]{:S(2)}, u32[]{:S(2)}) collective-permute-start(bf16[3,4,1024]{2,1,0:T(4,128)(2,1)S(1)} %broadcast_select_fusion.1), channel_id=1, source_target_pairs={{0,24},{8,32},{16,40},{24,0},{32,8},{40,16},{1,25},{9,33},{17,41},... | collective-permute-start | bytes 73736 | tf_op jit(solution)/shard_map/ppermute | solution.py:50
  120.7 10.5 %collective-permute-start.8 = (bf16[6,4,1024]{2,1,0:T(4,128)(2,1)S(1)}, bf16[6,4,1024]{2,1,0:T(4,128)(2,1)S(1)}, u32[]{:S(2)}, u32[]{:S(2)}) collective-permute-start(bf16[6,4,1024]{2,1,0:T(4,128)(2,1)S(1)} %bitcast_select_fusion.2), channel_id=1, source_target_pairs={{0,48},{48,96},{96,144},{144,0},{192,240},{240,288},{288,336},{336... | collective-permute-start | bytes 147464 | tf_op jit(solution)/shard_map/ppermute | solution.py:50
  124.2 7.0 %collective-permute-start.9 = (bf16[6,4,1024]{2,1,0:T(4,128)(2,1)S(1)}, bf16[6,4,1024]{2,1,0:T(4,128)(2,1)S(1)}, u32[]{:S(2)}, u32[]{:S(2)}) collective-permute-start(bf16[6,4,1024]{2,1,0:T(4,128)(2,1)S(1)} %bitcast_select_fusion.2), channel_id=1, source_target_pairs={{0,96},{48,144},{96,0},{144,48},{192,288},{240,336},{288,192},{336... | collective-permute-start | bytes 147464 | tf_op jit(solution)/shard_map/ppermute | solution.py:50
  127.4 6.0 %collective-permute-start.10 = (bf16[6,4,1024]{2,1,0:T(4,128)(2,1)S(1)}, bf16[6,4,1024]{2,1,0:T(4,128)(2,1)S(1)}, u32[]{:S(2)}, u32[]{:S(2)}) collective-permute-start(bf16[6,4,1024]{2,1,0:T(4,128)(2,1)S(1)} %bitcast_select_fusion.2), channel_id=1, source_target_pairs={{0,144},{48,0},{96,48},{144,96},{192,336},{240,192},{288,240},{336... | collective-permute-start | bytes 147464 | tf_op jit(solution)/shard_map/ppermute | solution.py:50
  134.4 32.2 %copy-start.105 = (pred[16]{0:T(512)(128)(4,1)S(1)}, pred[16]{0:T(512)(128)(4,1)}, u32[]{:S(2)}) copy-start(pred[16]{0:T(512)(128)(4,1)} %broadcast_in_dim.96) | copy-start | bytes 52
  135.2 17.2 %collective-permute-start.11 = (bf16[4,6,4,1024]{3,2,1,0:T(4,128)(2,1)S(1)}, bf16[4,6,4,1024]{3,2,1,0:T(4,128)(2,1)S(1)}, u32[]{:S(2)}, u32[]{:S(2)}) collective-permute-start(bf16[4,6,4,1024]{3,2,1,0:T(4,128)(2,1)S(1)} %broadcast_select_fusion), channel_id=1, source_target_pairs={{0,192},{48,240},{96,288},{144,336},{192,384},{240,432},{288,480},... | collective-permute-start | bytes 589832 | tf_op jit(solution)/shard_map/ppermute | solution.py:50
  143.0 9.5 %collective-permute-start.12 = (bf16[4,6,4,1024]{3,2,1,0:T(4,128)(2,1)S(1)}, bf16[4,6,4,1024]{3,2,1,0:T(4,128)(2,1)S(1)}, u32[]{:S(2)}, u32[]{:S(2)}) collective-permute-start(bf16[4,6,4,1024]{3,2,1,0:T(4,128)(2,1)S(1)} %broadcast_select_fusion), channel_id=1, source_target_pairs={{0,384},{48,432},{96,480},{144,528},{192,576},{240,624},{288,672},... | collective-permute-start | bytes 589832 | tf_op jit(solution)/shard_map/ppermute | solution.py:50
  147.0 14.7 %collective-permute-start.13 = (bf16[4,6,4,1024]{3,2,1,0:T(4,128)(2,1)S(1)}, bf16[4,6,4,1024]{3,2,1,0:T(4,128)(2,1)S(1)}, u32[]{:S(2)}, u32[]{:S(2)}) collective-permute-start(bf16[4,6,4,1024]{3,2,1,0:T(4,128)(2,1)S(1)} %broadcast_select_fusion), channel_id=1, source_target_pairs={{0,576},{48,624},{96,672},{144,720},{192,0},{240,48},{288,96},{336... | collective-permute-start | bytes 589832 | tf_op jit(solution)/shard_map/ppermute | solution.py:50
  214.2 30.4 %collective-permute-start.14 = (bf16[2,3,32,3072]{3,2,1,0:T(8,128)(2,1)}, bf16[2,3,32,3072]{3,2,1,0:T(8,128)(2,1)S(1)}, u32[]{:S(2)}, u32[]{:S(2)}) collective-permute-start(bf16[2,3,32,3072]{3,2,1,0:T(8,128)(2,1)} %get-tuple-element.13), channel_id=1, source_target_pairs={{0,1},{1,2},{2,3},{3,4},{4,5},{5,6},{6,7},{8,9},{9,10},{10,11},{11... | collective-permute-start | bytes 3538952 | tf_op jit(solution)/shard_map/ppermute | solution.py:23
  216.1 28.4 %collective-permute-start.15 = (bf16[2,3,32,3072]{3,2,1,0:T(8,128)(2,1)}, bf16[2,3,32,3072]{3,2,1,0:T(8,128)(2,1)S(1)}, u32[]{:S(2)}, u32[]{:S(2)}) collective-permute-start(bf16[2,3,32,3072]{3,2,1,0:T(8,128)(2,1)} %get-tuple-element.14), channel_id=1, source_target_pairs={{1,0},{2,1},{3,2},{4,3},{5,4},{6,5},{7,6},{9,8},{10,9},{11,10},{12... | collective-permute-start | bytes 3538952 | tf_op jit(solution)/shard_map/ppermute | solution.py:24
  (77 other events, 1406.9 us)

commit v3 on v2

--- a/solution.py
+++ b/solution.py
@@ -57,7 +57,7 @@
 
 def radix_split(count):
     parts = []
-    for radix in (4, 3, 2):
+    for radix in (3, 2):
         while count % radix == 0 and count > 1:
             parts.append(radix)
             count //= radix
@@ -117,37 +117,46 @@
     text_f = texts.astype(jnp.float32)
     text_vec = unit_rows(text_f).astype(jnp.bfloat16)
     text_count = texts.shape[0]
-    share = text_count // img_count
-    text_share = lax.dynamic_slice_in_dim(text_vec, img_at * share, share)
-    payload = jnp.concatenate([image_vec, text_share], axis=0)
-    gathered = gather_stages(payload, "img", radix_split(img_count))
+    text_all = gather_stages(text_vec, "dp", radix_split(dp_count)).reshape(
+        dp_count * text_count, -1
+    )
+    count = text_all.shape[0]
+    source_table = (sources[:, None] == jnp.arange(SOURCES)[None, :]).astype(jnp.float32)
+    weights = (
+        SOURCES
+        * jnp.sum(source_table * numerators.astype(jnp.float32)[None, :], axis=1)
+        / jnp.sum(numerators).astype(jnp.float32)
+    )
+    own_rows = (dp_at * batch_rows + jnp.arange(batch_rows)) * img_count + img_at
+    own_logits = (
+        LOGIT_SCALE * jnp.dot(image_vec, text_all.T, preferred_element_type=jnp.float32)
+        + LOGIT_BIAS
+    )
+    own_labels = jnp.where(
+        jnp.take(positives, own_rows)[:, None] == jnp.arange(count)[None, :], 1.0, -1.0
+    ).astype(jnp.float32)
+    own_weights = jnp.take(weights, own_rows)
+    own_pair = (
+        own_weights[:, None] * -own_labels * jax.nn.sigmoid(-own_labels * own_logits)
+    ).astype(jnp.bfloat16)
+    image_dir = LOGIT_SCALE * jnp.dot(own_pair, text_all, preferred_element_type=jnp.float32)
+    gathered = gather_stages(image_vec, "img", radix_split(img_count))
     gathered = gather_stages(gathered, "dp", radix_split(dp_count))
-    image_all = jnp.transpose(gathered[:, :, :batch_rows, :], (0, 2, 1, 3)).reshape(
+    image_all = jnp.transpose(gathered, (0, 2, 1, 3)).reshape(
         dp_count * batch_rows * img_count, -1
     )
-    text_all = gathered[:, :, batch_rows:, :].reshape(dp_count * text_count, -1)
-    count = text_all.shape[0]
     logits = (
         LOGIT_SCALE * jnp.dot(image_all, text_all.T, preferred_element_type=jnp.float32)
         + LOGIT_BIAS
     )
     labels = jnp.where(positives[:, None] == jnp.arange(count)[None, :], 1.0, -1.0).astype(
         jnp.float32
-    )
-    source_table = (sources[:, None] == jnp.arange(SOURCES)[None, :]).astype(jnp.float32)
-    weights = (
-        SOURCES
-        * numerators[sources].astype(jnp.float32)
-        / jnp.sum(numerators).astype(jnp.float32)
     )
     row_loss = lax.optimization_barrier(jnp.sum(jax.nn.softplus(-labels * logits), axis=1))
     group_sums = jnp.sum(source_table * (weights * row_loss)[:, None], axis=0)
     pair_grad = (weights[:, None] * -labels * jax.nn.sigmoid(-labels * logits)).astype(
         jnp.bfloat16
     )
-    own_rows = (dp_at * batch_rows + jnp.arange(batch_rows)) * img_count + img_at
-    own_pair = jnp.take(pair_grad, own_rows, axis=0)
-    image_dir = LOGIT_SCALE * jnp.dot(own_pair, text_all, preferred_element_type=jnp.float32)
     text_pair = lax.dynamic_slice_in_dim(pair_grad, dp_at * text_count, text_count, axis=1)
     text_dir = LOGIT_SCALE * lax.dot_general(
         text_pair, image_all, (((0,), (0,)), ((), ())), preferred_element_type=jnp.float32

time: 276 us -> 268 us (0.971)
  the two profiles are of different devices: /device:TPU:10 before, /device:TPU:6 now
where the time goes in v3:
time: 268 us; the launch traced here: 267 us
  other arithmetic  83.7 us (31%)
  starting transfers between devices  74.7 us (28%)
  waiting for transfers between devices  60.3 us (22%)
  local copies, waits for them, and re-layouts  29.3 us (11%)
  matrix products  14.5 us (5%)
  between operations  3.91 us (1%)
    ppermute x11, starting transfers between devices, gather_stages(): got.append(lax.ppermute(value, axis, pairs))  58 us
    ppermute x11, waiting for transfers between devices, gather_stages(): got.append(lax.ppermute(value, axis, pairs))  36.9 us
    reduce_sum x4, other arithmetic, cell_norm(): center = values - jnp.mean(values, axis=-1, keepdims=True)  27.8 us
    convert_element_type x1, other arithmetic, local(): grad_map = (own_grad[:, None, None, :] + spread).astype(jnp.bfloat16)  25.6 us
    ppermute x2, waiting for transfers between devices, halo_rows(): before = lax.ppermute(last, 'row', up)  14.7 us
    gather x12, local copies, waits for them, and re-layouts, gather_stages(): value = jnp.take(stacked, order, axis=0)  12.8 us
    ppermute x2, waiting for transfers between devices, halo_rows(): after = lax.ppermute(leading, 'row', down)  8.79 us
    concatenate x2, other arithmetic, halo_rows(): return jnp.concatenate([before, value, after], axis=1)  7.02 us
  transfers between devices with their start and end apart: 18, of which 11 were waited for; matrix products, arithmetic and copies ran while one was open for 9% of the time, Pallas kernels for 0%

profile of v3, /device:TPU:6, one launch (start us, length us, event | category | flops | bytes accessed | tf_op | source)
XLA Modules:
  0.0 266.6 jit_solution(10109028781040491317)
XLA Ops:
  0.7 3.2 %fusion.114 = (bf16[2,3,32,3072]{3,2,1,0:T(8,128)(2,1)}, bf16[2,3,32,3072]{3,2,1,0:T(8,128)(2,1)}) fusion(bf16[2,4,32,3072]{3,2,1,0:T(8,128)(2,1)} %param.11), kind=kLoop, calls=%fused_computation.329 | loop fusion | bytes 4718592 | tf_op jit(solution)/shard_map/slice | solution.py:21
  3.9 1.9 collective-permute-start
  5.8 3.6 %collective-permute-start.1 = (bf16[2,3,32,3072]{3,2,1,0:T(8,128)(2,1)}, bf16[2,3,32,3072]{3,2,1,0:T(8,128)(2,1)}, u32[]{:S(2)}, u32[]{:S(2)}) collective-permute-start(bf16[2,3,32,3072]{3,2,1,0:T(8,128)(2,1)} %get-tuple-element.18), channel_id=1, source_target_pairs={{1,0},{2,1},{3,2},{4,3},{5,4},{6,5},{7,6},{9,8},{10,9},{11,10},{12... | collective-permute-start | bytes 3538952 | tf_op jit(solution)/shard_map/ppermute | solution.py:24
  9.7 3.5 %collective-permute-start.5 = (bf16[12,1024]{1,0:T(8,128)(2,1)S(1)}, bf16[12,1024]{1,0:T(8,128)(2,1)S(1)}, u32[]{:S(2)}, u32[]{:S(2)}) collective-permute-start(bf16[12,1024]{1,0:T(8,128)(2,1)S(1)} %fusion.54), channel_id=1, source_target_pairs={{0,48},{48,0},{96,144},{144,96},{192,240},{240,192},{288,336},{336... | collective-permute-start | bytes 73736 | tf_op jit(solution)/shard_map/ppermute | solution.py:50
  23.9 4.5 %collective-permute-start.6 = (bf16[2,12,1024]{2,1,0:T(8,128)(2,1)S(1)}, bf16[2,12,1024]{2,1,0:T(8,128)(2,1)S(1)}, u32[]{:S(2)}, u32[]{:S(2)}) collective-permute-start(bf16[2,12,1024]{2,1,0:T(8,128)(2,1)S(1)} %broadcast_select_fusion.9), channel_id=1, source_target_pairs={{0,96},{48,144},{96,0},{144,48},{192,288},{240,336},{288,192},{336... | collective-permute-start | bytes 147464 | tf_op jit(solution)/shard_map/ppermute | solution.py:50
  28.5 4.2 %collective-permute-done.6 = bf16[2,12,1024]{2,1,0:T(8,128)(2,1)S(1)} collective-permute-done((bf16[2,12,1024]{2,1,0:T(8,128)(2,1)S(1)}, bf16[2,12,1024]{2,1,0:T(8,128)(2,1)S(1)}, u32[]{:S(2)}, u32[]{:S(2)}) %collective-permute-start.6) | collective-permute-done | bytes 49184 | tf_op jit(solution)/shard_map/ppermute | solution.py:50
  33.4 6.9 %collective-permute-start.7 = (bf16[2,2,12,1024]{3,2,1,0:T(8,128)(2,1)S(1)}, bf16[2,2,12,1024]{3,2,1,0:T(8,128)(2,1)S(1)}, u32[]{:S(2)}, u32[]{:S(2)}) collective-permute-start(bf16[2,2,12,1024]{3,2,1,0:T(8,128)(2,1)S(1)} %broadcast_select_fusion.6), channel_id=1, source_target_pairs={{0,192},{48,240},{96,288},{144,336},{192,0},{240,48},{288,96},{336... | collective-permute-start | bytes 294920 | tf_op jit(solution)/shard_map/ppermute | solution.py:50
  40.5 7.1 %collective-permute-done.7 = bf16[2,2,12,1024]{3,2,1,0:T(8,128)(2,1)S(1)} collective-permute-done((bf16[2,2,12,1024]{3,2,1,0:T(8,128)(2,1)S(1)}, bf16[2,2,12,1024]{3,2,1,0:T(8,128)(2,1)S(1)}, u32[]{:S(2)}, u32[]{:S(2)}) %collective-permute-start.7) | collective-permute-done | bytes 98336 | tf_op jit(solution)/shard_map/ppermute | solution.py:50
  49.2 3.5 %select_maximum_fusion.2 = bf16[2,10,38,3072]{3,2,1,0:T(8,128)(2,1)S(1)} fusion(bf16[2,3,32,3072]{3,2,1,0:T(8,128)(2,1)} %collective-permute-done.1, bf16[2,4,32,3072]{3,2,1,0:T(8,128)(2,1)S(1)} %copy-done.1, bf16[2,3,32,3072]{3,2,1,0:T(8,128)(2,1)S(1)} %collective-permute-done), kind=kLoop, calls=%fused_computation.17 | loop fusion | flops 28016640 | bytes 8601600 | tf_op jit(solution)/shard_map/concatenate | solution.py:25
  52.7 1.5 constant_dynamic-update-slice_fusion.2
  54.7 26.6 %fusion.111 = (f32[2,4,32]{2,1,0:T(4,128)S(1)}, f32[2,4,32,3072]{3,2,1,0:T(8,128)S(1)}) fusion(f32[3072]{0:T(1024)S(1)} %copy-done.112, f32[3072]{0:T(1024)S(1)} %bitcast.129, bf16[2,10,38,3072]{3,2,1,0:T(8,128)(2,1)S(1)} %select_maximum_fusion.2, f32[3072]{0:T(1024)S(1)} %bitcast.131, f32[3072]{0:T(1024)S(1)} %bitcast.135, f32[3072]{0:T(1024)S(1)} %bitcast.137, ...), kind=kLoop, calls=%fused_computation.327 | loop fusion | flops 116391680 | bytes 80831488 | tf_op jit(solution)/shard_map/reduce_sum | solution.py:69
  83.1 1.9 collective-permute-start.2
  85.1 3.0 %collective-permute-start.8 = (bf16[2,2,2,12,1024]{4,3,2,1,0:T(8,128)(2,1)S(1)}, bf16[2,2,2,12,1024]{4,3,2,1,0:T(8,128)(2,1)S(1)}, u32[]{:S(2)}, u32[]{:S(2)}) collective-permute-start(bf16[2,2,2,12,1024]{4,3,2,1,0:T(8,128)(2,1)S(1)} %broadcast_select_fusion.3), channel_id=1, source_target_pairs={{0,384},{48,432},{96,480},{144,528},{192,576},{240,624},{288,672},... | collective-permute-start | bytes 589832 | tf_op jit(solution)/shard_map/ppermute | solution.py:50
  88.1 3.1 %collective-permute-start.3 = (f32[2,3072]{1,0:T(2,128)S(1)}, f32[2,3072]{1,0:T(2,128)S(1)}, u32[]{:S(2)}, u32[]{:S(2)}) collective-permute-start(f32[2,3072]{1,0:T(2,128)S(1)} %fusion.107), channel_id=1, source_target_pairs={{0,2},{1,3},{2,0},{3,1},{4,6},{5,7},{6,4},{7,5},{8,10},{9,11},{10,... | collective-permute-start | bytes 73736 | tf_op jit(solution)/shard_map/ppermute | solution.py:33
  91.2 6.3 %collective-permute-done.8 = bf16[2,2,2,12,1024]{4,3,2,1,0:T(8,128)(2,1)S(1)} collective-permute-done((bf16[2,2,2,12,1024]{4,3,2,1,0:T(8,128)(2,1)S(1)}, bf16[2,2,2,12,1024]{4,3,2,1,0:T(8,128)(2,1)S(1)}, u32[]{:S(2)}, u32[]{:S(2)}) %collective-permute-start.8) | collective-permute-done | bytes 196640 | tf_op jit(solution)/shard_map/ppermute | solution.py:50
  98.3 2.5 gather_fusion.5
  100.9 1.9 collective-permute-start.4
  102.8 1.9 broadcast_select_fusion
  104.8 1.9 gather.79
  106.6 1.9 select_n.495
  109.6 3.9 %multiply_reduce_fusion.4 = (f32[2]{0:T(128)S(1)}, f32[2,1024]{1,0:T(2,128)S(1)}) fusion(bf16[3072,1024]{1,0:T(8,128)(2,1)} %param.17, f32[2]{0:T(128)S(1)} %fusion.99, f32[3072]{0:T(1024)S(1)} %copy-done.101, f32[2,3072]{1,0:T(2,128)S(1)} %get-tuple-element.10, f32[2]{0:T(128)S(1)} %broadcast_multiply_fusion.5), kind=kOutput, calls=%fused_computation.208 | convolution fusion | flops 12611582 | bytes 6336536 | tf_op jit(solution)/shard_map/dot_general | solution.py:115
  113.6 6.1 %collective-permute-start.11 = (bf16[2,1024]{1,0:T(2,128)(2,1)S(1)}, bf16[2,1024]{1,0:T(2,128)(2,1)S(1)}, u32[]{:S(2)}, u32[]{:S(2)}) collective-permute-start(bf16[2,1024]{1,0:T(2,128)(2,1)S(1)} %multiply_convert_fusion.2), channel_id=1, source_target_pairs={{0,8},{8,16},{16,0},{24,32},{32,40},{40,24},{1,9},{9,17},{17,1},{2... | collective-permute-start | bytes 12296 | tf_op jit(solution)/shard_map/ppermute | solution.py:50
  119.6 6.7 %collective-permute-start.12 = (bf16[2,1024]{1,0:T(2,128)(2,1)S(1)}, bf16[2,1024]{1,0:T(2,128)(2,1)S(1)}, u32[]{:S(2)}, u32[]{:S(2)}) collective-permute-start(bf16[2,1024]{1,0:T(2,128)(2,1)S(1)} %multiply_convert_fusion.2), channel_id=1, source_target_pairs={{0,16},{8,0},{16,8},{24,40},{32,24},{40,32},{1,17},{9,1},{17,9},{2... | collective-permute-start | bytes 12296 | tf_op jit(solution)/shard_map/ppermute | solution.py:50
  126.5 2.0 collective-permute-done.12
  129.4 11.3 %collective-permute-start.13 = (bf16[3,2,1024]{2,1,0:T(2,128)(2,1)S(1)}, bf16[3,2,1024]{2,1,0:T(2,128)(2,1)S(1)}, u32[]{:S(2)}, u32[]{:S(2)}) collective-permute-start(bf16[3,2,1024]{2,1,0:T(2,128)(2,1)S(1)} %broadcast_select_fusion.12), channel_id=1, source_target_pairs={{0,24},{8,32},{16,40},{24,0},{32,8},{40,16},{1,25},{9,33},{17,41},... | collective-permute-start | bytes 36872 | tf_op jit(solution)/shard_map/ppermute | solution.py:50
  140.8 1.6 collective-permute-done.13
  143.2 1.9 collective-permute-start.14
  145.3 3.7 %collective-permute-done.14 = bf16[6,2,1024]{2,1,0:T(2,128)(2,1)S(1)} collective-permute-done((bf16[6,2,1024]{2,1,0:T(2,128)(2,1)S(1)}, bf16[6,2,1024]{2,1,0:T(2,128)(2,1)S(1)}, u32[]{:S(2)}, u32[]{:S(2)}) %collective-permute-start.14) | collective-permute-done | bytes 24608 | tf_op jit(solution)/shard_map/ppermute | solution.py:50
  149.9 3.9 %collective-permute-start.15 = (bf16[2,6,2,1024]{3,2,1,0:T(2,128)(2,1)S(1)}, bf16[2,6,2,1024]{3,2,1,0:T(2,128)(2,1)S(1)}, u32[]{:S(2)}, u32[]{:S(2)}) collective-permute-start(bf16[2,6,2,1024]{3,2,1,0:T(2,128)(2,1)S(1)} %broadcast_select_fusion.7), channel_id=1, source_target_pairs={{0,96},{48,144},{96,0},{144,48},{192,288},{240,336},{288,192},{336... | collective-permute-start | bytes 147464 | tf_op jit(solution)/shard_map/ppermute | solution.py:50
  154.0 2.8 %collective-permute-done.15 = bf16[2,6,2,1024]{3,2,1,0:T(2,128)(2,1)S(1)} collective-permute-done((bf16[2,6,2,1024]{3,2,1,0:T(2,128)(2,1)S(1)}, bf16[2,6,2,1024]{3,2,1,0:T(2,128)(2,1)S(1)}, u32[]{:S(2)}, u32[]{:S(2)}) %collective-permute-start.15) | collective-permute-done | bytes 49184 | tf_op jit(solution)/shard_map/ppermute | solution.py:50
  158.0 7.1 %collective-permute-start.16 = (bf16[2,2,6,2,1024]{4,3,2,1,0:T(2,128)(2,1)S(1)}, bf16[2,2,6,2,1024]{4,3,2,1,0:T(2,128)(2,1)S(1)}, u32[]{:S(2)}, u32[]{:S(2)}) collective-permute-start(bf16[2,2,6,2,1024]{4,3,2,1,0:T(2,128)(2,1)S(1)} %broadcast_select_fusion.4), channel_id=1, source_target_pairs={{0,192},{48,240},{96,288},{144,336},{192,0},{240,48},{288,96},{336... | collective-permute-start | bytes 294920 | tf_op jit(solution)/shard_map/ppermute | solution.py:50
  165.3 3.2 %collective-permute-done.16 = bf16[2,2,6,2,1024]{4,3,2,1,0:T(2,128)(2,1)S(1)} collective-permute-done((bf16[2,2,6,2,1024]{4,3,2,1,0:T(2,128)(2,1)S(1)}, bf16[2,2,6,2,1024]{4,3,2,1,0:T(2,128)(2,1)S(1)}, u32[]{:S(2)}, u32[]{:S(2)}) %collective-permute-start.16) | collective-permute-done | bytes 98336 | tf_op jit(solution)/shard_map/ppermute | solution.py:50
  170.1 2.9 %collective-permute-start.17 = (bf16[2,2,2,6,2,1024]{5,4,3,2,1,0:T(2,128)(2,1)S(1)}, bf16[2,2,2,6,2,1024]{5,4,3,2,1,0:T(2,128)(2,1)S(1)}, u32[]{:S(2)}, u32[]{:S(2)}) collective-permute-start(bf16[2,2,2,6,2,1024]{5,4,3,2,1,0:T(2,128)(2,1)S(1)} %broadcast_select_fusion.1), channel_id=1, source_target_pairs={{0,384},{48,432},{96,480},{144,528},{192,576},{240,624},{288,672},... | collective-permute-start | bytes 589832 | tf_op jit(solution)/shard_map/ppermute | solution.py:50
  173.3 5.9 %collective-permute-done.17 = bf16[2,2,2,6,2,1024]{5,4,3,2,1,0:T(2,128)(2,1)S(1)} collective-permute-done((bf16[2,2,2,6,2,1024]{5,4,3,2,1,0:T(2,128)(2,1)S(1)}, bf16[2,2,2,6,2,1024]{5,4,3,2,1,0:T(2,128)(2,1)S(1)}, u32[]{:S(2)}, u32[]{:S(2)}) %collective-permute-start.17) | collective-permute-done | bytes 196640 | tf_op jit(solution)/shard_map/ppermute | solution.py:50
  179.2 1.3 pad_maximum_fusion.3
  180.5 2.5 gather_fusion.11
  183.1 1.6 bitcast_select_fusion
  185.8 2.1 fusion.50
  189.1 1.3 gather_fusion
  191.7 2.9 %multiply_reduce_fusion.3 = (f32[2]{0:T(128)}, f32[2,1024]{1,0:T(2,128)}) fusion(f32[2,1024]{1,0:T(2,128)} %copy-done.12, bf16[192,1024]{1,0:T(8,128)(2,1)} %gather.79, pred[192]{0:T(512)(128)(4,1)} %broadcast_in_dim.185, bf16[2,1024]{1,0:T(2,128)(2,1)} %copy-done.121, f32[2]{0:T(128)} %broadcast_select_fusion.15, s32[2]{0:T(128)} %broadcast_select_fusion.14), kind=kOutput, calls=%fused_computation.206 | convolution fusion | flops 1976830 | bytes 413912 | tf_op jit(solution)/shard_map/dot_general | solution.py:142
  195.3 4.7 %multiply_reduce_fusion.1 = (f32[2]{0:T(128)S(1)}, f32[2,3072]{1,0:T(2,128)S(1)}) fusion(f32[2,3072]{1,0:T(2,128)} %copy-done.8, f32[2]{0:T(128)} %copy-done.113, f32[3072]{0:T(1024)} %param.16, bf16[3072,1024]{1,0:T(8,128)(2,1)} %param.17, f32[2,1024]{1,0:T(2,128)} %copy-done.12, f32[2,1024]{1,0:T(2,128)} %get-tuple-element.79, ...), kind=kOutput, calls=%fused_computation.129 | convolution fusion | flops 12617726 | bytes 6369312 | tf_op jit(solution)/shard_map/dot_general | solution.py:168
  204.6 1.7 fusion.113
  206.2 1.9 collective-permute-start.10
  208.2 2.4 collective-permute-start.9
  213.4 8.8 %collective-permute-done.10 = bf16[2,3,32,3072]{3,2,1,0:T(8,128)(2,1)S(1)} collective-permute-done((bf16[2,3,32,3072]{3,2,1,0:T(8,128)(2,1)}, bf16[2,3,32,3072]{3,2,1,0:T(8,128)(2,1)S(1)}, u32[]{:S(2)}, u32[]{:S(2)}) %collective-permute-start.10) | collective-permute-done | bytes 1179680 | tf_op jit(solution)/shard_map/ppermute | solution.py:24
  222.2 14.7 %collective-permute-done.9 = bf16[2,3,32,3072]{3,2,1,0:T(8,128)(2,1)S(1)} collective-permute-done((bf16[2,3,32,3072]{3,2,1,0:T(8,128)(2,1)}, bf16[2,3,32,3072]{3,2,1,0:T(8,128)(2,1)S(1)}, u32[]{:S(2)}, u32[]{:S(2)}) %collective-permute-start.9) | collective-permute-done | bytes 1179680 | tf_op jit(solution)/shard_map/ppermute | solution.py:23
  236.8 3.5 %select_maximum_fusion = bf16[2,10,38,3072]{3,2,1,0:T(8,128)(2,1)S(1)} fusion(bf16[2,3,32,3072]{3,2,1,0:T(8,128)(2,1)S(1)} %collective-permute-done.10, bf16[2,4,32,3072]{3,2,1,0:T(8,128)(2,1)} %copy-done.3, bf16[2,3,32,3072]{3,2,1,0:T(8,128)(2,1)S(1)} %collective-permute-done.9), kind=kLoop, calls=%fused_computation.15 | loop fusion | flops 28016640 | bytes 8601600 | tf_op jit(solution)/shard_map/concatenate | solution.py:25
  240.8 25.6 %add_convert_fusion = bf16[2,4,32,3072]{3,2,1,0:T(8,128)(2,1)} fusion(bf16[2,4,32,3072]{3,2,1,0:T(8,128)(2,1)S(1)} %copy-done.4, bf16[2,3,32,3072]{3,2,1,0:T(8,128)(2,1)S(1)} %collective-permute-done.10, bf16[2,3,32,3072]{3,2,1,0:T(8,128)(2,1)S(1)} %collective-permute-done.9, bf16[2,10,38,3072]{3,2,1,0:T(8,128)(2,1)S(1)} %select_maximum_fusion, ...), kind=kLoop, calls=%fused_computation.57 | loop fusion | flops 121110528 | bytes 72192000 | tf_op jit(solution)/shard_map/convert_element_type | solution.py:175
  (379 shorter events, 33.6 us)
Async XLA Ops:
  3.9 44.3 %collective-permute-start = (bf16[2,3,32,3072]{3,2,1,0:T(8,128)(2,1)}, bf16[2,3,32,3072]{3,2,1,0:T(8,128)(2,1)S(1)}, u32[]{:S(2)}, u32[]{:S(2)}) collective-permute-start(bf16[2,3,32,3072]{3,2,1,0:T(8,128)(2,1)} %get-tuple-element.17), channel_id=1, source_target_pairs={{0,1},{1,2},{2,3},{3,4},{4,5},{5,6},{6,7},{8,9},{9,10},{10,11},{11... | collective-permute-start | bytes 3538952 | tf_op jit(solution)/shard_map/ppermute | solution.py:23
  5.8 43.3 %collective-permute-start.1 = (bf16[2,3,32,3072]{3,2,1,0:T(8,128)(2,1)}, bf16[2,3,32,3072]{3,2,1,0:T(8,128)(2,1)}, u32[]{:S(2)}, u32[]{:S(2)}) collective-permute-start(bf16[2,3,32,3072]{3,2,1,0:T(8,128)(2,1)} %get-tuple-element.18), channel_id=1, source_target_pairs={{1,0},{2,1},{3,2},{4,3},{5,4},{6,5},{7,6},{9,8},{10,9},{11,10},{12... | collective-permute-start | bytes 3538952 | tf_op jit(solution)/shard_map/ppermute | solution.py:24
  9.7 13.5 %collective-permute-start.5 = (bf16[12,1024]{1,0:T(8,128)(2,1)S(1)}, bf16[12,1024]{1,0:T(8,128)(2,1)S(1)}, u32[]{:S(2)}, u32[]{:S(2)}) collective-permute-start(bf16[12,1024]{1,0:T(8,128)(2,1)S(1)} %fusion.54), channel_id=1, source_target_pairs={{0,48},{48,0},{96,144},{144,96},{192,240},{240,192},{288,336},{336... | collective-permute-start | bytes 73736 | tf_op jit(solution)/shard_map/ppermute | solution.py:50
  15.0 39.2 %copy-start.13 = (f32[1,1,3072]{2,1,0:T(1,128)}, f32[1,1,3072]{2,1,0:T(1,128)S(1)}, u32[]{:S(2)}) copy-start(f32[1,1,3072]{2,1,0:T(1,128)S(1)} %get-tuple-element.57) | copy-start | bytes 36868
  15.0 39.2 %copy-start.15 = (f32[1,1,3072]{2,1,0:T(1,128)}, f32[1,1,3072]{2,1,0:T(1,128)S(1)}, u32[]{:S(2)}) copy-start(f32[1,1,3072]{2,1,0:T(1,128)S(1)} %get-tuple-element.58) | copy-start | bytes 36868
  15.0 39.2 %copy-start.17 = (f32[1,1,3072]{2,1,0:T(1,128)}, f32[1,1,3072]{2,1,0:T(1,128)S(1)}, u32[]{:S(2)}) copy-start(f32[1,1,3072]{2,1,0:T(1,128)S(1)} %get-tuple-element.59) | copy-start | bytes 36868
  15.0 39.2 %copy-start.19 = (f32[1,1,3072]{2,1,0:T(1,128)}, f32[1,1,3072]{2,1,0:T(1,128)S(1)}, u32[]{:S(2)}) copy-start(f32[1,1,3072]{2,1,0:T(1,128)S(1)} %get-tuple-element.60) | copy-start | bytes 36868
  15.0 39.2 %copy-start.21 = (f32[1,1,3072]{2,1,0:T(1,128)}, f32[1,1,3072]{2,1,0:T(1,128)S(1)}, u32[]{:S(2)}) copy-start(f32[1,1,3072]{2,1,0:T(1,128)S(1)} %get-tuple-element.61) | copy-start | bytes 36868
  15.0 39.2 %copy-start.23 = (f32[1,1,3072]{2,1,0:T(1,128)}, f32[1,1,3072]{2,1,0:T(1,128)S(1)}, u32[]{:S(2)}) copy-start(f32[1,1,3072]{2,1,0:T(1,128)S(1)} %get-tuple-element.62) | copy-start | bytes 36868
  15.0 39.2 %copy-start.25 = (f32[1,1,3072]{2,1,0:T(1,128)}, f32[1,1,3072]{2,1,0:T(1,128)S(1)}, u32[]{:S(2)}) copy-start(f32[1,1,3072]{2,1,0:T(1,128)S(1)} %get-tuple-element.63) | copy-start | bytes 36868
  15.1 39.2 %copy-start.27 = (f32[1,1,3072]{2,1,0:T(1,128)}, f32[1,1,3072]{2,1,0:T(1,128)S(1)}, u32[]{:S(2)}) copy-start(f32[1,1,3072]{2,1,0:T(1,128)S(1)} %get-tuple-element.64) | copy-start | bytes 36868
  15.1 39.2 %copy-start.29 = (f32[1,1,3072]{2,1,0:T(1,128)}, f32[1,1,3072]{2,1,0:T(1,128)S(1)}, u32[]{:S(2)}) copy-start(f32[1,1,3072]{2,1,0:T(1,128)S(1)} %get-tuple-element.65) | copy-start | bytes 36868
  15.1 39.2 %copy-start.31 = (f32[1,1,3072]{2,1,0:T(1,128)}, f32[1,1,3072]{2,1,0:T(1,128)S(1)}, u32[]{:S(2)}) copy-start(f32[1,1,3072]{2,1,0:T(1,128)S(1)} %get-tuple-element.66) | copy-start | bytes 36868
  15.1 39.2 %copy-start.33 = (f32[1,1,3072]{2,1,0:T(1,128)}, f32[1,1,3072]{2,1,0:T(1,128)S(1)}, u32[]{:S(2)}) copy-start(f32[1,1,3072]{2,1,0:T(1,128)S(1)} %get-tuple-element.67) | copy-start | bytes 36868
  15.8 32.5 %copy-start.1 = (bf16[2,4,32,3072]{3,2,1,0:T(8,128)(2,1)S(1)}, bf16[2,4,32,3072]{3,2,1,0:T(8,128)(2,1)}, u32[]{:S(2)}) copy-start(bf16[2,4,32,3072]{3,2,1,0:T(8,128)(2,1)} %param.11) | copy-start | bytes 4718596
  15.9 32.8 %copy-start.108 = (pred[2]{0:T(512)(128)(4,1)}, pred[2]{0:T(512)(128)(4,1)S(1)}, u32[]{:S(2)}) copy-start(pred[2]{0:T(512)(128)(4,1)S(1)} %get-tuple-element.87) | copy-start | bytes 10
  15.9 32.8 %copy-start.110 = (pred[2]{0:T(512)(128)(4,1)}, pred[2]{0:T(512)(128)(4,1)S(1)}, u32[]{:S(2)}) copy-start(pred[2]{0:T(512)(128)(4,1)S(1)} %get-tuple-element.86) | copy-start | bytes 10
  17.3 31.5 %copy-start.116 = (s32[1024]{0:T(1024)}, s32[1024]{0:T(1024)S(1)}, u32[]{:S(2)}) copy-start(s32[1024]{0:T(1024)S(1)} %pad_clamp_fusion.4) | copy-start | bytes 12292
  17.3 31.5 %copy-start.115 = (s32[1024]{0:T(1024)}, s32[1024]{0:T(1024)S(1)}, u32[]{:S(2)}) copy-start(s32[1024]{0:T(1024)S(1)} %pad_clamp_fusion.3) | copy-start | bytes 12292
  23.9 8.8 %collective-permute-start.6 = (bf16[2,12,1024]{2,1,0:T(8,128)(2,1)S(1)}, bf16[2,12,1024]{2,1,0:T(8,128)(2,1)S(1)}, u32[]{:S(2)}, u32[]{:S(2)}) collective-permute-start(bf16[2,12,1024]{2,1,0:T(8,128)(2,1)S(1)} %broadcast_select_fusion.9), channel_id=1, source_target_pairs={{0,96},{48,144},{96,0},{144,48},{192,288},{240,336},{288,192},{336... | collective-permute-start | bytes 147464 | tf_op jit(solution)/shard_map/ppermute | solution.py:50
  33.4 14.2 %collective-permute-start.7 = (bf16[2,2,12,1024]{3,2,1,0:T(8,128)(2,1)S(1)}, bf16[2,2,12,1024]{3,2,1,0:T(8,128)(2,1)S(1)}, u32[]{:S(2)}, u32[]{:S(2)}) collective-permute-start(bf16[2,2,12,1024]{3,2,1,0:T(8,128)(2,1)S(1)} %broadcast_select_fusion.6), channel_id=1, source_target_pairs={{0,192},{48,240},{96,288},{144,336},{192,0},{240,48},{288,96},{336... | collective-permute-start | bytes 294920 | tf_op jit(solution)/shard_map/ppermute | solution.py:50
  83.1 5.0 %collective-permute-start.2 = (f32[2,3072]{1,0:T(2,128)S(1)}, f32[2,3072]{1,0:T(2,128)S(1)}, u32[]{:S(2)}, u32[]{:S(2)}) collective-permute-start(f32[2,3072]{1,0:T(2,128)S(1)} %broadcast_multiply_fusion.1), channel_id=1, source_target_pairs={{0,1},{1,0},{2,3},{3,2},{4,5},{5,4},{6,7},{7,6},{8,9},{9,8},{10,11... | collective-permute-start | bytes 73736 | tf_op jit(solution)/shard_map/ppermute | solution.py:33
  85.1 12.4 %collective-permute-start.8 = (bf16[2,2,2,12,1024]{4,3,2,1,0:T(8,128)(2,1)S(1)}, bf16[2,2,2,12,1024]{4,3,2,1,0:T(8,128)(2,1)S(1)}, u32[]{:S(2)}, u32[]{:S(2)}) collective-permute-start(bf16[2,2,2,12,1024]{4,3,2,1,0:T(8,128)(2,1)S(1)} %broadcast_select_fusion.3), channel_id=1, source_target_pairs={{0,384},{48,432},{96,480},{144,528},{192,576},{240,624},{288,672},... | collective-permute-start | bytes 589832 | tf_op jit(solution)/shard_map/ppermute | solution.py:50
  88.1 12.7 %collective-permute-start.3 = (f32[2,3072]{1,0:T(2,128)S(1)}, f32[2,3072]{1,0:T(2,128)S(1)}, u32[]{:S(2)}, u32[]{:S(2)}) collective-permute-start(f32[2,3072]{1,0:T(2,128)S(1)} %fusion.107), channel_id=1, source_target_pairs={{0,2},{1,3},{2,0},{3,1},{4,6},{5,7},{6,4},{7,5},{8,10},{9,11},{10,... | collective-permute-start | bytes 73736 | tf_op jit(solution)/shard_map/ppermute | solution.py:33
  100.9 7.7 %collective-permute-start.4 = (f32[2,3072]{1,0:T(2,128)S(1)}, f32[2,3072]{1,0:T(2,128)S(1)}, u32[]{:S(2)}, u32[]{:S(2)}) collective-permute-start(f32[2,3072]{1,0:T(2,128)S(1)} %add.754), channel_id=1, source_target_pairs={{0,4},{1,5},{2,6},{3,7},{4,0},{5,1},{6,2},{7,3},{8,12},{9,13},{10,... | collective-permute-start | bytes 73736 | tf_op jit(solution)/shard_map/ppermute | solution.py:33
  109.5 33.6 %copy-start.125 = (pred[6]{0:T(512)(128)(4,1)S(1)}, pred[6]{0:T(512)(128)(4,1)}, u32[]{:S(2)}) copy-start(pred[6]{0:T(512)(128)(4,1)} %broadcast_in_dim.353) | copy-start | bytes 22
  109.5 40.3 %copy-start.107 = (pred[2]{0:T(512)(128)(4,1)S(1)}, pred[2]{0:T(512)(128)(4,1)}, u32[]{:S(2)}) copy-start(pred[2]{0:T(512)(128)(4,1)} %copy-done.106) | copy-start | bytes 10
  109.6 48.3 %copy-start.111 = (pred[2]{0:T(512)(128)(4,1)S(1)}, pred[2]{0:T(512)(128)(4,1)}, u32[]{:S(2)}) copy-start(pred[2]{0:T(512)(128)(4,1)} %copy-done.110) | copy-start | bytes 10
  113.5 28.9 %copy-start.12 = (f32[2,1024]{1,0:T(2,128)}, f32[2,1024]{1,0:T(2,128)S(1)}, u32[]{:S(2)}) copy-start(f32[2,1024]{1,0:T(2,128)S(1)} %get-tuple-element.75) | copy-start | bytes 24580
  113.6 12.9 %collective-permute-start.11 = (bf16[2,1024]{1,0:T(2,128)(2,1)S(1)}, bf16[2,1024]{1,0:T(2,128)(2,1)S(1)}, u32[]{:S(2)}, u32[]{:S(2)}) collective-permute-start(bf16[2,1024]{1,0:T(2,128)(2,1)S(1)} %multiply_convert_fusion.2), channel_id=1, source_target_pairs={{0,8},{8,16},{16,0},{24,32},{32,40},{40,24},{1,9},{9,17},{17,1},{2... | collective-permute-start | bytes 12296 | tf_op jit(solution)/shard_map/ppermute | solution.py:50
  119.6 8.9 %collective-permute-start.12 = (bf16[2,1024]{1,0:T(2,128)(2,1)S(1)}, bf16[2,1024]{1,0:T(2,128)(2,1)S(1)}, u32[]{:S(2)}, u32[]{:S(2)}) collective-permute-start(bf16[2,1024]{1,0:T(2,128)(2,1)S(1)} %multiply_convert_fusion.2), channel_id=1, source_target_pairs={{0,16},{8,0},{16,8},{24,40},{32,24},{40,32},{1,17},{9,1},{17,9},{2... | collective-permute-start | bytes 12296 | tf_op jit(solution)/shard_map/ppermute | solution.py:50
  129.4 13.0 %collective-permute-start.13 = (bf16[3,2,1024]{2,1,0:T(2,128)(2,1)S(1)}, bf16[3,2,1024]{2,1,0:T(2,128)(2,1)S(1)}, u32[]{:S(2)}, u32[]{:S(2)}) collective-permute-start(bf16[3,2,1024]{2,1,0:T(2,128)(2,1)S(1)} %broadcast_select_fusion.12), channel_id=1, source_target_pairs={{0,24},{8,32},{16,40},{24,0},{32,8},{40,16},{1,25},{9,33},{17,41},... | collective-permute-start | bytes 36872 | tf_op jit(solution)/shard_map/ppermute | solution.py:50
  143.2 5.7 %collective-permute-start.14 = (bf16[6,2,1024]{2,1,0:T(2,128)(2,1)S(1)}, bf16[6,2,1024]{2,1,0:T(2,128)(2,1)S(1)}, u32[]{:S(2)}, u32[]{:S(2)}) collective-permute-start(bf16[6,2,1024]{2,1,0:T(2,128)(2,1)S(1)} %broadcast_select_fusion.10), channel_id=1, source_target_pairs={{0,48},{48,0},{96,144},{144,96},{192,240},{240,192},{288,336},{336... | collective-permute-start | bytes 73736 | tf_op jit(solution)/shard_map/ppermute | solution.py:50
  149.9 6.9 %collective-permute-start.15 = (bf16[2,6,2,1024]{3,2,1,0:T(2,128)(2,1)S(1)}, bf16[2,6,2,1024]{3,2,1,0:T(2,128)(2,1)S(1)}, u32[]{:S(2)}, u32[]{:S(2)}) collective-permute-start(bf16[2,6,2,1024]{3,2,1,0:T(2,128)(2,1)S(1)} %broadcast_select_fusion.7), channel_id=1, source_target_pairs={{0,96},{48,144},{96,0},{144,48},{192,288},{240,336},{288,192},{336... | collective-permute-start | bytes 147464 | tf_op jit(solution)/shard_map/ppermute | solution.py:50
  158.0 10.5 %collective-permute-start.16 = (bf16[2,2,6,2,1024]{4,3,2,1,0:T(2,128)(2,1)S(1)}, bf16[2,2,6,2,1024]{4,3,2,1,0:T(2,128)(2,1)S(1)}, u32[]{:S(2)}, u32[]{:S(2)}) collective-permute-start(bf16[2,2,6,2,1024]{4,3,2,1,0:T(2,128)(2,1)S(1)} %broadcast_select_fusion.4), channel_id=1, source_target_pairs={{0,192},{48,240},{96,288},{144,336},{192,0},{240,48},{288,96},{336... | collective-permute-start | bytes 294920 | tf_op jit(solution)/shard_map/ppermute | solution.py:50
  170.1 9.1 %collective-permute-start.17 = (bf16[2,2,2,6,2,1024]{5,4,3,2,1,0:T(2,128)(2,1)S(1)}, bf16[2,2,2,6,2,1024]{5,4,3,2,1,0:T(2,128)(2,1)S(1)}, u32[]{:S(2)}, u32[]{:S(2)}) collective-permute-start(bf16[2,2,2,6,2,1024]{5,4,3,2,1,0:T(2,128)(2,1)S(1)} %broadcast_select_fusion.1), channel_id=1, source_target_pairs={{0,384},{48,432},{96,480},{144,528},{192,576},{240,624},{288,672},... | collective-permute-start | bytes 589832 | tf_op jit(solution)/shard_map/ppermute | solution.py:50
  206.2 15.9 %collective-permute-start.10 = (bf16[2,3,32,3072]{3,2,1,0:T(8,128)(2,1)}, bf16[2,3,32,3072]{3,2,1,0:T(8,128)(2,1)S(1)}, u32[]{:S(2)}, u32[]{:S(2)}) collective-permute-start(bf16[2,3,32,3072]{3,2,1,0:T(8,128)(2,1)} %get-tuple-element.14), channel_id=1, source_target_pairs={{1,0},{2,1},{3,2},{4,3},{5,4},{6,5},{7,6},{9,8},{10,9},{11,10},{12... | collective-permute-start | bytes 3538952 | tf_op jit(solution)/shard_map/ppermute | solution.py:24
  208.2 28.7 %collective-permute-start.9 = (bf16[2,3,32,3072]{3,2,1,0:T(8,128)(2,1)}, bf16[2,3,32,3072]{3,2,1,0:T(8,128)(2,1)S(1)}, u32[]{:S(2)}, u32[]{:S(2)}) collective-permute-start(bf16[2,3,32,3072]{3,2,1,0:T(8,128)(2,1)} %get-tuple-element.13), channel_id=1, source_target_pairs={{0,1},{1,2},{2,3},{3,4},{4,5},{5,6},{6,7},{8,9},{9,10},{10,11},{11... | collective-permute-start | bytes 3538952 | tf_op jit(solution)/shard_map/ppermute | solution.py:23
  213.0 27.4 %copy-start.20 = (f32[1,1,3072]{2,1,0:T(1,128)S(1)}, f32[1,1,3072]{2,1,0:T(1,128)}, u32[]{:S(2)}) copy-start(f32[1,1,3072]{2,1,0:T(1,128)} %copy-done.19) | copy-start | bytes 36868
  213.0 27.4 %copy-start.22 = (f32[1,1,3072]{2,1,0:T(1,128)S(1)}, f32[1,1,3072]{2,1,0:T(1,128)}, u32[]{:S(2)}) copy-start(f32[1,1,3072]{2,1,0:T(1,128)} %copy-done.21) | copy-start | bytes 36868
  213.0 27.4 %copy-start.24 = (f32[1,1,3072]{2,1,0:T(1,128)S(1)}, f32[1,1,3072]{2,1,0:T(1,128)}, u32[]{:S(2)}) copy-start(f32[1,1,3072]{2,1,0:T(1,128)} %copy-done.23) | copy-start | bytes 36868
  213.1 27.4 %copy-start.26 = (f32[1,1,3072]{2,1,0:T(1,128)S(1)}, f32[1,1,3072]{2,1,0:T(1,128)}, u32[]{:S(2)}) copy-start(f32[1,1,3072]{2,1,0:T(1,128)} %copy-done.25) | copy-start | bytes 36868
  213.1 27.4 %copy-start.28 = (f32[1,1,3072]{2,1,0:T(1,128)S(1)}, f32[1,1,3072]{2,1,0:T(1,128)}, u32[]{:S(2)}) copy-start(f32[1,1,3072]{2,1,0:T(1,128)} %copy-done.27) | copy-start | bytes 36868
  213.1 27.4 %copy-start.30 = (f32[1,1,3072]{2,1,0:T(1,128)S(1)}, f32[1,1,3072]{2,1,0:T(1,128)}, u32[]{:S(2)}) copy-start(f32[1,1,3072]{2,1,0:T(1,128)} %copy-done.29) | copy-start | bytes 36868
  213.1 27.4 %copy-start.32 = (f32[1,1,3072]{2,1,0:T(1,128)S(1)}, f32[1,1,3072]{2,1,0:T(1,128)}, u32[]{:S(2)}) copy-start(f32[1,1,3072]{2,1,0:T(1,128)} %copy-done.31) | copy-start | bytes 36868
  213.1 27.4 %copy-start.34 = (f32[1,1,3072]{2,1,0:T(1,128)S(1)}, f32[1,1,3072]{2,1,0:T(1,128)}, u32[]{:S(2)}) copy-start(f32[1,1,3072]{2,1,0:T(1,128)} %copy-done.33) | copy-start | bytes 36868
  213.1 27.4 %copy-start.36 = (f32[1,1,3072]{2,1,0:T(1,128)S(1)}, f32[1,1,3072]{2,1,0:T(1,128)}, u32[]{:S(2)}) copy-start(f32[1,1,3072]{2,1,0:T(1,128)} %get-tuple-element.19) | copy-start | bytes 36868
  213.1 27.4 %copy-start.38 = (f32[1,1,3072]{2,1,0:T(1,128)S(1)}, f32[1,1,3072]{2,1,0:T(1,128)}, u32[]{:S(2)}) copy-start(f32[1,1,3072]{2,1,0:T(1,128)} %get-tuple-element.20) | copy-start | bytes 36868
  (105 other events, 1346.6 us)

commit v4 on v3

--- a/solution.py
+++ b/solution.py
@@ -110,17 +110,18 @@
     conved = depthwise_rows(section_map, dw_kernel) + conv_bias
     section_out = section_map.astype(jnp.float32) + layer_scale * cell_norm(conved, ln_gain)
     partial_value = jnp.sum(section_out, axis=(1, 2)) / (H * W)
+    text_f = texts.astype(jnp.float32)
+    text_vec = unit_rows(text_f).astype(jnp.bfloat16)
+    text_count = texts.shape[0]
+    text_vec, partial_value = lax.optimization_barrier((text_vec, partial_value))
+    text_all = gather_stages(text_vec, "dp", radix_split(dp_count)).reshape(
+        dp_count * text_count, -1
+    )
+    count = text_all.shape[0]
     pooled = group_sum(partial_value)
     head_in = cell_norm(pooled, head_gain).astype(jnp.bfloat16)
     embed = jnp.dot(head_in, head_weight, preferred_element_type=jnp.float32)
     image_vec = unit_rows(embed).astype(jnp.bfloat16)
-    text_f = texts.astype(jnp.float32)
-    text_vec = unit_rows(text_f).astype(jnp.bfloat16)
-    text_count = texts.shape[0]
-    text_all = gather_stages(text_vec, "dp", radix_split(dp_count)).reshape(
-        dp_count * text_count, -1
-    )
-    count = text_all.shape[0]
     source_table = (sources[:, None] == jnp.arange(SOURCES)[None, :]).astype(jnp.float32)
     weights = (
         SOURCES
@@ -140,29 +141,6 @@
         own_weights[:, None] * -own_labels * jax.nn.sigmoid(-own_labels * own_logits)
     ).astype(jnp.bfloat16)
     image_dir = LOGIT_SCALE * jnp.dot(own_pair, text_all, preferred_element_type=jnp.float32)
-    gathered = gather_stages(image_vec, "img", radix_split(img_count))
-    gathered = gather_stages(gathered, "dp", radix_split(dp_count))
-    image_all = jnp.transpose(gathered, (0, 2, 1, 3)).reshape(
-        dp_count * batch_rows * img_count, -1
-    )
-    logits = (
-        LOGIT_SCALE * jnp.dot(image_all, text_all.T, preferred_element_type=jnp.float32)
-        + LOGIT_BIAS
-    )
-    labels = jnp.where(positives[:, None] == jnp.arange(count)[None, :], 1.0, -1.0).astype(
-        jnp.float32
-    )
-    row_loss = lax.optimization_barrier(jnp.sum(jax.nn.softplus(-labels * logits), axis=1))
-    group_sums = jnp.sum(source_table * (weights * row_loss)[:, None], axis=0)
-    pair_grad = (weights[:, None] * -labels * jax.nn.sigmoid(-labels * logits)).astype(
-        jnp.bfloat16
-    )
-    text_pair = lax.dynamic_slice_in_dim(pair_grad, dp_at * text_count, text_count, axis=1)
-    text_dir = LOGIT_SCALE * lax.dot_general(
-        text_pair, image_all, (((0,), (0,)), ((), ())), preferred_element_type=jnp.float32
-    )
-    text_back = jax.vjp(unit_rows, text_f)[1]
-    text_grad = text_back(text_dir)[0]
     embed_back = jax.vjp(unit_rows, embed)[1]
     embed_grad = embed_back(image_dir)[0].astype(jnp.bfloat16)
     head_grad = jnp.dot(embed_grad, head_weight.T, preferred_element_type=jnp.float32)
@@ -171,6 +149,30 @@
     norm_back = jax.vjp(lambda values: cell_norm(values, ln_gain), conved)[1]
     seeded = jnp.broadcast_to((layer_scale * own_grad)[:, None, None, :], conved.shape)
     conv_grad = norm_back(seeded)[0].astype(jnp.bfloat16)
+    image_vec, conv_grad = lax.optimization_barrier((image_vec, conv_grad))
+    gathered = gather_stages(image_vec, "img", radix_split(img_count))
+    gathered = gather_stages(gathered, "dp", radix_split(dp_count))
+    image_all = jnp.transpose(gathered, (0, 2, 1, 3)).reshape(
+        dp_count * batch_rows * img_count, -1
+    )
+    logits = (
+        LOGIT_SCALE * jnp.dot(image_all, text_all.T, preferred_element_type=jnp.float32)
+        + LOGIT_BIAS
+    )
+    labels = jnp.where(positives[:, None] == jnp.arange(count)[None, :], 1.0, -1.0).astype(
+        jnp.float32
+    )
+    row_loss = lax.optimization_barrier(jnp.sum(jax.nn.softplus(-labels * logits), axis=1))
+    group_sums = jnp.sum(source_table * (weights * row_loss)[:, None], axis=0)
+    pair_grad = (weights[:, None] * -labels * jax.nn.sigmoid(-labels * logits)).astype(
+        jnp.bfloat16
+    )
+    text_pair = lax.dynamic_slice_in_dim(pair_grad, dp_at * text_count, text_count, axis=1)
+    text_dir = LOGIT_SCALE * lax.dot_general(
+        text_pair, image_all, (((0,), (0,)), ((), ())), preferred_element_type=jnp.float32
+    )
+    text_back = jax.vjp(unit_rows, text_f)[1]
+    text_grad = text_back(text_dir)[0]
     spread = depthwise_rows(conv_grad, dw_kernel[::-1, ::-1, :])
     grad_map = (own_grad[:, None, None, :] + spread).astype(jnp.bfloat16)
     return (grad_map, text_grad, group_sums)

time: 268 us -> 267 us (level)
  the two profiles are of different devices: /device:TPU:6 before, /device:TPU:120 now
where the time goes in v4:
time: 267 us; the launch traced here: 265 us
  other arithmetic  90.9 us (34%)
  starting transfers between devices  80.4 us (30%)
  waiting for transfers between devices  46.8 us (18%)
  local copies, waits for them, and re-layouts  30.4 us (11%)
  matrix products  13.1 us (5%)
  between operations  3.64 us (1%)
    ppermute x11, starting transfers between devices, gather_stages(): got.append(lax.ppermute(value, axis, pairs))  50 us
    ppermute x11, waiting for transfers between devices, gather_stages(): got.append(lax.ppermute(value, axis, pairs))  46.1 us
    reduce_sum x4, other arithmetic, cell_norm(): center = values - jnp.mean(values, axis=-1, keepdims=True)  29.3 us
    convert_element_type x1, other arithmetic, local(): grad_map = (own_grad[:, None, None, :] + spread).astype(jnp.bfloat16)  25.8 us
    ppermute x3, starting transfers between devices, group_sum(): value = value + lax.ppermute(value, 'row', pairs)  17.3 us
    gather x12, local copies, waits for them, and re-layouts, gather_stages(): value = jnp.take(stacked, order, axis=0)  13.1 us
    ppermute x2, starting transfers between devices, halo_rows(): after = lax.ppermute(leading, 'row', down)  9.08 us
    select_n x24, other arithmetic, gather_stages(): value = jnp.take(stacked, order, axis=0)  8.06 us
  transfers between devices with their start and end apart: 18, of which 9 were waited for; matrix products, arithmetic and copies ran while one was open for 16% of the time, Pallas kernels for 0%

profile of v4, /device:TPU:120, one launch (start us, length us, event | category | flops | bytes accessed | tf_op | source)
XLA Modules:
  0.0 265.2 jit_solution(7656042972698629864)
XLA Ops:
  0.7 3.2 %fusion.108 = (bf16[2,3,32,3072]{3,2,1,0:T(8,128)(2,1)}, bf16[2,3,32,3072]{3,2,1,0:T(8,128)(2,1)}) fusion(bf16[2,4,32,3072]{3,2,1,0:T(8,128)(2,1)} %param.11), kind=kLoop, calls=%fused_computation.317 | loop fusion | bytes 4718592 | tf_op jit(solution)/shard_map/slice | solution.py:21
  3.9 2.0 collective-permute-start
  6.0 4.5 %collective-permute-start.1 = (bf16[2,3,32,3072]{3,2,1,0:T(8,128)(2,1)}, bf16[2,3,32,3072]{3,2,1,0:T(8,128)(2,1)}, u32[]{:S(2)}, u32[]{:S(2)}) collective-permute-start(bf16[2,3,32,3072]{3,2,1,0:T(8,128)(2,1)} %get-tuple-element.26), channel_id=1, source_target_pairs={{1,0},{2,1},{3,2},{4,3},{5,4},{6,5},{7,6},{9,8},{10,9},{11,10},{12... | collective-permute-start | bytes 3538952 | tf_op jit(solution)/shard_map/ppermute | solution.py:24
  24.6 3.4 %select_maximum_fusion.2 = bf16[2,10,38,3072]{3,2,1,0:T(8,128)(2,1)S(1)} fusion(bf16[2,3,32,3072]{3,2,1,0:T(8,128)(2,1)} %collective-permute-done.1, bf16[2,4,32,3072]{3,2,1,0:T(8,128)(2,1)S(1)} %copy-done.1, bf16[2,3,32,3072]{3,2,1,0:T(8,128)(2,1)S(1)} %collective-permute-done), kind=kLoop, calls=%fused_computation.17 | loop fusion | flops 28016640 | bytes 8601600 | tf_op jit(solution)/shard_map/concatenate | solution.py:25
  28.0 1.5 constant_dynamic-update-slice_fusion.2
  30.0 27.4 %fusion.105 = (f32[2,4,32]{2,1,0:T(4,128)S(1)}, f32[2,4,32,3072]{3,2,1,0:T(8,128)S(1)}) fusion(f32[3072]{0:T(1024)S(1)} %copy-done.103, f32[3072]{0:T(1024)S(1)} %bitcast.128, bf16[2,10,38,3072]{3,2,1,0:T(8,128)(2,1)S(1)} %select_maximum_fusion.2, f32[3072]{0:T(1024)S(1)} %bitcast.130, f32[3072]{0:T(1024)S(1)} %bitcast.134, f32[3072]{0:T(1024)S(1)} %bitcast.136, ...), kind=kLoop, calls=%fused_computation.315 | loop fusion | flops 116391680 | bytes 80831488 | tf_op jit(solution)/shard_map/reduce_sum | solution.py:69
  58.5 1.0 fusion.27
  59.5 12.5 %collective-permute-start.2 = (f32[2,3072]{1,0:T(2,128)S(1)}, f32[2,3072]{1,0:T(2,128)S(1)}, u32[]{:S(2)}, u32[]{:S(2)}) collective-permute-start(f32[2,3072]{1,0:T(2,128)S(1)} %broadcast_multiply_fusion.1), channel_id=1, source_target_pairs={{0,1},{1,0},{2,3},{3,2},{4,5},{5,4},{6,7},{7,6},{8,9},{9,8},{10,11... | collective-permute-start | bytes 73736 | tf_op jit(solution)/shard_map/ppermute | solution.py:33
  72.1 3.3 %collective-permute-start.5 = (bf16[12,1024]{1,0:T(8,128)(2,1)S(1)}, bf16[12,1024]{1,0:T(8,128)(2,1)S(1)}, u32[]{:S(2)}, u32[]{:S(2)}) collective-permute-start(bf16[12,1024]{1,0:T(8,128)(2,1)S(1)} %fusion.50), channel_id=1, source_target_pairs={{0,48},{48,0},{96,144},{144,96},{192,240},{240,192},{288,336},{336... | collective-permute-start | bytes 73736 | tf_op jit(solution)/shard_map/ppermute | solution.py:50
  79.3 1.9 collective-permute-start.3
  82.7 4.0 %collective-permute-start.6 = (bf16[2,12,1024]{2,1,0:T(8,128)(2,1)S(1)}, bf16[2,12,1024]{2,1,0:T(8,128)(2,1)S(1)}, u32[]{:S(2)}, u32[]{:S(2)}) collective-permute-start(bf16[2,12,1024]{2,1,0:T(8,128)(2,1)S(1)} %broadcast_select_fusion.9), channel_id=1, source_target_pairs={{0,96},{48,144},{96,0},{144,48},{192,288},{240,336},{288,192},{336... | collective-permute-start | bytes 147464 | tf_op jit(solution)/shard_map/ppermute | solution.py:50
  87.5 2.9 %collective-permute-start.4 = (f32[2,3072]{1,0:T(2,128)S(1)}, f32[2,3072]{1,0:T(2,128)}, u32[]{:S(2)}, u32[]{:S(2)}) collective-permute-start(f32[2,3072]{1,0:T(2,128)S(1)} %add.755), channel_id=1, source_target_pairs={{0,4},{1,5},{2,6},{3,7},{4,0},{5,1},{6,2},{7,3},{8,12},{9,13},{10,... | collective-permute-start | bytes 73736 | tf_op jit(solution)/shard_map/ppermute | solution.py:33
  93.3 0.9 fusion.104
  95.0 3.9 %multiply_reduce_fusion.4 = (f32[2]{0:T(128)S(1)}, f32[2,1024]{1,0:T(2,128)S(1)}) fusion(bf16[3072,1024]{1,0:T(8,128)(2,1)} %param.17, f32[2]{0:T(128)S(1)} %fusion.95, f32[3072]{0:T(1024)} %param.16, f32[2,3072]{1,0:T(2,128)S(1)} %get-tuple-element.16, f32[2]{0:T(128)S(1)} %broadcast_multiply_fusion.5), kind=kOutput, calls=%fused_computation.198 | convolution fusion | flops 12611582 | bytes 6336536 | tf_op jit(solution)/shard_map/dot_general | solution.py:123
  99.4 3.5 %collective-permute-start.7 = (bf16[2,2,12,1024]{3,2,1,0:T(8,128)(2,1)S(1)}, bf16[2,2,12,1024]{3,2,1,0:T(8,128)(2,1)S(1)}, u32[]{:S(2)}, u32[]{:S(2)}) collective-permute-start(bf16[2,2,12,1024]{3,2,1,0:T(8,128)(2,1)S(1)} %broadcast_select_fusion.6), channel_id=1, source_target_pairs={{0,192},{48,240},{96,288},{144,336},{192,0},{240,48},{288,96},{336... | collective-permute-start | bytes 294920 | tf_op jit(solution)/shard_map/ppermute | solution.py:50
  103.5 8.3 %collective-permute-done.7 = bf16[2,2,12,1024]{3,2,1,0:T(8,128)(2,1)S(1)} collective-permute-done((bf16[2,2,12,1024]{3,2,1,0:T(8,128)(2,1)S(1)}, bf16[2,2,12,1024]{3,2,1,0:T(8,128)(2,1)S(1)}, u32[]{:S(2)}, u32[]{:S(2)}) %collective-permute-start.7) | collective-permute-done | bytes 98336 | tf_op jit(solution)/shard_map/ppermute | solution.py:50
  112.6 1.6 gather_fusion.4
  115.0 4.9 %collective-permute-start.8 = (bf16[2,2,2,12,1024]{4,3,2,1,0:T(8,128)(2,1)S(1)}, bf16[2,2,2,12,1024]{4,3,2,1,0:T(8,128)(2,1)S(1)}, u32[]{:S(2)}, u32[]{:S(2)}) collective-permute-start(bf16[2,2,2,12,1024]{4,3,2,1,0:T(8,128)(2,1)S(1)} %broadcast_select_fusion.3), channel_id=1, source_target_pairs={{0,384},{48,432},{96,480},{144,528},{192,576},{240,624},{288,672},... | collective-permute-start | bytes 589832 | tf_op jit(solution)/shard_map/ppermute | solution.py:50
  120.7 4.3 %collective-permute-done.8 = bf16[2,2,2,12,1024]{4,3,2,1,0:T(8,128)(2,1)S(1)} collective-permute-done((bf16[2,2,2,12,1024]{4,3,2,1,0:T(8,128)(2,1)S(1)}, bf16[2,2,2,12,1024]{4,3,2,1,0:T(8,128)(2,1)S(1)}, u32[]{:S(2)}, u32[]{:S(2)}) %collective-permute-start.8) | collective-permute-done | bytes 196640 | tf_op jit(solution)/shard_map/ppermute | solution.py:50
  125.9 2.5 gather_fusion.5
  128.4 1.9 gather.79
  130.3 1.8 multiply_reduce_fusion.3
  132.7 4.6 %multiply_reduce_fusion.1 = (f32[2]{0:T(128)S(1)}, f32[2,3072]{1,0:T(2,128)S(1)}) fusion(f32[2,3072]{1,0:T(2,128)S(1)} %get-tuple-element.16, f32[2]{0:T(128)} %copy-done.104, f32[3072]{0:T(1024)S(1)} %copy-done.95, bf16[3072,1024]{1,0:T(8,128)(2,1)} %param.17, f32[2,1024]{1,0:T(2,128)S(1)} %copy-done.94, f32[2,1024]{1,0:T(2,128)S(1)} %get-tuple-element.85, ...), kind=kOutput, calls=%fused_computation.115 | convolution fusion | flops 12617726 | bytes 6369312 | tf_op jit(solution)/shard_map/dot_general | solution.py:146
  139.1 1.1 add_convert_fusion.1
  140.2 11.0 %collective-permute-start.12 = (bf16[2,1024]{1,0:T(2,128)(2,1)S(1)}, bf16[2,1024]{1,0:T(2,128)(2,1)S(1)}, u32[]{:S(2)}, u32[]{:S(2)}) collective-permute-start(bf16[2,1024]{1,0:T(2,128)(2,1)S(1)} %copy-done.100), channel_id=1, source_target_pairs={{0,16},{8,0},{16,8},{24,40},{32,24},{40,32},{1,17},{9,1},{17,9},{2... | collective-permute-start | bytes 12296 | tf_op jit(solution)/shard_map/ppermute | solution.py:50
  151.3 1.9 collective-permute-start.11
  153.2 1.6 fusion.107
  156.4 1.9 collective-permute-start.9
  158.4 4.5 %collective-permute-start.10 = (bf16[2,3,32,3072]{3,2,1,0:T(8,128)(2,1)}, bf16[2,3,32,3072]{3,2,1,0:T(8,128)(2,1)}, u32[]{:S(2)}, u32[]{:S(2)}) collective-permute-start(bf16[2,3,32,3072]{3,2,1,0:T(8,128)(2,1)} %get-tuple-element.22), channel_id=1, source_target_pairs={{1,0},{2,1},{3,2},{4,3},{5,4},{6,5},{7,6},{9,8},{10,9},{11,10},{12... | collective-permute-start | bytes 3538952 | tf_op jit(solution)/shard_map/ppermute | solution.py:24
  163.8 10.1 %collective-permute-start.13 = (bf16[3,2,1024]{2,1,0:T(2,128)(2,1)S(1)}, bf16[3,2,1024]{2,1,0:T(2,128)(2,1)S(1)}, u32[]{:S(2)}, u32[]{:S(2)}) collective-permute-start(bf16[3,2,1024]{2,1,0:T(2,128)(2,1)S(1)} %broadcast_select_fusion.12), channel_id=1, source_target_pairs={{0,24},{8,32},{16,40},{24,0},{32,8},{40,16},{1,25},{9,33},{17,41},... | collective-permute-start | bytes 36872 | tf_op jit(solution)/shard_map/ppermute | solution.py:50
  174.0 12.0 %collective-permute-done.13 = bf16[3,2,1024]{2,1,0:T(2,128)(2,1)S(1)} collective-permute-done((bf16[3,2,1024]{2,1,0:T(2,128)(2,1)S(1)}, bf16[3,2,1024]{2,1,0:T(2,128)(2,1)S(1)}, u32[]{:S(2)}, u32[]{:S(2)}) %collective-permute-start.13) | collective-permute-done | bytes 12320 | tf_op jit(solution)/shard_map/ppermute | solution.py:50
  186.9 2.6 collective-permute-start.14
  189.6 3.2 %collective-permute-done.14 = bf16[6,2,1024]{2,1,0:T(2,128)(2,1)S(1)} collective-permute-done((bf16[6,2,1024]{2,1,0:T(2,128)(2,1)S(1)}, bf16[6,2,1024]{2,1,0:T(2,128)(2,1)S(1)}, u32[]{:S(2)}, u32[]{:S(2)}) %collective-permute-start.14) | collective-permute-done | bytes 24608 | tf_op jit(solution)/shard_map/ppermute | solution.py:50
  194.5 1.9 collective-permute-start.15
  197.2 4.6 %collective-permute-done.15 = bf16[2,6,2,1024]{3,2,1,0:T(2,128)(2,1)S(1)} collective-permute-done((bf16[2,6,2,1024]{3,2,1,0:T(2,128)(2,1)S(1)}, bf16[2,6,2,1024]{3,2,1,0:T(2,128)(2,1)S(1)}, u32[]{:S(2)}, u32[]{:S(2)}) %collective-permute-start.15) | collective-permute-done | bytes 49184 | tf_op jit(solution)/shard_map/ppermute | solution.py:50
  201.9 0.9 gather_fusion.9
  203.0 2.0 collective-permute-start.16
  205.1 9.3 %collective-permute-done.16 = bf16[2,2,6,2,1024]{4,3,2,1,0:T(2,128)(2,1)S(1)} collective-permute-done((bf16[2,2,6,2,1024]{4,3,2,1,0:T(2,128)(2,1)S(1)}, bf16[2,2,6,2,1024]{4,3,2,1,0:T(2,128)(2,1)S(1)}, u32[]{:S(2)}, u32[]{:S(2)}) %collective-permute-start.16) | collective-permute-done | bytes 98336 | tf_op jit(solution)/shard_map/ppermute | solution.py:50
  214.7 1.1 gather_fusion.10
  216.1 4.8 %collective-permute-start.17 = (bf16[2,2,2,6,2,1024]{5,4,3,2,1,0:T(2,128)(2,1)S(1)}, bf16[2,2,2,6,2,1024]{5,4,3,2,1,0:T(2,128)(2,1)S(1)}, u32[]{:S(2)}, u32[]{:S(2)}) collective-permute-start(bf16[2,2,2,6,2,1024]{5,4,3,2,1,0:T(2,128)(2,1)S(1)} %broadcast_select_fusion.1), channel_id=1, source_target_pairs={{0,384},{48,432},{96,480},{144,528},{192,576},{240,624},{288,672},... | collective-permute-start | bytes 589832 | tf_op jit(solution)/shard_map/ppermute | solution.py:50
  221.1 4.1 %collective-permute-done.17 = bf16[2,2,2,6,2,1024]{5,4,3,2,1,0:T(2,128)(2,1)S(1)} collective-permute-done((bf16[2,2,2,6,2,1024]{5,4,3,2,1,0:T(2,128)(2,1)S(1)}, bf16[2,2,2,6,2,1024]{5,4,3,2,1,0:T(2,128)(2,1)S(1)}, u32[]{:S(2)}, u32[]{:S(2)}) %collective-permute-start.17) | collective-permute-done | bytes 196640 | tf_op jit(solution)/shard_map/ppermute | solution.py:50
  225.7 1.5 gather_fusion.11
  227.4 0.9 reshape.937
  228.3 1.5 fusion.46
  231.2 1.3 fusion.51
  234.2 3.5 %select_maximum_fusion = bf16[2,10,38,3072]{3,2,1,0:T(8,128)(2,1)S(1)} fusion(bf16[2,3,32,3072]{3,2,1,0:T(8,128)(2,1)} %collective-permute-done.10, bf16[2,4,32,3072]{3,2,1,0:T(8,128)(2,1)S(1)} %copy-done.4, bf16[2,3,32,3072]{3,2,1,0:T(8,128)(2,1)S(1)} %collective-permute-done.9), kind=kLoop, calls=%fused_computation.15 | loop fusion | flops 28016640 | bytes 8601600 | tf_op jit(solution)/shard_map/concatenate | solution.py:25
  237.6 1.4 constant_dynamic-update-slice_fusion.6
  239.4 25.8 %add_convert_fusion = bf16[2,4,32,3072]{3,2,1,0:T(8,128)(2,1)} fusion(bf16[2,4,32,3072]{3,2,1,0:T(8,128)(2,1)S(1)} %copy-done.4, bf16[2,10,38,3072]{3,2,1,0:T(8,128)(2,1)S(1)} %select_maximum_fusion, bf16[2,7,32,3072]{3,2,1,0:T(8,128)(2,1)S(1)} %constant_dynamic-update-slice_fusion.6, bf16[2,7,32,3072]{3,2,1,0:T(8,128)(2,1)S(1)} %get-tuple-element.19, ...), kind=kLoop, calls=%fused_computation.53 | loop fusion | flops 116391936 | bytes 79269888 | tf_op jit(solution)/shard_map/convert_element_type | solution.py:177
  (351 shorter events, 41.1 us)
Async XLA Ops:
  0.7 16.8 %copy-start.106 = (s32[192]{0:T(256)S(1)}, s32[192]{0:T(256)}, u32[]{:S(2)}) copy-start(s32[192]{0:T(256)} %param.20) | copy-start | bytes 2308
  0.7 20.5 %copy-start = (s32[192]{0:T(256)S(1)}, s32[192]{0:T(256)}, u32[]{:S(2)}) copy-start(s32[192]{0:T(256)} %param.19) | copy-start | bytes 2308
  3.9 20.1 %copy-start.1 = (bf16[2,4,32,3072]{3,2,1,0:T(8,128)(2,1)S(1)}, bf16[2,4,32,3072]{3,2,1,0:T(8,128)(2,1)}, u32[]{:S(2)}) copy-start(bf16[2,4,32,3072]{3,2,1,0:T(8,128)(2,1)} %param.11) | copy-start | bytes 4718596
  3.9 20.0 %collective-permute-start = (bf16[2,3,32,3072]{3,2,1,0:T(8,128)(2,1)}, bf16[2,3,32,3072]{3,2,1,0:T(8,128)(2,1)S(1)}, u32[]{:S(2)}, u32[]{:S(2)}) collective-permute-start(bf16[2,3,32,3072]{3,2,1,0:T(8,128)(2,1)} %get-tuple-element.25), channel_id=1, source_target_pairs={{0,1},{1,2},{2,3},{3,4},{4,5},{5,6},{6,7},{8,9},{9,10},{10,11},{11... | collective-permute-start | bytes 3538952 | tf_op jit(solution)/shard_map/ppermute | solution.py:23
  6.0 18.6 %collective-permute-start.1 = (bf16[2,3,32,3072]{3,2,1,0:T(8,128)(2,1)}, bf16[2,3,32,3072]{3,2,1,0:T(8,128)(2,1)}, u32[]{:S(2)}, u32[]{:S(2)}) collective-permute-start(bf16[2,3,32,3072]{3,2,1,0:T(8,128)(2,1)} %get-tuple-element.26), channel_id=1, source_target_pairs={{1,0},{2,1},{3,2},{4,3},{5,4},{6,5},{7,6},{9,8},{10,9},{11,10},{12... | collective-permute-start | bytes 3538952 | tf_op jit(solution)/shard_map/ppermute | solution.py:24
  12.0 17.5 %copy-start.9 = (f32[1,1,3072]{2,1,0:T(1,128)}, f32[1,1,3072]{2,1,0:T(1,128)S(1)}, u32[]{:S(2)}) copy-start(f32[1,1,3072]{2,1,0:T(1,128)S(1)} %get-tuple-element.70) | copy-start | bytes 36868
  12.0 17.5 %copy-start.11 = (f32[1,1,3072]{2,1,0:T(1,128)}, f32[1,1,3072]{2,1,0:T(1,128)S(1)}, u32[]{:S(2)}) copy-start(f32[1,1,3072]{2,1,0:T(1,128)S(1)} %get-tuple-element.71) | copy-start | bytes 36868
  12.1 17.5 %copy-start.13 = (f32[1,1,3072]{2,1,0:T(1,128)}, f32[1,1,3072]{2,1,0:T(1,128)S(1)}, u32[]{:S(2)}) copy-start(f32[1,1,3072]{2,1,0:T(1,128)S(1)} %get-tuple-element.72) | copy-start | bytes 36868
  12.1 17.5 %copy-start.15 = (f32[1,1,3072]{2,1,0:T(1,128)}, f32[1,1,3072]{2,1,0:T(1,128)S(1)}, u32[]{:S(2)}) copy-start(f32[1,1,3072]{2,1,0:T(1,128)S(1)} %get-tuple-element.73) | copy-start | bytes 36868
  12.1 17.5 %copy-start.17 = (f32[1,1,3072]{2,1,0:T(1,128)}, f32[1,1,3072]{2,1,0:T(1,128)S(1)}, u32[]{:S(2)}) copy-start(f32[1,1,3072]{2,1,0:T(1,128)S(1)} %get-tuple-element.74) | copy-start | bytes 36868
  12.1 17.5 %copy-start.19 = (f32[1,1,3072]{2,1,0:T(1,128)}, f32[1,1,3072]{2,1,0:T(1,128)S(1)}, u32[]{:S(2)}) copy-start(f32[1,1,3072]{2,1,0:T(1,128)S(1)} %get-tuple-element.75) | copy-start | bytes 36868
  12.9 16.7 %copy-start.21 = (f32[1,1,3072]{2,1,0:T(1,128)}, f32[1,1,3072]{2,1,0:T(1,128)S(1)}, u32[]{:S(2)}) copy-start(f32[1,1,3072]{2,1,0:T(1,128)S(1)} %get-tuple-element.27) | copy-start | bytes 36868
  12.9 16.7 %copy-start.23 = (f32[1,1,3072]{2,1,0:T(1,128)}, f32[1,1,3072]{2,1,0:T(1,128)S(1)}, u32[]{:S(2)}) copy-start(f32[1,1,3072]{2,1,0:T(1,128)S(1)} %get-tuple-element.28) | copy-start | bytes 36868
  12.9 16.7 %copy-start.25 = (f32[1,1,3072]{2,1,0:T(1,128)}, f32[1,1,3072]{2,1,0:T(1,128)S(1)}, u32[]{:S(2)}) copy-start(f32[1,1,3072]{2,1,0:T(1,128)S(1)} %get-tuple-element.29) | copy-start | bytes 36868
  12.9 16.7 %copy-start.27 = (f32[1,1,3072]{2,1,0:T(1,128)}, f32[1,1,3072]{2,1,0:T(1,128)S(1)}, u32[]{:S(2)}) copy-start(f32[1,1,3072]{2,1,0:T(1,128)S(1)} %get-tuple-element.30) | copy-start | bytes 36868
  12.9 16.7 %copy-start.29 = (f32[1,1,3072]{2,1,0:T(1,128)}, f32[1,1,3072]{2,1,0:T(1,128)S(1)}, u32[]{:S(2)}) copy-start(f32[1,1,3072]{2,1,0:T(1,128)S(1)} %get-tuple-element.31) | copy-start | bytes 36868
  12.9 16.7 %copy-start.31 = (f32[1,1,3072]{2,1,0:T(1,128)}, f32[1,1,3072]{2,1,0:T(1,128)S(1)}, u32[]{:S(2)}) copy-start(f32[1,1,3072]{2,1,0:T(1,128)S(1)} %get-tuple-element.32) | copy-start | bytes 36868
  12.9 16.7 %copy-start.33 = (f32[1,1,3072]{2,1,0:T(1,128)}, f32[1,1,3072]{2,1,0:T(1,128)S(1)}, u32[]{:S(2)}) copy-start(f32[1,1,3072]{2,1,0:T(1,128)S(1)} %get-tuple-element.33) | copy-start | bytes 36868
  12.9 16.7 %copy-start.35 = (f32[1,1,3072]{2,1,0:T(1,128)}, f32[1,1,3072]{2,1,0:T(1,128)S(1)}, u32[]{:S(2)}) copy-start(f32[1,1,3072]{2,1,0:T(1,128)S(1)} %get-tuple-element.34) | copy-start | bytes 36868
  12.9 16.7 %copy-start.37 = (f32[1,1,3072]{2,1,0:T(1,128)}, f32[1,1,3072]{2,1,0:T(1,128)S(1)}, u32[]{:S(2)}) copy-start(f32[1,1,3072]{2,1,0:T(1,128)S(1)} %get-tuple-element.35) | copy-start | bytes 36868
  12.9 16.7 %copy-start.39 = (f32[1,1,3072]{2,1,0:T(1,128)}, f32[1,1,3072]{2,1,0:T(1,128)S(1)}, u32[]{:S(2)}) copy-start(f32[1,1,3072]{2,1,0:T(1,128)S(1)} %get-tuple-element.36) | copy-start | bytes 36868
  12.9 16.7 %copy-start.41 = (f32[1,1,3072]{2,1,0:T(1,128)}, f32[1,1,3072]{2,1,0:T(1,128)S(1)}, u32[]{:S(2)}) copy-start(f32[1,1,3072]{2,1,0:T(1,128)S(1)} %get-tuple-element.37) | copy-start | bytes 36868
  12.9 16.7 %copy-start.43 = (f32[1,1,3072]{2,1,0:T(1,128)}, f32[1,1,3072]{2,1,0:T(1,128)S(1)}, u32[]{:S(2)}) copy-start(f32[1,1,3072]{2,1,0:T(1,128)S(1)} %get-tuple-element.38) | copy-start | bytes 36868
  13.0 16.7 %copy-start.45 = (f32[1,1,3072]{2,1,0:T(1,128)}, f32[1,1,3072]{2,1,0:T(1,128)S(1)}, u32[]{:S(2)}) copy-start(f32[1,1,3072]{2,1,0:T(1,128)S(1)} %get-tuple-element.39) | copy-start | bytes 36868
  13.0 16.7 %copy-start.47 = (f32[1,1,3072]{2,1,0:T(1,128)}, f32[1,1,3072]{2,1,0:T(1,128)S(1)}, u32[]{:S(2)}) copy-start(f32[1,1,3072]{2,1,0:T(1,128)S(1)} %get-tuple-element.40) | copy-start | bytes 36868
  13.0 16.7 %copy-start.49 = (f32[1,1,3072]{2,1,0:T(1,128)}, f32[1,1,3072]{2,1,0:T(1,128)S(1)}, u32[]{:S(2)}) copy-start(f32[1,1,3072]{2,1,0:T(1,128)S(1)} %get-tuple-element.41) | copy-start | bytes 36868
  58.5 17.4 %copy-start.118 = (pred[2]{0:T(512)(128)(4,1)S(1)}, pred[2]{0:T(512)(128)(4,1)}, u32[]{:S(2)}) copy-start(pred[2]{0:T(512)(128)(4,1)} %get-tuple-element.92) | copy-start | bytes 10
  59.5 19.7 %collective-permute-start.2 = (f32[2,3072]{1,0:T(2,128)S(1)}, f32[2,3072]{1,0:T(2,128)S(1)}, u32[]{:S(2)}, u32[]{:S(2)}) collective-permute-start(f32[2,3072]{1,0:T(2,128)S(1)} %broadcast_multiply_fusion.1), channel_id=1, source_target_pairs={{0,1},{1,0},{2,3},{3,2},{4,5},{5,4},{6,7},{7,6},{8,9},{9,8},{10,11... | collective-permute-start | bytes 73736 | tf_op jit(solution)/shard_map/ppermute | solution.py:33
  72.1 9.1 %collective-permute-start.5 = (bf16[12,1024]{1,0:T(8,128)(2,1)S(1)}, bf16[12,1024]{1,0:T(8,128)(2,1)S(1)}, u32[]{:S(2)}, u32[]{:S(2)}) collective-permute-start(bf16[12,1024]{1,0:T(8,128)(2,1)S(1)} %fusion.50), channel_id=1, source_target_pairs={{0,48},{48,0},{96,144},{144,96},{192,240},{240,192},{288,336},{336... | collective-permute-start | bytes 73736 | tf_op jit(solution)/shard_map/ppermute | solution.py:50
  79.3 8.2 %collective-permute-start.3 = (f32[2,3072]{1,0:T(2,128)S(1)}, f32[2,3072]{1,0:T(2,128)S(1)}, u32[]{:S(2)}, u32[]{:S(2)}) collective-permute-start(f32[2,3072]{1,0:T(2,128)S(1)} %add.754), channel_id=1, source_target_pairs={{0,2},{1,3},{2,0},{3,1},{4,6},{5,7},{6,4},{7,5},{8,10},{9,11},{10,... | collective-permute-start | bytes 73736 | tf_op jit(solution)/shard_map/ppermute | solution.py:33
  82.7 7.9 %collective-permute-start.6 = (bf16[2,12,1024]{2,1,0:T(8,128)(2,1)S(1)}, bf16[2,12,1024]{2,1,0:T(8,128)(2,1)S(1)}, u32[]{:S(2)}, u32[]{:S(2)}) collective-permute-start(bf16[2,12,1024]{2,1,0:T(8,128)(2,1)S(1)} %broadcast_select_fusion.9), channel_id=1, source_target_pairs={{0,96},{48,144},{96,0},{144,48},{192,288},{240,336},{288,192},{336... | collective-permute-start | bytes 147464 | tf_op jit(solution)/shard_map/ppermute | solution.py:50
  87.5 5.8 %collective-permute-start.4 = (f32[2,3072]{1,0:T(2,128)S(1)}, f32[2,3072]{1,0:T(2,128)}, u32[]{:S(2)}, u32[]{:S(2)}) collective-permute-start(f32[2,3072]{1,0:T(2,128)S(1)} %add.755), channel_id=1, source_target_pairs={{0,4},{1,5},{2,6},{3,7},{4,0},{5,1},{6,2},{7,3},{8,12},{9,13},{10,... | collective-permute-start | bytes 73736 | tf_op jit(solution)/shard_map/ppermute | solution.py:33
  99.4 12.5 %collective-permute-start.7 = (bf16[2,2,12,1024]{3,2,1,0:T(8,128)(2,1)S(1)}, bf16[2,2,12,1024]{3,2,1,0:T(8,128)(2,1)S(1)}, u32[]{:S(2)}, u32[]{:S(2)}) collective-permute-start(bf16[2,2,12,1024]{3,2,1,0:T(8,128)(2,1)S(1)} %broadcast_select_fusion.6), channel_id=1, source_target_pairs={{0,192},{48,240},{96,288},{144,336},{192,0},{240,48},{288,96},{336... | collective-permute-start | bytes 294920 | tf_op jit(solution)/shard_map/ppermute | solution.py:50
  115.0 10.0 %collective-permute-start.8 = (bf16[2,2,2,12,1024]{4,3,2,1,0:T(8,128)(2,1)S(1)}, bf16[2,2,2,12,1024]{4,3,2,1,0:T(8,128)(2,1)S(1)}, u32[]{:S(2)}, u32[]{:S(2)}) collective-permute-start(bf16[2,2,2,12,1024]{4,3,2,1,0:T(8,128)(2,1)S(1)} %broadcast_select_fusion.3), channel_id=1, source_target_pairs={{0,384},{48,432},{96,480},{144,528},{192,576},{240,624},{288,672},... | collective-permute-start | bytes 589832 | tf_op jit(solution)/shard_map/ppermute | solution.py:50
  140.2 23.5 %copy-start.115 = (pred[3]{0:T(512)(128)(4,1)S(1)}, pred[3]{0:T(512)(128)(4,1)}, u32[]{:S(2)}) copy-start(pred[3]{0:T(512)(128)(4,1)} %compare_and_fusion) | copy-start | bytes 13
  140.2 46.6 %copy-start.108 = (pred[6]{0:T(512)(128)(4,1)S(1)}, pred[6]{0:T(512)(128)(4,1)}, u32[]{:S(2)}) copy-start(pred[6]{0:T(512)(128)(4,1)} %broadcast_in_dim.353) | copy-start | bytes 22
  140.2 62.6 %copy-start.102 = (pred[2]{0:T(512)(128)(4,1)S(1)}, pred[2]{0:T(512)(128)(4,1)}, u32[]{:S(2)}) copy-start(pred[2]{0:T(512)(128)(4,1)} %get-tuple-element.94) | copy-start | bytes 10
  140.2 22.7 %collective-permute-start.12 = (bf16[2,1024]{1,0:T(2,128)(2,1)S(1)}, bf16[2,1024]{1,0:T(2,128)(2,1)S(1)}, u32[]{:S(2)}, u32[]{:S(2)}) collective-permute-start(bf16[2,1024]{1,0:T(2,128)(2,1)S(1)} %copy-done.100), channel_id=1, source_target_pairs={{0,16},{8,0},{16,8},{24,40},{32,24},{40,32},{1,17},{9,1},{17,9},{2... | collective-permute-start | bytes 12296 | tf_op jit(solution)/shard_map/ppermute | solution.py:50
  151.3 11.7 %collective-permute-start.11 = (bf16[2,1024]{1,0:T(2,128)(2,1)S(1)}, bf16[2,1024]{1,0:T(2,128)(2,1)S(1)}, u32[]{:S(2)}, u32[]{:S(2)}) collective-permute-start(bf16[2,1024]{1,0:T(2,128)(2,1)S(1)} %copy-done.100), channel_id=1, source_target_pairs={{0,8},{8,16},{16,0},{24,32},{32,40},{40,24},{1,9},{9,17},{17,1},{2... | collective-permute-start | bytes 12296 | tf_op jit(solution)/shard_map/ppermute | solution.py:50
  154.9 60.9 %copy-start.101 = (pred[2]{0:T(512)(128)(4,1)S(1)}, pred[2]{0:T(512)(128)(4,1)}, u32[]{:S(2)}) copy-start(pred[2]{0:T(512)(128)(4,1)} %get-tuple-element.95) | copy-start | bytes 10
  155.6 71.7 %copy-start.111 = (pred[16]{0:T(512)(128)(4,1)S(1)}, pred[16]{0:T(512)(128)(4,1)}, u32[]{:S(2)}) copy-start(pred[16]{0:T(512)(128)(4,1)} %broadcast_in_dim.209) | copy-start | bytes 52
  156.4 76.8 %collective-permute-start.9 = (bf16[2,3,32,3072]{3,2,1,0:T(8,128)(2,1)}, bf16[2,3,32,3072]{3,2,1,0:T(8,128)(2,1)S(1)}, u32[]{:S(2)}, u32[]{:S(2)}) collective-permute-start(bf16[2,3,32,3072]{3,2,1,0:T(8,128)(2,1)} %get-tuple-element.21), channel_id=1, source_target_pairs={{0,1},{1,2},{2,3},{3,4},{4,5},{5,6},{6,7},{8,9},{9,10},{10,11},{11... | collective-permute-start | bytes 3538952 | tf_op jit(solution)/shard_map/ppermute | solution.py:23
  158.4 75.8 %collective-permute-start.10 = (bf16[2,3,32,3072]{3,2,1,0:T(8,128)(2,1)}, bf16[2,3,32,3072]{3,2,1,0:T(8,128)(2,1)}, u32[]{:S(2)}, u32[]{:S(2)}) collective-permute-start(bf16[2,3,32,3072]{3,2,1,0:T(8,128)(2,1)} %get-tuple-element.22), channel_id=1, source_target_pairs={{1,0},{2,1},{3,2},{4,3},{5,4},{6,5},{7,6},{9,8},{10,9},{11,10},{12... | collective-permute-start | bytes 3538952 | tf_op jit(solution)/shard_map/ppermute | solution.py:24
  163.8 22.2 %collective-permute-start.13 = (bf16[3,2,1024]{2,1,0:T(2,128)(2,1)S(1)}, bf16[3,2,1024]{2,1,0:T(2,128)(2,1)S(1)}, u32[]{:S(2)}, u32[]{:S(2)}) collective-permute-start(bf16[3,2,1024]{2,1,0:T(2,128)(2,1)S(1)} %broadcast_select_fusion.12), channel_id=1, source_target_pairs={{0,24},{8,32},{16,40},{24,0},{32,8},{40,16},{1,25},{9,33},{17,41},... | collective-permute-start | bytes 36872 | tf_op jit(solution)/shard_map/ppermute | solution.py:50
  186.9 5.9 %collective-permute-start.14 = (bf16[6,2,1024]{2,1,0:T(2,128)(2,1)S(1)}, bf16[6,2,1024]{2,1,0:T(2,128)(2,1)S(1)}, u32[]{:S(2)}, u32[]{:S(2)}) collective-permute-start(bf16[6,2,1024]{2,1,0:T(2,128)(2,1)S(1)} %broadcast_select_fusion.10), channel_id=1, source_target_pairs={{0,48},{48,0},{96,144},{144,96},{192,240},{240,192},{288,336},{336... | collective-permute-start | bytes 73736 | tf_op jit(solution)/shard_map/ppermute | solution.py:50
  194.5 7.3 %collective-permute-start.15 = (bf16[2,6,2,1024]{3,2,1,0:T(2,128)(2,1)S(1)}, bf16[2,6,2,1024]{3,2,1,0:T(2,128)(2,1)S(1)}, u32[]{:S(2)}, u32[]{:S(2)}) collective-permute-start(bf16[2,6,2,1024]{3,2,1,0:T(2,128)(2,1)S(1)} %broadcast_select_fusion.7), channel_id=1, source_target_pairs={{0,96},{48,144},{96,0},{144,48},{192,288},{240,336},{288,192},{336... | collective-permute-start | bytes 147464 | tf_op jit(solution)/shard_map/ppermute | solution.py:50
  203.0 11.5 %collective-permute-start.16 = (bf16[2,2,6,2,1024]{4,3,2,1,0:T(2,128)(2,1)S(1)}, bf16[2,2,6,2,1024]{4,3,2,1,0:T(2,128)(2,1)S(1)}, u32[]{:S(2)}, u32[]{:S(2)}) collective-permute-start(bf16[2,2,6,2,1024]{4,3,2,1,0:T(2,128)(2,1)S(1)} %broadcast_select_fusion.4), channel_id=1, source_target_pairs={{0,192},{48,240},{96,288},{144,336},{192,0},{240,48},{288,96},{336... | collective-permute-start | bytes 294920 | tf_op jit(solution)/shard_map/ppermute | solution.py:50
  216.1 9.1 %collective-permute-start.17 = (bf16[2,2,2,6,2,1024]{5,4,3,2,1,0:T(2,128)(2,1)S(1)}, bf16[2,2,2,6,2,1024]{5,4,3,2,1,0:T(2,128)(2,1)S(1)}, u32[]{:S(2)}, u32[]{:S(2)}) collective-permute-start(bf16[2,2,2,6,2,1024]{5,4,3,2,1,0:T(2,128)(2,1)S(1)} %broadcast_select_fusion.1), channel_id=1, source_target_pairs={{0,384},{48,432},{96,480},{144,528},{192,576},{240,624},{288,672},... | collective-permute-start | bytes 589832 | tf_op jit(solution)/shard_map/ppermute | solution.py:50
  (90 other events, 540.8 us)

commit v5 on v2

--- a/solution.py
+++ b/solution.py
@@ -48,16 +48,22 @@
                 d = (src // place) % radix
                 pairs.append((src, src + ((d + shift) % radix - d) * place))
             got.append(lax.ppermute(value, axis, pairs))
-        stacked = jnp.stack(got)
-        order = (digit - jnp.arange(radix)) % radix
-        value = jnp.take(stacked, order, axis=0)
+        if radix == 2:
+            first = digit == 0
+            value = jnp.stack(
+                [jnp.where(first, got[0], got[1]), jnp.where(first, got[1], got[0])]
+            )
+        else:
+            stacked = jnp.stack(got)
+            order = (digit - jnp.arange(radix)) % radix
+            value = jnp.take(stacked, order, axis=0)
         place *= radix
     return value.reshape((devices,) + value.shape[len(radices) :])
 
 
 def radix_split(count):
     parts = []
-    for radix in (4, 3, 2):
+    for radix in (3, 2):
         while count % radix == 0 and count > 1:
             parts.append(radix)
             count //= radix
@@ -137,7 +143,7 @@
     source_table = (sources[:, None] == jnp.arange(SOURCES)[None, :]).astype(jnp.float32)
     weights = (
         SOURCES
-        * numerators[sources].astype(jnp.float32)
+        * jnp.sum(source_table * numerators.astype(jnp.float32)[None, :], axis=1)
         / jnp.sum(numerators).astype(jnp.float32)
     )
     row_loss = lax.optimization_barrier(jnp.sum(jax.nn.softplus(-labels * logits), axis=1))

time: 276 us -> 249 us (0.902)
  the two profiles are of different devices: /device:TPU:10 before, /device:TPU:6 now
where the time goes in v5:
time: 249 us; the launch traced here: 248 us
  other arithmetic  81.5 us (33%)
  waiting for transfers between devices  68 us (27%)
  starting transfers between devices  66.1 us (27%)
  local copies, waits for them, and re-layouts  16.6 us (7%)
  matrix products  12.2 us (5%)
  between operations  3.45 us (1%)
    ppermute x7, starting transfers between devices, gather_stages(): got.append(lax.ppermute(value, axis, pairs))  48.1 us
    ppermute x2, waiting for transfers between devices, halo_rows(): before = lax.ppermute(last, 'row', up)  43 us
    reduce_sum x4, other arithmetic, cell_norm(): center = values - jnp.mean(values, axis=-1, keepdims=True)  28.7 us
    convert_element_type x1, other arithmetic, local(): grad_map = (own_grad[:, None, None, :] + spread).astype(jnp.bfloat16)  26.4 us
    ppermute x7, waiting for transfers between devices, gather_stages(): got.append(lax.ppermute(value, axis, pairs))  18.1 us
    ppermute x2, starting transfers between devices, halo_rows(): after = lax.ppermute(leading, 'row', down)  7.29 us
    ppermute x3, waiting for transfers between devices, group_sum(): value = value + lax.ppermute(value, 'row', pairs)  6.85 us
    ppermute x3, starting transfers between devices, group_sum(): value = value + lax.ppermute(value, 'row', pairs)  6.84 us
  transfers between devices with their start and end apart: 14, of which 11 were waited for; matrix products, arithmetic and copies ran while one was open for 4% of the time, Pallas kernels for 0%

profile of v5, /device:TPU:6, one launch (start us, length us, event | category | flops | bytes accessed | tf_op | source)
XLA Modules:
  0.0 247.9 jit_solution(4708181596754098373)
XLA Ops:
  0.7 1.9 fusion.62
  2.6 1.9 collective-permute-start
  4.5 3.6 %collective-permute-start.1 = (bf16[2,3,32,3072]{3,2,1,0:T(8,128)(2,1)S(1)}, bf16[2,3,32,3072]{3,2,1,0:T(8,128)(2,1)S(1)}, u32[]{:S(2)}, u32[]{:S(2)}) collective-permute-start(bf16[2,3,32,3072]{3,2,1,0:T(8,128)(2,1)S(1)} %get-tuple-element.18), channel_id=1, source_target_pairs={{1,0},{2,1},{3,2},{4,3},{5,4},{6,5},{7,6},{9,8},{10,9},{11,10},{12... | collective-permute-start | bytes 3538952 | tf_op jit(solution)/shard_map/ppermute | solution.py:24
  10.4 22.4 %collective-permute-done = bf16[2,3,32,3072]{3,2,1,0:T(8,128)(2,1)S(1)} collective-permute-done((bf16[2,3,32,3072]{3,2,1,0:T(8,128)(2,1)S(1)}, bf16[2,3,32,3072]{3,2,1,0:T(8,128)(2,1)S(1)}, u32[]{:S(2)}, u32[]{:S(2)}) %collective-permute-start) | collective-permute-done | bytes 1179680 | tf_op jit(solution)/shard_map/ppermute | solution.py:23
  33.3 2.2 select_maximum_fusion.2
  36.0 27.6 %fusion.59 = (f32[2,4,32]{2,1,0:T(4,128)S(1)}, f32[2,4,32,3072]{3,2,1,0:T(8,128)S(1)}) fusion(f32[3072]{0:T(1024)S(1)} %copy-done.95, f32[3072]{0:T(1024)S(1)} %bitcast.109, bf16[2,10,38,3072]{3,2,1,0:T(8,128)(2,1)S(1)} %select_maximum_fusion.2, f32[3072]{0:T(1024)S(1)} %bitcast.111, f32[3072]{0:T(1024)S(1)} %bitcast.115, f32[3072]{0:T(1024)S(1)} %bitcast.117, ...), kind=kLoop, calls=%fused_computation.207 | loop fusion | flops 116391680 | bytes 80831488 | tf_op jit(solution)/shard_map/reduce_sum | solution.py:75
  65.6 1.9 collective-permute-start.2
  68.8 1.9 collective-permute-start.3
  70.7 3.8 %collective-permute-done.3 = f32[2,3072]{1,0:T(2,128)S(1)} collective-permute-done((f32[2,3072]{1,0:T(2,128)S(1)}, f32[2,3072]{1,0:T(2,128)S(1)}, u32[]{:S(2)}, u32[]{:S(2)}) %collective-permute-start.3) | collective-permute-done | bytes 24608 | tf_op jit(solution)/shard_map/ppermute | solution.py:33
  74.5 3.0 %collective-permute-start.4 = (f32[2,3072]{1,0:T(2,128)S(1)}, f32[2,3072]{1,0:T(2,128)S(1)}, u32[]{:S(2)}, u32[]{:S(2)}) collective-permute-start(f32[2,3072]{1,0:T(2,128)S(1)} %add.559), channel_id=1, source_target_pairs={{0,4},{1,5},{2,6},{3,7},{4,0},{5,1},{6,2},{7,3},{8,12},{9,13},{10,... | collective-permute-start | bytes 73736 | tf_op jit(solution)/shard_map/ppermute | solution.py:33
  77.6 2.6 %collective-permute-done.4 = f32[2,3072]{1,0:T(2,128)S(1)} collective-permute-done((f32[2,3072]{1,0:T(2,128)S(1)}, f32[2,3072]{1,0:T(2,128)S(1)}, u32[]{:S(2)}, u32[]{:S(2)}) %collective-permute-start.4) | collective-permute-done | bytes 24608 | tf_op jit(solution)/shard_map/ppermute | solution.py:33
  81.2 3.9 %multiply_reduce_fusion.6 = (f32[2]{0:T(128)S(1)}, f32[2,1024]{1,0:T(2,128)S(1)}) fusion(bf16[3072,1024]{1,0:T(8,128)(2,1)} %param.17, f32[2]{0:T(128)S(1)} %fusion.52, f32[3072]{0:T(1024)S(1)} %copy-done.90, f32[2,3072]{1,0:T(2,128)S(1)} %get-tuple-element.10, f32[2]{0:T(128)S(1)} %broadcast_multiply_fusion.5), kind=kOutput, calls=%fused_computation.166 | convolution fusion | flops 12611582 | bytes 6336536 | tf_op jit(solution)/shard_map/dot_general | solution.py:121
  85.2 6.1 %collective-permute-start.5 = (bf16[4,1024]{1,0:T(4,128)(2,1)S(1)}, bf16[4,1024]{1,0:T(4,128)(2,1)S(1)}, u32[]{:S(2)}, u32[]{:S(2)}) collective-permute-start(bf16[4,1024]{1,0:T(4,128)(2,1)S(1)} %get-tuple-element.81), channel_id=1, source_target_pairs={{0,8},{8,16},{16,0},{24,32},{32,40},{40,24},{1,9},{9,17},{17,1},{2... | collective-permute-start | bytes 24584 | tf_op jit(solution)/shard_map/ppermute | solution.py:50
  91.3 6.7 %collective-permute-start.6 = (bf16[4,1024]{1,0:T(4,128)(2,1)S(1)}, bf16[4,1024]{1,0:T(4,128)(2,1)S(1)}, u32[]{:S(2)}, u32[]{:S(2)}) collective-permute-start(bf16[4,1024]{1,0:T(4,128)(2,1)S(1)} %get-tuple-element.81), channel_id=1, source_target_pairs={{0,16},{8,0},{16,8},{24,40},{32,24},{40,32},{1,17},{9,1},{17,9},{2... | collective-permute-start | bytes 24584 | tf_op jit(solution)/shard_map/ppermute | solution.py:50
  98.1 2.1 collective-permute-done.6
  100.9 12.7 %collective-permute-start.7 = (bf16[3,4,1024]{2,1,0:T(4,128)(2,1)S(1)}, bf16[3,4,1024]{2,1,0:T(4,128)(2,1)S(1)}, u32[]{:S(2)}, u32[]{:S(2)}) collective-permute-start(bf16[3,4,1024]{2,1,0:T(4,128)(2,1)S(1)} %broadcast_select_fusion), channel_id=1, source_target_pairs={{0,24},{8,32},{16,40},{24,0},{32,8},{40,16},{1,25},{9,33},{17,41},... | collective-permute-start | bytes 73736 | tf_op jit(solution)/shard_map/ppermute | solution.py:50
  113.7 1.8 collective-permute-done.7
  115.6 3.5 %collective-permute-start.8 = (bf16[6,4,1024]{2,1,0:T(4,128)(2,1)S(1)}, bf16[6,4,1024]{2,1,0:T(4,128)(2,1)S(1)}, u32[]{:S(2)}, u32[]{:S(2)}) collective-permute-start(bf16[6,4,1024]{2,1,0:T(4,128)(2,1)S(1)} %bitcast.90), channel_id=1, source_target_pairs={{0,48},{48,0},{96,144},{144,96},{192,240},{240,192},{288,336},{336... | collective-permute-start | bytes 147464 | tf_op jit(solution)/shard_map/ppermute | solution.py:50
  119.1 2.5 collective-permute-done.8
  121.7 5.0 %collective-permute-start.9 = (bf16[2,6,4,1024]{3,2,1,0:T(4,128)(2,1)S(1)}, bf16[2,6,4,1024]{3,2,1,0:T(4,128)(2,1)S(1)}, u32[]{:S(2)}, u32[]{:S(2)}) collective-permute-start(bf16[2,6,4,1024]{3,2,1,0:T(4,128)(2,1)S(1)} %pad_maximum_fusion.5), channel_id=1, source_target_pairs={{0,96},{48,144},{96,0},{144,48},{192,288},{240,336},{288,192},{336... | collective-permute-start | bytes 294920 | tf_op jit(solution)/shard_map/ppermute | solution.py:50
  126.8 3.6 %collective-permute-done.9 = bf16[2,6,4,1024]{3,2,1,0:T(4,128)(2,1)S(1)} collective-permute-done((bf16[2,6,4,1024]{3,2,1,0:T(4,128)(2,1)S(1)}, bf16[2,6,4,1024]{3,2,1,0:T(4,128)(2,1)S(1)}, u32[]{:S(2)}, u32[]{:S(2)}) %collective-permute-start.9) | collective-permute-done | bytes 98336 | tf_op jit(solution)/shard_map/ppermute | solution.py:50
  130.6 10.6 %collective-permute-start.10 = (bf16[2,2,6,4,1024]{4,3,2,1,0:T(4,128)(2,1)S(1)}, bf16[2,2,6,4,1024]{4,3,2,1,0:T(4,128)(2,1)S(1)}, u32[]{:S(2)}, u32[]{:S(2)}) collective-permute-start(bf16[2,2,6,4,1024]{4,3,2,1,0:T(4,128)(2,1)S(1)} %pad_maximum_fusion.4), channel_id=1, source_target_pairs={{0,192},{48,240},{96,288},{144,336},{192,0},{240,48},{288,96},{336... | collective-permute-start | bytes 589832 | tf_op jit(solution)/shard_map/ppermute | solution.py:50
  141.3 1.2 fusion.63
  142.5 4.5 %collective-permute-done.10 = bf16[2,2,6,4,1024]{4,3,2,1,0:T(4,128)(2,1)S(1)} collective-permute-done((bf16[2,2,6,4,1024]{4,3,2,1,0:T(4,128)(2,1)S(1)}, bf16[2,2,6,4,1024]{4,3,2,1,0:T(4,128)(2,1)S(1)}, u32[]{:S(2)}, u32[]{:S(2)}) %collective-permute-start.10) | collective-permute-done | bytes 196640 | tf_op jit(solution)/shard_map/ppermute | solution.py:50
  147.2 1.0 pad_maximum_fusion.3
  148.2 3.5 %collective-permute-start.11 = (bf16[2,2,2,6,4,1024]{5,4,3,2,1,0:T(4,128)(2,1)}, bf16[2,2,2,6,4,1024]{5,4,3,2,1,0:T(4,128)(2,1)}, u32[]{:S(2)}, u32[]{:S(2)}) collective-permute-start(bf16[2,2,2,6,4,1024]{5,4,3,2,1,0:T(4,128)(2,1)} %pad_maximum_fusion.3), channel_id=1, source_target_pairs={{0,384},{48,432},{96,480},{144,528},{192,576},{240,624},{288,672},... | collective-permute-start | bytes 1179656 | tf_op jit(solution)/shard_map/ppermute | solution.py:50
  153.6 1.2 pad_clamp_fusion
  154.7 1.4 select_reduce_fusion.1
  156.1 3.6 %collective-permute-done.11 = bf16[2,2,2,6,4,1024]{5,4,3,2,1,0:T(4,128)(2,1)} collective-permute-done((bf16[2,2,2,6,4,1024]{5,4,3,2,1,0:T(4,128)(2,1)}, bf16[2,2,2,6,4,1024]{5,4,3,2,1,0:T(4,128)(2,1)}, u32[]{:S(2)}, u32[]{:S(2)}) %collective-permute-start.11) | collective-permute-done | bytes 393248 | tf_op jit(solution)/shard_map/ppermute | solution.py:50
  159.7 1.5 select_bitcast_fusion.1
  161.7 1.3 slice_bitcast_fusion
  163.9 1.2 reshape.567
  165.1 1.9 reshape.568
  167.0 1.4 fusion.37
  168.4 1.3 fusion.56
  169.7 1.4 multiply_convert_fusion
  171.1 1.6 copy.20
  172.7 2.2 gather_fusion.1
  174.9 1.3 multiply_reduce_fusion.5
  176.8 4.6 %multiply_reduce_fusion.3 = (f32[2]{0:T(128)S(1)}, f32[2,3072]{1,0:T(2,128)S(1)}) fusion(f32[2,3072]{1,0:T(2,128)} %copy-done.4, f32[2]{0:T(128)} %copy-done.96, f32[3072]{0:T(1024)} %param.16, bf16[3072,1024]{1,0:T(8,128)(2,1)} %param.17, f32[2,1024]{1,0:T(2,128)} %copy-done.87, f32[2,1024]{1,0:T(2,128)S(1)} %get-tuple-element.93, ...), kind=kOutput, calls=%fused_computation.92 | convolution fusion | flops 12617726 | bytes 6369312 | tf_op jit(solution)/shard_map/dot_general | solution.py:165
  183.8 1.0 add_convert_fusion.1
  184.8 1.1 copy-done.1
  185.9 1.7 fusion.61
  187.6 1.9 collective-permute-start.12
  189.5 3.6 %collective-permute-start.13 = (bf16[2,3,32,3072]{3,2,1,0:T(8,128)(2,1)}, bf16[2,3,32,3072]{3,2,1,0:T(8,128)(2,1)}, u32[]{:S(2)}, u32[]{:S(2)}) collective-permute-start(bf16[2,3,32,3072]{3,2,1,0:T(8,128)(2,1)} %get-tuple-element.14), channel_id=1, source_target_pairs={{1,0},{2,1},{3,2},{4,3},{5,4},{6,5},{7,6},{9,8},{10,9},{11,10},{12... | collective-permute-start | bytes 3538952 | tf_op jit(solution)/shard_map/ppermute | solution.py:24
  196.6 20.7 %collective-permute-done.12 = bf16[2,3,32,3072]{3,2,1,0:T(8,128)(2,1)S(1)} collective-permute-done((bf16[2,3,32,3072]{3,2,1,0:T(8,128)(2,1)}, bf16[2,3,32,3072]{3,2,1,0:T(8,128)(2,1)S(1)}, u32[]{:S(2)}, u32[]{:S(2)}) %collective-permute-start.12) | collective-permute-done | bytes 1179680 | tf_op jit(solution)/shard_map/ppermute | solution.py:23
  217.3 3.7 %select_maximum_fusion = bf16[2,10,38,3072]{3,2,1,0:T(8,128)(2,1)S(1)} fusion(bf16[2,3,32,3072]{3,2,1,0:T(8,128)(2,1)} %collective-permute-done.13, bf16[2,4,32,3072]{3,2,1,0:T(8,128)(2,1)} %copy-done.1, bf16[2,3,32,3072]{3,2,1,0:T(8,128)(2,1)S(1)} %collective-permute-done.12), kind=kLoop, calls=%fused_computation.5 | loop fusion | flops 28016640 | bytes 8601600 | tf_op jit(solution)/shard_map/concatenate | solution.py:25
  221.4 26.4 %add_convert_fusion = bf16[2,4,32,3072]{3,2,1,0:T(8,128)(2,1)} fusion(bf16[2,4,32,3072]{3,2,1,0:T(8,128)(2,1)S(1)} %copy-done.2, bf16[2,3,32,3072]{3,2,1,0:T(8,128)(2,1)} %collective-permute-done.13, bf16[2,3,32,3072]{3,2,1,0:T(8,128)(2,1)S(1)} %collective-permute-done.12, bf16[2,10,38,3072]{3,2,1,0:T(8,128)(2,1)S(1)} %select_maximum_fusion, ...), kind=kLoop, calls=%fused_computation.47 | loop fusion | flops 121110528 | bytes 72192000 | tf_op jit(solution)/shard_map/convert_element_type | solution.py:172
  (269 shorter events, 17.0 us)
Async XLA Ops:
  0.6 32.2 %copy-start = (bf16[2,4,32,3072]{3,2,1,0:T(8,128)(2,1)S(1)}, bf16[2,4,32,3072]{3,2,1,0:T(8,128)(2,1)}, u32[]{:S(2)}) copy-start(bf16[2,4,32,3072]{3,2,1,0:T(8,128)(2,1)} %param.11) | copy-start | bytes 4718596
  2.6 30.2 %collective-permute-start = (bf16[2,3,32,3072]{3,2,1,0:T(8,128)(2,1)S(1)}, bf16[2,3,32,3072]{3,2,1,0:T(8,128)(2,1)S(1)}, u32[]{:S(2)}, u32[]{:S(2)}) collective-permute-start(bf16[2,3,32,3072]{3,2,1,0:T(8,128)(2,1)S(1)} %get-tuple-element.17), channel_id=1, source_target_pairs={{0,1},{1,2},{2,3},{3,4},{4,5},{5,6},{6,7},{8,9},{9,10},{10,11},{11... | collective-permute-start | bytes 3538952 | tf_op jit(solution)/shard_map/ppermute | solution.py:23
  4.5 28.7 %collective-permute-start.1 = (bf16[2,3,32,3072]{3,2,1,0:T(8,128)(2,1)S(1)}, bf16[2,3,32,3072]{3,2,1,0:T(8,128)(2,1)S(1)}, u32[]{:S(2)}, u32[]{:S(2)}) collective-permute-start(bf16[2,3,32,3072]{3,2,1,0:T(8,128)(2,1)S(1)} %get-tuple-element.18), channel_id=1, source_target_pairs={{1,0},{2,1},{3,2},{4,3},{5,4},{6,5},{7,6},{9,8},{10,9},{11,10},{12... | collective-permute-start | bytes 3538952 | tf_op jit(solution)/shard_map/ppermute | solution.py:24
  8.3 27.2 %copy-start.31 = (f32[1,1,3072]{2,1,0:T(1,128)}, f32[1,1,3072]{2,1,0:T(1,128)S(1)}, u32[]{:S(2)}) copy-start(f32[1,1,3072]{2,1,0:T(1,128)S(1)} %get-tuple-element.25) | copy-start | bytes 36868
  8.4 27.2 %copy-start.33 = (f32[1,1,3072]{2,1,0:T(1,128)}, f32[1,1,3072]{2,1,0:T(1,128)S(1)}, u32[]{:S(2)}) copy-start(f32[1,1,3072]{2,1,0:T(1,128)S(1)} %get-tuple-element.26) | copy-start | bytes 36868
  8.4 27.2 %copy-start.35 = (f32[1,1,3072]{2,1,0:T(1,128)}, f32[1,1,3072]{2,1,0:T(1,128)S(1)}, u32[]{:S(2)}) copy-start(f32[1,1,3072]{2,1,0:T(1,128)S(1)} %get-tuple-element.27) | copy-start | bytes 36868
  8.4 27.2 %copy-start.37 = (f32[1,1,3072]{2,1,0:T(1,128)}, f32[1,1,3072]{2,1,0:T(1,128)S(1)}, u32[]{:S(2)}) copy-start(f32[1,1,3072]{2,1,0:T(1,128)S(1)} %get-tuple-element.28) | copy-start | bytes 36868
  8.4 27.2 %copy-start.39 = (f32[1,1,3072]{2,1,0:T(1,128)}, f32[1,1,3072]{2,1,0:T(1,128)S(1)}, u32[]{:S(2)}) copy-start(f32[1,1,3072]{2,1,0:T(1,128)S(1)} %get-tuple-element.29) | copy-start | bytes 36868
  8.4 27.2 %copy-start.41 = (f32[1,1,3072]{2,1,0:T(1,128)}, f32[1,1,3072]{2,1,0:T(1,128)S(1)}, u32[]{:S(2)}) copy-start(f32[1,1,3072]{2,1,0:T(1,128)S(1)} %get-tuple-element.30) | copy-start | bytes 36868
  8.4 27.2 %copy-start.43 = (f32[1,1,3072]{2,1,0:T(1,128)}, f32[1,1,3072]{2,1,0:T(1,128)S(1)}, u32[]{:S(2)}) copy-start(f32[1,1,3072]{2,1,0:T(1,128)S(1)} %get-tuple-element.31) | copy-start | bytes 36868
  8.4 27.2 %copy-start.45 = (f32[1,1,3072]{2,1,0:T(1,128)}, f32[1,1,3072]{2,1,0:T(1,128)S(1)}, u32[]{:S(2)}) copy-start(f32[1,1,3072]{2,1,0:T(1,128)S(1)} %get-tuple-element.32) | copy-start | bytes 36868
  8.4 27.2 %copy-start.47 = (f32[1,1,3072]{2,1,0:T(1,128)}, f32[1,1,3072]{2,1,0:T(1,128)S(1)}, u32[]{:S(2)}) copy-start(f32[1,1,3072]{2,1,0:T(1,128)S(1)} %get-tuple-element.33) | copy-start | bytes 36868
  8.4 27.2 %copy-start.49 = (f32[1,1,3072]{2,1,0:T(1,128)}, f32[1,1,3072]{2,1,0:T(1,128)S(1)}, u32[]{:S(2)}) copy-start(f32[1,1,3072]{2,1,0:T(1,128)S(1)} %get-tuple-element.34) | copy-start | bytes 36868
  8.4 27.2 %copy-start.51 = (f32[1,1,3072]{2,1,0:T(1,128)}, f32[1,1,3072]{2,1,0:T(1,128)S(1)}, u32[]{:S(2)}) copy-start(f32[1,1,3072]{2,1,0:T(1,128)S(1)} %get-tuple-element.35) | copy-start | bytes 36868
  8.5 27.2 %copy-start.53 = (f32[1,1,3072]{2,1,0:T(1,128)}, f32[1,1,3072]{2,1,0:T(1,128)S(1)}, u32[]{:S(2)}) copy-start(f32[1,1,3072]{2,1,0:T(1,128)S(1)} %get-tuple-element.36) | copy-start | bytes 36868
  8.5 27.2 %copy-start.55 = (f32[1,1,3072]{2,1,0:T(1,128)}, f32[1,1,3072]{2,1,0:T(1,128)S(1)}, u32[]{:S(2)}) copy-start(f32[1,1,3072]{2,1,0:T(1,128)S(1)} %get-tuple-element.37) | copy-start | bytes 36868
  8.5 27.2 %copy-start.57 = (f32[1,1,3072]{2,1,0:T(1,128)}, f32[1,1,3072]{2,1,0:T(1,128)S(1)}, u32[]{:S(2)}) copy-start(f32[1,1,3072]{2,1,0:T(1,128)S(1)} %get-tuple-element.38) | copy-start | bytes 36868
  8.5 27.2 %copy-start.59 = (f32[1,1,3072]{2,1,0:T(1,128)}, f32[1,1,3072]{2,1,0:T(1,128)S(1)}, u32[]{:S(2)}) copy-start(f32[1,1,3072]{2,1,0:T(1,128)S(1)} %get-tuple-element.39) | copy-start | bytes 36868
  8.5 27.2 %copy-start.61 = (f32[1,1,3072]{2,1,0:T(1,128)}, f32[1,1,3072]{2,1,0:T(1,128)S(1)}, u32[]{:S(2)}) copy-start(f32[1,1,3072]{2,1,0:T(1,128)S(1)} %get-tuple-element.40) | copy-start | bytes 36868
  8.5 27.2 %copy-start.63 = (f32[1,1,3072]{2,1,0:T(1,128)}, f32[1,1,3072]{2,1,0:T(1,128)S(1)}, u32[]{:S(2)}) copy-start(f32[1,1,3072]{2,1,0:T(1,128)S(1)} %get-tuple-element.41) | copy-start | bytes 36868
  8.5 27.2 %copy-start.65 = (f32[1,1,3072]{2,1,0:T(1,128)}, f32[1,1,3072]{2,1,0:T(1,128)S(1)}, u32[]{:S(2)}) copy-start(f32[1,1,3072]{2,1,0:T(1,128)S(1)} %get-tuple-element.42) | copy-start | bytes 36868
  8.5 27.2 %copy-start.67 = (f32[1,1,3072]{2,1,0:T(1,128)}, f32[1,1,3072]{2,1,0:T(1,128)S(1)}, u32[]{:S(2)}) copy-start(f32[1,1,3072]{2,1,0:T(1,128)S(1)} %get-tuple-element.43) | copy-start | bytes 36868
  10.1 25.7 %copy-start.69 = (f32[1,1,3072]{2,1,0:T(1,128)}, f32[1,1,3072]{2,1,0:T(1,128)S(1)}, u32[]{:S(2)}) copy-start(f32[1,1,3072]{2,1,0:T(1,128)S(1)} %get-tuple-element.44) | copy-start | bytes 36868
  10.1 25.7 %copy-start.71 = (f32[1,1,3072]{2,1,0:T(1,128)}, f32[1,1,3072]{2,1,0:T(1,128)S(1)}, u32[]{:S(2)}) copy-start(f32[1,1,3072]{2,1,0:T(1,128)S(1)} %get-tuple-element.45) | copy-start | bytes 36868
  10.1 25.7 %copy-start.73 = (f32[1,1,3072]{2,1,0:T(1,128)}, f32[1,1,3072]{2,1,0:T(1,128)S(1)}, u32[]{:S(2)}) copy-start(f32[1,1,3072]{2,1,0:T(1,128)S(1)} %get-tuple-element.46) | copy-start | bytes 36868
  10.1 25.7 %copy-start.75 = (f32[1,1,3072]{2,1,0:T(1,128)}, f32[1,1,3072]{2,1,0:T(1,128)S(1)}, u32[]{:S(2)}) copy-start(f32[1,1,3072]{2,1,0:T(1,128)S(1)} %get-tuple-element.47) | copy-start | bytes 36868
  10.1 25.7 %copy-start.77 = (f32[1,1,3072]{2,1,0:T(1,128)}, f32[1,1,3072]{2,1,0:T(1,128)S(1)}, u32[]{:S(2)}) copy-start(f32[1,1,3072]{2,1,0:T(1,128)S(1)} %get-tuple-element.48) | copy-start | bytes 36868
  10.1 25.7 %copy-start.79 = (f32[1,1,3072]{2,1,0:T(1,128)}, f32[1,1,3072]{2,1,0:T(1,128)S(1)}, u32[]{:S(2)}) copy-start(f32[1,1,3072]{2,1,0:T(1,128)S(1)} %get-tuple-element.49) | copy-start | bytes 36868
  10.1 25.7 %copy-start.81 = (f32[1,1,3072]{2,1,0:T(1,128)}, f32[1,1,3072]{2,1,0:T(1,128)S(1)}, u32[]{:S(2)}) copy-start(f32[1,1,3072]{2,1,0:T(1,128)S(1)} %get-tuple-element.50) | copy-start | bytes 36868
  10.1 25.7 %copy-start.83 = (f32[1,1,3072]{2,1,0:T(1,128)}, f32[1,1,3072]{2,1,0:T(1,128)S(1)}, u32[]{:S(2)}) copy-start(f32[1,1,3072]{2,1,0:T(1,128)S(1)} %get-tuple-element.51) | copy-start | bytes 36868
  10.2 25.7 %copy-start.85 = (f32[1,1,3072]{2,1,0:T(1,128)}, f32[1,1,3072]{2,1,0:T(1,128)S(1)}, u32[]{:S(2)}) copy-start(f32[1,1,3072]{2,1,0:T(1,128)S(1)} %get-tuple-element.52) | copy-start | bytes 36868
  10.3 25.6 %copy-start.9 = (f32[1,1,3072]{2,1,0:T(1,128)}, f32[1,1,3072]{2,1,0:T(1,128)S(1)}, u32[]{:S(2)}) copy-start(f32[1,1,3072]{2,1,0:T(1,128)S(1)} %get-tuple-element.63) | copy-start | bytes 36868
  10.3 25.6 %copy-start.11 = (f32[1,1,3072]{2,1,0:T(1,128)}, f32[1,1,3072]{2,1,0:T(1,128)S(1)}, u32[]{:S(2)}) copy-start(f32[1,1,3072]{2,1,0:T(1,128)S(1)} %get-tuple-element.64) | copy-start | bytes 36868
  65.6 3.1 %collective-permute-start.2 = (f32[2,3072]{1,0:T(2,128)S(1)}, f32[2,3072]{1,0:T(2,128)S(1)}, u32[]{:S(2)}, u32[]{:S(2)}) collective-permute-start(f32[2,3072]{1,0:T(2,128)S(1)} %broadcast_multiply_fusion.1), channel_id=1, source_target_pairs={{0,1},{1,0},{2,3},{3,2},{4,5},{5,4},{6,7},{7,6},{8,9},{9,8},{10,11... | collective-permute-start | bytes 73736 | tf_op jit(solution)/shard_map/ppermute | solution.py:33
  68.8 5.7 %collective-permute-start.3 = (f32[2,3072]{1,0:T(2,128)S(1)}, f32[2,3072]{1,0:T(2,128)S(1)}, u32[]{:S(2)}, u32[]{:S(2)}) collective-permute-start(f32[2,3072]{1,0:T(2,128)S(1)} %fusion.55), channel_id=1, source_target_pairs={{0,2},{1,3},{2,0},{3,1},{4,6},{5,7},{6,4},{7,5},{8,10},{9,11},{10,... | collective-permute-start | bytes 73736 | tf_op jit(solution)/shard_map/ppermute | solution.py:33
  74.5 5.7 %collective-permute-start.4 = (f32[2,3072]{1,0:T(2,128)S(1)}, f32[2,3072]{1,0:T(2,128)S(1)}, u32[]{:S(2)}, u32[]{:S(2)}) collective-permute-start(f32[2,3072]{1,0:T(2,128)S(1)} %add.559), channel_id=1, source_target_pairs={{0,4},{1,5},{2,6},{3,7},{4,0},{5,1},{6,2},{7,3},{8,12},{9,13},{10,... | collective-permute-start | bytes 73736 | tf_op jit(solution)/shard_map/ppermute | solution.py:33
  81.2 60.1 %copy-start.105 = (s32[32]{0:T(128)S(1)}, s32[32]{0:T(128)}, u32[]{:S(2)}) copy-start(s32[32]{0:T(128)} %param.21) | copy-start | bytes 388
  85.1 30.4 %copy-start.87 = (f32[2,1024]{1,0:T(2,128)}, f32[2,1024]{1,0:T(2,128)S(1)}, u32[]{:S(2)}) copy-start(f32[2,1024]{1,0:T(2,128)S(1)} %get-tuple-element.89) | copy-start | bytes 24580
  85.1 30.5 %copy-start.102 = (f32[2]{0:T(128)}, f32[2]{0:T(128)S(1)}, u32[]{:S(2)}) copy-start(f32[2]{0:T(128)S(1)} %get-tuple-element.88) | copy-start | bytes 28
  85.2 12.9 %collective-permute-start.5 = (bf16[4,1024]{1,0:T(4,128)(2,1)S(1)}, bf16[4,1024]{1,0:T(4,128)(2,1)S(1)}, u32[]{:S(2)}, u32[]{:S(2)}) collective-permute-start(bf16[4,1024]{1,0:T(4,128)(2,1)S(1)} %get-tuple-element.81), channel_id=1, source_target_pairs={{0,8},{8,16},{16,0},{24,32},{32,40},{40,24},{1,9},{9,17},{17,1},{2... | collective-permute-start | bytes 24584 | tf_op jit(solution)/shard_map/ppermute | solution.py:50
  91.3 8.9 %collective-permute-start.6 = (bf16[4,1024]{1,0:T(4,128)(2,1)S(1)}, bf16[4,1024]{1,0:T(4,128)(2,1)S(1)}, u32[]{:S(2)}, u32[]{:S(2)}) collective-permute-start(bf16[4,1024]{1,0:T(4,128)(2,1)S(1)} %get-tuple-element.81), channel_id=1, source_target_pairs={{0,16},{8,0},{16,8},{24,40},{32,24},{40,32},{1,17},{9,1},{17,9},{2... | collective-permute-start | bytes 24584 | tf_op jit(solution)/shard_map/ppermute | solution.py:50
  100.9 14.5 %collective-permute-start.7 = (bf16[3,4,1024]{2,1,0:T(4,128)(2,1)S(1)}, bf16[3,4,1024]{2,1,0:T(4,128)(2,1)S(1)}, u32[]{:S(2)}, u32[]{:S(2)}) collective-permute-start(bf16[3,4,1024]{2,1,0:T(4,128)(2,1)S(1)} %broadcast_select_fusion), channel_id=1, source_target_pairs={{0,24},{8,32},{16,40},{24,0},{32,8},{40,16},{1,25},{9,33},{17,41},... | collective-permute-start | bytes 73736 | tf_op jit(solution)/shard_map/ppermute | solution.py:50
  115.6 6.0 %collective-permute-start.8 = (bf16[6,4,1024]{2,1,0:T(4,128)(2,1)S(1)}, bf16[6,4,1024]{2,1,0:T(4,128)(2,1)S(1)}, u32[]{:S(2)}, u32[]{:S(2)}) collective-permute-start(bf16[6,4,1024]{2,1,0:T(4,128)(2,1)S(1)} %bitcast.90), channel_id=1, source_target_pairs={{0,48},{48,0},{96,144},{144,96},{192,240},{240,192},{288,336},{336... | collective-permute-start | bytes 147464 | tf_op jit(solution)/shard_map/ppermute | solution.py:50
  121.7 8.7 %collective-permute-start.9 = (bf16[2,6,4,1024]{3,2,1,0:T(4,128)(2,1)S(1)}, bf16[2,6,4,1024]{3,2,1,0:T(4,128)(2,1)S(1)}, u32[]{:S(2)}, u32[]{:S(2)}) collective-permute-start(bf16[2,6,4,1024]{3,2,1,0:T(4,128)(2,1)S(1)} %pad_maximum_fusion.5), channel_id=1, source_target_pairs={{0,96},{48,144},{96,0},{144,48},{192,288},{240,336},{288,192},{336... | collective-permute-start | bytes 294920 | tf_op jit(solution)/shard_map/ppermute | solution.py:50
  130.6 16.4 %collective-permute-start.10 = (bf16[2,2,6,4,1024]{4,3,2,1,0:T(4,128)(2,1)S(1)}, bf16[2,2,6,4,1024]{4,3,2,1,0:T(4,128)(2,1)S(1)}, u32[]{:S(2)}, u32[]{:S(2)}) collective-permute-start(bf16[2,2,6,4,1024]{4,3,2,1,0:T(4,128)(2,1)S(1)} %pad_maximum_fusion.4), channel_id=1, source_target_pairs={{0,192},{48,240},{96,288},{144,336},{192,0},{240,48},{288,96},{336... | collective-permute-start | bytes 589832 | tf_op jit(solution)/shard_map/ppermute | solution.py:50
  148.2 11.5 %collective-permute-start.11 = (bf16[2,2,2,6,4,1024]{5,4,3,2,1,0:T(4,128)(2,1)}, bf16[2,2,2,6,4,1024]{5,4,3,2,1,0:T(4,128)(2,1)}, u32[]{:S(2)}, u32[]{:S(2)}) collective-permute-start(bf16[2,2,2,6,4,1024]{5,4,3,2,1,0:T(4,128)(2,1)} %pad_maximum_fusion.3), channel_id=1, source_target_pairs={{0,384},{48,432},{96,480},{144,528},{192,576},{240,624},{288,672},... | collective-permute-start | bytes 1179656 | tf_op jit(solution)/shard_map/ppermute | solution.py:50
  187.6 29.7 %collective-permute-start.12 = (bf16[2,3,32,3072]{3,2,1,0:T(8,128)(2,1)}, bf16[2,3,32,3072]{3,2,1,0:T(8,128)(2,1)S(1)}, u32[]{:S(2)}, u32[]{:S(2)}) collective-permute-start(bf16[2,3,32,3072]{3,2,1,0:T(8,128)(2,1)} %get-tuple-element.13), channel_id=1, source_target_pairs={{0,1},{1,2},{2,3},{3,4},{4,5},{5,6},{6,7},{8,9},{9,10},{10,11},{11... | collective-permute-start | bytes 3538952 | tf_op jit(solution)/shard_map/ppermute | solution.py:23
  189.5 27.7 %collective-permute-start.13 = (bf16[2,3,32,3072]{3,2,1,0:T(8,128)(2,1)}, bf16[2,3,32,3072]{3,2,1,0:T(8,128)(2,1)}, u32[]{:S(2)}, u32[]{:S(2)}) collective-permute-start(bf16[2,3,32,3072]{3,2,1,0:T(8,128)(2,1)} %get-tuple-element.14), channel_id=1, source_target_pairs={{1,0},{2,1},{3,2},{4,3},{5,4},{6,5},{7,6},{9,8},{10,9},{11,10},{12... | collective-permute-start | bytes 3538952 | tf_op jit(solution)/shard_map/ppermute | solution.py:24
  (72 other events, 1326.7 us)

commit v6 on v5

--- a/solution.py
+++ b/solution.py
@@ -128,38 +128,34 @@
     payload = jnp.concatenate([image_vec, text_share], axis=0)
     gathered = gather_stages(payload, "img", radix_split(img_count))
     gathered = gather_stages(gathered, "dp", radix_split(dp_count))
-    image_all = jnp.transpose(gathered[:, :, :batch_rows, :], (0, 2, 1, 3)).reshape(
-        dp_count * batch_rows * img_count, -1
-    )
+    image_all = gathered[:, :, :batch_rows, :].reshape(dp_count * img_count * batch_rows, -1)
     text_all = gathered[:, :, batch_rows:, :].reshape(dp_count * text_count, -1)
     count = text_all.shape[0]
+
+    def in_gathered_order(vector):
+        return jnp.transpose(vector.reshape(dp_count, batch_rows, img_count), (0, 2, 1)).reshape(-1)
+
+    positives_g = in_gathered_order(positives)
+    sources_g = in_gathered_order(sources)
     logits = (
         LOGIT_SCALE * jnp.dot(image_all, text_all.T, preferred_element_type=jnp.float32)
         + LOGIT_BIAS
     )
-    labels = jnp.where(positives[:, None] == jnp.arange(count)[None, :], 1.0, -1.0).astype(
+    labels = jnp.where(positives_g[:, None] == jnp.arange(count)[None, :], 1.0, -1.0).astype(
         jnp.float32
     )
-    source_table = (sources[:, None] == jnp.arange(SOURCES)[None, :]).astype(jnp.float32)
+    source_table = (sources_g[:, None] == jnp.arange(SOURCES)[None, :]).astype(jnp.float32)
     weights = (
         SOURCES
         * jnp.sum(source_table * numerators.astype(jnp.float32)[None, :], axis=1)
         / jnp.sum(numerators).astype(jnp.float32)
     )
-    row_loss = lax.optimization_barrier(jnp.sum(jax.nn.softplus(-labels * logits), axis=1))
-    group_sums = jnp.sum(source_table * (weights * row_loss)[:, None], axis=0)
     pair_grad = (weights[:, None] * -labels * jax.nn.sigmoid(-labels * logits)).astype(
         jnp.bfloat16
     )
-    own_rows = (dp_at * batch_rows + jnp.arange(batch_rows)) * img_count + img_at
-    own_pair = jnp.take(pair_grad, own_rows, axis=0)
+    own_at = (dp_at * img_count + img_at) * batch_rows
+    own_pair = lax.dynamic_slice_in_dim(pair_grad, own_at, batch_rows, axis=0)
     image_dir = LOGIT_SCALE * jnp.dot(own_pair, text_all, preferred_element_type=jnp.float32)
-    text_pair = lax.dynamic_slice_in_dim(pair_grad, dp_at * text_count, text_count, axis=1)
-    text_dir = LOGIT_SCALE * lax.dot_general(
-        text_pair, image_all, (((0,), (0,)), ((), ())), preferred_element_type=jnp.float32
-    )
-    text_back = jax.vjp(unit_rows, text_f)[1]
-    text_grad = text_back(text_dir)[0]
     embed_back = jax.vjp(unit_rows, embed)[1]
     embed_grad = embed_back(image_dir)[0].astype(jnp.bfloat16)
     head_grad = jnp.dot(embed_grad, head_weight.T, preferred_element_type=jnp.float32)
@@ -168,6 +164,15 @@
     norm_back = jax.vjp(lambda values: cell_norm(values, ln_gain), conved)[1]
     seeded = jnp.broadcast_to((layer_scale * own_grad)[:, None, None, :], conved.shape)
     conv_grad = norm_back(seeded)[0].astype(jnp.bfloat16)
+    logits, pair_grad, conv_grad = lax.optimization_barrier((logits, pair_grad, conv_grad))
+    row_loss = lax.optimization_barrier(jnp.sum(jax.nn.softplus(-labels * logits), axis=1))
+    group_sums = jnp.sum(source_table * (weights * row_loss)[:, None], axis=0)
+    text_pair = lax.dynamic_slice_in_dim(pair_grad, dp_at * text_count, text_count, axis=1)
+    text_dir = LOGIT_SCALE * lax.dot_general(
+        text_pair, image_all, (((0,), (0,)), ((), ())), preferred_element_type=jnp.float32
+    )
+    text_back = jax.vjp(unit_rows, text_f)[1]
+    text_grad = text_back(text_dir)[0]
     spread = depthwise_rows(conv_grad, dw_kernel[::-1, ::-1, :])
     grad_map = (own_grad[:, None, None, :] + spread).astype(jnp.bfloat16)
     return (grad_map, text_grad, group_sums)

time: 249 us -> 246 us (0.988); the launches traced: 248 us -> 242 us
  other arithmetic: 81.5 us -> 76.7 us
  local copies, waits for them, and re-layouts: 16.6 us -> 20.9 us
  starting transfers between devices: 66.1 us -> 63.2 us
  waiting for transfers between devices: 68 us -> 65.5 us
    ppermute x7, waiting for transfers between devices: 18.1 us -> 14 us  [gather_stages(): got.append(lax.ppermute(value, axis, pairs))]
    eq x0 -> x2, local copies, waits for them, and re-layouts: none -> 3.1 us  [the longest x1 1.56 us: local(): sources_g[:, None] == jnp.arange(SOURCES)[None, :]]
    ppermute x7, starting transfers between devices: 48.1 us -> 45.1 us  [gather_stages(): got.append(lax.ppermute(value, axis, pairs))]
    reshape x1 -> x3, local copies, waits for them, and re-layouts: 1.17 us -> 3.95 us  [the longest x2 2.81 us: in_gathered_order(): vector.reshape(dp_count, batch_rows, img_count)]
    convert_element_type x2 -> x0, other arithmetic: 2.6 us -> none  [the longest x1 1.39 us: local(): (weights[:, None] * -labels * jax.nn.sigmoid(-labels * logits)).astype(jn...]
  transfers between devices with their start and end apart: 14 -> 14, of which waited for: 11 -> 10; matrix products, arithmetic and copies ran while one was open for 4% -> 8% of each run, Pallas kernels for 0% -> 0%
where the time goes in v6:
time: 246 us; the launch traced here: 242 us
  other arithmetic  76.7 us (31%)
  waiting for transfers between devices  65.5 us (27%)
  starting transfers between devices  63.2 us (26%)
  local copies, waits for them, and re-layouts  20.9 us (8%)
  matrix products  12.2 us (5%)
  between operations  3.56 us (1%)
    ppermute x7, starting transfers between devices, gather_stages(): got.append(lax.ppermute(value, axis, pairs))  45.1 us
    ppermute x2, waiting for transfers between devices, halo_rows(): before = lax.ppermute(last, 'row', up)  44.6 us
    reduce_sum x4, other arithmetic, cell_norm(): center = values - jnp.mean(values, axis=-1, keepdims=True)  28.7 us
    convert_element_type x1, other arithmetic, local(): grad_map = (own_grad[:, None, None, :] + spread).astype(jnp.bfloat16)  26.1 us
    ppermute x7, waiting for transfers between devices, gather_stages(): got.append(lax.ppermute(value, axis, pairs))  14 us
    ppermute x2, starting transfers between devices, halo_rows(): after = lax.ppermute(leading, 'row', down)  7.28 us
    ppermute x3, waiting for transfers between devices, group_sum(): value = value + lax.ppermute(value, 'row', pairs)  6.91 us
    ppermute x3, starting transfers between devices, group_sum(): value = value + lax.ppermute(value, 'row', pairs)  6.84 us
  transfers between devices with their start and end apart: 14, of which 10 were waited for; matrix products, arithmetic and copies ran while one was open for 8% of the time, Pallas kernels for 0%

profile of v6, /device:TPU:6, one launch (start us, length us, event | category | flops | bytes accessed | tf_op | source)
XLA Modules:
  0.0 242.0 jit_solution(12487081410276410718)
XLA Ops:
  0.7 1.9 fusion.55
  2.6 1.9 collective-permute-start
  4.5 3.6 %collective-permute-start.1 = (bf16[2,3,32,3072]{3,2,1,0:T(8,128)(2,1)S(1)}, bf16[2,3,32,3072]{3,2,1,0:T(8,128)(2,1)S(1)}, u32[]{:S(2)}, u32[]{:S(2)}) collective-permute-start(bf16[2,3,32,3072]{3,2,1,0:T(8,128)(2,1)S(1)} %get-tuple-element.24), channel_id=1, source_target_pairs={{1,0},{2,1},{3,2},{4,3},{5,4},{6,5},{7,6},{9,8},{10,9},{11,10},{12... | collective-permute-start | bytes 3538952 | tf_op jit(solution)/shard_map/ppermute | solution.py:24
  10.3 22.5 %collective-permute-done = bf16[2,3,32,3072]{3,2,1,0:T(8,128)(2,1)S(1)} collective-permute-done((bf16[2,3,32,3072]{3,2,1,0:T(8,128)(2,1)S(1)}, bf16[2,3,32,3072]{3,2,1,0:T(8,128)(2,1)S(1)}, u32[]{:S(2)}, u32[]{:S(2)}) %collective-permute-start) | collective-permute-done | bytes 1179680 | tf_op jit(solution)/shard_map/ppermute | solution.py:23
  33.3 2.2 select_maximum_fusion.2
  36.0 27.6 %fusion.52 = (f32[2,4,32]{2,1,0:T(4,128)S(1)}, f32[2,4,32,3072]{3,2,1,0:T(8,128)S(1)}) fusion(f32[3072]{0:T(1024)S(1)} %copy-done.101, f32[3072]{0:T(1024)S(1)} %bitcast.107, bf16[2,10,38,3072]{3,2,1,0:T(8,128)(2,1)S(1)} %select_maximum_fusion.2, f32[3072]{0:T(1024)S(1)} %bitcast.109, f32[3072]{0:T(1024)S(1)} %bitcast.113, f32[3072]{0:T(1024)S(1)} %bitcast.115, ...), kind=kLoop, calls=%fused_computation.187 | loop fusion | flops 116391680 | bytes 80831488 | tf_op jit(solution)/shard_map/reduce_sum | solution.py:75
  64.7 1.0 fusion.27
  65.7 1.9 collective-permute-start.2
  68.8 1.9 collective-permute-start.3
  70.7 3.8 %collective-permute-done.3 = f32[2,3072]{1,0:T(2,128)S(1)} collective-permute-done((f32[2,3072]{1,0:T(2,128)S(1)}, f32[2,3072]{1,0:T(2,128)S(1)}, u32[]{:S(2)}, u32[]{:S(2)}) %collective-permute-start.3) | collective-permute-done | bytes 24608 | tf_op jit(solution)/shard_map/ppermute | solution.py:33
  74.5 3.0 %collective-permute-start.4 = (f32[2,3072]{1,0:T(2,128)S(1)}, f32[2,3072]{1,0:T(2,128)S(1)}, u32[]{:S(2)}, u32[]{:S(2)}) collective-permute-start(f32[2,3072]{1,0:T(2,128)S(1)} %add.507), channel_id=1, source_target_pairs={{0,4},{1,5},{2,6},{3,7},{4,0},{5,1},{6,2},{7,3},{8,12},{9,13},{10,... | collective-permute-start | bytes 73736 | tf_op jit(solution)/shard_map/ppermute | solution.py:33
  77.6 2.6 %collective-permute-done.4 = f32[2,3072]{1,0:T(2,128)S(1)} collective-permute-done((f32[2,3072]{1,0:T(2,128)S(1)}, f32[2,3072]{1,0:T(2,128)S(1)}, u32[]{:S(2)}, u32[]{:S(2)}) %collective-permute-start.4) | collective-permute-done | bytes 24608 | tf_op jit(solution)/shard_map/ppermute | solution.py:33
  81.1 3.9 %multiply_reduce_fusion.6 = (f32[2]{0:T(128)S(1)}, f32[2,1024]{1,0:T(2,128)S(1)}) fusion(bf16[3072,1024]{1,0:T(8,128)(2,1)} %param.17, f32[2]{0:T(128)S(1)} %fusion.47, f32[3072]{0:T(1024)S(1)} %copy-done.94, f32[2,3072]{1,0:T(2,128)S(1)} %get-tuple-element.14, f32[2]{0:T(128)S(1)} %broadcast_multiply_fusion.5), kind=kOutput, calls=%fused_computation.153 | convolution fusion | flops 12611582 | bytes 6336536 | tf_op jit(solution)/shard_map/dot_general | solution.py:121
  85.1 6.1 %collective-permute-start.5 = (bf16[4,1024]{1,0:T(4,128)(2,1)S(1)}, bf16[4,1024]{1,0:T(4,128)(2,1)S(1)}, u32[]{:S(2)}, u32[]{:S(2)}) collective-permute-start(bf16[4,1024]{1,0:T(4,128)(2,1)S(1)} %get-tuple-element.87), channel_id=1, source_target_pairs={{0,8},{8,16},{16,0},{24,32},{32,40},{40,24},{1,9},{9,17},{17,1},{2... | collective-permute-start | bytes 24584 | tf_op jit(solution)/shard_map/ppermute | solution.py:50
  91.2 6.7 %collective-permute-start.6 = (bf16[4,1024]{1,0:T(4,128)(2,1)S(1)}, bf16[4,1024]{1,0:T(4,128)(2,1)S(1)}, u32[]{:S(2)}, u32[]{:S(2)}) collective-permute-start(bf16[4,1024]{1,0:T(4,128)(2,1)S(1)} %get-tuple-element.87), channel_id=1, source_target_pairs={{0,16},{8,0},{16,8},{24,40},{32,24},{40,32},{1,17},{9,1},{17,9},{2... | collective-permute-start | bytes 24584 | tf_op jit(solution)/shard_map/ppermute | solution.py:50
  98.0 2.1 collective-permute-done.6
  100.9 12.7 %collective-permute-start.7 = (bf16[3,4,1024]{2,1,0:T(4,128)(2,1)S(1)}, bf16[3,4,1024]{2,1,0:T(4,128)(2,1)S(1)}, u32[]{:S(2)}, u32[]{:S(2)}) collective-permute-start(bf16[3,4,1024]{2,1,0:T(4,128)(2,1)S(1)} %broadcast_select_fusion), channel_id=1, source_target_pairs={{0,24},{8,32},{16,40},{24,0},{32,8},{40,16},{1,25},{9,33},{17,41},... | collective-permute-start | bytes 73736 | tf_op jit(solution)/shard_map/ppermute | solution.py:50
  113.6 1.8 collective-permute-done.7
  115.5 3.5 %collective-permute-start.8 = (bf16[6,4,1024]{2,1,0:T(4,128)(2,1)S(1)}, bf16[6,4,1024]{2,1,0:T(4,128)(2,1)S(1)}, u32[]{:S(2)}, u32[]{:S(2)}) collective-permute-start(bf16[6,4,1024]{2,1,0:T(4,128)(2,1)S(1)} %bitcast.88), channel_id=1, source_target_pairs={{0,48},{48,0},{96,144},{144,96},{192,240},{240,192},{288,336},{336... | collective-permute-start | bytes 147464 | tf_op jit(solution)/shard_map/ppermute | solution.py:50
  119.0 2.5 %collective-permute-done.8 = bf16[6,4,1024]{2,1,0:T(4,128)(2,1)S(1)} collective-permute-done((bf16[6,4,1024]{2,1,0:T(4,128)(2,1)S(1)}, bf16[6,4,1024]{2,1,0:T(4,128)(2,1)S(1)}, u32[]{:S(2)}, u32[]{:S(2)}) %collective-permute-start.8) | collective-permute-done | bytes 49184 | tf_op jit(solution)/shard_map/ppermute | solution.py:50
  121.6 5.0 %collective-permute-start.9 = (bf16[2,6,4,1024]{3,2,1,0:T(4,128)(2,1)S(1)}, bf16[2,6,4,1024]{3,2,1,0:T(4,128)(2,1)S(1)}, u32[]{:S(2)}, u32[]{:S(2)}) collective-permute-start(bf16[2,6,4,1024]{3,2,1,0:T(4,128)(2,1)S(1)} %pad_maximum_fusion.3), channel_id=1, source_target_pairs={{0,96},{48,144},{96,0},{144,48},{192,288},{240,336},{288,192},{336... | collective-permute-start | bytes 294920 | tf_op jit(solution)/shard_map/ppermute | solution.py:50
  126.7 3.6 %collective-permute-done.9 = bf16[2,6,4,1024]{3,2,1,0:T(4,128)(2,1)S(1)} collective-permute-done((bf16[2,6,4,1024]{3,2,1,0:T(4,128)(2,1)S(1)}, bf16[2,6,4,1024]{3,2,1,0:T(4,128)(2,1)S(1)}, u32[]{:S(2)}, u32[]{:S(2)}) %collective-permute-start.9) | collective-permute-done | bytes 98336 | tf_op jit(solution)/shard_map/ppermute | solution.py:50
  131.2 7.6 %collective-permute-start.10 = (bf16[2,2,6,4,1024]{4,3,2,1,0:T(4,128)(2,1)S(1)}, bf16[2,2,6,4,1024]{4,3,2,1,0:T(4,128)(2,1)}, u32[]{:S(2)}, u32[]{:S(2)}) collective-permute-start(bf16[2,2,6,4,1024]{4,3,2,1,0:T(4,128)(2,1)S(1)} %pad_maximum_fusion.2), channel_id=1, source_target_pairs={{0,192},{48,240},{96,288},{144,336},{192,0},{240,48},{288,96},{336... | collective-permute-start | bytes 589832 | tf_op jit(solution)/shard_map/ppermute | solution.py:50
  138.8 4.0 %collective-permute-done.10 = bf16[2,2,6,4,1024]{4,3,2,1,0:T(4,128)(2,1)} collective-permute-done((bf16[2,2,6,4,1024]{4,3,2,1,0:T(4,128)(2,1)S(1)}, bf16[2,2,6,4,1024]{4,3,2,1,0:T(4,128)(2,1)}, u32[]{:S(2)}, u32[]{:S(2)}) %collective-permute-start.10) | collective-permute-done | bytes 196640 | tf_op jit(solution)/shard_map/ppermute | solution.py:50
  142.9 1.3 select_bitcast_fusion.3
  144.1 1.0 pad_maximum_fusion.1
  145.1 3.5 %collective-permute-start.11 = (bf16[2,2,2,6,4,1024]{5,4,3,2,1,0:T(4,128)(2,1)}, bf16[2,2,2,6,4,1024]{5,4,3,2,1,0:T(4,128)(2,1)}, u32[]{:S(2)}, u32[]{:S(2)}) collective-permute-start(bf16[2,2,2,6,4,1024]{5,4,3,2,1,0:T(4,128)(2,1)} %pad_maximum_fusion.1), channel_id=1, source_target_pairs={{0,384},{48,432},{96,480},{144,528},{192,576},{240,624},{288,672},... | collective-permute-start | bytes 1179656 | tf_op jit(solution)/shard_map/ppermute | solution.py:50
  148.6 1.9 fusion.57
  151.2 1.4 reshape.545
  152.6 1.4 reshape.544
  154.0 1.5 copy.16
  155.5 1.6 eq.54
  157.1 1.5 copy.17
  158.6 1.5 eq.58
  161.5 1.5 select_bitcast_fusion.1
  163.5 1.3 fusion.56
  165.7 1.1 reshape.548
  166.9 2.0 multiply_convert_fusion
  168.9 1.3 multiply_reduce_fusion.5
  170.9 4.6 %multiply_reduce_fusion.3 = (f32[2]{0:T(128)S(1)}, f32[2,3072]{1,0:T(2,128)S(1)}) fusion(f32[2,3072]{1,0:T(2,128)} %copy-done.6, f32[2]{0:T(128)} %copy-done.105, f32[3072]{0:T(1024)} %param.16, bf16[3072,1024]{1,0:T(8,128)(2,1)} %param.17, f32[2,1024]{1,0:T(2,128)} %copy-done.12, f32[2,1024]{1,0:T(2,128)S(1)} %get-tuple-element.99, ...), kind=kOutput, calls=%fused_computation.77 | convolution fusion | flops 12617726 | bytes 6369312 | tf_op jit(solution)/shard_map/dot_general | solution.py:161
  177.8 1.0 add_convert_fusion.1
  178.9 1.1 copy-done.1
  180.0 1.7 fusion.54
  181.6 2.0 collective-permute-start.12
  184.0 3.6 %collective-permute-start.13 = (bf16[2,3,32,3072]{3,2,1,0:T(8,128)(2,1)}, bf16[2,3,32,3072]{3,2,1,0:T(8,128)(2,1)S(1)}, u32[]{:S(2)}, u32[]{:S(2)}) collective-permute-start(bf16[2,3,32,3072]{3,2,1,0:T(8,128)(2,1)} %get-tuple-element.20), channel_id=1, source_target_pairs={{1,0},{2,1},{3,2},{4,3},{5,4},{6,5},{7,6},{9,8},{10,9},{11,10},{12... | collective-permute-start | bytes 3538952 | tf_op jit(solution)/shard_map/ppermute | solution.py:24
  190.1 22.1 %collective-permute-done.12 = bf16[2,3,32,3072]{3,2,1,0:T(8,128)(2,1)S(1)} collective-permute-done((bf16[2,3,32,3072]{3,2,1,0:T(8,128)(2,1)}, bf16[2,3,32,3072]{3,2,1,0:T(8,128)(2,1)S(1)}, u32[]{:S(2)}, u32[]{:S(2)}) %collective-permute-start.12) | collective-permute-done | bytes 1179680 | tf_op jit(solution)/shard_map/ppermute | solution.py:23
  213.0 2.2 select_maximum_fusion
  215.7 26.1 %add_convert_fusion = bf16[2,4,32,3072]{3,2,1,0:T(8,128)(2,1)} fusion(bf16[2,4,32,3072]{3,2,1,0:T(8,128)(2,1)S(1)} %copy-done.2, bf16[2,10,38,3072]{3,2,1,0:T(8,128)(2,1)S(1)} %select_maximum_fusion, bf16[2,7,32,3072]{3,2,1,0:T(8,128)(2,1)S(1)} %constant_dynamic-update-slice_fusion.6, bf16[2,7,32,3072]{3,2,1,0:T(8,128)(2,1)S(1)} %get-tuple-element.17, ...), kind=kLoop, calls=%fused_computation.42 | loop fusion | flops 116391936 | bytes 79269888 | tf_op jit(solution)/shard_map/convert_element_type | solution.py:177
  (287 shorter events, 16.7 us)
Async XLA Ops:
  0.6 32.2 %copy-start = (bf16[2,4,32,3072]{3,2,1,0:T(8,128)(2,1)S(1)}, bf16[2,4,32,3072]{3,2,1,0:T(8,128)(2,1)}, u32[]{:S(2)}) copy-start(bf16[2,4,32,3072]{3,2,1,0:T(8,128)(2,1)} %param.11) | copy-start | bytes 4718596
  2.6 30.2 %collective-permute-start = (bf16[2,3,32,3072]{3,2,1,0:T(8,128)(2,1)S(1)}, bf16[2,3,32,3072]{3,2,1,0:T(8,128)(2,1)S(1)}, u32[]{:S(2)}, u32[]{:S(2)}) collective-permute-start(bf16[2,3,32,3072]{3,2,1,0:T(8,128)(2,1)S(1)} %get-tuple-element.23), channel_id=1, source_target_pairs={{0,1},{1,2},{2,3},{3,4},{4,5},{5,6},{6,7},{8,9},{9,10},{10,11},{11... | collective-permute-start | bytes 3538952 | tf_op jit(solution)/shard_map/ppermute | solution.py:23
  4.5 28.7 %collective-permute-start.1 = (bf16[2,3,32,3072]{3,2,1,0:T(8,128)(2,1)S(1)}, bf16[2,3,32,3072]{3,2,1,0:T(8,128)(2,1)S(1)}, u32[]{:S(2)}, u32[]{:S(2)}) collective-permute-start(bf16[2,3,32,3072]{3,2,1,0:T(8,128)(2,1)S(1)} %get-tuple-element.24), channel_id=1, source_target_pairs={{1,0},{2,1},{3,2},{4,3},{5,4},{6,5},{7,6},{9,8},{10,9},{11,10},{12... | collective-permute-start | bytes 3538952 | tf_op jit(solution)/shard_map/ppermute | solution.py:24
  9.0 26.6 %copy-start.35 = (f32[1,1,3072]{2,1,0:T(1,128)}, f32[1,1,3072]{2,1,0:T(1,128)S(1)}, u32[]{:S(2)}) copy-start(f32[1,1,3072]{2,1,0:T(1,128)S(1)} %get-tuple-element.31) | copy-start | bytes 36868
  9.0 26.6 %copy-start.37 = (f32[1,1,3072]{2,1,0:T(1,128)}, f32[1,1,3072]{2,1,0:T(1,128)S(1)}, u32[]{:S(2)}) copy-start(f32[1,1,3072]{2,1,0:T(1,128)S(1)} %get-tuple-element.32) | copy-start | bytes 36868
  9.0 26.6 %copy-start.39 = (f32[1,1,3072]{2,1,0:T(1,128)}, f32[1,1,3072]{2,1,0:T(1,128)S(1)}, u32[]{:S(2)}) copy-start(f32[1,1,3072]{2,1,0:T(1,128)S(1)} %get-tuple-element.33) | copy-start | bytes 36868
  9.0 26.6 %copy-start.41 = (f32[1,1,3072]{2,1,0:T(1,128)}, f32[1,1,3072]{2,1,0:T(1,128)S(1)}, u32[]{:S(2)}) copy-start(f32[1,1,3072]{2,1,0:T(1,128)S(1)} %get-tuple-element.34) | copy-start | bytes 36868
  9.0 26.6 %copy-start.43 = (f32[1,1,3072]{2,1,0:T(1,128)}, f32[1,1,3072]{2,1,0:T(1,128)S(1)}, u32[]{:S(2)}) copy-start(f32[1,1,3072]{2,1,0:T(1,128)S(1)} %get-tuple-element.35) | copy-start | bytes 36868
  9.0 26.6 %copy-start.45 = (f32[1,1,3072]{2,1,0:T(1,128)}, f32[1,1,3072]{2,1,0:T(1,128)S(1)}, u32[]{:S(2)}) copy-start(f32[1,1,3072]{2,1,0:T(1,128)S(1)} %get-tuple-element.36) | copy-start | bytes 36868
  9.1 26.6 %copy-start.47 = (f32[1,1,3072]{2,1,0:T(1,128)}, f32[1,1,3072]{2,1,0:T(1,128)S(1)}, u32[]{:S(2)}) copy-start(f32[1,1,3072]{2,1,0:T(1,128)S(1)} %get-tuple-element.37) | copy-start | bytes 36868
  9.1 26.6 %copy-start.49 = (f32[1,1,3072]{2,1,0:T(1,128)}, f32[1,1,3072]{2,1,0:T(1,128)S(1)}, u32[]{:S(2)}) copy-start(f32[1,1,3072]{2,1,0:T(1,128)S(1)} %get-tuple-element.38) | copy-start | bytes 36868
  9.1 26.6 %copy-start.51 = (f32[1,1,3072]{2,1,0:T(1,128)}, f32[1,1,3072]{2,1,0:T(1,128)S(1)}, u32[]{:S(2)}) copy-start(f32[1,1,3072]{2,1,0:T(1,128)S(1)} %get-tuple-element.39) | copy-start | bytes 36868
  9.1 26.6 %copy-start.53 = (f32[1,1,3072]{2,1,0:T(1,128)}, f32[1,1,3072]{2,1,0:T(1,128)S(1)}, u32[]{:S(2)}) copy-start(f32[1,1,3072]{2,1,0:T(1,128)S(1)} %get-tuple-element.40) | copy-start | bytes 36868
  9.1 26.6 %copy-start.55 = (f32[1,1,3072]{2,1,0:T(1,128)}, f32[1,1,3072]{2,1,0:T(1,128)S(1)}, u32[]{:S(2)}) copy-start(f32[1,1,3072]{2,1,0:T(1,128)S(1)} %get-tuple-element.41) | copy-start | bytes 36868
  9.1 26.6 %copy-start.57 = (f32[1,1,3072]{2,1,0:T(1,128)}, f32[1,1,3072]{2,1,0:T(1,128)S(1)}, u32[]{:S(2)}) copy-start(f32[1,1,3072]{2,1,0:T(1,128)S(1)} %get-tuple-element.42) | copy-start | bytes 36868
  9.1 26.6 %copy-start.59 = (f32[1,1,3072]{2,1,0:T(1,128)}, f32[1,1,3072]{2,1,0:T(1,128)S(1)}, u32[]{:S(2)}) copy-start(f32[1,1,3072]{2,1,0:T(1,128)S(1)} %get-tuple-element.43) | copy-start | bytes 36868
  9.1 26.6 %copy-start.61 = (f32[1,1,3072]{2,1,0:T(1,128)}, f32[1,1,3072]{2,1,0:T(1,128)S(1)}, u32[]{:S(2)}) copy-start(f32[1,1,3072]{2,1,0:T(1,128)S(1)} %get-tuple-element.44) | copy-start | bytes 36868
  9.1 26.6 %copy-start.63 = (f32[1,1,3072]{2,1,0:T(1,128)}, f32[1,1,3072]{2,1,0:T(1,128)S(1)}, u32[]{:S(2)}) copy-start(f32[1,1,3072]{2,1,0:T(1,128)S(1)} %get-tuple-element.45) | copy-start | bytes 36868
  9.1 26.6 %copy-start.65 = (f32[1,1,3072]{2,1,0:T(1,128)}, f32[1,1,3072]{2,1,0:T(1,128)S(1)}, u32[]{:S(2)}) copy-start(f32[1,1,3072]{2,1,0:T(1,128)S(1)} %get-tuple-element.46) | copy-start | bytes 36868
  9.2 26.6 %copy-start.67 = (f32[1,1,3072]{2,1,0:T(1,128)}, f32[1,1,3072]{2,1,0:T(1,128)S(1)}, u32[]{:S(2)}) copy-start(f32[1,1,3072]{2,1,0:T(1,128)S(1)} %get-tuple-element.47) | copy-start | bytes 36868
  9.2 26.6 %copy-start.69 = (f32[1,1,3072]{2,1,0:T(1,128)}, f32[1,1,3072]{2,1,0:T(1,128)S(1)}, u32[]{:S(2)}) copy-start(f32[1,1,3072]{2,1,0:T(1,128)S(1)} %get-tuple-element.48) | copy-start | bytes 36868
  9.2 26.6 %copy-start.71 = (f32[1,1,3072]{2,1,0:T(1,128)}, f32[1,1,3072]{2,1,0:T(1,128)S(1)}, u32[]{:S(2)}) copy-start(f32[1,1,3072]{2,1,0:T(1,128)S(1)} %get-tuple-element.49) | copy-start | bytes 36868
  10.0 25.8 %copy-start.73 = (f32[1,1,3072]{2,1,0:T(1,128)}, f32[1,1,3072]{2,1,0:T(1,128)S(1)}, u32[]{:S(2)}) copy-start(f32[1,1,3072]{2,1,0:T(1,128)S(1)} %get-tuple-element.50) | copy-start | bytes 36868
  10.0 25.8 %copy-start.75 = (f32[1,1,3072]{2,1,0:T(1,128)}, f32[1,1,3072]{2,1,0:T(1,128)S(1)}, u32[]{:S(2)}) copy-start(f32[1,1,3072]{2,1,0:T(1,128)S(1)} %get-tuple-element.51) | copy-start | bytes 36868
  10.0 25.8 %copy-start.77 = (f32[1,1,3072]{2,1,0:T(1,128)}, f32[1,1,3072]{2,1,0:T(1,128)S(1)}, u32[]{:S(2)}) copy-start(f32[1,1,3072]{2,1,0:T(1,128)S(1)} %get-tuple-element.52) | copy-start | bytes 36868
  10.0 25.8 %copy-start.79 = (f32[1,1,3072]{2,1,0:T(1,128)}, f32[1,1,3072]{2,1,0:T(1,128)S(1)}, u32[]{:S(2)}) copy-start(f32[1,1,3072]{2,1,0:T(1,128)S(1)} %get-tuple-element.53) | copy-start | bytes 36868
  10.0 25.8 %copy-start.81 = (f32[1,1,3072]{2,1,0:T(1,128)}, f32[1,1,3072]{2,1,0:T(1,128)S(1)}, u32[]{:S(2)}) copy-start(f32[1,1,3072]{2,1,0:T(1,128)S(1)} %get-tuple-element.54) | copy-start | bytes 36868
  10.0 25.8 %copy-start.83 = (f32[1,1,3072]{2,1,0:T(1,128)}, f32[1,1,3072]{2,1,0:T(1,128)S(1)}, u32[]{:S(2)}) copy-start(f32[1,1,3072]{2,1,0:T(1,128)S(1)} %get-tuple-element.55) | copy-start | bytes 36868
  10.0 25.8 %copy-start.85 = (f32[1,1,3072]{2,1,0:T(1,128)}, f32[1,1,3072]{2,1,0:T(1,128)S(1)}, u32[]{:S(2)}) copy-start(f32[1,1,3072]{2,1,0:T(1,128)S(1)} %get-tuple-element.56) | copy-start | bytes 36868
  10.0 25.8 %copy-start.87 = (f32[1,1,3072]{2,1,0:T(1,128)}, f32[1,1,3072]{2,1,0:T(1,128)S(1)}, u32[]{:S(2)}) copy-start(f32[1,1,3072]{2,1,0:T(1,128)S(1)} %get-tuple-element.57) | copy-start | bytes 36868
  10.0 25.8 %copy-start.89 = (f32[1,1,3072]{2,1,0:T(1,128)}, f32[1,1,3072]{2,1,0:T(1,128)S(1)}, u32[]{:S(2)}) copy-start(f32[1,1,3072]{2,1,0:T(1,128)S(1)} %get-tuple-element.58) | copy-start | bytes 36868
  10.2 25.7 %copy-start.13 = (f32[1,1,3072]{2,1,0:T(1,128)}, f32[1,1,3072]{2,1,0:T(1,128)S(1)}, u32[]{:S(2)}) copy-start(f32[1,1,3072]{2,1,0:T(1,128)S(1)} %get-tuple-element.69) | copy-start | bytes 36868
  10.2 25.7 %copy-start.15 = (f32[1,1,3072]{2,1,0:T(1,128)}, f32[1,1,3072]{2,1,0:T(1,128)S(1)}, u32[]{:S(2)}) copy-start(f32[1,1,3072]{2,1,0:T(1,128)S(1)} %get-tuple-element.70) | copy-start | bytes 36868
  10.2 25.7 %copy-start.17 = (f32[1,1,3072]{2,1,0:T(1,128)}, f32[1,1,3072]{2,1,0:T(1,128)S(1)}, u32[]{:S(2)}) copy-start(f32[1,1,3072]{2,1,0:T(1,128)S(1)} %get-tuple-element.71) | copy-start | bytes 36868
  65.7 3.1 %collective-permute-start.2 = (f32[2,3072]{1,0:T(2,128)S(1)}, f32[2,3072]{1,0:T(2,128)S(1)}, u32[]{:S(2)}, u32[]{:S(2)}) collective-permute-start(f32[2,3072]{1,0:T(2,128)S(1)} %broadcast_multiply_fusion.1), channel_id=1, source_target_pairs={{0,1},{1,0},{2,3},{3,2},{4,5},{5,4},{6,7},{7,6},{8,9},{9,8},{10,11... | collective-permute-start | bytes 73736 | tf_op jit(solution)/shard_map/ppermute | solution.py:33
  68.8 5.7 %collective-permute-start.3 = (f32[2,3072]{1,0:T(2,128)S(1)}, f32[2,3072]{1,0:T(2,128)S(1)}, u32[]{:S(2)}, u32[]{:S(2)}) collective-permute-start(f32[2,3072]{1,0:T(2,128)S(1)} %fusion.49), channel_id=1, source_target_pairs={{0,2},{1,3},{2,0},{3,1},{4,6},{5,7},{6,4},{7,5},{8,10},{9,11},{10,... | collective-permute-start | bytes 73736 | tf_op jit(solution)/shard_map/ppermute | solution.py:33
  74.5 5.7 %collective-permute-start.4 = (f32[2,3072]{1,0:T(2,128)S(1)}, f32[2,3072]{1,0:T(2,128)S(1)}, u32[]{:S(2)}, u32[]{:S(2)}) collective-permute-start(f32[2,3072]{1,0:T(2,128)S(1)} %add.507), channel_id=1, source_target_pairs={{0,4},{1,5},{2,6},{3,7},{4,0},{5,1},{6,2},{7,3},{8,12},{9,13},{10,... | collective-permute-start | bytes 73736 | tf_op jit(solution)/shard_map/ppermute | solution.py:33
  85.0 30.4 %copy-start.110 = (f32[2]{0:T(128)}, f32[2]{0:T(128)S(1)}, u32[]{:S(2)}) copy-start(f32[2]{0:T(128)S(1)} %get-tuple-element.94) | copy-start | bytes 28
  85.1 12.9 %collective-permute-start.5 = (bf16[4,1024]{1,0:T(4,128)(2,1)S(1)}, bf16[4,1024]{1,0:T(4,128)(2,1)S(1)}, u32[]{:S(2)}, u32[]{:S(2)}) collective-permute-start(bf16[4,1024]{1,0:T(4,128)(2,1)S(1)} %get-tuple-element.87), channel_id=1, source_target_pairs={{0,8},{8,16},{16,0},{24,32},{32,40},{40,24},{1,9},{9,17},{17,1},{2... | collective-permute-start | bytes 24584 | tf_op jit(solution)/shard_map/ppermute | solution.py:50
  91.2 8.9 %collective-permute-start.6 = (bf16[4,1024]{1,0:T(4,128)(2,1)S(1)}, bf16[4,1024]{1,0:T(4,128)(2,1)S(1)}, u32[]{:S(2)}, u32[]{:S(2)}) collective-permute-start(bf16[4,1024]{1,0:T(4,128)(2,1)S(1)} %get-tuple-element.87), channel_id=1, source_target_pairs={{0,16},{8,0},{16,8},{24,40},{32,24},{40,32},{1,17},{9,1},{17,9},{2... | collective-permute-start | bytes 24584 | tf_op jit(solution)/shard_map/ppermute | solution.py:50
  100.9 14.5 %collective-permute-start.7 = (bf16[3,4,1024]{2,1,0:T(4,128)(2,1)S(1)}, bf16[3,4,1024]{2,1,0:T(4,128)(2,1)S(1)}, u32[]{:S(2)}, u32[]{:S(2)}) collective-permute-start(bf16[3,4,1024]{2,1,0:T(4,128)(2,1)S(1)} %broadcast_select_fusion), channel_id=1, source_target_pairs={{0,24},{8,32},{16,40},{24,0},{32,8},{40,16},{1,25},{9,33},{17,41},... | collective-permute-start | bytes 73736 | tf_op jit(solution)/shard_map/ppermute | solution.py:50
  115.5 6.0 %collective-permute-start.8 = (bf16[6,4,1024]{2,1,0:T(4,128)(2,1)S(1)}, bf16[6,4,1024]{2,1,0:T(4,128)(2,1)S(1)}, u32[]{:S(2)}, u32[]{:S(2)}) collective-permute-start(bf16[6,4,1024]{2,1,0:T(4,128)(2,1)S(1)} %bitcast.88), channel_id=1, source_target_pairs={{0,48},{48,0},{96,144},{144,96},{192,240},{240,192},{288,336},{336... | collective-permute-start | bytes 147464 | tf_op jit(solution)/shard_map/ppermute | solution.py:50
  121.6 8.7 %collective-permute-start.9 = (bf16[2,6,4,1024]{3,2,1,0:T(4,128)(2,1)S(1)}, bf16[2,6,4,1024]{3,2,1,0:T(4,128)(2,1)S(1)}, u32[]{:S(2)}, u32[]{:S(2)}) collective-permute-start(bf16[2,6,4,1024]{3,2,1,0:T(4,128)(2,1)S(1)} %pad_maximum_fusion.3), channel_id=1, source_target_pairs={{0,96},{48,144},{96,0},{144,48},{192,288},{240,336},{288,192},{336... | collective-permute-start | bytes 294920 | tf_op jit(solution)/shard_map/ppermute | solution.py:50
  131.2 11.7 %collective-permute-start.10 = (bf16[2,2,6,4,1024]{4,3,2,1,0:T(4,128)(2,1)S(1)}, bf16[2,2,6,4,1024]{4,3,2,1,0:T(4,128)(2,1)}, u32[]{:S(2)}, u32[]{:S(2)}) collective-permute-start(bf16[2,2,6,4,1024]{4,3,2,1,0:T(4,128)(2,1)S(1)} %pad_maximum_fusion.2), channel_id=1, source_target_pairs={{0,192},{48,240},{96,288},{144,336},{192,0},{240,48},{288,96},{336... | collective-permute-start | bytes 589832 | tf_op jit(solution)/shard_map/ppermute | solution.py:50
  145.1 16.4 %collective-permute-start.11 = (bf16[2,2,2,6,4,1024]{5,4,3,2,1,0:T(4,128)(2,1)}, bf16[2,2,2,6,4,1024]{5,4,3,2,1,0:T(4,128)(2,1)}, u32[]{:S(2)}, u32[]{:S(2)}) collective-permute-start(bf16[2,2,2,6,4,1024]{5,4,3,2,1,0:T(4,128)(2,1)} %pad_maximum_fusion.1), channel_id=1, source_target_pairs={{0,384},{48,432},{96,480},{144,528},{192,576},{240,624},{288,672},... | collective-permute-start | bytes 1179656 | tf_op jit(solution)/shard_map/ppermute | solution.py:50
  181.6 30.6 %copy-start.2 = (bf16[2,4,32,3072]{3,2,1,0:T(8,128)(2,1)S(1)}, bf16[2,4,32,3072]{3,2,1,0:T(8,128)(2,1)}, u32[]{:S(2)}) copy-start(bf16[2,4,32,3072]{3,2,1,0:T(8,128)(2,1)} %copy-done.1) | copy-start | bytes 4718596
  181.6 30.5 %collective-permute-start.12 = (bf16[2,3,32,3072]{3,2,1,0:T(8,128)(2,1)}, bf16[2,3,32,3072]{3,2,1,0:T(8,128)(2,1)S(1)}, u32[]{:S(2)}, u32[]{:S(2)}) collective-permute-start(bf16[2,3,32,3072]{3,2,1,0:T(8,128)(2,1)} %get-tuple-element.19), channel_id=1, source_target_pairs={{0,1},{1,2},{2,3},{3,4},{4,5},{5,6},{6,7},{8,9},{9,10},{10,11},{11... | collective-permute-start | bytes 3538952 | tf_op jit(solution)/shard_map/ppermute | solution.py:23
  184.0 29.0 %collective-permute-start.13 = (bf16[2,3,32,3072]{3,2,1,0:T(8,128)(2,1)}, bf16[2,3,32,3072]{3,2,1,0:T(8,128)(2,1)S(1)}, u32[]{:S(2)}, u32[]{:S(2)}) collective-permute-start(bf16[2,3,32,3072]{3,2,1,0:T(8,128)(2,1)} %get-tuple-element.20), channel_id=1, source_target_pairs={{1,0},{2,1},{3,2},{4,3},{5,4},{6,5},{7,6},{9,8},{10,9},{11,10},{12... | collective-permute-start | bytes 3538952 | tf_op jit(solution)/shard_map/ppermute | solution.py:24
  (79 other events, 461.4 us)

commit v7 on v6

--- a/solution.py
+++ b/solution.py
@@ -81,9 +81,10 @@
     return values * lax.rsqrt(jnp.sum(values * values, axis=-1, keepdims=True) + 1e-06)
 
 
-def depthwise_rows(field, kernel):
+def depthwise_rows(field, kernel, beside=None):
     batch_rows, row_count, width, channels = field.shape
     framed = halo_rows(field, 3)
+    framed, beside = lax.optimization_barrier((framed, beside))
     framed = jnp.pad(framed, ((0, 0), (0, 0), (3, 3), (0, 0)))
     summed = jnp.zeros(field.shape, jnp.float32)
     for tap_row in range(7):
@@ -92,7 +93,7 @@
                 jnp.float32
             )
             summed = summed + window * kernel[tap_row, tap_col].astype(jnp.float32)
-    return summed
+    return summed, beside
 
 
 def local(
@@ -113,42 +114,45 @@
     dp_count = lax.axis_size("dp")
     dp_at = lax.axis_index("dp")
     img_at = lax.axis_index("img")
-    conved = depthwise_rows(section_map, dw_kernel) + conv_bias
+    text_f = texts.astype(jnp.float32)
+    text_vec = unit_rows(text_f).astype(jnp.bfloat16)
+    text_count = texts.shape[0]
+    share = text_count // img_count
+    text_share = lax.dynamic_slice_in_dim(text_vec, img_at * share, share)
+    count = dp_count * text_count
+
+    def in_gathered_order(vector):
+        return jnp.transpose(vector.reshape(dp_count, batch_rows, img_count), (0, 2, 1)).reshape(-1)
+
+    positives_g = in_gathered_order(positives)
+    sources_g = in_gathered_order(sources)
+    labels = jnp.where(positives_g[:, None] == jnp.arange(count)[None, :], 1.0, -1.0).astype(
+        jnp.float32
+    )
+    source_table = (sources_g[:, None] == jnp.arange(SOURCES)[None, :]).astype(jnp.float32)
+    weights = (
+        SOURCES
+        * jnp.sum(source_table * numerators.astype(jnp.float32)[None, :], axis=1)
+        / jnp.sum(numerators).astype(jnp.float32)
+    )
+    early = (text_share, labels, source_table, weights)
+    conved, early = depthwise_rows(section_map, dw_kernel, early)
+    text_share, labels, source_table, weights = early
+    conved = conved + conv_bias
     section_out = section_map.astype(jnp.float32) + layer_scale * cell_norm(conved, ln_gain)
     partial_value = jnp.sum(section_out, axis=(1, 2)) / (H * W)
     pooled = group_sum(partial_value)
     head_in = cell_norm(pooled, head_gain).astype(jnp.bfloat16)
     embed = jnp.dot(head_in, head_weight, preferred_element_type=jnp.float32)
     image_vec = unit_rows(embed).astype(jnp.bfloat16)
-    text_f = texts.astype(jnp.float32)
-    text_vec = unit_rows(text_f).astype(jnp.bfloat16)
-    text_count = texts.shape[0]
-    share = text_count // img_count
-    text_share = lax.dynamic_slice_in_dim(text_vec, img_at * share, share)
     payload = jnp.concatenate([image_vec, text_share], axis=0)
     gathered = gather_stages(payload, "img", radix_split(img_count))
     gathered = gather_stages(gathered, "dp", radix_split(dp_count))
     image_all = gathered[:, :, :batch_rows, :].reshape(dp_count * img_count * batch_rows, -1)
     text_all = gathered[:, :, batch_rows:, :].reshape(dp_count * text_count, -1)
-    count = text_all.shape[0]
-
-    def in_gathered_order(vector):
-        return jnp.transpose(vector.reshape(dp_count, batch_rows, img_count), (0, 2, 1)).reshape(-1)
-
-    positives_g = in_gathered_order(positives)
-    sources_g = in_gathered_order(sources)
     logits = (
         LOGIT_SCALE * jnp.dot(image_all, text_all.T, preferred_element_type=jnp.float32)
         + LOGIT_BIAS
-    )
-    labels = jnp.where(positives_g[:, None] == jnp.arange(count)[None, :], 1.0, -1.0).astype(
-        jnp.float32
-    )
-    source_table = (sources_g[:, None] == jnp.arange(SOURCES)[None, :]).astype(jnp.float32)
-    weights = (
-        SOURCES
-        * jnp.sum(source_table * numerators.astype(jnp.float32)[None, :], axis=1)
-        / jnp.sum(numerators).astype(jnp.float32)
     )
     pair_grad = (weights[:, None] * -labels * jax.nn.sigmoid(-labels * logits)).astype(
         jnp.bfloat16
@@ -173,7 +177,7 @@
     )
     text_back = jax.vjp(unit_rows, text_f)[1]
     text_grad = text_back(text_dir)[0]
-    spread = depthwise_rows(conv_grad, dw_kernel[::-1, ::-1, :])
+    spread = depthwise_rows(conv_grad, dw_kernel[::-1, ::-1, :])[0]
     grad_map = (own_grad[:, None, None, :] + spread).astype(jnp.bfloat16)
     return (grad_map, text_grad, group_sums)
 

time: 246 us -> 242 us (0.984)
  local copies, waits for them, and re-layouts: 20.9 us -> 13.5 us
  waiting for transfers between devices: 65.5 us -> 68 us
    ppermute x7, waiting for transfers between devices: 14 us -> 21.9 us  [gather_stages(): got.append(lax.ppermute(value, axis, pairs))]
    ppermute x2, waiting for transfers between devices: 44.6 us -> 39.2 us  [halo_rows(): before = lax.ppermute(last, 'row', up)]
    transpose x2, local copies, waits for them, and re-layouts: 3.07 us -> 0.41 us  [in_gathered_order(): jnp.transpose(vector.reshape(dp_count, batch_rows, img_count), (0, 2, 1))]
    reshape x2, local copies, waits for them, and re-layouts: 2.81 us -> 0.22 us  [in_gathered_order(): vector.reshape(dp_count, batch_rows, img_count)]
  transfers between devices with their start and end apart: 14 -> 14, of which waited for: 10 -> 11; matrix products, arithmetic and copies ran while one was open for 8% -> 4% of each run, Pallas kernels for 0% -> 0%
where the time goes in v7:
time: 242 us; the launch traced here: 239 us
  other arithmetic  78.1 us (32%)
  waiting for transfers between devices  68 us (28%)
  starting transfers between devices  63.7 us (26%)
  local copies, waits for them, and re-layouts  13.5 us (6%)
  matrix products  12.3 us (5%)
  between operations  3.55 us (1%)
    ppermute x7, starting transfers between devices, gather_stages(): got.append(lax.ppermute(value, axis, pairs))  45.2 us
    ppermute x2, waiting for transfers between devices, halo_rows(): before = lax.ppermute(last, 'row', up)  39.2 us
    reduce_sum x4, other arithmetic, cell_norm(): center = values - jnp.mean(values, axis=-1, keepdims=True)  30.1 us
    convert_element_type x1, other arithmetic, local(): grad_map = (own_grad[:, None, None, :] + spread).astype(jnp.bfloat16)  27.3 us
    ppermute x7, waiting for transfers between devices, gather_stages(): got.append(lax.ppermute(value, axis, pairs))  21.9 us
    ppermute x3, starting transfers between devices, group_sum(): value = value + lax.ppermute(value, 'row', pairs)  7.47 us
    ppermute x2, starting transfers between devices, halo_rows(): after = lax.ppermute(leading, 'row', down)  7.29 us
    ppermute x3, waiting for transfers between devices, group_sum(): value = value + lax.ppermute(value, 'row', pairs)  6.97 us
  transfers between devices with their start and end apart: 14, of which 11 were waited for; matrix products, arithmetic and copies ran while one was open for 4% of the time, Pallas kernels for 0%

profile of v7, /device:TPU:6, one launch (start us, length us, event | category | flops | bytes accessed | tf_op | source)
XLA Modules:
  0.0 239.2 jit_solution(3952775361351055044)
XLA Ops:
  0.7 3.3 %fusion.27 = (bf16[2,3,32,3072]{3,2,1,0:T(8,128)(2,1)}, bf16[2,3,32,3072]{3,2,1,0:T(8,128)(2,1)}) fusion(bf16[2,4,32,3072]{3,2,1,0:T(8,128)(2,1)} %param.11), kind=kLoop, calls=%fused_computation.221 | loop fusion | bytes 4718592 | tf_op jit(solution)/shard_map/slice | solution.py:21
  4.0 1.9 collective-permute-start
  5.9 3.6 %collective-permute-start.1 = (bf16[2,3,32,3072]{3,2,1,0:T(8,128)(2,1)}, bf16[2,3,32,3072]{3,2,1,0:T(8,128)(2,1)}, u32[]{:S(2)}, u32[]{:S(2)}) collective-permute-start(bf16[2,3,32,3072]{3,2,1,0:T(8,128)(2,1)} %get-tuple-element.30), channel_id=1, source_target_pairs={{1,0},{2,1},{3,2},{4,3},{5,4},{6,5},{7,6},{9,8},{10,9},{11,10},{12... | collective-permute-start | bytes 3538952 | tf_op jit(solution)/shard_map/ppermute | solution.py:24
  14.0 0.8 fusion.4
  16.0 0.8 slice_convert_fusion.47
  16.9 17.4 %collective-permute-done = bf16[2,3,32,3072]{3,2,1,0:T(8,128)(2,1)S(1)} collective-permute-done((bf16[2,3,32,3072]{3,2,1,0:T(8,128)(2,1)}, bf16[2,3,32,3072]{3,2,1,0:T(8,128)(2,1)S(1)}, u32[]{:S(2)}, u32[]{:S(2)}) %collective-permute-start) | collective-permute-done | bytes 1179680 | tf_op jit(solution)/shard_map/ppermute | solution.py:23
  34.4 1.5 pad_maximum_fusion
  36.3 29.0 %fusion.25 = (f32[2,4,32]{2,1,0:T(4,128)S(1)}, f32[2,4,32,3072]{3,2,1,0:T(8,128)S(1)}) fusion(f32[3072]{0:T(1024)S(1)} %copy-done.103, f32[3072]{0:T(1024)S(1)} %bitcast.107, f32[3072]{0:T(1024)S(1)} %bitcast.109, f32[3072]{0:T(1024)S(1)} %bitcast.113, f32[3072]{0:T(1024)S(1)} %bitcast.115, bf16[2,10,32,3072]{3,2,1,0:T(8,128)(2,1)S(1)} %pad_maximum_fusion, ...), kind=kLoop, calls=%fused_computation.219 | loop fusion | flops 116391680 | bytes 18703360 | tf_op jit(solution)/shard_map/reduce_sum | solution.py:75
  65.9 0.9 copy-done.1
  66.8 1.0 add_reduce_fusion
  67.7 1.9 collective-permute-start.2
  69.7 1.1 collective-permute-done.2
  70.9 1.9 collective-permute-start.3
  72.8 3.8 %collective-permute-done.3 = f32[2,3072]{1,0:T(2,128)S(1)} collective-permute-done((f32[2,3072]{1,0:T(2,128)S(1)}, f32[2,3072]{1,0:T(2,128)S(1)}, u32[]{:S(2)}, u32[]{:S(2)}) %collective-permute-start.3) | collective-permute-done | bytes 24608 | tf_op jit(solution)/shard_map/ppermute | solution.py:33
  76.6 3.6 %collective-permute-start.4 = (f32[2,3072]{1,0:T(2,128)S(1)}, f32[2,3072]{1,0:T(2,128)S(1)}, u32[]{:S(2)}, u32[]{:S(2)}) collective-permute-start(f32[2,3072]{1,0:T(2,128)S(1)} %add.509), channel_id=1, source_target_pairs={{0,4},{1,5},{2,6},{3,7},{4,0},{5,1},{6,2},{7,3},{8,12},{9,13},{10,... | collective-permute-start | bytes 73736 | tf_op jit(solution)/shard_map/ppermute | solution.py:33
  80.2 2.1 collective-permute-done.4
  83.2 3.9 %multiply_reduce_fusion.7 = (f32[2]{0:T(128)S(1)}, f32[2,1024]{1,0:T(2,128)S(1)}) fusion(bf16[3072,1024]{1,0:T(8,128)(2,1)} %param.17, f32[2]{0:T(128)S(1)} %fusion.20, f32[3072]{0:T(1024)S(1)} %copy-done.96, f32[2,3072]{1,0:T(2,128)S(1)} %get-tuple-element.24, f32[2]{0:T(128)S(1)} %broadcast_multiply_fusion.5), kind=kOutput, calls=%fused_computation.185 | convolution fusion | flops 12611582 | bytes 6336536 | tf_op jit(solution)/shard_map/dot_general | solution.py:146
  87.6 6.1 %collective-permute-start.5 = (bf16[4,1024]{1,0:T(4,128)(2,1)S(1)}, bf16[4,1024]{1,0:T(4,128)(2,1)S(1)}, u32[]{:S(2)}, u32[]{:S(2)}) collective-permute-start(bf16[4,1024]{1,0:T(4,128)(2,1)S(1)} %get-tuple-element.93), channel_id=1, source_target_pairs={{0,8},{8,16},{16,0},{24,32},{32,40},{40,24},{1,9},{9,17},{17,1},{2... | collective-permute-start | bytes 24584 | tf_op jit(solution)/shard_map/ppermute | solution.py:50
  93.7 6.7 %collective-permute-start.6 = (bf16[4,1024]{1,0:T(4,128)(2,1)S(1)}, bf16[4,1024]{1,0:T(4,128)(2,1)S(1)}, u32[]{:S(2)}, u32[]{:S(2)}) collective-permute-start(bf16[4,1024]{1,0:T(4,128)(2,1)S(1)} %get-tuple-element.93), channel_id=1, source_target_pairs={{0,16},{8,0},{16,8},{24,40},{32,24},{40,32},{1,17},{9,1},{17,9},{2... | collective-permute-start | bytes 24584 | tf_op jit(solution)/shard_map/ppermute | solution.py:50
  100.5 2.1 collective-permute-done.6
  103.3 12.7 %collective-permute-start.7 = (bf16[3,4,1024]{2,1,0:T(4,128)(2,1)S(1)}, bf16[3,4,1024]{2,1,0:T(4,128)(2,1)S(1)}, u32[]{:S(2)}, u32[]{:S(2)}) collective-permute-start(bf16[3,4,1024]{2,1,0:T(4,128)(2,1)S(1)} %broadcast_select_fusion), channel_id=1, source_target_pairs={{0,24},{8,32},{16,40},{24,0},{32,8},{40,16},{1,25},{9,33},{17,41},... | collective-permute-start | bytes 73736 | tf_op jit(solution)/shard_map/ppermute | solution.py:50
  116.1 1.8 collective-permute-done.7
  118.0 3.5 %collective-permute-start.8 = (bf16[6,4,1024]{2,1,0:T(4,128)(2,1)S(1)}, bf16[6,4,1024]{2,1,0:T(4,128)(2,1)S(1)}, u32[]{:S(2)}, u32[]{:S(2)}) collective-permute-start(bf16[6,4,1024]{2,1,0:T(4,128)(2,1)S(1)} %bitcast.88), channel_id=1, source_target_pairs={{0,48},{48,0},{96,144},{144,96},{192,240},{240,192},{288,336},{336... | collective-permute-start | bytes 147464 | tf_op jit(solution)/shard_map/ppermute | solution.py:50
  121.5 2.5 %collective-permute-done.8 = bf16[6,4,1024]{2,1,0:T(4,128)(2,1)S(1)} collective-permute-done((bf16[6,4,1024]{2,1,0:T(4,128)(2,1)S(1)}, bf16[6,4,1024]{2,1,0:T(4,128)(2,1)S(1)}, u32[]{:S(2)}, u32[]{:S(2)}) %collective-permute-start.8) | collective-permute-done | bytes 49184 | tf_op jit(solution)/shard_map/ppermute | solution.py:50
  124.1 5.0 %collective-permute-start.9 = (bf16[2,6,4,1024]{3,2,1,0:T(4,128)(2,1)S(1)}, bf16[2,6,4,1024]{3,2,1,0:T(4,128)(2,1)S(1)}, u32[]{:S(2)}, u32[]{:S(2)}) collective-permute-start(bf16[2,6,4,1024]{3,2,1,0:T(4,128)(2,1)S(1)} %pad_maximum_fusion.5), channel_id=1, source_target_pairs={{0,96},{48,144},{96,0},{144,48},{192,288},{240,336},{288,192},{336... | collective-permute-start | bytes 294920 | tf_op jit(solution)/shard_map/ppermute | solution.py:50
  129.1 3.6 %collective-permute-done.9 = bf16[2,6,4,1024]{3,2,1,0:T(4,128)(2,1)S(1)} collective-permute-done((bf16[2,6,4,1024]{3,2,1,0:T(4,128)(2,1)S(1)}, bf16[2,6,4,1024]{3,2,1,0:T(4,128)(2,1)S(1)}, u32[]{:S(2)}, u32[]{:S(2)}) %collective-permute-start.9) | collective-permute-done | bytes 98336 | tf_op jit(solution)/shard_map/ppermute | solution.py:50
  133.6 7.6 %collective-permute-start.10 = (bf16[2,2,6,4,1024]{4,3,2,1,0:T(4,128)(2,1)S(1)}, bf16[2,2,6,4,1024]{4,3,2,1,0:T(4,128)(2,1)}, u32[]{:S(2)}, u32[]{:S(2)}) collective-permute-start(bf16[2,2,6,4,1024]{4,3,2,1,0:T(4,128)(2,1)S(1)} %pad_maximum_fusion.4), channel_id=1, source_target_pairs={{0,192},{48,240},{96,288},{144,336},{192,0},{240,48},{288,96},{336... | collective-permute-start | bytes 589832 | tf_op jit(solution)/shard_map/ppermute | solution.py:50
  141.3 4.0 %collective-permute-done.10 = bf16[2,2,6,4,1024]{4,3,2,1,0:T(4,128)(2,1)} collective-permute-done((bf16[2,2,6,4,1024]{4,3,2,1,0:T(4,128)(2,1)S(1)}, bf16[2,2,6,4,1024]{4,3,2,1,0:T(4,128)(2,1)}, u32[]{:S(2)}, u32[]{:S(2)}) %collective-permute-start.10) | collective-permute-done | bytes 196640 | tf_op jit(solution)/shard_map/ppermute | solution.py:50
  145.3 1.3 select_bitcast_fusion.3
  146.6 1.0 pad_maximum_fusion.3
  147.6 3.5 %collective-permute-start.11 = (bf16[2,2,2,6,4,1024]{5,4,3,2,1,0:T(4,128)(2,1)}, bf16[2,2,2,6,4,1024]{5,4,3,2,1,0:T(4,128)(2,1)}, u32[]{:S(2)}, u32[]{:S(2)}) collective-permute-start(bf16[2,2,2,6,4,1024]{5,4,3,2,1,0:T(4,128)(2,1)} %pad_maximum_fusion.3), channel_id=1, source_target_pairs={{0,384},{48,432},{96,480},{144,528},{192,576},{240,624},{288,672},... | collective-permute-start | bytes 1179656 | tf_op jit(solution)/shard_map/ppermute | solution.py:50
  151.2 7.9 %collective-permute-done.11 = bf16[2,2,2,6,4,1024]{5,4,3,2,1,0:T(4,128)(2,1)} collective-permute-done((bf16[2,2,2,6,4,1024]{5,4,3,2,1,0:T(4,128)(2,1)}, bf16[2,2,2,6,4,1024]{5,4,3,2,1,0:T(4,128)(2,1)}, u32[]{:S(2)}, u32[]{:S(2)}) %collective-permute-start.11) | collective-permute-done | bytes 393248 | tf_op jit(solution)/shard_map/ppermute | solution.py:50
  159.1 1.5 select_bitcast_fusion.1
  161.1 1.3 fusion.28
  162.4 0.9 reshape.546
  163.3 1.1 reshape.545
  164.5 2.1 multiply_convert_fusion
  166.6 1.3 multiply_reduce_fusion.6
  168.6 4.6 %multiply_reduce_fusion.4 = (f32[2]{0:T(128)S(1)}, f32[2,3072]{1,0:T(2,128)S(1)}) fusion(f32[2,3072]{1,0:T(2,128)} %copy-done.7, f32[2]{0:T(128)} %copy-done.104, f32[3072]{0:T(1024)} %param.16, bf16[3072,1024]{1,0:T(8,128)(2,1)} %param.17, f32[2,1024]{1,0:T(2,128)} %copy-done.13, f32[2,1024]{1,0:T(2,128)S(1)} %get-tuple-element.105, ...), kind=kOutput, calls=%fused_computation.117 | convolution fusion | flops 12617726 | bytes 6369312 | tf_op jit(solution)/shard_map/dot_general | solution.py:165
  174.7 0.8 fusion.1
  175.5 1.0 add_convert_fusion.1
  176.6 1.1 copy-done.2
  177.7 1.3 fusion.26
  179.0 1.9 collective-permute-start.12
  180.9 3.6 %collective-permute-start.13 = (bf16[2,3,32,3072]{3,2,1,0:T(8,128)(2,1)S(1)}, bf16[2,3,32,3072]{3,2,1,0:T(8,128)(2,1)}, u32[]{:S(2)}, u32[]{:S(2)}) collective-permute-start(bf16[2,3,32,3072]{3,2,1,0:T(8,128)(2,1)S(1)} %get-tuple-element.28), channel_id=1, source_target_pairs={{1,0},{2,1},{3,2},{4,3},{5,4},{6,5},{7,6},{9,8},{10,9},{11,10},{12... | collective-permute-start | bytes 3538952 | tf_op jit(solution)/shard_map/ppermute | solution.py:24
  187.6 21.7 %collective-permute-done.12 = bf16[2,3,32,3072]{3,2,1,0:T(8,128)(2,1)S(1)} collective-permute-done((bf16[2,3,32,3072]{3,2,1,0:T(8,128)(2,1)}, bf16[2,3,32,3072]{3,2,1,0:T(8,128)(2,1)S(1)}, u32[]{:S(2)}, u32[]{:S(2)}) %collective-permute-start.12) | collective-permute-done | bytes 1179680 | tf_op jit(solution)/shard_map/ppermute | solution.py:23
  209.3 2.0 pad_maximum_fusion.1
  211.7 27.3 %add_convert_fusion = bf16[2,4,32,3072]{3,2,1,0:T(8,128)(2,1)} fusion(bf16[2,10,32,3072]{3,2,1,0:T(8,128)(2,1)S(1)} %pad_maximum_fusion.1, f32[2,3072]{1,0:T(2,128)S(1)} %copy-done.93, f32[3072]{0:T(1024)S(1)} %bitcast.108, f32[3072]{0:T(1024)S(1)} %bitcast.110, f32[3072]{0:T(1024)S(1)} %bitcast.114, f32[3072]{0:T(1024)S(1)} %bitcast.116, ...), kind=kLoop, calls=%fused_computation.8 | loop fusion | flops 116391936 | bytes 17141760 | tf_op jit(solution)/shard_map/convert_element_type | solution.py:181
  (288 shorter events, 14.2 us)
Async XLA Ops:
  0.6 33.7 %copy-start = (bf16[2,4,32,3072]{3,2,1,0:T(8,128)(2,1)S(1)}, bf16[2,4,32,3072]{3,2,1,0:T(8,128)(2,1)}, u32[]{:S(2)}) copy-start(bf16[2,4,32,3072]{3,2,1,0:T(8,128)(2,1)} %param.11) | copy-start | bytes 4718596
  4.0 30.4 %collective-permute-start = (bf16[2,3,32,3072]{3,2,1,0:T(8,128)(2,1)}, bf16[2,3,32,3072]{3,2,1,0:T(8,128)(2,1)S(1)}, u32[]{:S(2)}, u32[]{:S(2)}) collective-permute-start(bf16[2,3,32,3072]{3,2,1,0:T(8,128)(2,1)} %get-tuple-element.29), channel_id=1, source_target_pairs={{0,1},{1,2},{2,3},{3,4},{4,5},{5,6},{6,7},{8,9},{9,10},{10,11},{11... | collective-permute-start | bytes 3538952 | tf_op jit(solution)/shard_map/ppermute | solution.py:23
  5.9 28.4 %collective-permute-start.1 = (bf16[2,3,32,3072]{3,2,1,0:T(8,128)(2,1)}, bf16[2,3,32,3072]{3,2,1,0:T(8,128)(2,1)}, u32[]{:S(2)}, u32[]{:S(2)}) collective-permute-start(bf16[2,3,32,3072]{3,2,1,0:T(8,128)(2,1)} %get-tuple-element.30), channel_id=1, source_target_pairs={{1,0},{2,1},{3,2},{4,3},{5,4},{6,5},{7,6},{9,8},{10,9},{11,10},{12... | collective-permute-start | bytes 3538952 | tf_op jit(solution)/shard_map/ppermute | solution.py:24
  67.7 3.1 %collective-permute-start.2 = (f32[2,3072]{1,0:T(2,128)S(1)}, f32[2,3072]{1,0:T(2,128)S(1)}, u32[]{:S(2)}, u32[]{:S(2)}) collective-permute-start(f32[2,3072]{1,0:T(2,128)S(1)} %broadcast_multiply_fusion.1), channel_id=1, source_target_pairs={{0,1},{1,0},{2,3},{3,2},{4,5},{5,4},{6,7},{7,6},{8,9},{9,8},{10,11... | collective-permute-start | bytes 73736 | tf_op jit(solution)/shard_map/ppermute | solution.py:33
  70.9 5.7 %collective-permute-start.3 = (f32[2,3072]{1,0:T(2,128)S(1)}, f32[2,3072]{1,0:T(2,128)S(1)}, u32[]{:S(2)}, u32[]{:S(2)}) collective-permute-start(f32[2,3072]{1,0:T(2,128)S(1)} %fusion.22), channel_id=1, source_target_pairs={{0,2},{1,3},{2,0},{3,1},{4,6},{5,7},{6,4},{7,5},{8,10},{9,11},{10,... | collective-permute-start | bytes 73736 | tf_op jit(solution)/shard_map/ppermute | solution.py:33
  76.6 5.7 %collective-permute-start.4 = (f32[2,3072]{1,0:T(2,128)S(1)}, f32[2,3072]{1,0:T(2,128)S(1)}, u32[]{:S(2)}, u32[]{:S(2)}) collective-permute-start(f32[2,3072]{1,0:T(2,128)S(1)} %add.509), channel_id=1, source_target_pairs={{0,4},{1,5},{2,6},{3,7},{4,0},{5,1},{6,2},{7,3},{8,12},{9,13},{10,... | collective-permute-start | bytes 73736 | tf_op jit(solution)/shard_map/ppermute | solution.py:33
  87.6 12.9 %collective-permute-start.5 = (bf16[4,1024]{1,0:T(4,128)(2,1)S(1)}, bf16[4,1024]{1,0:T(4,128)(2,1)S(1)}, u32[]{:S(2)}, u32[]{:S(2)}) collective-permute-start(bf16[4,1024]{1,0:T(4,128)(2,1)S(1)} %get-tuple-element.93), channel_id=1, source_target_pairs={{0,8},{8,16},{16,0},{24,32},{32,40},{40,24},{1,9},{9,17},{17,1},{2... | collective-permute-start | bytes 24584 | tf_op jit(solution)/shard_map/ppermute | solution.py:50
  93.7 8.9 %collective-permute-start.6 = (bf16[4,1024]{1,0:T(4,128)(2,1)S(1)}, bf16[4,1024]{1,0:T(4,128)(2,1)S(1)}, u32[]{:S(2)}, u32[]{:S(2)}) collective-permute-start(bf16[4,1024]{1,0:T(4,128)(2,1)S(1)} %get-tuple-element.93), channel_id=1, source_target_pairs={{0,16},{8,0},{16,8},{24,40},{32,24},{40,32},{1,17},{9,1},{17,9},{2... | collective-permute-start | bytes 24584 | tf_op jit(solution)/shard_map/ppermute | solution.py:50
  103.3 14.5 %collective-permute-start.7 = (bf16[3,4,1024]{2,1,0:T(4,128)(2,1)S(1)}, bf16[3,4,1024]{2,1,0:T(4,128)(2,1)S(1)}, u32[]{:S(2)}, u32[]{:S(2)}) collective-permute-start(bf16[3,4,1024]{2,1,0:T(4,128)(2,1)S(1)} %broadcast_select_fusion), channel_id=1, source_target_pairs={{0,24},{8,32},{16,40},{24,0},{32,8},{40,16},{1,25},{9,33},{17,41},... | collective-permute-start | bytes 73736 | tf_op jit(solution)/shard_map/ppermute | solution.py:50
  118.0 6.0 %collective-permute-start.8 = (bf16[6,4,1024]{2,1,0:T(4,128)(2,1)S(1)}, bf16[6,4,1024]{2,1,0:T(4,128)(2,1)S(1)}, u32[]{:S(2)}, u32[]{:S(2)}) collective-permute-start(bf16[6,4,1024]{2,1,0:T(4,128)(2,1)S(1)} %bitcast.88), channel_id=1, source_target_pairs={{0,48},{48,0},{96,144},{144,96},{192,240},{240,192},{288,336},{336... | collective-permute-start | bytes 147464 | tf_op jit(solution)/shard_map/ppermute | solution.py:50
  124.1 8.7 %collective-permute-start.9 = (bf16[2,6,4,1024]{3,2,1,0:T(4,128)(2,1)S(1)}, bf16[2,6,4,1024]{3,2,1,0:T(4,128)(2,1)S(1)}, u32[]{:S(2)}, u32[]{:S(2)}) collective-permute-start(bf16[2,6,4,1024]{3,2,1,0:T(4,128)(2,1)S(1)} %pad_maximum_fusion.5), channel_id=1, source_target_pairs={{0,96},{48,144},{96,0},{144,48},{192,288},{240,336},{288,192},{336... | collective-permute-start | bytes 294920 | tf_op jit(solution)/shard_map/ppermute | solution.py:50
  133.6 11.7 %collective-permute-start.10 = (bf16[2,2,6,4,1024]{4,3,2,1,0:T(4,128)(2,1)S(1)}, bf16[2,2,6,4,1024]{4,3,2,1,0:T(4,128)(2,1)}, u32[]{:S(2)}, u32[]{:S(2)}) collective-permute-start(bf16[2,2,6,4,1024]{4,3,2,1,0:T(4,128)(2,1)S(1)} %pad_maximum_fusion.4), channel_id=1, source_target_pairs={{0,192},{48,240},{96,288},{144,336},{192,0},{240,48},{288,96},{336... | collective-permute-start | bytes 589832 | tf_op jit(solution)/shard_map/ppermute | solution.py:50
  147.6 11.5 %collective-permute-start.11 = (bf16[2,2,2,6,4,1024]{5,4,3,2,1,0:T(4,128)(2,1)}, bf16[2,2,2,6,4,1024]{5,4,3,2,1,0:T(4,128)(2,1)}, u32[]{:S(2)}, u32[]{:S(2)}) collective-permute-start(bf16[2,2,2,6,4,1024]{5,4,3,2,1,0:T(4,128)(2,1)} %pad_maximum_fusion.3), channel_id=1, source_target_pairs={{0,384},{48,432},{96,480},{144,528},{192,576},{240,624},{288,672},... | collective-permute-start | bytes 1179656 | tf_op jit(solution)/shard_map/ppermute | solution.py:50
  179.0 30.4 %collective-permute-start.12 = (bf16[2,3,32,3072]{3,2,1,0:T(8,128)(2,1)}, bf16[2,3,32,3072]{3,2,1,0:T(8,128)(2,1)S(1)}, u32[]{:S(2)}, u32[]{:S(2)}) collective-permute-start(bf16[2,3,32,3072]{3,2,1,0:T(8,128)(2,1)} %get-tuple-element.27), channel_id=1, source_target_pairs={{0,1},{1,2},{2,3},{3,4},{4,5},{5,6},{6,7},{8,9},{9,10},{10,11},{11... | collective-permute-start | bytes 3538952 | tf_op jit(solution)/shard_map/ppermute | solution.py:23
  180.9 28.4 %collective-permute-start.13 = (bf16[2,3,32,3072]{3,2,1,0:T(8,128)(2,1)S(1)}, bf16[2,3,32,3072]{3,2,1,0:T(8,128)(2,1)}, u32[]{:S(2)}, u32[]{:S(2)}) collective-permute-start(bf16[2,3,32,3072]{3,2,1,0:T(8,128)(2,1)S(1)} %get-tuple-element.28), channel_id=1, source_target_pairs={{1,0},{2,1},{3,2},{4,3},{5,4},{6,5},{7,6},{9,8},{10,9},{11,10},{12... | collective-permute-start | bytes 3538952 | tf_op jit(solution)/shard_map/ppermute | solution.py:24
  187.2 24.1 %copy-start.24 = (f32[1,1,3072]{2,1,0:T(1,128)S(1)}, f32[1,1,3072]{2,1,0:T(1,128)}, u32[]{:S(2)}) copy-start(f32[1,1,3072]{2,1,0:T(1,128)} %copy-done.23) | copy-start | bytes 36868
  187.2 24.1 %copy-start.26 = (f32[1,1,3072]{2,1,0:T(1,128)S(1)}, f32[1,1,3072]{2,1,0:T(1,128)}, u32[]{:S(2)}) copy-start(f32[1,1,3072]{2,1,0:T(1,128)} %copy-done.25) | copy-start | bytes 36868
  187.3 24.1 %copy-start.28 = (f32[1,1,3072]{2,1,0:T(1,128)S(1)}, f32[1,1,3072]{2,1,0:T(1,128)}, u32[]{:S(2)}) copy-start(f32[1,1,3072]{2,1,0:T(1,128)} %copy-done.27) | copy-start | bytes 36868
  187.3 24.1 %copy-start.30 = (f32[1,1,3072]{2,1,0:T(1,128)S(1)}, f32[1,1,3072]{2,1,0:T(1,128)}, u32[]{:S(2)}) copy-start(f32[1,1,3072]{2,1,0:T(1,128)} %copy-done.29) | copy-start | bytes 36868
  187.3 24.1 %copy-start.32 = (f32[1,1,3072]{2,1,0:T(1,128)S(1)}, f32[1,1,3072]{2,1,0:T(1,128)}, u32[]{:S(2)}) copy-start(f32[1,1,3072]{2,1,0:T(1,128)} %copy-done.31) | copy-start | bytes 36868
  187.3 24.1 %copy-start.34 = (f32[1,1,3072]{2,1,0:T(1,128)S(1)}, f32[1,1,3072]{2,1,0:T(1,128)}, u32[]{:S(2)}) copy-start(f32[1,1,3072]{2,1,0:T(1,128)} %copy-done.33) | copy-start | bytes 36868
  187.3 24.1 %copy-start.36 = (f32[1,1,3072]{2,1,0:T(1,128)S(1)}, f32[1,1,3072]{2,1,0:T(1,128)}, u32[]{:S(2)}) copy-start(f32[1,1,3072]{2,1,0:T(1,128)} %copy-done.35) | copy-start | bytes 36868
  187.3 24.1 %copy-start.38 = (f32[1,1,3072]{2,1,0:T(1,128)S(1)}, f32[1,1,3072]{2,1,0:T(1,128)}, u32[]{:S(2)}) copy-start(f32[1,1,3072]{2,1,0:T(1,128)} %copy-done.37) | copy-start | bytes 36868
  187.3 24.1 %copy-start.40 = (f32[1,1,3072]{2,1,0:T(1,128)S(1)}, f32[1,1,3072]{2,1,0:T(1,128)}, u32[]{:S(2)}) copy-start(f32[1,1,3072]{2,1,0:T(1,128)} %copy-done.39) | copy-start | bytes 36868
  187.3 24.1 %copy-start.42 = (f32[1,1,3072]{2,1,0:T(1,128)S(1)}, f32[1,1,3072]{2,1,0:T(1,128)}, u32[]{:S(2)}) copy-start(f32[1,1,3072]{2,1,0:T(1,128)} %copy-done.41) | copy-start | bytes 36868
  187.3 24.1 %copy-start.44 = (f32[1,1,3072]{2,1,0:T(1,128)S(1)}, f32[1,1,3072]{2,1,0:T(1,128)}, u32[]{:S(2)}) copy-start(f32[1,1,3072]{2,1,0:T(1,128)} %copy-done.43) | copy-start | bytes 36868
  187.3 24.1 %copy-start.46 = (f32[1,1,3072]{2,1,0:T(1,128)S(1)}, f32[1,1,3072]{2,1,0:T(1,128)}, u32[]{:S(2)}) copy-start(f32[1,1,3072]{2,1,0:T(1,128)} %copy-done.45) | copy-start | bytes 36868
  187.4 24.1 %copy-start.48 = (f32[1,1,3072]{2,1,0:T(1,128)S(1)}, f32[1,1,3072]{2,1,0:T(1,128)}, u32[]{:S(2)}) copy-start(f32[1,1,3072]{2,1,0:T(1,128)} %copy-done.47) | copy-start | bytes 36868
  187.4 24.1 %copy-start.50 = (f32[1,1,3072]{2,1,0:T(1,128)S(1)}, f32[1,1,3072]{2,1,0:T(1,128)}, u32[]{:S(2)}) copy-start(f32[1,1,3072]{2,1,0:T(1,128)} %copy-done.49) | copy-start | bytes 36868
  187.4 24.1 %copy-start.52 = (f32[1,1,3072]{2,1,0:T(1,128)S(1)}, f32[1,1,3072]{2,1,0:T(1,128)}, u32[]{:S(2)}) copy-start(f32[1,1,3072]{2,1,0:T(1,128)} %copy-done.51) | copy-start | bytes 36868
  187.4 24.1 %copy-start.54 = (f32[1,1,3072]{2,1,0:T(1,128)S(1)}, f32[1,1,3072]{2,1,0:T(1,128)}, u32[]{:S(2)}) copy-start(f32[1,1,3072]{2,1,0:T(1,128)} %copy-done.53) | copy-start | bytes 36868
  187.4 24.1 %copy-start.56 = (f32[1,1,3072]{2,1,0:T(1,128)S(1)}, f32[1,1,3072]{2,1,0:T(1,128)}, u32[]{:S(2)}) copy-start(f32[1,1,3072]{2,1,0:T(1,128)} %copy-done.55) | copy-start | bytes 36868
  187.4 24.1 %copy-start.58 = (f32[1,1,3072]{2,1,0:T(1,128)S(1)}, f32[1,1,3072]{2,1,0:T(1,128)}, u32[]{:S(2)}) copy-start(f32[1,1,3072]{2,1,0:T(1,128)} %copy-done.57) | copy-start | bytes 36868
  187.4 24.1 %copy-start.60 = (f32[1,1,3072]{2,1,0:T(1,128)S(1)}, f32[1,1,3072]{2,1,0:T(1,128)}, u32[]{:S(2)}) copy-start(f32[1,1,3072]{2,1,0:T(1,128)} %copy-done.59) | copy-start | bytes 36868
  187.4 24.1 %copy-start.62 = (f32[1,1,3072]{2,1,0:T(1,128)S(1)}, f32[1,1,3072]{2,1,0:T(1,128)}, u32[]{:S(2)}) copy-start(f32[1,1,3072]{2,1,0:T(1,128)} %copy-done.61) | copy-start | bytes 36868
  187.4 24.1 %copy-start.64 = (f32[1,1,3072]{2,1,0:T(1,128)S(1)}, f32[1,1,3072]{2,1,0:T(1,128)}, u32[]{:S(2)}) copy-start(f32[1,1,3072]{2,1,0:T(1,128)} %copy-done.63) | copy-start | bytes 36868
  187.4 24.1 %copy-start.66 = (f32[1,1,3072]{2,1,0:T(1,128)S(1)}, f32[1,1,3072]{2,1,0:T(1,128)}, u32[]{:S(2)}) copy-start(f32[1,1,3072]{2,1,0:T(1,128)} %copy-done.65) | copy-start | bytes 36868
  187.5 24.1 %copy-start.68 = (f32[1,1,3072]{2,1,0:T(1,128)S(1)}, f32[1,1,3072]{2,1,0:T(1,128)}, u32[]{:S(2)}) copy-start(f32[1,1,3072]{2,1,0:T(1,128)} %copy-done.67) | copy-start | bytes 36868
  187.5 24.1 %copy-start.70 = (f32[1,1,3072]{2,1,0:T(1,128)S(1)}, f32[1,1,3072]{2,1,0:T(1,128)}, u32[]{:S(2)}) copy-start(f32[1,1,3072]{2,1,0:T(1,128)} %copy-done.69) | copy-start | bytes 36868
  187.5 24.1 %copy-start.72 = (f32[1,1,3072]{2,1,0:T(1,128)S(1)}, f32[1,1,3072]{2,1,0:T(1,128)}, u32[]{:S(2)}) copy-start(f32[1,1,3072]{2,1,0:T(1,128)} %copy-done.71) | copy-start | bytes 36868
  187.5 24.1 %copy-start.74 = (f32[1,1,3072]{2,1,0:T(1,128)S(1)}, f32[1,1,3072]{2,1,0:T(1,128)}, u32[]{:S(2)}) copy-start(f32[1,1,3072]{2,1,0:T(1,128)} %copy-done.73) | copy-start | bytes 36868
  187.5 24.1 %copy-start.76 = (f32[1,1,3072]{2,1,0:T(1,128)S(1)}, f32[1,1,3072]{2,1,0:T(1,128)}, u32[]{:S(2)}) copy-start(f32[1,1,3072]{2,1,0:T(1,128)} %copy-done.75) | copy-start | bytes 36868
  187.5 24.1 %copy-start.78 = (f32[1,1,3072]{2,1,0:T(1,128)S(1)}, f32[1,1,3072]{2,1,0:T(1,128)}, u32[]{:S(2)}) copy-start(f32[1,1,3072]{2,1,0:T(1,128)} %copy-done.77) | copy-start | bytes 36868
  187.5 24.1 %copy-start.80 = (f32[1,1,3072]{2,1,0:T(1,128)S(1)}, f32[1,1,3072]{2,1,0:T(1,128)}, u32[]{:S(2)}) copy-start(f32[1,1,3072]{2,1,0:T(1,128)} %copy-done.79) | copy-start | bytes 36868
  187.5 24.1 %copy-start.82 = (f32[1,1,3072]{2,1,0:T(1,128)S(1)}, f32[1,1,3072]{2,1,0:T(1,128)}, u32[]{:S(2)}) copy-start(f32[1,1,3072]{2,1,0:T(1,128)} %copy-done.81) | copy-start | bytes 36868
  187.5 24.1 %copy-start.84 = (f32[1,1,3072]{2,1,0:T(1,128)S(1)}, f32[1,1,3072]{2,1,0:T(1,128)}, u32[]{:S(2)}) copy-start(f32[1,1,3072]{2,1,0:T(1,128)} %copy-done.83) | copy-start | bytes 36868
  187.5 24.1 %copy-start.86 = (f32[1,1,3072]{2,1,0:T(1,128)S(1)}, f32[1,1,3072]{2,1,0:T(1,128)}, u32[]{:S(2)}) copy-start(f32[1,1,3072]{2,1,0:T(1,128)} %copy-done.85) | copy-start | bytes 36868
  187.6 24.1 %copy-start.88 = (f32[1,1,3072]{2,1,0:T(1,128)S(1)}, f32[1,1,3072]{2,1,0:T(1,128)}, u32[]{:S(2)}) copy-start(f32[1,1,3072]{2,1,0:T(1,128)} %copy-done.87) | copy-start | bytes 36868
  (81 other events, 1180.2 us)

commit v8 on v7

--- a/solution.py
+++ b/solution.py
@@ -63,7 +63,7 @@
 
 def radix_split(count):
     parts = []
-    for radix in (3, 2):
+    for radix in (2, 3):
         while count % radix == 0 and count > 1:
             parts.append(radix)
             count //= radix

time: 242 us -> 244 us (level)
  waiting for transfers between devices: 68 us -> 73.5 us
  starting transfers between devices: 63.7 us -> 59.5 us
    ppermute x7, starting transfers between devices: 45.2 us -> 40.9 us  [gather_stages(): got.append(lax.ppermute(value, axis, pairs))]
    ppermute x7, waiting for transfers between devices: 21.9 us -> 25.4 us  [gather_stages(): got.append(lax.ppermute(value, axis, pairs))]
  transfers between devices with their start and end apart: 14 -> 14, of which waited for: 11 -> 11; matrix products, arithmetic and copies ran while one was open for 4% -> 3% of each run, Pallas kernels for 0% -> 0%
where the time goes in v8:
time: 244 us; the launch traced here: 240 us
  other arithmetic  77.3 us (32%)
  waiting for transfers between devices  73.5 us (30%)
  starting transfers between devices  59.5 us (24%)
  local copies, waits for them, and re-layouts  13.9 us (6%)
  matrix products  12.3 us (5%)
  between operations  3.55 us (1%)
    ppermute x2, waiting for transfers between devices, halo_rows(): before = lax.ppermute(last, 'row', up)  41 us
    ppermute x7, starting transfers between devices, gather_stages(): got.append(lax.ppermute(value, axis, pairs))  40.9 us
    reduce_sum x4, other arithmetic, cell_norm(): center = values - jnp.mean(values, axis=-1, keepdims=True)  30.1 us
    convert_element_type x1, other arithmetic, local(): grad_map = (own_grad[:, None, None, :] + spread).astype(jnp.bfloat16)  27.3 us
    ppermute x7, waiting for transfers between devices, gather_stages(): got.append(lax.ppermute(value, axis, pairs))  25.4 us
    ppermute x3, starting transfers between devices, group_sum(): value = value + lax.ppermute(value, 'row', pairs)  7.47 us
    ppermute x2, starting transfers between devices, halo_rows(): after = lax.ppermute(leading, 'row', down)  7.29 us
    ppermute x3, waiting for transfers between devices, group_sum(): value = value + lax.ppermute(value, 'row', pairs)  6.97 us
  transfers between devices with their start and end apart: 14, of which 11 were waited for; matrix products, arithmetic and copies ran while one was open for 3% of the time, Pallas kernels for 0%

profile of v8, /device:TPU:6, one launch (start us, length us, event | category | flops | bytes accessed | tf_op | source)
XLA Modules:
  0.0 240.0 jit_solution(2707511949847633712)
XLA Ops:
  0.7 3.3 %fusion.27 = (bf16[2,3,32,3072]{3,2,1,0:T(8,128)(2,1)}, bf16[2,3,32,3072]{3,2,1,0:T(8,128)(2,1)}) fusion(bf16[2,4,32,3072]{3,2,1,0:T(8,128)(2,1)} %param.11), kind=kLoop, calls=%fused_computation.221 | loop fusion | bytes 4718592 | tf_op jit(solution)/shard_map/slice | solution.py:21
  4.0 1.9 collective-permute-start
  5.9 3.6 %collective-permute-start.1 = (bf16[2,3,32,3072]{3,2,1,0:T(8,128)(2,1)}, bf16[2,3,32,3072]{3,2,1,0:T(8,128)(2,1)}, u32[]{:S(2)}, u32[]{:S(2)}) collective-permute-start(bf16[2,3,32,3072]{3,2,1,0:T(8,128)(2,1)} %get-tuple-element.30), channel_id=1, source_target_pairs={{1,0},{2,1},{3,2},{4,3},{5,4},{6,5},{7,6},{9,8},{10,9},{11,10},{12... | collective-permute-start | bytes 3538952 | tf_op jit(solution)/shard_map/ppermute | solution.py:24
  12.7 0.8 fusion.4
  14.8 0.8 slice_convert_fusion.47
  15.7 18.6 %collective-permute-done = bf16[2,3,32,3072]{3,2,1,0:T(8,128)(2,1)S(1)} collective-permute-done((bf16[2,3,32,3072]{3,2,1,0:T(8,128)(2,1)}, bf16[2,3,32,3072]{3,2,1,0:T(8,128)(2,1)S(1)}, u32[]{:S(2)}, u32[]{:S(2)}) %collective-permute-start) | collective-permute-done | bytes 1179680 | tf_op jit(solution)/shard_map/ppermute | solution.py:23
  34.4 1.5 pad_maximum_fusion
  36.3 29.0 %fusion.25 = (f32[2,4,32]{2,1,0:T(4,128)S(1)}, f32[2,4,32,3072]{3,2,1,0:T(8,128)S(1)}) fusion(f32[3072]{0:T(1024)S(1)} %copy-done.102, f32[3072]{0:T(1024)S(1)} %bitcast.107, f32[3072]{0:T(1024)S(1)} %bitcast.109, f32[3072]{0:T(1024)S(1)} %bitcast.113, f32[3072]{0:T(1024)S(1)} %bitcast.115, bf16[2,10,32,3072]{3,2,1,0:T(8,128)(2,1)S(1)} %pad_maximum_fusion, ...), kind=kLoop, calls=%fused_computation.219 | loop fusion | flops 116391680 | bytes 18703360 | tf_op jit(solution)/shard_map/reduce_sum | solution.py:75
  65.9 0.9 copy-done.1
  66.8 1.0 add_reduce_fusion
  67.8 1.9 collective-permute-start.2
  69.7 1.1 collective-permute-done.2
  70.9 1.9 collective-permute-start.3
  72.8 3.8 %collective-permute-done.3 = f32[2,3072]{1,0:T(2,128)S(1)} collective-permute-done((f32[2,3072]{1,0:T(2,128)S(1)}, f32[2,3072]{1,0:T(2,128)S(1)}, u32[]{:S(2)}, u32[]{:S(2)}) %collective-permute-start.3) | collective-permute-done | bytes 24608 | tf_op jit(solution)/shard_map/ppermute | solution.py:33
  76.6 3.6 %collective-permute-start.4 = (f32[2,3072]{1,0:T(2,128)S(1)}, f32[2,3072]{1,0:T(2,128)S(1)}, u32[]{:S(2)}, u32[]{:S(2)}) collective-permute-start(f32[2,3072]{1,0:T(2,128)S(1)} %add.509), channel_id=1, source_target_pairs={{0,4},{1,5},{2,6},{3,7},{4,0},{5,1},{6,2},{7,3},{8,12},{9,13},{10,... | collective-permute-start | bytes 73736 | tf_op jit(solution)/shard_map/ppermute | solution.py:33
  80.3 2.1 collective-permute-done.4
  83.3 3.9 %multiply_reduce_fusion.7 = (f32[2]{0:T(128)S(1)}, f32[2,1024]{1,0:T(2,128)S(1)}) fusion(bf16[3072,1024]{1,0:T(8,128)(2,1)} %param.17, f32[2]{0:T(128)S(1)} %fusion.20, f32[3072]{0:T(1024)S(1)} %copy-done.95, f32[2,3072]{1,0:T(2,128)S(1)} %get-tuple-element.24, f32[2]{0:T(128)S(1)} %broadcast_multiply_fusion.5), kind=kOutput, calls=%fused_computation.185 | convolution fusion | flops 12611582 | bytes 6336536 | tf_op jit(solution)/shard_map/dot_general | solution.py:146
  87.3 6.1 %collective-permute-start.5 = (bf16[4,1024]{1,0:T(4,128)(2,1)S(1)}, bf16[4,1024]{1,0:T(4,128)(2,1)S(1)}, u32[]{:S(2)}, u32[]{:S(2)}) collective-permute-start(bf16[4,1024]{1,0:T(4,128)(2,1)S(1)} %pad_maximum_fusion.8), channel_id=1, source_target_pairs={{0,8},{8,0},{16,24},{24,16},{32,40},{40,32},{1,9},{9,1},{17,25},{2... | collective-permute-start | bytes 24584 | tf_op jit(solution)/shard_map/ppermute | solution.py:50
  93.4 1.6 collective-permute-done.5
  95.1 10.9 %collective-permute-start.6 = (bf16[2,4,1024]{2,1,0:T(4,128)(2,1)S(1)}, bf16[2,4,1024]{2,1,0:T(4,128)(2,1)S(1)}, u32[]{:S(2)}, u32[]{:S(2)}) collective-permute-start(bf16[2,4,1024]{2,1,0:T(4,128)(2,1)S(1)} %get-tuple-element.91), channel_id=1, source_target_pairs={{0,16},{8,24},{16,32},{24,40},{32,0},{40,8},{1,17},{9,25},{17,33},... | collective-permute-start | bytes 49160 | tf_op jit(solution)/shard_map/ppermute | solution.py:50
  106.0 4.3 %collective-permute-start.7 = (bf16[2,4,1024]{2,1,0:T(4,128)(2,1)S(1)}, bf16[2,4,1024]{2,1,0:T(4,128)(2,1)S(1)}, u32[]{:S(2)}, u32[]{:S(2)}) collective-permute-start(bf16[2,4,1024]{2,1,0:T(4,128)(2,1)S(1)} %get-tuple-element.91), channel_id=1, source_target_pairs={{0,32},{8,40},{16,0},{24,8},{32,16},{40,24},{1,33},{9,41},{17,1},{... | collective-permute-start | bytes 49160 | tf_op jit(solution)/shard_map/ppermute | solution.py:50
  110.5 5.1 %collective-permute-done.7 = bf16[2,4,1024]{2,1,0:T(4,128)(2,1)S(1)} collective-permute-done((bf16[2,4,1024]{2,1,0:T(4,128)(2,1)S(1)}, bf16[2,4,1024]{2,1,0:T(4,128)(2,1)S(1)}, u32[]{:S(2)}, u32[]{:S(2)}) %collective-permute-start.7) | collective-permute-done | bytes 16416 | tf_op jit(solution)/shard_map/ppermute | solution.py:50
  116.3 3.5 %collective-permute-start.8 = (bf16[6,4,1024]{2,1,0:T(4,128)(2,1)S(1)}, bf16[6,4,1024]{2,1,0:T(4,128)(2,1)S(1)}, u32[]{:S(2)}, u32[]{:S(2)}) collective-permute-start(bf16[6,4,1024]{2,1,0:T(4,128)(2,1)S(1)} %bitcast_select_fusion), channel_id=1, source_target_pairs={{0,48},{48,0},{96,144},{144,96},{192,240},{240,192},{288,336},{336... | collective-permute-start | bytes 147464 | tf_op jit(solution)/shard_map/ppermute | solution.py:50
  119.8 2.5 %collective-permute-done.8 = bf16[6,4,1024]{2,1,0:T(4,128)(2,1)S(1)} collective-permute-done((bf16[6,4,1024]{2,1,0:T(4,128)(2,1)S(1)}, bf16[6,4,1024]{2,1,0:T(4,128)(2,1)S(1)}, u32[]{:S(2)}, u32[]{:S(2)}) %collective-permute-start.8) | collective-permute-done | bytes 49184 | tf_op jit(solution)/shard_map/ppermute | solution.py:50
  122.4 4.9 %collective-permute-start.9 = (bf16[2,6,4,1024]{3,2,1,0:T(4,128)(2,1)S(1)}, bf16[2,6,4,1024]{3,2,1,0:T(4,128)(2,1)S(1)}, u32[]{:S(2)}, u32[]{:S(2)}) collective-permute-start(bf16[2,6,4,1024]{3,2,1,0:T(4,128)(2,1)S(1)} %pad_maximum_fusion.5), channel_id=1, source_target_pairs={{0,96},{48,144},{96,0},{144,48},{192,288},{240,336},{288,192},{336... | collective-permute-start | bytes 294920 | tf_op jit(solution)/shard_map/ppermute | solution.py:50
  127.4 3.6 %collective-permute-done.9 = bf16[2,6,4,1024]{3,2,1,0:T(4,128)(2,1)S(1)} collective-permute-done((bf16[2,6,4,1024]{3,2,1,0:T(4,128)(2,1)S(1)}, bf16[2,6,4,1024]{3,2,1,0:T(4,128)(2,1)S(1)}, u32[]{:S(2)}, u32[]{:S(2)}) %collective-permute-start.9) | collective-permute-done | bytes 98336 | tf_op jit(solution)/shard_map/ppermute | solution.py:50
  131.9 7.7 %collective-permute-start.10 = (bf16[2,2,6,4,1024]{4,3,2,1,0:T(4,128)(2,1)S(1)}, bf16[2,2,6,4,1024]{4,3,2,1,0:T(4,128)(2,1)}, u32[]{:S(2)}, u32[]{:S(2)}) collective-permute-start(bf16[2,2,6,4,1024]{4,3,2,1,0:T(4,128)(2,1)S(1)} %pad_maximum_fusion.4), channel_id=1, source_target_pairs={{0,192},{48,240},{96,288},{144,336},{192,0},{240,48},{288,96},{336... | collective-permute-start | bytes 589832 | tf_op jit(solution)/shard_map/ppermute | solution.py:50
  139.7 4.8 %collective-permute-done.10 = bf16[2,2,6,4,1024]{4,3,2,1,0:T(4,128)(2,1)} collective-permute-done((bf16[2,2,6,4,1024]{4,3,2,1,0:T(4,128)(2,1)S(1)}, bf16[2,2,6,4,1024]{4,3,2,1,0:T(4,128)(2,1)}, u32[]{:S(2)}, u32[]{:S(2)}) %collective-permute-start.10) | collective-permute-done | bytes 196640 | tf_op jit(solution)/shard_map/ppermute | solution.py:50
  144.5 1.3 select_bitcast_fusion.3
  145.7 1.0 pad_maximum_fusion.3
  146.8 3.5 %collective-permute-start.11 = (bf16[2,2,2,6,4,1024]{5,4,3,2,1,0:T(4,128)(2,1)}, bf16[2,2,2,6,4,1024]{5,4,3,2,1,0:T(4,128)(2,1)}, u32[]{:S(2)}, u32[]{:S(2)}) collective-permute-start(bf16[2,2,2,6,4,1024]{5,4,3,2,1,0:T(4,128)(2,1)} %pad_maximum_fusion.3), channel_id=1, source_target_pairs={{0,384},{48,432},{96,480},{144,528},{192,576},{240,624},{288,672},... | collective-permute-start | bytes 1179656 | tf_op jit(solution)/shard_map/ppermute | solution.py:50
  150.3 8.0 %collective-permute-done.11 = bf16[2,2,2,6,4,1024]{5,4,3,2,1,0:T(4,128)(2,1)} collective-permute-done((bf16[2,2,2,6,4,1024]{5,4,3,2,1,0:T(4,128)(2,1)}, bf16[2,2,2,6,4,1024]{5,4,3,2,1,0:T(4,128)(2,1)}, u32[]{:S(2)}, u32[]{:S(2)}) %collective-permute-start.11) | collective-permute-done | bytes 393248 | tf_op jit(solution)/shard_map/ppermute | solution.py:50
  158.2 1.5 select_bitcast_fusion.1
  160.3 1.3 fusion.28
  161.5 0.9 reshape.545
  162.5 1.1 reshape.544
  163.6 2.1 multiply_convert_fusion
  165.7 1.3 multiply_reduce_fusion.6
  167.7 4.6 %multiply_reduce_fusion.4 = (f32[2]{0:T(128)S(1)}, f32[2,3072]{1,0:T(2,128)S(1)}) fusion(f32[2,3072]{1,0:T(2,128)} %copy-done.6, f32[2]{0:T(128)} %copy-done.103, f32[3072]{0:T(1024)} %param.16, bf16[3072,1024]{1,0:T(8,128)(2,1)} %param.17, f32[2,1024]{1,0:T(2,128)} %copy-done.12, f32[2,1024]{1,0:T(2,128)S(1)} %get-tuple-element.105, ...), kind=kOutput, calls=%fused_computation.117 | convolution fusion | flops 12617726 | bytes 6369312 | tf_op jit(solution)/shard_map/dot_general | solution.py:165
  173.8 0.8 fusion.1
  174.6 2.1 add_convert_fusion.1
  176.8 2.9 %fusion.26 = (bf16[2,3,32,3072]{3,2,1,0:T(8,128)(2,1)}, bf16[2,3,32,3072]{3,2,1,0:T(8,128)(2,1)S(1)}) fusion(bf16[2,4,32,3072]{3,2,1,0:T(8,128)(2,1)} %add_convert_fusion.1), kind=kLoop, calls=%fused_computation.220 | loop fusion | bytes 4718592 | tf_op jit(solution)/shard_map/slice | solution.py:21
  179.7 1.9 collective-permute-start.12
  181.6 3.6 %collective-permute-start.13 = (bf16[2,3,32,3072]{3,2,1,0:T(8,128)(2,1)S(1)}, bf16[2,3,32,3072]{3,2,1,0:T(8,128)(2,1)}, u32[]{:S(2)}, u32[]{:S(2)}) collective-permute-start(bf16[2,3,32,3072]{3,2,1,0:T(8,128)(2,1)S(1)} %get-tuple-element.28), channel_id=1, source_target_pairs={{1,0},{2,1},{3,2},{4,3},{5,4},{6,5},{7,6},{9,8},{10,9},{11,10},{12... | collective-permute-start | bytes 3538952 | tf_op jit(solution)/shard_map/ppermute | solution.py:24
  186.6 0.7 add_add_fusion.2
  187.7 22.4 %collective-permute-done.12 = bf16[2,3,32,3072]{3,2,1,0:T(8,128)(2,1)S(1)} collective-permute-done((bf16[2,3,32,3072]{3,2,1,0:T(8,128)(2,1)}, bf16[2,3,32,3072]{3,2,1,0:T(8,128)(2,1)S(1)}, u32[]{:S(2)}, u32[]{:S(2)}) %collective-permute-start.12) | collective-permute-done | bytes 1179680 | tf_op jit(solution)/shard_map/ppermute | solution.py:23
  210.1 2.0 pad_maximum_fusion.1
  212.5 27.3 %add_convert_fusion = bf16[2,4,32,3072]{3,2,1,0:T(8,128)(2,1)} fusion(bf16[2,10,32,3072]{3,2,1,0:T(8,128)(2,1)S(1)} %pad_maximum_fusion.1, f32[2,3072]{1,0:T(2,128)S(1)} %copy-done.92, f32[3072]{0:T(1024)S(1)} %bitcast.108, f32[3072]{0:T(1024)S(1)} %bitcast.110, f32[3072]{0:T(1024)S(1)} %bitcast.114, f32[3072]{0:T(1024)S(1)} %bitcast.116, ...), kind=kLoop, calls=%fused_computation.8 | loop fusion | flops 116391936 | bytes 17141760 | tf_op jit(solution)/shard_map/convert_element_type | solution.py:181
  (292 shorter events, 11.3 us)
Async XLA Ops:
  0.6 33.8 %copy-start = (bf16[2,4,32,3072]{3,2,1,0:T(8,128)(2,1)S(1)}, bf16[2,4,32,3072]{3,2,1,0:T(8,128)(2,1)}, u32[]{:S(2)}) copy-start(bf16[2,4,32,3072]{3,2,1,0:T(8,128)(2,1)} %param.11) | copy-start | bytes 4718596
  4.0 30.4 %collective-permute-start = (bf16[2,3,32,3072]{3,2,1,0:T(8,128)(2,1)}, bf16[2,3,32,3072]{3,2,1,0:T(8,128)(2,1)S(1)}, u32[]{:S(2)}, u32[]{:S(2)}) collective-permute-start(bf16[2,3,32,3072]{3,2,1,0:T(8,128)(2,1)} %get-tuple-element.29), channel_id=1, source_target_pairs={{0,1},{1,2},{2,3},{3,4},{4,5},{5,6},{6,7},{8,9},{9,10},{10,11},{11... | collective-permute-start | bytes 3538952 | tf_op jit(solution)/shard_map/ppermute | solution.py:23
  5.9 28.4 %collective-permute-start.1 = (bf16[2,3,32,3072]{3,2,1,0:T(8,128)(2,1)}, bf16[2,3,32,3072]{3,2,1,0:T(8,128)(2,1)}, u32[]{:S(2)}, u32[]{:S(2)}) collective-permute-start(bf16[2,3,32,3072]{3,2,1,0:T(8,128)(2,1)} %get-tuple-element.30), channel_id=1, source_target_pairs={{1,0},{2,1},{3,2},{4,3},{5,4},{6,5},{7,6},{9,8},{10,9},{11,10},{12... | collective-permute-start | bytes 3538952 | tf_op jit(solution)/shard_map/ppermute | solution.py:24
  67.8 3.1 %collective-permute-start.2 = (f32[2,3072]{1,0:T(2,128)S(1)}, f32[2,3072]{1,0:T(2,128)S(1)}, u32[]{:S(2)}, u32[]{:S(2)}) collective-permute-start(f32[2,3072]{1,0:T(2,128)S(1)} %broadcast_multiply_fusion.1), channel_id=1, source_target_pairs={{0,1},{1,0},{2,3},{3,2},{4,5},{5,4},{6,7},{7,6},{8,9},{9,8},{10,11... | collective-permute-start | bytes 73736 | tf_op jit(solution)/shard_map/ppermute | solution.py:33
  70.9 5.7 %collective-permute-start.3 = (f32[2,3072]{1,0:T(2,128)S(1)}, f32[2,3072]{1,0:T(2,128)S(1)}, u32[]{:S(2)}, u32[]{:S(2)}) collective-permute-start(f32[2,3072]{1,0:T(2,128)S(1)} %fusion.21), channel_id=1, source_target_pairs={{0,2},{1,3},{2,0},{3,1},{4,6},{5,7},{6,4},{7,5},{8,10},{9,11},{10,... | collective-permute-start | bytes 73736 | tf_op jit(solution)/shard_map/ppermute | solution.py:33
  76.6 5.7 %collective-permute-start.4 = (f32[2,3072]{1,0:T(2,128)S(1)}, f32[2,3072]{1,0:T(2,128)S(1)}, u32[]{:S(2)}, u32[]{:S(2)}) collective-permute-start(f32[2,3072]{1,0:T(2,128)S(1)} %add.509), channel_id=1, source_target_pairs={{0,4},{1,5},{2,6},{3,7},{4,0},{5,1},{6,2},{7,3},{8,12},{9,13},{10,... | collective-permute-start | bytes 73736 | tf_op jit(solution)/shard_map/ppermute | solution.py:33
  87.2 28.3 %copy-start.12 = (f32[2,1024]{1,0:T(2,128)}, f32[2,1024]{1,0:T(2,128)S(1)}, u32[]{:S(2)}) copy-start(f32[2,1024]{1,0:T(2,128)S(1)} %get-tuple-element.101) | copy-start | bytes 24580
  87.3 7.7 %collective-permute-start.5 = (bf16[4,1024]{1,0:T(4,128)(2,1)S(1)}, bf16[4,1024]{1,0:T(4,128)(2,1)S(1)}, u32[]{:S(2)}, u32[]{:S(2)}) collective-permute-start(bf16[4,1024]{1,0:T(4,128)(2,1)S(1)} %pad_maximum_fusion.8), channel_id=1, source_target_pairs={{0,8},{8,0},{16,24},{24,16},{32,40},{40,32},{1,9},{9,1},{17,25},{2... | collective-permute-start | bytes 24584 | tf_op jit(solution)/shard_map/ppermute | solution.py:50
  95.1 15.4 %collective-permute-start.6 = (bf16[2,4,1024]{2,1,0:T(4,128)(2,1)S(1)}, bf16[2,4,1024]{2,1,0:T(4,128)(2,1)S(1)}, u32[]{:S(2)}, u32[]{:S(2)}) collective-permute-start(bf16[2,4,1024]{2,1,0:T(4,128)(2,1)S(1)} %get-tuple-element.91), channel_id=1, source_target_pairs={{0,16},{8,24},{16,32},{24,40},{32,0},{40,8},{1,17},{9,25},{17,33},... | collective-permute-start | bytes 49160 | tf_op jit(solution)/shard_map/ppermute | solution.py:50
  106.0 9.5 %collective-permute-start.7 = (bf16[2,4,1024]{2,1,0:T(4,128)(2,1)S(1)}, bf16[2,4,1024]{2,1,0:T(4,128)(2,1)S(1)}, u32[]{:S(2)}, u32[]{:S(2)}) collective-permute-start(bf16[2,4,1024]{2,1,0:T(4,128)(2,1)S(1)} %get-tuple-element.91), channel_id=1, source_target_pairs={{0,32},{8,40},{16,0},{24,8},{32,16},{40,24},{1,33},{9,41},{17,1},{... | collective-permute-start | bytes 49160 | tf_op jit(solution)/shard_map/ppermute | solution.py:50
  116.3 6.0 %collective-permute-start.8 = (bf16[6,4,1024]{2,1,0:T(4,128)(2,1)S(1)}, bf16[6,4,1024]{2,1,0:T(4,128)(2,1)S(1)}, u32[]{:S(2)}, u32[]{:S(2)}) collective-permute-start(bf16[6,4,1024]{2,1,0:T(4,128)(2,1)S(1)} %bitcast_select_fusion), channel_id=1, source_target_pairs={{0,48},{48,0},{96,144},{144,96},{192,240},{240,192},{288,336},{336... | collective-permute-start | bytes 147464 | tf_op jit(solution)/shard_map/ppermute | solution.py:50
  122.4 8.6 %collective-permute-start.9 = (bf16[2,6,4,1024]{3,2,1,0:T(4,128)(2,1)S(1)}, bf16[2,6,4,1024]{3,2,1,0:T(4,128)(2,1)S(1)}, u32[]{:S(2)}, u32[]{:S(2)}) collective-permute-start(bf16[2,6,4,1024]{3,2,1,0:T(4,128)(2,1)S(1)} %pad_maximum_fusion.5), channel_id=1, source_target_pairs={{0,96},{48,144},{96,0},{144,48},{192,288},{240,336},{288,192},{336... | collective-permute-start | bytes 294920 | tf_op jit(solution)/shard_map/ppermute | solution.py:50
  131.9 12.5 %collective-permute-start.10 = (bf16[2,2,6,4,1024]{4,3,2,1,0:T(4,128)(2,1)S(1)}, bf16[2,2,6,4,1024]{4,3,2,1,0:T(4,128)(2,1)}, u32[]{:S(2)}, u32[]{:S(2)}) collective-permute-start(bf16[2,2,6,4,1024]{4,3,2,1,0:T(4,128)(2,1)S(1)} %pad_maximum_fusion.4), channel_id=1, source_target_pairs={{0,192},{48,240},{96,288},{144,336},{192,0},{240,48},{288,96},{336... | collective-permute-start | bytes 589832 | tf_op jit(solution)/shard_map/ppermute | solution.py:50
  146.8 11.5 %collective-permute-start.11 = (bf16[2,2,2,6,4,1024]{5,4,3,2,1,0:T(4,128)(2,1)}, bf16[2,2,2,6,4,1024]{5,4,3,2,1,0:T(4,128)(2,1)}, u32[]{:S(2)}, u32[]{:S(2)}) collective-permute-start(bf16[2,2,2,6,4,1024]{5,4,3,2,1,0:T(4,128)(2,1)} %pad_maximum_fusion.3), channel_id=1, source_target_pairs={{0,384},{48,432},{96,480},{144,528},{192,576},{240,624},{288,672},... | collective-permute-start | bytes 1179656 | tf_op jit(solution)/shard_map/ppermute | solution.py:50
  179.7 30.4 %collective-permute-start.12 = (bf16[2,3,32,3072]{3,2,1,0:T(8,128)(2,1)}, bf16[2,3,32,3072]{3,2,1,0:T(8,128)(2,1)S(1)}, u32[]{:S(2)}, u32[]{:S(2)}) collective-permute-start(bf16[2,3,32,3072]{3,2,1,0:T(8,128)(2,1)} %get-tuple-element.27), channel_id=1, source_target_pairs={{0,1},{1,2},{2,3},{3,4},{4,5},{5,6},{6,7},{8,9},{9,10},{10,11},{11... | collective-permute-start | bytes 3538952 | tf_op jit(solution)/shard_map/ppermute | solution.py:23
  181.6 28.4 %collective-permute-start.13 = (bf16[2,3,32,3072]{3,2,1,0:T(8,128)(2,1)S(1)}, bf16[2,3,32,3072]{3,2,1,0:T(8,128)(2,1)}, u32[]{:S(2)}, u32[]{:S(2)}) collective-permute-start(bf16[2,3,32,3072]{3,2,1,0:T(8,128)(2,1)S(1)} %get-tuple-element.28), channel_id=1, source_target_pairs={{1,0},{2,1},{3,2},{4,3},{5,4},{6,5},{7,6},{9,8},{10,9},{11,10},{12... | collective-permute-start | bytes 3538952 | tf_op jit(solution)/shard_map/ppermute | solution.py:24
  187.3 24.8 %copy-start.23 = (f32[1,1,3072]{2,1,0:T(1,128)S(1)}, f32[1,1,3072]{2,1,0:T(1,128)}, u32[]{:S(2)}) copy-start(f32[1,1,3072]{2,1,0:T(1,128)} %copy-done.22) | copy-start | bytes 36868
  187.3 24.8 %copy-start.25 = (f32[1,1,3072]{2,1,0:T(1,128)S(1)}, f32[1,1,3072]{2,1,0:T(1,128)}, u32[]{:S(2)}) copy-start(f32[1,1,3072]{2,1,0:T(1,128)} %copy-done.24) | copy-start | bytes 36868
  187.3 24.8 %copy-start.27 = (f32[1,1,3072]{2,1,0:T(1,128)S(1)}, f32[1,1,3072]{2,1,0:T(1,128)}, u32[]{:S(2)}) copy-start(f32[1,1,3072]{2,1,0:T(1,128)} %copy-done.26) | copy-start | bytes 36868
  187.3 24.8 %copy-start.29 = (f32[1,1,3072]{2,1,0:T(1,128)S(1)}, f32[1,1,3072]{2,1,0:T(1,128)}, u32[]{:S(2)}) copy-start(f32[1,1,3072]{2,1,0:T(1,128)} %copy-done.28) | copy-start | bytes 36868
  187.3 24.8 %copy-start.31 = (f32[1,1,3072]{2,1,0:T(1,128)S(1)}, f32[1,1,3072]{2,1,0:T(1,128)}, u32[]{:S(2)}) copy-start(f32[1,1,3072]{2,1,0:T(1,128)} %copy-done.30) | copy-start | bytes 36868
  187.3 24.8 %copy-start.33 = (f32[1,1,3072]{2,1,0:T(1,128)S(1)}, f32[1,1,3072]{2,1,0:T(1,128)}, u32[]{:S(2)}) copy-start(f32[1,1,3072]{2,1,0:T(1,128)} %copy-done.32) | copy-start | bytes 36868
  187.4 24.8 %copy-start.35 = (f32[1,1,3072]{2,1,0:T(1,128)S(1)}, f32[1,1,3072]{2,1,0:T(1,128)}, u32[]{:S(2)}) copy-start(f32[1,1,3072]{2,1,0:T(1,128)} %copy-done.34) | copy-start | bytes 36868
  187.4 24.8 %copy-start.37 = (f32[1,1,3072]{2,1,0:T(1,128)S(1)}, f32[1,1,3072]{2,1,0:T(1,128)}, u32[]{:S(2)}) copy-start(f32[1,1,3072]{2,1,0:T(1,128)} %copy-done.36) | copy-start | bytes 36868
  187.4 24.8 %copy-start.39 = (f32[1,1,3072]{2,1,0:T(1,128)S(1)}, f32[1,1,3072]{2,1,0:T(1,128)}, u32[]{:S(2)}) copy-start(f32[1,1,3072]{2,1,0:T(1,128)} %copy-done.38) | copy-start | bytes 36868
  187.4 24.8 %copy-start.41 = (f32[1,1,3072]{2,1,0:T(1,128)S(1)}, f32[1,1,3072]{2,1,0:T(1,128)}, u32[]{:S(2)}) copy-start(f32[1,1,3072]{2,1,0:T(1,128)} %copy-done.40) | copy-start | bytes 36868
  187.4 24.8 %copy-start.43 = (f32[1,1,3072]{2,1,0:T(1,128)S(1)}, f32[1,1,3072]{2,1,0:T(1,128)}, u32[]{:S(2)}) copy-start(f32[1,1,3072]{2,1,0:T(1,128)} %copy-done.42) | copy-start | bytes 36868
  187.4 24.8 %copy-start.45 = (f32[1,1,3072]{2,1,0:T(1,128)S(1)}, f32[1,1,3072]{2,1,0:T(1,128)}, u32[]{:S(2)}) copy-start(f32[1,1,3072]{2,1,0:T(1,128)} %copy-done.44) | copy-start | bytes 36868
  187.4 24.8 %copy-start.47 = (f32[1,1,3072]{2,1,0:T(1,128)S(1)}, f32[1,1,3072]{2,1,0:T(1,128)}, u32[]{:S(2)}) copy-start(f32[1,1,3072]{2,1,0:T(1,128)} %copy-done.46) | copy-start | bytes 36868
  187.4 24.8 %copy-start.49 = (f32[1,1,3072]{2,1,0:T(1,128)S(1)}, f32[1,1,3072]{2,1,0:T(1,128)}, u32[]{:S(2)}) copy-start(f32[1,1,3072]{2,1,0:T(1,128)} %copy-done.48) | copy-start | bytes 36868
  187.4 24.8 %copy-start.51 = (f32[1,1,3072]{2,1,0:T(1,128)S(1)}, f32[1,1,3072]{2,1,0:T(1,128)}, u32[]{:S(2)}) copy-start(f32[1,1,3072]{2,1,0:T(1,128)} %copy-done.50) | copy-start | bytes 36868
  187.4 24.8 %copy-start.53 = (f32[1,1,3072]{2,1,0:T(1,128)S(1)}, f32[1,1,3072]{2,1,0:T(1,128)}, u32[]{:S(2)}) copy-start(f32[1,1,3072]{2,1,0:T(1,128)} %copy-done.52) | copy-start | bytes 36868
  187.5 24.8 %copy-start.55 = (f32[1,1,3072]{2,1,0:T(1,128)S(1)}, f32[1,1,3072]{2,1,0:T(1,128)}, u32[]{:S(2)}) copy-start(f32[1,1,3072]{2,1,0:T(1,128)} %copy-done.54) | copy-start | bytes 36868
  187.5 24.8 %copy-start.57 = (f32[1,1,3072]{2,1,0:T(1,128)S(1)}, f32[1,1,3072]{2,1,0:T(1,128)}, u32[]{:S(2)}) copy-start(f32[1,1,3072]{2,1,0:T(1,128)} %copy-done.56) | copy-start | bytes 36868
  187.5 24.8 %copy-start.59 = (f32[1,1,3072]{2,1,0:T(1,128)S(1)}, f32[1,1,3072]{2,1,0:T(1,128)}, u32[]{:S(2)}) copy-start(f32[1,1,3072]{2,1,0:T(1,128)} %copy-done.58) | copy-start | bytes 36868
  187.5 24.8 %copy-start.61 = (f32[1,1,3072]{2,1,0:T(1,128)S(1)}, f32[1,1,3072]{2,1,0:T(1,128)}, u32[]{:S(2)}) copy-start(f32[1,1,3072]{2,1,0:T(1,128)} %copy-done.60) | copy-start | bytes 36868
  187.5 24.8 %copy-start.63 = (f32[1,1,3072]{2,1,0:T(1,128)S(1)}, f32[1,1,3072]{2,1,0:T(1,128)}, u32[]{:S(2)}) copy-start(f32[1,1,3072]{2,1,0:T(1,128)} %copy-done.62) | copy-start | bytes 36868
  187.5 24.8 %copy-start.65 = (f32[1,1,3072]{2,1,0:T(1,128)S(1)}, f32[1,1,3072]{2,1,0:T(1,128)}, u32[]{:S(2)}) copy-start(f32[1,1,3072]{2,1,0:T(1,128)} %copy-done.64) | copy-start | bytes 36868
  187.5 24.8 %copy-start.67 = (f32[1,1,3072]{2,1,0:T(1,128)S(1)}, f32[1,1,3072]{2,1,0:T(1,128)}, u32[]{:S(2)}) copy-start(f32[1,1,3072]{2,1,0:T(1,128)} %copy-done.66) | copy-start | bytes 36868
  187.5 24.8 %copy-start.69 = (f32[1,1,3072]{2,1,0:T(1,128)S(1)}, f32[1,1,3072]{2,1,0:T(1,128)}, u32[]{:S(2)}) copy-start(f32[1,1,3072]{2,1,0:T(1,128)} %copy-done.68) | copy-start | bytes 36868
  187.5 24.8 %copy-start.71 = (f32[1,1,3072]{2,1,0:T(1,128)S(1)}, f32[1,1,3072]{2,1,0:T(1,128)}, u32[]{:S(2)}) copy-start(f32[1,1,3072]{2,1,0:T(1,128)} %copy-done.70) | copy-start | bytes 36868
  187.5 24.8 %copy-start.73 = (f32[1,1,3072]{2,1,0:T(1,128)S(1)}, f32[1,1,3072]{2,1,0:T(1,128)}, u32[]{:S(2)}) copy-start(f32[1,1,3072]{2,1,0:T(1,128)} %copy-done.72) | copy-start | bytes 36868
  187.6 24.8 %copy-start.75 = (f32[1,1,3072]{2,1,0:T(1,128)S(1)}, f32[1,1,3072]{2,1,0:T(1,128)}, u32[]{:S(2)}) copy-start(f32[1,1,3072]{2,1,0:T(1,128)} %copy-done.74) | copy-start | bytes 36868
  187.6 24.8 %copy-start.77 = (f32[1,1,3072]{2,1,0:T(1,128)S(1)}, f32[1,1,3072]{2,1,0:T(1,128)}, u32[]{:S(2)}) copy-start(f32[1,1,3072]{2,1,0:T(1,128)} %copy-done.76) | copy-start | bytes 36868
  187.6 24.8 %copy-start.79 = (f32[1,1,3072]{2,1,0:T(1,128)S(1)}, f32[1,1,3072]{2,1,0:T(1,128)}, u32[]{:S(2)}) copy-start(f32[1,1,3072]{2,1,0:T(1,128)} %copy-done.78) | copy-start | bytes 36868
  187.6 24.8 %copy-start.81 = (f32[1,1,3072]{2,1,0:T(1,128)S(1)}, f32[1,1,3072]{2,1,0:T(1,128)}, u32[]{:S(2)}) copy-start(f32[1,1,3072]{2,1,0:T(1,128)} %copy-done.80) | copy-start | bytes 36868
  187.6 24.8 %copy-start.83 = (f32[1,1,3072]{2,1,0:T(1,128)S(1)}, f32[1,1,3072]{2,1,0:T(1,128)}, u32[]{:S(2)}) copy-start(f32[1,1,3072]{2,1,0:T(1,128)} %copy-done.82) | copy-start | bytes 36868
  187.6 24.8 %copy-start.85 = (f32[1,1,3072]{2,1,0:T(1,128)S(1)}, f32[1,1,3072]{2,1,0:T(1,128)}, u32[]{:S(2)}) copy-start(f32[1,1,3072]{2,1,0:T(1,128)} %copy-done.84) | copy-start | bytes 36868
  (82 other events, 1258.4 us)

commit v9 on v7

--- a/solution.py
+++ b/solution.py
@@ -36,10 +36,14 @@
 
 
 def gather_stages(value, axis, radices):
-    place = 1
     devices = lax.axis_size(axis)
     at = lax.axis_index(axis)
+    places = []
+    place = 1
     for radix in radices:
+        places.append(place)
+        place *= radix
+    for stage, (radix, place) in enumerate(reversed(list(zip(radices, places)))):
         digit = (at // place) % radix
         got = [value]
         for shift in range(1, radix):
@@ -51,13 +55,12 @@
         if radix == 2:
             first = digit == 0
             value = jnp.stack(
-                [jnp.where(first, got[0], got[1]), jnp.where(first, got[1], got[0])]
+                [jnp.where(first, got[0], got[1]), jnp.where(first, got[1], got[0])], axis=stage
             )
         else:
-            stacked = jnp.stack(got)
+            stacked = jnp.stack(got, axis=stage)
             order = (digit - jnp.arange(radix)) % radix
-            value = jnp.take(stacked, order, axis=0)
-        place *= radix
+            value = jnp.take(stacked, order, axis=stage)
     return value.reshape((devices,) + value.shape[len(radices) :])
 
 

time: 242 us -> 242 us (level)
  no operation moved by 1% of the time
where the time goes in v9:
time: 242 us; the launch traced here: 240 us
  other arithmetic  78.1 us (32%)
  waiting for transfers between devices  70 us (29%)
  starting transfers between devices  61.6 us (25%)
  local copies, waits for them, and re-layouts  14.1 us (6%)
  matrix products  12.3 us (5%)
  between operations  3.55 us (1%)
    ppermute x7, starting transfers between devices, gather_stages(): got.append(lax.ppermute(value, axis, pairs))  43 us
    ppermute x2, waiting for transfers between devices, halo_rows(): before = lax.ppermute(last, 'row', up)  39.2 us
    reduce_sum x4, other arithmetic, cell_norm(): center = values - jnp.mean(values, axis=-1, keepdims=True)  30.1 us
    convert_element_type x1, other arithmetic, local(): grad_map = (own_grad[:, None, None, :] + spread).astype(jnp.bfloat16)  27.3 us
    ppermute x7, waiting for transfers between devices, gather_stages(): got.append(lax.ppermute(value, axis, pairs))  23.8 us
    ppermute x3, starting transfers between devices, group_sum(): value = value + lax.ppermute(value, 'row', pairs)  7.47 us
    ppermute x2, starting transfers between devices, halo_rows(): after = lax.ppermute(leading, 'row', down)  7.29 us
    ppermute x3, waiting for transfers between devices, group_sum(): value = value + lax.ppermute(value, 'row', pairs)  7 us
  transfers between devices with their start and end apart: 14, of which 11 were waited for; matrix products, arithmetic and copies ran while one was open for 4% of the time, Pallas kernels for 0%

profile of v9, /device:TPU:6, one launch (start us, length us, event | category | flops | bytes accessed | tf_op | source)
XLA Modules:
  0.0 239.6 jit_solution(15842515290141968196)
XLA Ops:
  0.7 3.3 %fusion.27 = (bf16[2,3,32,3072]{3,2,1,0:T(8,128)(2,1)}, bf16[2,3,32,3072]{3,2,1,0:T(8,128)(2,1)}) fusion(bf16[2,4,32,3072]{3,2,1,0:T(8,128)(2,1)} %param.11), kind=kLoop, calls=%fused_computation.221 | loop fusion | bytes 4718592 | tf_op jit(solution)/shard_map/slice | solution.py:21
  4.0 1.9 collective-permute-start
  5.9 3.6 %collective-permute-start.1 = (bf16[2,3,32,3072]{3,2,1,0:T(8,128)(2,1)}, bf16[2,3,32,3072]{3,2,1,0:T(8,128)(2,1)}, u32[]{:S(2)}, u32[]{:S(2)}) collective-permute-start(bf16[2,3,32,3072]{3,2,1,0:T(8,128)(2,1)} %get-tuple-element.30), channel_id=1, source_target_pairs={{1,0},{2,1},{3,2},{4,3},{5,4},{6,5},{7,6},{9,8},{10,9},{11,10},{12... | collective-permute-start | bytes 3538952 | tf_op jit(solution)/shard_map/ppermute | solution.py:24
  9.6 0.7 multiply_reduce_fusion.2
  14.0 0.8 fusion.4
  16.0 0.8 slice_convert_fusion.47
  16.9 17.4 %collective-permute-done = bf16[2,3,32,3072]{3,2,1,0:T(8,128)(2,1)S(1)} collective-permute-done((bf16[2,3,32,3072]{3,2,1,0:T(8,128)(2,1)}, bf16[2,3,32,3072]{3,2,1,0:T(8,128)(2,1)S(1)}, u32[]{:S(2)}, u32[]{:S(2)}) %collective-permute-start) | collective-permute-done | bytes 1179680 | tf_op jit(solution)/shard_map/ppermute | solution.py:23
  34.4 1.5 pad_maximum_fusion
  36.3 29.0 %fusion.25 = (f32[2,4,32]{2,1,0:T(4,128)S(1)}, f32[2,4,32,3072]{3,2,1,0:T(8,128)S(1)}) fusion(f32[3072]{0:T(1024)S(1)} %copy-done.103, f32[3072]{0:T(1024)S(1)} %bitcast.109, f32[3072]{0:T(1024)S(1)} %bitcast.111, f32[3072]{0:T(1024)S(1)} %bitcast.115, f32[3072]{0:T(1024)S(1)} %bitcast.117, bf16[2,10,32,3072]{3,2,1,0:T(8,128)(2,1)S(1)} %pad_maximum_fusion, ...), kind=kLoop, calls=%fused_computation.219 | loop fusion | flops 116391680 | bytes 18703360 | tf_op jit(solution)/shard_map/reduce_sum | solution.py:78
  66.8 1.0 add_reduce_fusion
  67.7 1.9 collective-permute-start.2
  69.7 1.2 collective-permute-done.2
  70.9 1.9 collective-permute-start.3
  72.8 3.8 %collective-permute-done.3 = f32[2,3072]{1,0:T(2,128)S(1)} collective-permute-done((f32[2,3072]{1,0:T(2,128)S(1)}, f32[2,3072]{1,0:T(2,128)S(1)}, u32[]{:S(2)}, u32[]{:S(2)}) %collective-permute-start.3) | collective-permute-done | bytes 24608 | tf_op jit(solution)/shard_map/ppermute | solution.py:33
  76.6 3.6 %collective-permute-start.4 = (f32[2,3072]{1,0:T(2,128)S(1)}, f32[2,3072]{1,0:T(2,128)S(1)}, u32[]{:S(2)}, u32[]{:S(2)}) collective-permute-start(f32[2,3072]{1,0:T(2,128)S(1)} %add.509), channel_id=1, source_target_pairs={{0,4},{1,5},{2,6},{3,7},{4,0},{5,1},{6,2},{7,3},{8,12},{9,13},{10,... | collective-permute-start | bytes 73736 | tf_op jit(solution)/shard_map/ppermute | solution.py:33
  80.3 2.1 collective-permute-done.4
  83.2 3.9 %multiply_reduce_fusion.7 = (f32[2]{0:T(128)S(1)}, f32[2,1024]{1,0:T(2,128)S(1)}) fusion(bf16[3072,1024]{1,0:T(8,128)(2,1)} %param.17, f32[2]{0:T(128)S(1)} %fusion.20, f32[3072]{0:T(1024)S(1)} %copy-done.96, f32[2,3072]{1,0:T(2,128)S(1)} %get-tuple-element.24, f32[2]{0:T(128)S(1)} %broadcast_multiply_fusion.5), kind=kOutput, calls=%fused_computation.185 | convolution fusion | flops 12611582 | bytes 6336536 | tf_op jit(solution)/shard_map/dot_general | solution.py:149
  87.8 15.1 %collective-permute-start.5 = (bf16[4,1024]{1,0:T(4,128)(2,1)S(1)}, bf16[4,1024]{1,0:T(4,128)(2,1)S(1)}, u32[]{:S(2)}, u32[]{:S(2)}) collective-permute-start(bf16[4,1024]{1,0:T(4,128)(2,1)S(1)} %pad_maximum_fusion.8), channel_id=1, source_target_pairs={{0,24},{8,32},{16,40},{24,0},{32,8},{40,16},{1,25},{9,33},{17,41},... | collective-permute-start | bytes 24584 | tf_op jit(solution)/shard_map/ppermute | solution.py:54
  103.0 1.6 collective-permute-done.5
  104.6 3.7 %collective-permute-start.6 = (bf16[2,4,1024]{2,1,0:T(4,128)(2,1)S(1)}, bf16[2,4,1024]{2,1,0:T(4,128)(2,1)S(1)}, u32[]{:S(2)}, u32[]{:S(2)}) collective-permute-start(bf16[2,4,1024]{2,1,0:T(4,128)(2,1)S(1)} %get-tuple-element.91), channel_id=1, source_target_pairs={{0,8},{8,16},{16,0},{24,32},{32,40},{40,24},{1,9},{9,17},{17,1},{2... | collective-permute-start | bytes 49160 | tf_op jit(solution)/shard_map/ppermute | solution.py:54
  108.3 6.1 %collective-permute-start.7 = (bf16[2,4,1024]{2,1,0:T(4,128)(2,1)S(1)}, bf16[2,4,1024]{2,1,0:T(4,128)(2,1)S(1)}, u32[]{:S(2)}, u32[]{:S(2)}) collective-permute-start(bf16[2,4,1024]{2,1,0:T(4,128)(2,1)S(1)} %get-tuple-element.91), channel_id=1, source_target_pairs={{0,16},{8,0},{16,8},{24,40},{32,24},{40,32},{1,17},{9,1},{17,9},{2... | collective-permute-start | bytes 49160 | tf_op jit(solution)/shard_map/ppermute | solution.py:54
  114.5 1.3 collective-permute-done.7
  116.5 3.3 %collective-permute-start.8 = (bf16[6,4,1024]{2,1,0:T(4,128)(2,1)S(1)}, bf16[6,4,1024]{2,1,0:T(4,128)(2,1)S(1)}, u32[]{:S(2)}, u32[]{:S(2)}) collective-permute-start(bf16[6,4,1024]{2,1,0:T(4,128)(2,1)S(1)} %bitcast_select_fusion), channel_id=1, source_target_pairs={{0,384},{48,432},{96,480},{144,528},{192,576},{240,624},{288,672},... | collective-permute-start | bytes 147464 | tf_op jit(solution)/shard_map/ppermute | solution.py:54
  119.9 4.1 %collective-permute-done.8 = bf16[6,4,1024]{2,1,0:T(4,128)(2,1)S(1)} collective-permute-done((bf16[6,4,1024]{2,1,0:T(4,128)(2,1)S(1)}, bf16[6,4,1024]{2,1,0:T(4,128)(2,1)S(1)}, u32[]{:S(2)}, u32[]{:S(2)}) %collective-permute-start.8) | collective-permute-done | bytes 49184 | tf_op jit(solution)/shard_map/ppermute | solution.py:54
  124.2 7.7 %collective-permute-start.9 = (bf16[2,6,4,1024]{3,2,1,0:T(4,128)(2,1)S(1)}, bf16[2,6,4,1024]{3,2,1,0:T(4,128)(2,1)S(1)}, u32[]{:S(2)}, u32[]{:S(2)}) collective-permute-start(bf16[2,6,4,1024]{3,2,1,0:T(4,128)(2,1)S(1)} %pad_maximum_fusion.5), channel_id=1, source_target_pairs={{0,192},{48,240},{96,288},{144,336},{192,0},{240,48},{288,96},{336... | collective-permute-start | bytes 294920 | tf_op jit(solution)/shard_map/ppermute | solution.py:54
  132.0 3.1 %collective-permute-done.9 = bf16[2,6,4,1024]{3,2,1,0:T(4,128)(2,1)S(1)} collective-permute-done((bf16[2,6,4,1024]{3,2,1,0:T(4,128)(2,1)S(1)}, bf16[2,6,4,1024]{3,2,1,0:T(4,128)(2,1)S(1)}, u32[]{:S(2)}, u32[]{:S(2)}) %collective-permute-start.9) | collective-permute-done | bytes 98336 | tf_op jit(solution)/shard_map/ppermute | solution.py:54
  136.0 5.0 %collective-permute-start.10 = (bf16[2,2,6,4,1024]{4,3,2,0,1:T(4,128)(2,1)S(1)}, bf16[2,2,6,4,1024]{4,3,2,0,1:T(4,128)(2,1)}, u32[]{:S(2)}, u32[]{:S(2)}) collective-permute-start(bf16[2,2,6,4,1024]{4,3,2,0,1:T(4,128)(2,1)S(1)} %pad_maximum_fusion.4), channel_id=1, source_target_pairs={{0,96},{48,144},{96,0},{144,48},{192,288},{240,336},{288,192},{336... | collective-permute-start | bytes 589832 | tf_op jit(solution)/shard_map/ppermute | solution.py:54
  141.1 5.8 %collective-permute-done.10 = bf16[2,2,6,4,1024]{4,3,2,0,1:T(4,128)(2,1)} collective-permute-done((bf16[2,2,6,4,1024]{4,3,2,0,1:T(4,128)(2,1)S(1)}, bf16[2,2,6,4,1024]{4,3,2,0,1:T(4,128)(2,1)}, u32[]{:S(2)}, u32[]{:S(2)}) %collective-permute-start.10) | collective-permute-done | bytes 196640 | tf_op jit(solution)/shard_map/ppermute | solution.py:54
  146.9 1.3 select_bitcast_fusion.3
  148.2 1.0 pad_maximum_fusion.3
  149.2 2.1 collective-permute-start.11
  151.3 7.9 %collective-permute-done.11 = bf16[2,2,2,6,4,1024]{5,4,3,0,1,2:T(4,128)(2,1)} collective-permute-done((bf16[2,2,2,6,4,1024]{5,4,3,0,1,2:T(4,128)(2,1)}, bf16[2,2,2,6,4,1024]{5,4,3,0,1,2:T(4,128)(2,1)}, u32[]{:S(2)}, u32[]{:S(2)}) %collective-permute-start.11) | collective-permute-done | bytes 393248 | tf_op jit(solution)/shard_map/ppermute | solution.py:54
  159.2 1.5 select_bitcast_fusion.1
  161.5 1.3 fusion.28
  162.8 0.9 reshape.545
  163.7 1.1 reshape.544
  164.9 2.1 multiply_convert_fusion
  166.9 1.3 multiply_reduce_fusion.6
  169.0 4.6 %multiply_reduce_fusion.4 = (f32[2]{0:T(128)S(1)}, f32[2,3072]{1,0:T(2,128)S(1)}) fusion(f32[2,3072]{1,0:T(2,128)} %copy-done.7, f32[2]{0:T(128)} %copy-done.104, f32[3072]{0:T(1024)} %param.16, bf16[3072,1024]{1,0:T(8,128)(2,1)} %param.17, f32[2,1024]{1,0:T(2,128)} %copy-done.13, f32[2,1024]{1,0:T(2,128)S(1)} %get-tuple-element.105, ...), kind=kOutput, calls=%fused_computation.117 | convolution fusion | flops 12617726 | bytes 6369312 | tf_op jit(solution)/shard_map/dot_general | solution.py:168
  175.1 0.8 fusion.1
  175.9 1.0 add_convert_fusion.1
  177.0 1.1 copy-done.2
  178.1 1.3 fusion.26
  179.3 1.9 collective-permute-start.12
  181.3 3.6 %collective-permute-start.13 = (bf16[2,3,32,3072]{3,2,1,0:T(8,128)(2,1)S(1)}, bf16[2,3,32,3072]{3,2,1,0:T(8,128)(2,1)}, u32[]{:S(2)}, u32[]{:S(2)}) collective-permute-start(bf16[2,3,32,3072]{3,2,1,0:T(8,128)(2,1)S(1)} %get-tuple-element.28), channel_id=1, source_target_pairs={{1,0},{2,1},{3,2},{4,3},{5,4},{6,5},{7,6},{9,8},{10,9},{11,10},{12... | collective-permute-start | bytes 3538952 | tf_op jit(solution)/shard_map/ppermute | solution.py:24
  188.0 21.7 %collective-permute-done.12 = bf16[2,3,32,3072]{3,2,1,0:T(8,128)(2,1)S(1)} collective-permute-done((bf16[2,3,32,3072]{3,2,1,0:T(8,128)(2,1)}, bf16[2,3,32,3072]{3,2,1,0:T(8,128)(2,1)S(1)}, u32[]{:S(2)}, u32[]{:S(2)}) %collective-permute-start.12) | collective-permute-done | bytes 1179680 | tf_op jit(solution)/shard_map/ppermute | solution.py:23
  209.7 2.0 pad_maximum_fusion.1
  212.1 27.3 %add_convert_fusion = bf16[2,4,32,3072]{3,2,1,0:T(8,128)(2,1)} fusion(bf16[2,10,32,3072]{3,2,1,0:T(8,128)(2,1)S(1)} %pad_maximum_fusion.1, f32[2,3072]{1,0:T(2,128)S(1)} %copy-done.93, f32[3072]{0:T(1024)S(1)} %bitcast.110, f32[3072]{0:T(1024)S(1)} %bitcast.112, f32[3072]{0:T(1024)S(1)} %bitcast.116, f32[3072]{0:T(1024)S(1)} %bitcast.118, ...), kind=kLoop, calls=%fused_computation.8 | loop fusion | flops 116391936 | bytes 17141760 | tf_op jit(solution)/shard_map/convert_element_type | solution.py:184
  (292 shorter events, 14.9 us)
Async XLA Ops:
  0.6 33.7 %copy-start = (bf16[2,4,32,3072]{3,2,1,0:T(8,128)(2,1)S(1)}, bf16[2,4,32,3072]{3,2,1,0:T(8,128)(2,1)}, u32[]{:S(2)}) copy-start(bf16[2,4,32,3072]{3,2,1,0:T(8,128)(2,1)} %param.11) | copy-start | bytes 4718596
  4.0 30.4 %collective-permute-start = (bf16[2,3,32,3072]{3,2,1,0:T(8,128)(2,1)}, bf16[2,3,32,3072]{3,2,1,0:T(8,128)(2,1)S(1)}, u32[]{:S(2)}, u32[]{:S(2)}) collective-permute-start(bf16[2,3,32,3072]{3,2,1,0:T(8,128)(2,1)} %get-tuple-element.29), channel_id=1, source_target_pairs={{0,1},{1,2},{2,3},{3,4},{4,5},{5,6},{6,7},{8,9},{9,10},{10,11},{11... | collective-permute-start | bytes 3538952 | tf_op jit(solution)/shard_map/ppermute | solution.py:23
  5.9 28.4 %collective-permute-start.1 = (bf16[2,3,32,3072]{3,2,1,0:T(8,128)(2,1)}, bf16[2,3,32,3072]{3,2,1,0:T(8,128)(2,1)}, u32[]{:S(2)}, u32[]{:S(2)}) collective-permute-start(bf16[2,3,32,3072]{3,2,1,0:T(8,128)(2,1)} %get-tuple-element.30), channel_id=1, source_target_pairs={{1,0},{2,1},{3,2},{4,3},{5,4},{6,5},{7,6},{9,8},{10,9},{11,10},{12... | collective-permute-start | bytes 3538952 | tf_op jit(solution)/shard_map/ppermute | solution.py:24
  67.7 3.1 %collective-permute-start.2 = (f32[2,3072]{1,0:T(2,128)S(1)}, f32[2,3072]{1,0:T(2,128)S(1)}, u32[]{:S(2)}, u32[]{:S(2)}) collective-permute-start(f32[2,3072]{1,0:T(2,128)S(1)} %broadcast_multiply_fusion.1), channel_id=1, source_target_pairs={{0,1},{1,0},{2,3},{3,2},{4,5},{5,4},{6,7},{7,6},{8,9},{9,8},{10,11... | collective-permute-start | bytes 73736 | tf_op jit(solution)/shard_map/ppermute | solution.py:33
  70.9 5.7 %collective-permute-start.3 = (f32[2,3072]{1,0:T(2,128)S(1)}, f32[2,3072]{1,0:T(2,128)S(1)}, u32[]{:S(2)}, u32[]{:S(2)}) collective-permute-start(f32[2,3072]{1,0:T(2,128)S(1)} %fusion.21), channel_id=1, source_target_pairs={{0,2},{1,3},{2,0},{3,1},{4,6},{5,7},{6,4},{7,5},{8,10},{9,11},{10,... | collective-permute-start | bytes 73736 | tf_op jit(solution)/shard_map/ppermute | solution.py:33
  76.6 5.7 %collective-permute-start.4 = (f32[2,3072]{1,0:T(2,128)S(1)}, f32[2,3072]{1,0:T(2,128)S(1)}, u32[]{:S(2)}, u32[]{:S(2)}) collective-permute-start(f32[2,3072]{1,0:T(2,128)S(1)} %add.509), channel_id=1, source_target_pairs={{0,4},{1,5},{2,6},{3,7},{4,0},{5,1},{6,2},{7,3},{8,12},{9,13},{10,... | collective-permute-start | bytes 73736 | tf_op jit(solution)/shard_map/ppermute | solution.py:33
  87.8 16.8 %collective-permute-start.5 = (bf16[4,1024]{1,0:T(4,128)(2,1)S(1)}, bf16[4,1024]{1,0:T(4,128)(2,1)S(1)}, u32[]{:S(2)}, u32[]{:S(2)}) collective-permute-start(bf16[4,1024]{1,0:T(4,128)(2,1)S(1)} %pad_maximum_fusion.8), channel_id=1, source_target_pairs={{0,24},{8,32},{16,40},{24,0},{32,8},{40,16},{1,25},{9,33},{17,41},... | collective-permute-start | bytes 24584 | tf_op jit(solution)/shard_map/ppermute | solution.py:54
  104.6 9.9 %collective-permute-start.6 = (bf16[2,4,1024]{2,1,0:T(4,128)(2,1)S(1)}, bf16[2,4,1024]{2,1,0:T(4,128)(2,1)S(1)}, u32[]{:S(2)}, u32[]{:S(2)}) collective-permute-start(bf16[2,4,1024]{2,1,0:T(4,128)(2,1)S(1)} %get-tuple-element.91), channel_id=1, source_target_pairs={{0,8},{8,16},{16,0},{24,32},{32,40},{40,24},{1,9},{9,17},{17,1},{2... | collective-permute-start | bytes 49160 | tf_op jit(solution)/shard_map/ppermute | solution.py:54
  108.3 7.5 %collective-permute-start.7 = (bf16[2,4,1024]{2,1,0:T(4,128)(2,1)S(1)}, bf16[2,4,1024]{2,1,0:T(4,128)(2,1)S(1)}, u32[]{:S(2)}, u32[]{:S(2)}) collective-permute-start(bf16[2,4,1024]{2,1,0:T(4,128)(2,1)S(1)} %get-tuple-element.91), channel_id=1, source_target_pairs={{0,16},{8,0},{16,8},{24,40},{32,24},{40,32},{1,17},{9,1},{17,9},{2... | collective-permute-start | bytes 49160 | tf_op jit(solution)/shard_map/ppermute | solution.py:54
  116.5 7.5 %collective-permute-start.8 = (bf16[6,4,1024]{2,1,0:T(4,128)(2,1)S(1)}, bf16[6,4,1024]{2,1,0:T(4,128)(2,1)S(1)}, u32[]{:S(2)}, u32[]{:S(2)}) collective-permute-start(bf16[6,4,1024]{2,1,0:T(4,128)(2,1)S(1)} %bitcast_select_fusion), channel_id=1, source_target_pairs={{0,384},{48,432},{96,480},{144,528},{192,576},{240,624},{288,672},... | collective-permute-start | bytes 147464 | tf_op jit(solution)/shard_map/ppermute | solution.py:54
  124.2 10.9 %collective-permute-start.9 = (bf16[2,6,4,1024]{3,2,1,0:T(4,128)(2,1)S(1)}, bf16[2,6,4,1024]{3,2,1,0:T(4,128)(2,1)S(1)}, u32[]{:S(2)}, u32[]{:S(2)}) collective-permute-start(bf16[2,6,4,1024]{3,2,1,0:T(4,128)(2,1)S(1)} %pad_maximum_fusion.5), channel_id=1, source_target_pairs={{0,192},{48,240},{96,288},{144,336},{192,0},{240,48},{288,96},{336... | collective-permute-start | bytes 294920 | tf_op jit(solution)/shard_map/ppermute | solution.py:54
  136.0 10.9 %collective-permute-start.10 = (bf16[2,2,6,4,1024]{4,3,2,0,1:T(4,128)(2,1)S(1)}, bf16[2,2,6,4,1024]{4,3,2,0,1:T(4,128)(2,1)}, u32[]{:S(2)}, u32[]{:S(2)}) collective-permute-start(bf16[2,2,6,4,1024]{4,3,2,0,1:T(4,128)(2,1)S(1)} %pad_maximum_fusion.4), channel_id=1, source_target_pairs={{0,96},{48,144},{96,0},{144,48},{192,288},{240,336},{288,192},{336... | collective-permute-start | bytes 589832 | tf_op jit(solution)/shard_map/ppermute | solution.py:54
  149.2 10.0 %collective-permute-start.11 = (bf16[2,2,2,6,4,1024]{5,4,3,0,1,2:T(4,128)(2,1)}, bf16[2,2,2,6,4,1024]{5,4,3,0,1,2:T(4,128)(2,1)}, u32[]{:S(2)}, u32[]{:S(2)}) collective-permute-start(bf16[2,2,2,6,4,1024]{5,4,3,0,1,2:T(4,128)(2,1)} %pad_maximum_fusion.3), channel_id=1, source_target_pairs={{0,48},{48,0},{96,144},{144,96},{192,240},{240,192},{288,336},{336... | collective-permute-start | bytes 1179656 | tf_op jit(solution)/shard_map/ppermute | solution.py:54
  179.3 30.4 %collective-permute-start.12 = (bf16[2,3,32,3072]{3,2,1,0:T(8,128)(2,1)}, bf16[2,3,32,3072]{3,2,1,0:T(8,128)(2,1)S(1)}, u32[]{:S(2)}, u32[]{:S(2)}) collective-permute-start(bf16[2,3,32,3072]{3,2,1,0:T(8,128)(2,1)} %get-tuple-element.27), channel_id=1, source_target_pairs={{0,1},{1,2},{2,3},{3,4},{4,5},{5,6},{6,7},{8,9},{9,10},{10,11},{11... | collective-permute-start | bytes 3538952 | tf_op jit(solution)/shard_map/ppermute | solution.py:23
  181.3 28.4 %collective-permute-start.13 = (bf16[2,3,32,3072]{3,2,1,0:T(8,128)(2,1)S(1)}, bf16[2,3,32,3072]{3,2,1,0:T(8,128)(2,1)}, u32[]{:S(2)}, u32[]{:S(2)}) collective-permute-start(bf16[2,3,32,3072]{3,2,1,0:T(8,128)(2,1)S(1)} %get-tuple-element.28), channel_id=1, source_target_pairs={{1,0},{2,1},{3,2},{4,3},{5,4},{6,5},{7,6},{9,8},{10,9},{11,10},{12... | collective-permute-start | bytes 3538952 | tf_op jit(solution)/shard_map/ppermute | solution.py:24
  187.6 24.1 %copy-start.24 = (f32[1,1,3072]{2,1,0:T(1,128)S(1)}, f32[1,1,3072]{2,1,0:T(1,128)}, u32[]{:S(2)}) copy-start(f32[1,1,3072]{2,1,0:T(1,128)} %copy-done.23) | copy-start | bytes 36868
  187.6 24.1 %copy-start.26 = (f32[1,1,3072]{2,1,0:T(1,128)S(1)}, f32[1,1,3072]{2,1,0:T(1,128)}, u32[]{:S(2)}) copy-start(f32[1,1,3072]{2,1,0:T(1,128)} %copy-done.25) | copy-start | bytes 36868
  187.6 24.1 %copy-start.28 = (f32[1,1,3072]{2,1,0:T(1,128)S(1)}, f32[1,1,3072]{2,1,0:T(1,128)}, u32[]{:S(2)}) copy-start(f32[1,1,3072]{2,1,0:T(1,128)} %copy-done.27) | copy-start | bytes 36868
  187.6 24.1 %copy-start.30 = (f32[1,1,3072]{2,1,0:T(1,128)S(1)}, f32[1,1,3072]{2,1,0:T(1,128)}, u32[]{:S(2)}) copy-start(f32[1,1,3072]{2,1,0:T(1,128)} %copy-done.29) | copy-start | bytes 36868
  187.7 24.1 %copy-start.32 = (f32[1,1,3072]{2,1,0:T(1,128)S(1)}, f32[1,1,3072]{2,1,0:T(1,128)}, u32[]{:S(2)}) copy-start(f32[1,1,3072]{2,1,0:T(1,128)} %copy-done.31) | copy-start | bytes 36868
  187.7 24.1 %copy-start.34 = (f32[1,1,3072]{2,1,0:T(1,128)S(1)}, f32[1,1,3072]{2,1,0:T(1,128)}, u32[]{:S(2)}) copy-start(f32[1,1,3072]{2,1,0:T(1,128)} %copy-done.33) | copy-start | bytes 36868
  187.7 24.1 %copy-start.36 = (f32[1,1,3072]{2,1,0:T(1,128)S(1)}, f32[1,1,3072]{2,1,0:T(1,128)}, u32[]{:S(2)}) copy-start(f32[1,1,3072]{2,1,0:T(1,128)} %copy-done.35) | copy-start | bytes 36868
  187.7 24.1 %copy-start.38 = (f32[1,1,3072]{2,1,0:T(1,128)S(1)}, f32[1,1,3072]{2,1,0:T(1,128)}, u32[]{:S(2)}) copy-start(f32[1,1,3072]{2,1,0:T(1,128)} %copy-done.37) | copy-start | bytes 36868
  187.7 24.1 %copy-start.40 = (f32[1,1,3072]{2,1,0:T(1,128)S(1)}, f32[1,1,3072]{2,1,0:T(1,128)}, u32[]{:S(2)}) copy-start(f32[1,1,3072]{2,1,0:T(1,128)} %copy-done.39) | copy-start | bytes 36868
  187.7 24.1 %copy-start.42 = (f32[1,1,3072]{2,1,0:T(1,128)S(1)}, f32[1,1,3072]{2,1,0:T(1,128)}, u32[]{:S(2)}) copy-start(f32[1,1,3072]{2,1,0:T(1,128)} %copy-done.41) | copy-start | bytes 36868
  187.7 24.1 %copy-start.44 = (f32[1,1,3072]{2,1,0:T(1,128)S(1)}, f32[1,1,3072]{2,1,0:T(1,128)}, u32[]{:S(2)}) copy-start(f32[1,1,3072]{2,1,0:T(1,128)} %copy-done.43) | copy-start | bytes 36868
  187.7 24.1 %copy-start.46 = (f32[1,1,3072]{2,1,0:T(1,128)S(1)}, f32[1,1,3072]{2,1,0:T(1,128)}, u32[]{:S(2)}) copy-start(f32[1,1,3072]{2,1,0:T(1,128)} %copy-done.45) | copy-start | bytes 36868
  187.7 24.1 %copy-start.48 = (f32[1,1,3072]{2,1,0:T(1,128)S(1)}, f32[1,1,3072]{2,1,0:T(1,128)}, u32[]{:S(2)}) copy-start(f32[1,1,3072]{2,1,0:T(1,128)} %copy-done.47) | copy-start | bytes 36868
  187.7 24.1 %copy-start.50 = (f32[1,1,3072]{2,1,0:T(1,128)S(1)}, f32[1,1,3072]{2,1,0:T(1,128)}, u32[]{:S(2)}) copy-start(f32[1,1,3072]{2,1,0:T(1,128)} %copy-done.49) | copy-start | bytes 36868
  187.8 24.1 %copy-start.52 = (f32[1,1,3072]{2,1,0:T(1,128)S(1)}, f32[1,1,3072]{2,1,0:T(1,128)}, u32[]{:S(2)}) copy-start(f32[1,1,3072]{2,1,0:T(1,128)} %copy-done.51) | copy-start | bytes 36868
  187.8 24.1 %copy-start.54 = (f32[1,1,3072]{2,1,0:T(1,128)S(1)}, f32[1,1,3072]{2,1,0:T(1,128)}, u32[]{:S(2)}) copy-start(f32[1,1,3072]{2,1,0:T(1,128)} %copy-done.53) | copy-start | bytes 36868
  187.8 24.1 %copy-start.56 = (f32[1,1,3072]{2,1,0:T(1,128)S(1)}, f32[1,1,3072]{2,1,0:T(1,128)}, u32[]{:S(2)}) copy-start(f32[1,1,3072]{2,1,0:T(1,128)} %copy-done.55) | copy-start | bytes 36868
  187.8 24.1 %copy-start.58 = (f32[1,1,3072]{2,1,0:T(1,128)S(1)}, f32[1,1,3072]{2,1,0:T(1,128)}, u32[]{:S(2)}) copy-start(f32[1,1,3072]{2,1,0:T(1,128)} %copy-done.57) | copy-start | bytes 36868
  187.8 24.1 %copy-start.60 = (f32[1,1,3072]{2,1,0:T(1,128)S(1)}, f32[1,1,3072]{2,1,0:T(1,128)}, u32[]{:S(2)}) copy-start(f32[1,1,3072]{2,1,0:T(1,128)} %copy-done.59) | copy-start | bytes 36868
  187.8 24.1 %copy-start.62 = (f32[1,1,3072]{2,1,0:T(1,128)S(1)}, f32[1,1,3072]{2,1,0:T(1,128)}, u32[]{:S(2)}) copy-start(f32[1,1,3072]{2,1,0:T(1,128)} %copy-done.61) | copy-start | bytes 36868
  187.8 24.1 %copy-start.64 = (f32[1,1,3072]{2,1,0:T(1,128)S(1)}, f32[1,1,3072]{2,1,0:T(1,128)}, u32[]{:S(2)}) copy-start(f32[1,1,3072]{2,1,0:T(1,128)} %copy-done.63) | copy-start | bytes 36868
  187.8 24.1 %copy-start.66 = (f32[1,1,3072]{2,1,0:T(1,128)S(1)}, f32[1,1,3072]{2,1,0:T(1,128)}, u32[]{:S(2)}) copy-start(f32[1,1,3072]{2,1,0:T(1,128)} %copy-done.65) | copy-start | bytes 36868
  187.8 24.1 %copy-start.68 = (f32[1,1,3072]{2,1,0:T(1,128)S(1)}, f32[1,1,3072]{2,1,0:T(1,128)}, u32[]{:S(2)}) copy-start(f32[1,1,3072]{2,1,0:T(1,128)} %copy-done.67) | copy-start | bytes 36868
  187.8 24.1 %copy-start.70 = (f32[1,1,3072]{2,1,0:T(1,128)S(1)}, f32[1,1,3072]{2,1,0:T(1,128)}, u32[]{:S(2)}) copy-start(f32[1,1,3072]{2,1,0:T(1,128)} %copy-done.69) | copy-start | bytes 36868
  187.9 24.1 %copy-start.72 = (f32[1,1,3072]{2,1,0:T(1,128)S(1)}, f32[1,1,3072]{2,1,0:T(1,128)}, u32[]{:S(2)}) copy-start(f32[1,1,3072]{2,1,0:T(1,128)} %copy-done.71) | copy-start | bytes 36868
  187.9 24.1 %copy-start.74 = (f32[1,1,3072]{2,1,0:T(1,128)S(1)}, f32[1,1,3072]{2,1,0:T(1,128)}, u32[]{:S(2)}) copy-start(f32[1,1,3072]{2,1,0:T(1,128)} %copy-done.73) | copy-start | bytes 36868
  187.9 24.1 %copy-start.76 = (f32[1,1,3072]{2,1,0:T(1,128)S(1)}, f32[1,1,3072]{2,1,0:T(1,128)}, u32[]{:S(2)}) copy-start(f32[1,1,3072]{2,1,0:T(1,128)} %copy-done.75) | copy-start | bytes 36868
  187.9 24.1 %copy-start.78 = (f32[1,1,3072]{2,1,0:T(1,128)S(1)}, f32[1,1,3072]{2,1,0:T(1,128)}, u32[]{:S(2)}) copy-start(f32[1,1,3072]{2,1,0:T(1,128)} %copy-done.77) | copy-start | bytes 36868
  187.9 24.1 %copy-start.80 = (f32[1,1,3072]{2,1,0:T(1,128)S(1)}, f32[1,1,3072]{2,1,0:T(1,128)}, u32[]{:S(2)}) copy-start(f32[1,1,3072]{2,1,0:T(1,128)} %copy-done.79) | copy-start | bytes 36868
  187.9 24.1 %copy-start.82 = (f32[1,1,3072]{2,1,0:T(1,128)S(1)}, f32[1,1,3072]{2,1,0:T(1,128)}, u32[]{:S(2)}) copy-start(f32[1,1,3072]{2,1,0:T(1,128)} %copy-done.81) | copy-start | bytes 36868
  187.9 24.1 %copy-start.84 = (f32[1,1,3072]{2,1,0:T(1,128)S(1)}, f32[1,1,3072]{2,1,0:T(1,128)}, u32[]{:S(2)}) copy-start(f32[1,1,3072]{2,1,0:T(1,128)} %copy-done.83) | copy-start | bytes 36868
  187.9 24.1 %copy-start.86 = (f32[1,1,3072]{2,1,0:T(1,128)S(1)}, f32[1,1,3072]{2,1,0:T(1,128)}, u32[]{:S(2)}) copy-start(f32[1,1,3072]{2,1,0:T(1,128)} %copy-done.85) | copy-start | bytes 36868
  187.9 24.1 %copy-start.88 = (f32[1,1,3072]{2,1,0:T(1,128)S(1)}, f32[1,1,3072]{2,1,0:T(1,128)}, u32[]{:S(2)}) copy-start(f32[1,1,3072]{2,1,0:T(1,128)} %copy-done.87) | copy-start | bytes 36868
  (81 other events, 1162.6 us)

commit v10 on v9

--- a/solution.py
+++ b/solution.py
@@ -153,15 +153,16 @@
     gathered = gather_stages(gathered, "dp", radix_split(dp_count))
     image_all = gathered[:, :, :batch_rows, :].reshape(dp_count * img_count * batch_rows, -1)
     text_all = gathered[:, :, batch_rows:, :].reshape(dp_count * text_count, -1)
-    logits = (
-        LOGIT_SCALE * jnp.dot(image_all, text_all.T, preferred_element_type=jnp.float32)
+    own_at = (dp_at * img_count + img_at) * batch_rows
+    own_labels = lax.dynamic_slice_in_dim(labels, own_at, batch_rows, axis=0)
+    own_weights = lax.dynamic_slice_in_dim(weights, own_at, batch_rows)
+    own_logits = (
+        LOGIT_SCALE * jnp.dot(image_vec, text_all.T, preferred_element_type=jnp.float32)
         + LOGIT_BIAS
     )
-    pair_grad = (weights[:, None] * -labels * jax.nn.sigmoid(-labels * logits)).astype(
-        jnp.bfloat16
-    )
-    own_at = (dp_at * img_count + img_at) * batch_rows
-    own_pair = lax.dynamic_slice_in_dim(pair_grad, own_at, batch_rows, axis=0)
+    own_pair = (
+        own_weights[:, None] * -own_labels * jax.nn.sigmoid(-own_labels * own_logits)
+    ).astype(jnp.bfloat16)
     image_dir = LOGIT_SCALE * jnp.dot(own_pair, text_all, preferred_element_type=jnp.float32)
     embed_back = jax.vjp(unit_rows, embed)[1]
     embed_grad = embed_back(image_dir)[0].astype(jnp.bfloat16)
@@ -171,7 +172,14 @@
     norm_back = jax.vjp(lambda values: cell_norm(values, ln_gain), conved)[1]
     seeded = jnp.broadcast_to((layer_scale * own_grad)[:, None, None, :], conved.shape)
     conv_grad = norm_back(seeded)[0].astype(jnp.bfloat16)
-    logits, pair_grad, conv_grad = lax.optimization_barrier((logits, pair_grad, conv_grad))
+    image_all, conv_grad = lax.optimization_barrier((image_all, conv_grad))
+    logits = (
+        LOGIT_SCALE * jnp.dot(image_all, text_all.T, preferred_element_type=jnp.float32)
+        + LOGIT_BIAS
+    )
+    pair_grad = (weights[:, None] * -labels * jax.nn.sigmoid(-labels * logits)).astype(
+        jnp.bfloat16
+    )
     row_loss = lax.optimization_barrier(jnp.sum(jax.nn.softplus(-labels * logits), axis=1))
     group_sums = jnp.sum(source_table * (weights * row_loss)[:, None], axis=0)
     text_pair = lax.dynamic_slice_in_dim(pair_grad, dp_at * text_count, text_count, axis=1)

time: 242 us -> 244 us (level)
  local copies, waits for them, and re-layouts: 14.1 us -> 17 us
  transfers between devices with their start and end apart: 14 -> 14, of which waited for: 11 -> 11; matrix products, arithmetic and copies ran while one was open for 4% -> 5% of each run, Pallas kernels for 0% -> 0%
where the time goes in v10:
time: 244 us; the launch traced here: 242 us
  other arithmetic  78.3 us (32%)
  waiting for transfers between devices  67.7 us (28%)
  starting transfers between devices  61.6 us (25%)
  local copies, waits for them, and re-layouts  17 us (7%)
  matrix products  13.4 us (5%)
  between operations  3.49 us (1%)
    ppermute x7, starting transfers between devices, gather_stages(): got.append(lax.ppermute(value, axis, pairs))  43 us
    ppermute x2, waiting for transfers between devices, halo_rows(): before = lax.ppermute(last, 'row', up)  38.1 us
    reduce_sum x4, other arithmetic, cell_norm(): center = values - jnp.mean(values, axis=-1, keepdims=True)  30.1 us
    convert_element_type x1, other arithmetic, local(): grad_map = (own_grad[:, None, None, :] + spread).astype(jnp.bfloat16)  27.3 us
    ppermute x7, waiting for transfers between devices, gather_stages(): got.append(lax.ppermute(value, axis, pairs))  22.6 us
    ppermute x3, starting transfers between devices, group_sum(): value = value + lax.ppermute(value, 'row', pairs)  7.47 us
    ppermute x2, starting transfers between devices, halo_rows(): after = lax.ppermute(leading, 'row', down)  7.29 us
    ppermute x3, waiting for transfers between devices, group_sum(): value = value + lax.ppermute(value, 'row', pairs)  7 us
  transfers between devices with their start and end apart: 14, of which 11 were waited for; matrix products, arithmetic and copies ran while one was open for 5% of the time, Pallas kernels for 0%

profile of v10, /device:TPU:6, one launch (start us, length us, event | category | flops | bytes accessed | tf_op | source)
XLA Modules:
  0.0 241.5 jit_solution(6109102733802083769)
XLA Ops:
  0.7 3.3 %fusion.53 = (bf16[2,3,32,3072]{3,2,1,0:T(8,128)(2,1)}, bf16[2,3,32,3072]{3,2,1,0:T(8,128)(2,1)}) fusion(bf16[2,4,32,3072]{3,2,1,0:T(8,128)(2,1)} %param.11), kind=kLoop, calls=%fused_computation.248 | loop fusion | bytes 4718592 | tf_op jit(solution)/shard_map/slice | solution.py:21
  4.0 1.9 collective-permute-start
  5.9 3.6 %collective-permute-start.1 = (bf16[2,3,32,3072]{3,2,1,0:T(8,128)(2,1)}, bf16[2,3,32,3072]{3,2,1,0:T(8,128)(2,1)}, u32[]{:S(2)}, u32[]{:S(2)}) collective-permute-start(bf16[2,3,32,3072]{3,2,1,0:T(8,128)(2,1)} %get-tuple-element.28), channel_id=1, source_target_pairs={{1,0},{2,1},{3,2},{4,3},{5,4},{6,5},{7,6},{9,8},{10,9},{11,10},{12... | collective-permute-start | bytes 3538952 | tf_op jit(solution)/shard_map/ppermute | solution.py:24
  13.8 0.8 fusion.14
  15.9 0.8 slice_convert_fusion.47
  16.7 17.6 %collective-permute-done = bf16[2,3,32,3072]{3,2,1,0:T(8,128)(2,1)S(1)} collective-permute-done((bf16[2,3,32,3072]{3,2,1,0:T(8,128)(2,1)}, bf16[2,3,32,3072]{3,2,1,0:T(8,128)(2,1)S(1)}, u32[]{:S(2)}, u32[]{:S(2)}) %collective-permute-start) | collective-permute-done | bytes 1179680 | tf_op jit(solution)/shard_map/ppermute | solution.py:23
  34.4 1.5 pad_maximum_fusion
  36.3 29.0 %fusion.51 = (f32[2,4,32]{2,1,0:T(4,128)S(1)}, f32[2,4,32,3072]{3,2,1,0:T(8,128)S(1)}) fusion(f32[3072]{0:T(1024)S(1)} %copy-done.100, f32[3072]{0:T(1024)S(1)} %bitcast.110, f32[3072]{0:T(1024)S(1)} %bitcast.112, f32[3072]{0:T(1024)S(1)} %bitcast.116, f32[3072]{0:T(1024)S(1)} %bitcast.118, bf16[2,10,32,3072]{3,2,1,0:T(8,128)(2,1)S(1)} %pad_maximum_fusion, ...), kind=kLoop, calls=%fused_computation.246 | loop fusion | flops 116391680 | bytes 18703360 | tf_op jit(solution)/shard_map/reduce_sum | solution.py:78
  66.8 1.0 add_reduce_fusion
  67.8 1.9 collective-permute-start.2
  69.7 1.2 collective-permute-done.2
  70.9 1.9 collective-permute-start.3
  72.8 3.8 %collective-permute-done.3 = f32[2,3072]{1,0:T(2,128)S(1)} collective-permute-done((f32[2,3072]{1,0:T(2,128)S(1)}, f32[2,3072]{1,0:T(2,128)S(1)}, u32[]{:S(2)}, u32[]{:S(2)}) %collective-permute-start.3) | collective-permute-done | bytes 24608 | tf_op jit(solution)/shard_map/ppermute | solution.py:33
  76.6 3.6 %collective-permute-start.4 = (f32[2,3072]{1,0:T(2,128)S(1)}, f32[2,3072]{1,0:T(2,128)S(1)}, u32[]{:S(2)}, u32[]{:S(2)}) collective-permute-start(f32[2,3072]{1,0:T(2,128)S(1)} %add.513), channel_id=1, source_target_pairs={{0,4},{1,5},{2,6},{3,7},{4,0},{5,1},{6,2},{7,3},{8,12},{9,13},{10,... | collective-permute-start | bytes 73736 | tf_op jit(solution)/shard_map/ppermute | solution.py:33
  80.3 2.1 collective-permute-done.4
  83.2 3.9 %multiply_reduce_fusion.7 = (f32[2]{0:T(128)S(1)}, f32[2,1024]{1,0:T(2,128)S(1)}) fusion(bf16[3072,1024]{1,0:T(8,128)(2,1)} %param.17, f32[2]{0:T(128)S(1)} %fusion.42, f32[3072]{0:T(1024)S(1)} %copy-done.95, f32[2,3072]{1,0:T(2,128)S(1)} %get-tuple-element.22, f32[2]{0:T(128)S(1)} %broadcast_multiply_fusion.5), kind=kOutput, calls=%fused_computation.203 | convolution fusion | flops 12611582 | bytes 6336536 | tf_op jit(solution)/shard_map/dot_general | solution.py:149
  87.8 15.1 %collective-permute-start.5 = (bf16[4,1024]{1,0:T(4,128)(2,1)S(1)}, bf16[4,1024]{1,0:T(4,128)(2,1)S(1)}, u32[]{:S(2)}, u32[]{:S(2)}) collective-permute-start(bf16[4,1024]{1,0:T(4,128)(2,1)S(1)} %pad_maximum_fusion.8), channel_id=1, source_target_pairs={{0,24},{8,32},{16,40},{24,0},{32,8},{40,16},{1,25},{9,33},{17,41},... | collective-permute-start | bytes 24584 | tf_op jit(solution)/shard_map/ppermute | solution.py:54
  103.0 1.6 collective-permute-done.5
  104.6 3.7 %collective-permute-start.6 = (bf16[2,4,1024]{2,1,0:T(4,128)(2,1)S(1)}, bf16[2,4,1024]{2,1,0:T(4,128)(2,1)S(1)}, u32[]{:S(2)}, u32[]{:S(2)}) collective-permute-start(bf16[2,4,1024]{2,1,0:T(4,128)(2,1)S(1)} %get-tuple-element.89), channel_id=1, source_target_pairs={{0,8},{8,16},{16,0},{24,32},{32,40},{40,24},{1,9},{9,17},{17,1},{2... | collective-permute-start | bytes 49160 | tf_op jit(solution)/shard_map/ppermute | solution.py:54
  108.3 6.1 %collective-permute-start.7 = (bf16[2,4,1024]{2,1,0:T(4,128)(2,1)S(1)}, bf16[2,4,1024]{2,1,0:T(4,128)(2,1)S(1)}, u32[]{:S(2)}, u32[]{:S(2)}) collective-permute-start(bf16[2,4,1024]{2,1,0:T(4,128)(2,1)S(1)} %get-tuple-element.89), channel_id=1, source_target_pairs={{0,16},{8,0},{16,8},{24,40},{32,24},{40,32},{1,17},{9,1},{17,9},{2... | collective-permute-start | bytes 49160 | tf_op jit(solution)/shard_map/ppermute | solution.py:54
  114.5 1.3 collective-permute-done.7
  116.6 3.3 %collective-permute-start.8 = (bf16[6,4,1024]{2,1,0:T(4,128)(2,1)S(1)}, bf16[6,4,1024]{2,1,0:T(4,128)(2,1)S(1)}, u32[]{:S(2)}, u32[]{:S(2)}) collective-permute-start(bf16[6,4,1024]{2,1,0:T(4,128)(2,1)S(1)} %bitcast_select_fusion), channel_id=1, source_target_pairs={{0,384},{48,432},{96,480},{144,528},{192,576},{240,624},{288,672},... | collective-permute-start | bytes 147464 | tf_op jit(solution)/shard_map/ppermute | solution.py:54
  119.9 4.1 %collective-permute-done.8 = bf16[6,4,1024]{2,1,0:T(4,128)(2,1)S(1)} collective-permute-done((bf16[6,4,1024]{2,1,0:T(4,128)(2,1)S(1)}, bf16[6,4,1024]{2,1,0:T(4,128)(2,1)S(1)}, u32[]{:S(2)}, u32[]{:S(2)}) %collective-permute-start.8) | collective-permute-done | bytes 49184 | tf_op jit(solution)/shard_map/ppermute | solution.py:54
  124.3 7.7 %collective-permute-start.9 = (bf16[2,6,4,1024]{3,2,1,0:T(4,128)(2,1)S(1)}, bf16[2,6,4,1024]{3,2,1,0:T(4,128)(2,1)S(1)}, u32[]{:S(2)}, u32[]{:S(2)}) collective-permute-start(bf16[2,6,4,1024]{3,2,1,0:T(4,128)(2,1)S(1)} %pad_maximum_fusion.5), channel_id=1, source_target_pairs={{0,192},{48,240},{96,288},{144,336},{192,0},{240,48},{288,96},{336... | collective-permute-start | bytes 294920 | tf_op jit(solution)/shard_map/ppermute | solution.py:54
  132.0 3.1 %collective-permute-done.9 = bf16[2,6,4,1024]{3,2,1,0:T(4,128)(2,1)S(1)} collective-permute-done((bf16[2,6,4,1024]{3,2,1,0:T(4,128)(2,1)S(1)}, bf16[2,6,4,1024]{3,2,1,0:T(4,128)(2,1)S(1)}, u32[]{:S(2)}, u32[]{:S(2)}) %collective-permute-start.9) | collective-permute-done | bytes 98336 | tf_op jit(solution)/shard_map/ppermute | solution.py:54
  136.1 5.0 %collective-permute-start.10 = (bf16[2,2,6,4,1024]{4,3,2,0,1:T(4,128)(2,1)S(1)}, bf16[2,2,6,4,1024]{4,3,2,0,1:T(4,128)(2,1)}, u32[]{:S(2)}, u32[]{:S(2)}) collective-permute-start(bf16[2,2,6,4,1024]{4,3,2,0,1:T(4,128)(2,1)S(1)} %pad_maximum_fusion.4), channel_id=1, source_target_pairs={{0,96},{48,144},{96,0},{144,48},{192,288},{240,336},{288,192},{336... | collective-permute-start | bytes 589832 | tf_op jit(solution)/shard_map/ppermute | solution.py:54
  141.1 5.8 %collective-permute-done.10 = bf16[2,2,6,4,1024]{4,3,2,0,1:T(4,128)(2,1)} collective-permute-done((bf16[2,2,6,4,1024]{4,3,2,0,1:T(4,128)(2,1)S(1)}, bf16[2,2,6,4,1024]{4,3,2,0,1:T(4,128)(2,1)}, u32[]{:S(2)}, u32[]{:S(2)}) %collective-permute-start.10) | collective-permute-done | bytes 196640 | tf_op jit(solution)/shard_map/ppermute | solution.py:54
  146.9 1.3 select_bitcast_fusion.3
  148.2 1.0 pad_maximum_fusion.3
  149.2 2.1 collective-permute-start.11
  151.4 1.2 dynamic_slice.13
  152.6 6.7 %collective-permute-done.11 = bf16[2,2,2,6,4,1024]{5,4,3,0,1,2:T(4,128)(2,1)} collective-permute-done((bf16[2,2,2,6,4,1024]{5,4,3,0,1,2:T(4,128)(2,1)}, bf16[2,2,2,6,4,1024]{5,4,3,0,1,2:T(4,128)(2,1)}, u32[]{:S(2)}, u32[]{:S(2)}) %collective-permute-start.11) | collective-permute-done | bytes 393248 | tf_op jit(solution)/shard_map/ppermute | solution.py:54
  159.2 1.5 select_bitcast_fusion.1
  161.5 1.3 fusion.54
  162.8 1.9 reshape.545
  164.7 2.9 %multiply_reduce_fusion.6 = (f32[2]{0:T(128)}, f32[2,1024]{1,0:T(2,128)}) fusion(f32[2,1024]{1,0:T(2,128)} %copy-done.92, bf16[192,1024]{1,0:T(8,128)(2,1)} %reshape.545, f32[192,192]{1,0:T(8,128)} %fusion.14, s32[]{:T(128)S(6)} %select_n.160, f32[2]{0:T(128)} %dynamic_slice.13, f32[2]{0:T(128)} %copy-done.111), kind=kOutput, calls=%fused_computation.199 | convolution fusion | flops 1586942 | bytes 814092 | tf_op jit(solution)/shard_map/dot_general | solution.py:166
  168.4 4.7 %multiply_reduce_fusion.4 = (f32[2]{0:T(128)S(1)}, f32[2,3072]{1,0:T(2,128)S(1)}) fusion(f32[2,3072]{1,0:T(2,128)} %copy-done.7, f32[2]{0:T(128)} %copy-done.101, f32[3072]{0:T(1024)} %param.16, bf16[3072,1024]{1,0:T(8,128)(2,1)} %param.17, f32[2,1024]{1,0:T(2,128)} %copy-done.92, f32[2,1024]{1,0:T(2,128)} %get-tuple-element.101, ...), kind=kOutput, calls=%fused_computation.135 | convolution fusion | flops 12617726 | bytes 6369312 | tf_op jit(solution)/shard_map/dot_general | solution.py:169
  174.6 0.8 fusion.1
  175.4 2.1 add_convert_fusion.1
  177.5 0.9 reshape.546
  178.5 3.3 %fusion.52 = (bf16[2,3,32,3072]{3,2,1,0:T(8,128)(2,1)}, bf16[2,3,32,3072]{3,2,1,0:T(8,128)(2,1)}) fusion(bf16[2,4,32,3072]{3,2,1,0:T(8,128)(2,1)} %add_convert_fusion.1), kind=kLoop, calls=%fused_computation.247 | loop fusion | bytes 4718592 | tf_op jit(solution)/shard_map/slice | solution.py:21
  181.8 1.9 collective-permute-start.12
  183.7 3.6 %collective-permute-start.13 = (bf16[2,3,32,3072]{3,2,1,0:T(8,128)(2,1)}, bf16[2,3,32,3072]{3,2,1,0:T(8,128)(2,1)}, u32[]{:S(2)}, u32[]{:S(2)}) collective-permute-start(bf16[2,3,32,3072]{3,2,1,0:T(8,128)(2,1)} %get-tuple-element.26), channel_id=1, source_target_pairs={{1,0},{2,1},{3,2},{4,3},{5,4},{6,5},{7,6},{9,8},{10,9},{11,10},{12... | collective-permute-start | bytes 3538952 | tf_op jit(solution)/shard_map/ppermute | solution.py:24
  187.4 1.5 fusion.13
  190.6 0.7 add_add_fusion.2
  191.7 20.5 %collective-permute-done.12 = bf16[2,3,32,3072]{3,2,1,0:T(8,128)(2,1)S(1)} collective-permute-done((bf16[2,3,32,3072]{3,2,1,0:T(8,128)(2,1)}, bf16[2,3,32,3072]{3,2,1,0:T(8,128)(2,1)S(1)}, u32[]{:S(2)}, u32[]{:S(2)}) %collective-permute-start.12) | collective-permute-done | bytes 1179680 | tf_op jit(solution)/shard_map/ppermute | solution.py:23
  212.1 1.5 pad_maximum_fusion.1
  214.1 27.3 %add_convert_fusion = bf16[2,4,32,3072]{3,2,1,0:T(8,128)(2,1)} fusion(bf16[2,10,32,3072]{3,2,1,0:T(8,128)(2,1)S(1)} %pad_maximum_fusion.1, f32[2,3072]{1,0:T(2,128)} %get-tuple-element.18, f32[3072]{0:T(1024)S(1)} %bitcast.111, f32[3072]{0:T(1024)S(1)} %bitcast.113, f32[3072]{0:T(1024)S(1)} %bitcast.117, f32[3072]{0:T(1024)S(1)} %bitcast.119, ...), kind=kLoop, calls=%fused_computation.8 | loop fusion | flops 116391936 | bytes 17141760 | tf_op jit(solution)/shard_map/convert_element_type | solution.py:192
  (289 shorter events, 14.5 us)
Async XLA Ops:
  0.6 33.8 %copy-start = (bf16[2,4,32,3072]{3,2,1,0:T(8,128)(2,1)S(1)}, bf16[2,4,32,3072]{3,2,1,0:T(8,128)(2,1)}, u32[]{:S(2)}) copy-start(bf16[2,4,32,3072]{3,2,1,0:T(8,128)(2,1)} %param.11) | copy-start | bytes 4718596
  4.0 30.4 %collective-permute-start = (bf16[2,3,32,3072]{3,2,1,0:T(8,128)(2,1)}, bf16[2,3,32,3072]{3,2,1,0:T(8,128)(2,1)S(1)}, u32[]{:S(2)}, u32[]{:S(2)}) collective-permute-start(bf16[2,3,32,3072]{3,2,1,0:T(8,128)(2,1)} %get-tuple-element.27), channel_id=1, source_target_pairs={{0,1},{1,2},{2,3},{3,4},{4,5},{5,6},{6,7},{8,9},{9,10},{10,11},{11... | collective-permute-start | bytes 3538952 | tf_op jit(solution)/shard_map/ppermute | solution.py:23
  5.9 28.4 %collective-permute-start.1 = (bf16[2,3,32,3072]{3,2,1,0:T(8,128)(2,1)}, bf16[2,3,32,3072]{3,2,1,0:T(8,128)(2,1)}, u32[]{:S(2)}, u32[]{:S(2)}) collective-permute-start(bf16[2,3,32,3072]{3,2,1,0:T(8,128)(2,1)} %get-tuple-element.28), channel_id=1, source_target_pairs={{1,0},{2,1},{3,2},{4,3},{5,4},{6,5},{7,6},{9,8},{10,9},{11,10},{12... | collective-permute-start | bytes 3538952 | tf_op jit(solution)/shard_map/ppermute | solution.py:24
  67.8 3.1 %collective-permute-start.2 = (f32[2,3072]{1,0:T(2,128)S(1)}, f32[2,3072]{1,0:T(2,128)S(1)}, u32[]{:S(2)}, u32[]{:S(2)}) collective-permute-start(f32[2,3072]{1,0:T(2,128)S(1)} %broadcast_multiply_fusion.1), channel_id=1, source_target_pairs={{0,1},{1,0},{2,3},{3,2},{4,5},{5,4},{6,7},{7,6},{8,9},{9,8},{10,11... | collective-permute-start | bytes 73736 | tf_op jit(solution)/shard_map/ppermute | solution.py:33
  70.9 5.7 %collective-permute-start.3 = (f32[2,3072]{1,0:T(2,128)S(1)}, f32[2,3072]{1,0:T(2,128)S(1)}, u32[]{:S(2)}, u32[]{:S(2)}) collective-permute-start(f32[2,3072]{1,0:T(2,128)S(1)} %fusion.47), channel_id=1, source_target_pairs={{0,2},{1,3},{2,0},{3,1},{4,6},{5,7},{6,4},{7,5},{8,10},{9,11},{10,... | collective-permute-start | bytes 73736 | tf_op jit(solution)/shard_map/ppermute | solution.py:33
  76.6 5.7 %collective-permute-start.4 = (f32[2,3072]{1,0:T(2,128)S(1)}, f32[2,3072]{1,0:T(2,128)S(1)}, u32[]{:S(2)}, u32[]{:S(2)}) collective-permute-start(f32[2,3072]{1,0:T(2,128)S(1)} %add.513), channel_id=1, source_target_pairs={{0,4},{1,5},{2,6},{3,7},{4,0},{5,1},{6,2},{7,3},{8,12},{9,13},{10,... | collective-permute-start | bytes 73736 | tf_op jit(solution)/shard_map/ppermute | solution.py:33
  87.8 16.8 %collective-permute-start.5 = (bf16[4,1024]{1,0:T(4,128)(2,1)S(1)}, bf16[4,1024]{1,0:T(4,128)(2,1)S(1)}, u32[]{:S(2)}, u32[]{:S(2)}) collective-permute-start(bf16[4,1024]{1,0:T(4,128)(2,1)S(1)} %pad_maximum_fusion.8), channel_id=1, source_target_pairs={{0,24},{8,32},{16,40},{24,0},{32,8},{40,16},{1,25},{9,33},{17,41},... | collective-permute-start | bytes 24584 | tf_op jit(solution)/shard_map/ppermute | solution.py:54
  104.6 9.9 %collective-permute-start.6 = (bf16[2,4,1024]{2,1,0:T(4,128)(2,1)S(1)}, bf16[2,4,1024]{2,1,0:T(4,128)(2,1)S(1)}, u32[]{:S(2)}, u32[]{:S(2)}) collective-permute-start(bf16[2,4,1024]{2,1,0:T(4,128)(2,1)S(1)} %get-tuple-element.89), channel_id=1, source_target_pairs={{0,8},{8,16},{16,0},{24,32},{32,40},{40,24},{1,9},{9,17},{17,1},{2... | collective-permute-start | bytes 49160 | tf_op jit(solution)/shard_map/ppermute | solution.py:54
  108.3 7.5 %collective-permute-start.7 = (bf16[2,4,1024]{2,1,0:T(4,128)(2,1)S(1)}, bf16[2,4,1024]{2,1,0:T(4,128)(2,1)S(1)}, u32[]{:S(2)}, u32[]{:S(2)}) collective-permute-start(bf16[2,4,1024]{2,1,0:T(4,128)(2,1)S(1)} %get-tuple-element.89), channel_id=1, source_target_pairs={{0,16},{8,0},{16,8},{24,40},{32,24},{40,32},{1,17},{9,1},{17,9},{2... | collective-permute-start | bytes 49160 | tf_op jit(solution)/shard_map/ppermute | solution.py:54
  116.6 7.5 %collective-permute-start.8 = (bf16[6,4,1024]{2,1,0:T(4,128)(2,1)S(1)}, bf16[6,4,1024]{2,1,0:T(4,128)(2,1)S(1)}, u32[]{:S(2)}, u32[]{:S(2)}) collective-permute-start(bf16[6,4,1024]{2,1,0:T(4,128)(2,1)S(1)} %bitcast_select_fusion), channel_id=1, source_target_pairs={{0,384},{48,432},{96,480},{144,528},{192,576},{240,624},{288,672},... | collective-permute-start | bytes 147464 | tf_op jit(solution)/shard_map/ppermute | solution.py:54
  124.3 10.9 %collective-permute-start.9 = (bf16[2,6,4,1024]{3,2,1,0:T(4,128)(2,1)S(1)}, bf16[2,6,4,1024]{3,2,1,0:T(4,128)(2,1)S(1)}, u32[]{:S(2)}, u32[]{:S(2)}) collective-permute-start(bf16[2,6,4,1024]{3,2,1,0:T(4,128)(2,1)S(1)} %pad_maximum_fusion.5), channel_id=1, source_target_pairs={{0,192},{48,240},{96,288},{144,336},{192,0},{240,48},{288,96},{336... | collective-permute-start | bytes 294920 | tf_op jit(solution)/shard_map/ppermute | solution.py:54
  136.1 10.9 %collective-permute-start.10 = (bf16[2,2,6,4,1024]{4,3,2,0,1:T(4,128)(2,1)S(1)}, bf16[2,2,6,4,1024]{4,3,2,0,1:T(4,128)(2,1)}, u32[]{:S(2)}, u32[]{:S(2)}) collective-permute-start(bf16[2,2,6,4,1024]{4,3,2,0,1:T(4,128)(2,1)S(1)} %pad_maximum_fusion.4), channel_id=1, source_target_pairs={{0,96},{48,144},{96,0},{144,48},{192,288},{240,336},{288,192},{336... | collective-permute-start | bytes 589832 | tf_op jit(solution)/shard_map/ppermute | solution.py:54
  149.2 10.0 %collective-permute-start.11 = (bf16[2,2,2,6,4,1024]{5,4,3,0,1,2:T(4,128)(2,1)}, bf16[2,2,2,6,4,1024]{5,4,3,0,1,2:T(4,128)(2,1)}, u32[]{:S(2)}, u32[]{:S(2)}) collective-permute-start(bf16[2,2,2,6,4,1024]{5,4,3,0,1,2:T(4,128)(2,1)} %pad_maximum_fusion.3), channel_id=1, source_target_pairs={{0,48},{48,0},{96,144},{144,96},{192,240},{240,192},{288,336},{336... | collective-permute-start | bytes 1179656 | tf_op jit(solution)/shard_map/ppermute | solution.py:54
  178.5 33.7 %copy-start.2 = (bf16[2,4,32,3072]{3,2,1,0:T(8,128)(2,1)S(1)}, bf16[2,4,32,3072]{3,2,1,0:T(8,128)(2,1)}, u32[]{:S(2)}) copy-start(bf16[2,4,32,3072]{3,2,1,0:T(8,128)(2,1)} %add_convert_fusion.1) | copy-start | bytes 4718596
  181.8 30.4 %collective-permute-start.12 = (bf16[2,3,32,3072]{3,2,1,0:T(8,128)(2,1)}, bf16[2,3,32,3072]{3,2,1,0:T(8,128)(2,1)S(1)}, u32[]{:S(2)}, u32[]{:S(2)}) collective-permute-start(bf16[2,3,32,3072]{3,2,1,0:T(8,128)(2,1)} %get-tuple-element.25), channel_id=1, source_target_pairs={{0,1},{1,2},{2,3},{3,4},{4,5},{5,6},{6,7},{8,9},{9,10},{10,11},{11... | collective-permute-start | bytes 3538952 | tf_op jit(solution)/shard_map/ppermute | solution.py:23
  183.7 28.4 %collective-permute-start.13 = (bf16[2,3,32,3072]{3,2,1,0:T(8,128)(2,1)}, bf16[2,3,32,3072]{3,2,1,0:T(8,128)(2,1)}, u32[]{:S(2)}, u32[]{:S(2)}) collective-permute-start(bf16[2,3,32,3072]{3,2,1,0:T(8,128)(2,1)} %get-tuple-element.26), channel_id=1, source_target_pairs={{1,0},{2,1},{3,2},{4,3},{5,4},{6,5},{7,6},{9,8},{10,9},{11,10},{12... | collective-permute-start | bytes 3538952 | tf_op jit(solution)/shard_map/ppermute | solution.py:24
  191.3 22.4 %copy-start.23 = (f32[1,1,3072]{2,1,0:T(1,128)S(1)}, f32[1,1,3072]{2,1,0:T(1,128)}, u32[]{:S(2)}) copy-start(f32[1,1,3072]{2,1,0:T(1,128)} %copy-done.22) | copy-start | bytes 36868
  191.3 22.4 %copy-start.25 = (f32[1,1,3072]{2,1,0:T(1,128)S(1)}, f32[1,1,3072]{2,1,0:T(1,128)}, u32[]{:S(2)}) copy-start(f32[1,1,3072]{2,1,0:T(1,128)} %copy-done.24) | copy-start | bytes 36868
  191.3 22.4 %copy-start.27 = (f32[1,1,3072]{2,1,0:T(1,128)S(1)}, f32[1,1,3072]{2,1,0:T(1,128)}, u32[]{:S(2)}) copy-start(f32[1,1,3072]{2,1,0:T(1,128)} %copy-done.26) | copy-start | bytes 36868
  191.3 22.4 %copy-start.29 = (f32[1,1,3072]{2,1,0:T(1,128)S(1)}, f32[1,1,3072]{2,1,0:T(1,128)}, u32[]{:S(2)}) copy-start(f32[1,1,3072]{2,1,0:T(1,128)} %copy-done.28) | copy-start | bytes 36868
  191.3 22.4 %copy-start.31 = (f32[1,1,3072]{2,1,0:T(1,128)S(1)}, f32[1,1,3072]{2,1,0:T(1,128)}, u32[]{:S(2)}) copy-start(f32[1,1,3072]{2,1,0:T(1,128)} %copy-done.30) | copy-start | bytes 36868
  191.4 22.4 %copy-start.33 = (f32[1,1,3072]{2,1,0:T(1,128)S(1)}, f32[1,1,3072]{2,1,0:T(1,128)}, u32[]{:S(2)}) copy-start(f32[1,1,3072]{2,1,0:T(1,128)} %copy-done.32) | copy-start | bytes 36868
  191.4 22.4 %copy-start.35 = (f32[1,1,3072]{2,1,0:T(1,128)S(1)}, f32[1,1,3072]{2,1,0:T(1,128)}, u32[]{:S(2)}) copy-start(f32[1,1,3072]{2,1,0:T(1,128)} %copy-done.34) | copy-start | bytes 36868
  191.4 22.4 %copy-start.37 = (f32[1,1,3072]{2,1,0:T(1,128)S(1)}, f32[1,1,3072]{2,1,0:T(1,128)}, u32[]{:S(2)}) copy-start(f32[1,1,3072]{2,1,0:T(1,128)} %copy-done.36) | copy-start | bytes 36868
  191.4 22.4 %copy-start.39 = (f32[1,1,3072]{2,1,0:T(1,128)S(1)}, f32[1,1,3072]{2,1,0:T(1,128)}, u32[]{:S(2)}) copy-start(f32[1,1,3072]{2,1,0:T(1,128)} %copy-done.38) | copy-start | bytes 36868
  191.4 22.4 %copy-start.41 = (f32[1,1,3072]{2,1,0:T(1,128)S(1)}, f32[1,1,3072]{2,1,0:T(1,128)}, u32[]{:S(2)}) copy-start(f32[1,1,3072]{2,1,0:T(1,128)} %copy-done.40) | copy-start | bytes 36868
  191.4 22.4 %copy-start.43 = (f32[1,1,3072]{2,1,0:T(1,128)S(1)}, f32[1,1,3072]{2,1,0:T(1,128)}, u32[]{:S(2)}) copy-start(f32[1,1,3072]{2,1,0:T(1,128)} %copy-done.42) | copy-start | bytes 36868
  191.4 22.4 %copy-start.45 = (f32[1,1,3072]{2,1,0:T(1,128)S(1)}, f32[1,1,3072]{2,1,0:T(1,128)}, u32[]{:S(2)}) copy-start(f32[1,1,3072]{2,1,0:T(1,128)} %copy-done.44) | copy-start | bytes 36868
  191.4 22.4 %copy-start.47 = (f32[1,1,3072]{2,1,0:T(1,128)S(1)}, f32[1,1,3072]{2,1,0:T(1,128)}, u32[]{:S(2)}) copy-start(f32[1,1,3072]{2,1,0:T(1,128)} %copy-done.46) | copy-start | bytes 36868
  191.4 22.4 %copy-start.49 = (f32[1,1,3072]{2,1,0:T(1,128)S(1)}, f32[1,1,3072]{2,1,0:T(1,128)}, u32[]{:S(2)}) copy-start(f32[1,1,3072]{2,1,0:T(1,128)} %copy-done.48) | copy-start | bytes 36868
  191.4 22.4 %copy-start.51 = (f32[1,1,3072]{2,1,0:T(1,128)S(1)}, f32[1,1,3072]{2,1,0:T(1,128)}, u32[]{:S(2)}) copy-start(f32[1,1,3072]{2,1,0:T(1,128)} %copy-done.50) | copy-start | bytes 36868
  191.5 22.4 %copy-start.53 = (f32[1,1,3072]{2,1,0:T(1,128)S(1)}, f32[1,1,3072]{2,1,0:T(1,128)}, u32[]{:S(2)}) copy-start(f32[1,1,3072]{2,1,0:T(1,128)} %copy-done.52) | copy-start | bytes 36868
  191.5 22.4 %copy-start.55 = (f32[1,1,3072]{2,1,0:T(1,128)S(1)}, f32[1,1,3072]{2,1,0:T(1,128)}, u32[]{:S(2)}) copy-start(f32[1,1,3072]{2,1,0:T(1,128)} %copy-done.54) | copy-start | bytes 36868
  191.5 22.4 %copy-start.57 = (f32[1,1,3072]{2,1,0:T(1,128)S(1)}, f32[1,1,3072]{2,1,0:T(1,128)}, u32[]{:S(2)}) copy-start(f32[1,1,3072]{2,1,0:T(1,128)} %copy-done.56) | copy-start | bytes 36868
  191.5 22.4 %copy-start.59 = (f32[1,1,3072]{2,1,0:T(1,128)S(1)}, f32[1,1,3072]{2,1,0:T(1,128)}, u32[]{:S(2)}) copy-start(f32[1,1,3072]{2,1,0:T(1,128)} %copy-done.58) | copy-start | bytes 36868
  191.5 22.4 %copy-start.61 = (f32[1,1,3072]{2,1,0:T(1,128)S(1)}, f32[1,1,3072]{2,1,0:T(1,128)}, u32[]{:S(2)}) copy-start(f32[1,1,3072]{2,1,0:T(1,128)} %copy-done.60) | copy-start | bytes 36868
  191.5 22.4 %copy-start.63 = (f32[1,1,3072]{2,1,0:T(1,128)S(1)}, f32[1,1,3072]{2,1,0:T(1,128)}, u32[]{:S(2)}) copy-start(f32[1,1,3072]{2,1,0:T(1,128)} %copy-done.62) | copy-start | bytes 36868
  191.5 22.4 %copy-start.65 = (f32[1,1,3072]{2,1,0:T(1,128)S(1)}, f32[1,1,3072]{2,1,0:T(1,128)}, u32[]{:S(2)}) copy-start(f32[1,1,3072]{2,1,0:T(1,128)} %copy-done.64) | copy-start | bytes 36868
  191.5 22.4 %copy-start.67 = (f32[1,1,3072]{2,1,0:T(1,128)S(1)}, f32[1,1,3072]{2,1,0:T(1,128)}, u32[]{:S(2)}) copy-start(f32[1,1,3072]{2,1,0:T(1,128)} %copy-done.66) | copy-start | bytes 36868
  191.5 22.4 %copy-start.69 = (f32[1,1,3072]{2,1,0:T(1,128)S(1)}, f32[1,1,3072]{2,1,0:T(1,128)}, u32[]{:S(2)}) copy-start(f32[1,1,3072]{2,1,0:T(1,128)} %copy-done.68) | copy-start | bytes 36868
  191.5 22.4 %copy-start.71 = (f32[1,1,3072]{2,1,0:T(1,128)S(1)}, f32[1,1,3072]{2,1,0:T(1,128)}, u32[]{:S(2)}) copy-start(f32[1,1,3072]{2,1,0:T(1,128)} %copy-done.70) | copy-start | bytes 36868
  191.6 22.4 %copy-start.73 = (f32[1,1,3072]{2,1,0:T(1,128)S(1)}, f32[1,1,3072]{2,1,0:T(1,128)}, u32[]{:S(2)}) copy-start(f32[1,1,3072]{2,1,0:T(1,128)} %copy-done.72) | copy-start | bytes 36868
  191.6 22.4 %copy-start.75 = (f32[1,1,3072]{2,1,0:T(1,128)S(1)}, f32[1,1,3072]{2,1,0:T(1,128)}, u32[]{:S(2)}) copy-start(f32[1,1,3072]{2,1,0:T(1,128)} %copy-done.74) | copy-start | bytes 36868
  191.6 22.4 %copy-start.77 = (f32[1,1,3072]{2,1,0:T(1,128)S(1)}, f32[1,1,3072]{2,1,0:T(1,128)}, u32[]{:S(2)}) copy-start(f32[1,1,3072]{2,1,0:T(1,128)} %copy-done.76) | copy-start | bytes 36868
  191.6 22.4 %copy-start.79 = (f32[1,1,3072]{2,1,0:T(1,128)S(1)}, f32[1,1,3072]{2,1,0:T(1,128)}, u32[]{:S(2)}) copy-start(f32[1,1,3072]{2,1,0:T(1,128)} %copy-done.78) | copy-start | bytes 36868
  191.6 22.4 %copy-start.81 = (f32[1,1,3072]{2,1,0:T(1,128)S(1)}, f32[1,1,3072]{2,1,0:T(1,128)}, u32[]{:S(2)}) copy-start(f32[1,1,3072]{2,1,0:T(1,128)} %copy-done.80) | copy-start | bytes 36868
  191.6 22.4 %copy-start.83 = (f32[1,1,3072]{2,1,0:T(1,128)S(1)}, f32[1,1,3072]{2,1,0:T(1,128)}, u32[]{:S(2)}) copy-start(f32[1,1,3072]{2,1,0:T(1,128)} %copy-done.82) | copy-start | bytes 36868
  191.6 22.4 %copy-start.85 = (f32[1,1,3072]{2,1,0:T(1,128)S(1)}, f32[1,1,3072]{2,1,0:T(1,128)}, u32[]{:S(2)}) copy-start(f32[1,1,3072]{2,1,0:T(1,128)} %copy-done.84) | copy-start | bytes 36868
  (79 other events, 1155.2 us)

commit v11 on v9

--- a/solution.py
+++ b/solution.py
@@ -66,7 +66,7 @@
 
 def radix_split(count):
     parts = []
-    for radix in (3, 2):
+    for radix in (4, 3, 2):
         while count % radix == 0 and count > 1:
             parts.append(radix)
             count //= radix

time: 242 us -> 247 us (1.021)
  local copies, waits for them, and re-layouts: 14.1 us -> 19.3 us
  starting transfers between devices: 61.6 us -> 66.5 us
  waiting for transfers between devices: 70 us -> 66.5 us
    gather x2 -> x5, local copies, waits for them, and re-layouts: 0.62 us -> 6.2 us  [gather_stages(): value = jnp.take(stacked, order, axis=stage)]
    ppermute x7 -> x9, starting transfers between devices: 43 us -> 48 us  [gather_stages(): got.append(lax.ppermute(value, axis, pairs))]
    another operation x9 -> x1, other arithmetic: 4.75 us -> 0.02 us  [gather_stages(): jnp.stack([jnp.where(first, got[0], got[1]), jnp.where(first, got[1], got...]
    ppermute x7 -> x9, waiting for transfers between devices: 23.8 us -> 19.7 us  [gather_stages(): got.append(lax.ppermute(value, axis, pairs))]
  transfers between devices with their start and end apart: 14 -> 16, of which waited for: 11 -> 11; matrix products, arithmetic and copies ran while one was open for 4% -> 4% of each run, Pallas kernels for 0% -> 0%
where the time goes in v11:
time: 247 us; the launch traced here: 245 us
  other arithmetic  77 us (31%)
  starting transfers between devices  66.5 us (27%)
  waiting for transfers between devices  66.5 us (27%)
  local copies, waits for them, and re-layouts  19.3 us (8%)
  matrix products  12.3 us (5%)
  between operations  3.52 us (1%)
    ppermute x9, starting transfers between devices, gather_stages(): got.append(lax.ppermute(value, axis, pairs))  48 us
    ppermute x2, waiting for transfers between devices, halo_rows(): before = lax.ppermute(last, 'row', up)  40.4 us
    reduce_sum x4, other arithmetic, cell_norm(): center = values - jnp.mean(values, axis=-1, keepdims=True)  30.1 us
    convert_element_type x1, other arithmetic, local(): grad_map = (own_grad[:, None, None, :] + spread).astype(jnp.bfloat16)  27.3 us
    ppermute x9, waiting for transfers between devices, gather_stages(): got.append(lax.ppermute(value, axis, pairs))  19.7 us
    ppermute x3, starting transfers between devices, group_sum(): value = value + lax.ppermute(value, 'row', pairs)  7.47 us
    ppermute x2, starting transfers between devices, halo_rows(): after = lax.ppermute(leading, 'row', down)  7.29 us
    ppermute x3, waiting for transfers between devices, group_sum(): value = value + lax.ppermute(value, 'row', pairs)  6.4 us
  transfers between devices with their start and end apart: 16, of which 11 were waited for; matrix products, arithmetic and copies ran while one was open for 4% of the time, Pallas kernels for 0%

profile of v11, /device:TPU:6, one launch (start us, length us, event | category | flops | bytes accessed | tf_op | source)
XLA Modules:
  0.0 245.1 jit_solution(13288303914927746122)
XLA Ops:
  0.7 3.3 %fusion.34 = (bf16[2,3,32,3072]{3,2,1,0:T(8,128)(2,1)}, bf16[2,3,32,3072]{3,2,1,0:T(8,128)(2,1)}) fusion(bf16[2,4,32,3072]{3,2,1,0:T(8,128)(2,1)} %param.11), kind=kLoop, calls=%fused_computation.244 | loop fusion | bytes 4718592 | tf_op jit(solution)/shard_map/slice | solution.py:21
  4.0 1.9 collective-permute-start
  5.9 3.6 %collective-permute-start.1 = (bf16[2,3,32,3072]{3,2,1,0:T(8,128)(2,1)}, bf16[2,3,32,3072]{3,2,1,0:T(8,128)(2,1)}, u32[]{:S(2)}, u32[]{:S(2)}) collective-permute-start(bf16[2,3,32,3072]{3,2,1,0:T(8,128)(2,1)} %get-tuple-element.30), channel_id=1, source_target_pairs={{1,0},{2,1},{3,2},{4,3},{5,4},{6,5},{7,6},{9,8},{10,9},{11,10},{12... | collective-permute-start | bytes 3538952 | tf_op jit(solution)/shard_map/ppermute | solution.py:24
  16.4 18.0 %collective-permute-done = bf16[2,3,32,3072]{3,2,1,0:T(8,128)(2,1)S(1)} collective-permute-done((bf16[2,3,32,3072]{3,2,1,0:T(8,128)(2,1)}, bf16[2,3,32,3072]{3,2,1,0:T(8,128)(2,1)S(1)}, u32[]{:S(2)}, u32[]{:S(2)}) %collective-permute-start) | collective-permute-done | bytes 1179680 | tf_op jit(solution)/shard_map/ppermute | solution.py:23
  34.4 1.5 pad_maximum_fusion
  36.3 29.0 %fusion.32 = (f32[2,4,32]{2,1,0:T(4,128)S(1)}, f32[2,4,32,3072]{3,2,1,0:T(8,128)S(1)}) fusion(f32[3072]{0:T(1024)S(1)} %copy-done.101, f32[3072]{0:T(1024)S(1)} %bitcast.120, f32[3072]{0:T(1024)S(1)} %bitcast.122, f32[3072]{0:T(1024)S(1)} %bitcast.126, f32[3072]{0:T(1024)S(1)} %bitcast.128, bf16[2,10,32,3072]{3,2,1,0:T(8,128)(2,1)S(1)} %pad_maximum_fusion, ...), kind=kLoop, calls=%fused_computation.242 | loop fusion | flops 116391680 | bytes 18703360 | tf_op jit(solution)/shard_map/reduce_sum | solution.py:78
  65.9 0.9 copy-done.1
  66.8 1.0 add_reduce_fusion
  67.7 1.9 collective-permute-start.2
  70.9 1.9 collective-permute-start.3
  72.8 3.8 %collective-permute-done.3 = f32[2,3072]{1,0:T(2,128)S(1)} collective-permute-done((f32[2,3072]{1,0:T(2,128)S(1)}, f32[2,3072]{1,0:T(2,128)S(1)}, u32[]{:S(2)}, u32[]{:S(2)}) %collective-permute-start.3) | collective-permute-done | bytes 24608 | tf_op jit(solution)/shard_map/ppermute | solution.py:33
  76.6 3.6 %collective-permute-start.4 = (f32[2,3072]{1,0:T(2,128)S(1)}, f32[2,3072]{1,0:T(2,128)S(1)}, u32[]{:S(2)}, u32[]{:S(2)}) collective-permute-start(f32[2,3072]{1,0:T(2,128)S(1)} %add.565), channel_id=1, source_target_pairs={{0,4},{1,5},{2,6},{3,7},{4,0},{5,1},{6,2},{7,3},{8,12},{9,13},{10,... | collective-permute-start | bytes 73736 | tf_op jit(solution)/shard_map/ppermute | solution.py:33
  80.2 2.1 collective-permute-done.4
  83.2 3.9 %multiply_reduce_fusion.7 = (f32[2]{0:T(128)S(1)}, f32[2,1024]{1,0:T(2,128)S(1)}) fusion(bf16[3072,1024]{1,0:T(8,128)(2,1)} %param.17, f32[2]{0:T(128)S(1)} %fusion.27, f32[3072]{0:T(1024)S(1)} %copy-done.94, f32[2,3072]{1,0:T(2,128)S(1)} %get-tuple-element.24, f32[2]{0:T(128)S(1)} %broadcast_multiply_fusion.5), kind=kOutput, calls=%fused_computation.182 | convolution fusion | flops 12611582 | bytes 6336536 | tf_op jit(solution)/shard_map/dot_general | solution.py:149
  87.8 15.1 %collective-permute-start.5 = (bf16[4,1024]{1,0:T(4,128)(2,1)S(1)}, bf16[4,1024]{1,0:T(4,128)(2,1)S(1)}, u32[]{:S(2)}, u32[]{:S(2)}) collective-permute-start(bf16[4,1024]{1,0:T(4,128)(2,1)S(1)} %pad_maximum_fusion.6), channel_id=1, source_target_pairs={{0,24},{8,32},{16,40},{24,0},{32,8},{40,16},{1,25},{9,33},{17,41},... | collective-permute-start | bytes 24584 | tf_op jit(solution)/shard_map/ppermute | solution.py:54
  103.4 1.1 collective-permute-done.5
  104.6 3.7 %collective-permute-start.6 = (bf16[2,4,1024]{2,1,0:T(4,128)(2,1)S(1)}, bf16[2,4,1024]{2,1,0:T(4,128)(2,1)S(1)}, u32[]{:S(2)}, u32[]{:S(2)}) collective-permute-start(bf16[2,4,1024]{2,1,0:T(4,128)(2,1)S(1)} %get-tuple-element.83), channel_id=1, source_target_pairs={{0,8},{8,16},{16,0},{24,32},{32,40},{40,24},{1,9},{9,17},{17,1},{2... | collective-permute-start | bytes 49160 | tf_op jit(solution)/shard_map/ppermute | solution.py:54
  108.3 6.1 %collective-permute-start.7 = (bf16[2,4,1024]{2,1,0:T(4,128)(2,1)S(1)}, bf16[2,4,1024]{2,1,0:T(4,128)(2,1)S(1)}, u32[]{:S(2)}, u32[]{:S(2)}) collective-permute-start(bf16[2,4,1024]{2,1,0:T(4,128)(2,1)S(1)} %get-tuple-element.83), channel_id=1, source_target_pairs={{0,16},{8,0},{16,8},{24,40},{32,24},{40,32},{1,17},{9,1},{17,9},{2... | collective-permute-start | bytes 49160 | tf_op jit(solution)/shard_map/ppermute | solution.py:54
  116.5 8.6 %collective-permute-start.10 = (bf16[6,4,1024]{2,1,0:T(4,128)(2,1)S(1)}, bf16[6,4,1024]{2,1,0:T(4,128)(2,1)S(1)}, u32[]{:S(2)}, u32[]{:S(2)}) collective-permute-start(bf16[6,4,1024]{2,1,0:T(4,128)(2,1)S(1)} %bitcast_select_fusion.2), channel_id=1, source_target_pairs={{0,576},{48,624},{96,672},{144,720},{192,0},{240,48},{288,96},{336... | collective-permute-start | bytes 147464 | tf_op jit(solution)/shard_map/ppermute | solution.py:54
  125.1 4.0 %collective-permute-start.9 = (bf16[6,4,1024]{2,1,0:T(4,128)(2,1)S(1)}, bf16[6,4,1024]{2,1,0:T(4,128)(2,1)S(1)}, u32[]{:S(2)}, u32[]{:S(2)}) collective-permute-start(bf16[6,4,1024]{2,1,0:T(4,128)(2,1)S(1)} %bitcast_select_fusion.2), channel_id=1, source_target_pairs={{0,384},{48,432},{96,480},{144,528},{192,576},{240,624},{288,672},... | collective-permute-start | bytes 147464 | tf_op jit(solution)/shard_map/ppermute | solution.py:54
  129.1 1.9 collective-permute-start.8
  131.2 1.4 collective-permute-done.9
  132.6 9.1 %collective-permute-done.8 = bf16[6,4,1024]{2,1,0:T(4,128)(2,1)S(1)} collective-permute-done((bf16[6,4,1024]{2,1,0:T(4,128)(2,1)S(1)}, bf16[6,4,1024]{2,1,0:T(4,128)(2,1)S(1)}, u32[]{:S(2)}, u32[]{:S(2)}) %collective-permute-start.8) | collective-permute-done | bytes 49184 | tf_op jit(solution)/shard_map/ppermute | solution.py:54
  141.8 0.8 gather_fusion.1
  142.7 0.8 broadcast_select_fusion
  143.5 2.8 %collective-permute-start.13 = (bf16[4,6,4,1024]{3,2,1,0:T(4,128)(2,1)S(1)}, bf16[4,6,4,1024]{3,2,1,0:T(4,128)(2,1)S(1)}, u32[]{:S(2)}, u32[]{:S(2)}) collective-permute-start(bf16[4,6,4,1024]{3,2,1,0:T(4,128)(2,1)S(1)} %broadcast_select_fusion), channel_id=1, source_target_pairs={{0,144},{48,0},{96,48},{144,96},{192,336},{240,192},{288,240},{336... | collective-permute-start | bytes 589832 | tf_op jit(solution)/shard_map/ppermute | solution.py:54
  146.3 3.7 %collective-permute-start.12 = (bf16[4,6,4,1024]{3,2,1,0:T(4,128)(2,1)S(1)}, bf16[4,6,4,1024]{3,2,1,0:T(4,128)(2,1)S(1)}, u32[]{:S(2)}, u32[]{:S(2)}) collective-permute-start(bf16[4,6,4,1024]{3,2,1,0:T(4,128)(2,1)S(1)} %broadcast_select_fusion), channel_id=1, source_target_pairs={{0,96},{48,144},{96,0},{144,48},{192,288},{240,336},{288,192},{336... | collective-permute-start | bytes 589832 | tf_op jit(solution)/shard_map/ppermute | solution.py:54
  150.0 2.1 collective-permute-start.11
  152.1 0.8 fusion.4
  152.9 1.1 collective-permute-done.13
  154.0 6.3 %collective-permute-done.12 = bf16[4,6,4,1024]{3,2,1,0:T(4,128)(2,1)S(1)} collective-permute-done((bf16[4,6,4,1024]{3,2,1,0:T(4,128)(2,1)S(1)}, bf16[4,6,4,1024]{3,2,1,0:T(4,128)(2,1)S(1)}, u32[]{:S(2)}, u32[]{:S(2)}) %collective-permute-start.12) | collective-permute-done | bytes 196640 | tf_op jit(solution)/shard_map/ppermute | solution.py:54
  160.3 1.6 pad_maximum_fusion.2
  161.9 3.3 %gather_fusion.2 = bf16[4,4,6,4,1024]{4,3,2,1,0:T(4,128)(2,1)} fusion(bf16[4,4,6,4,1024]{4,3,2,1,0:T(4,128)(2,1)} %pad_maximum_fusion.2, s32[1024]{0:T(1024)} %pad_clamp_fusion), kind=kCustom, calls=%fused_computation.2 | custom fusion | bytes 1572880 | tf_op jit(solution)/shard_map/jit(_take)/gather | solution.py:63
  165.2 1.4 copy.39
  167.1 1.3 fusion.35
  168.4 0.9 reshape.670
  169.3 1.1 reshape.669
  170.4 2.1 multiply_convert_fusion
  172.5 1.3 multiply_reduce_fusion.6
  174.5 4.6 %multiply_reduce_fusion.4 = (f32[2]{0:T(128)S(1)}, f32[2,3072]{1,0:T(2,128)S(1)}) fusion(f32[2,3072]{1,0:T(2,128)} %copy-done.5, f32[2]{0:T(128)} %copy-done.102, f32[3072]{0:T(1024)} %param.16, bf16[3072,1024]{1,0:T(8,128)(2,1)} %param.17, f32[2,1024]{1,0:T(2,128)} %copy-done.11, f32[2,1024]{1,0:T(2,128)S(1)} %get-tuple-element.97, ...), kind=kOutput, calls=%fused_computation.114 | convolution fusion | flops 12617726 | bytes 6369312 | tf_op jit(solution)/shard_map/dot_general | solution.py:168
  181.4 1.0 add_convert_fusion.1
  182.5 1.1 copy-done.2
  183.6 1.3 fusion.33
  184.9 1.9 collective-permute-start.14
  186.8 3.6 %collective-permute-start.15 = (bf16[2,3,32,3072]{3,2,1,0:T(8,128)(2,1)S(1)}, bf16[2,3,32,3072]{3,2,1,0:T(8,128)(2,1)}, u32[]{:S(2)}, u32[]{:S(2)}) collective-permute-start(bf16[2,3,32,3072]{3,2,1,0:T(8,128)(2,1)S(1)} %get-tuple-element.28), channel_id=1, source_target_pairs={{1,0},{2,1},{3,2},{4,3},{5,4},{6,5},{7,6},{9,8},{10,9},{11,10},{12... | collective-permute-start | bytes 3538952 | tf_op jit(solution)/shard_map/ppermute | solution.py:24
  192.8 22.4 %collective-permute-done.14 = bf16[2,3,32,3072]{3,2,1,0:T(8,128)(2,1)S(1)} collective-permute-done((bf16[2,3,32,3072]{3,2,1,0:T(8,128)(2,1)}, bf16[2,3,32,3072]{3,2,1,0:T(8,128)(2,1)S(1)}, u32[]{:S(2)}, u32[]{:S(2)}) %collective-permute-start.14) | collective-permute-done | bytes 1179680 | tf_op jit(solution)/shard_map/ppermute | solution.py:23
  215.3 2.0 pad_maximum_fusion.1
  217.6 27.3 %add_convert_fusion = bf16[2,4,32,3072]{3,2,1,0:T(8,128)(2,1)} fusion(bf16[2,10,32,3072]{3,2,1,0:T(8,128)(2,1)S(1)} %pad_maximum_fusion.1, f32[2,3072]{1,0:T(2,128)S(1)} %copy-done.91, f32[3072]{0:T(1024)S(1)} %bitcast.121, f32[3072]{0:T(1024)S(1)} %bitcast.123, f32[3072]{0:T(1024)S(1)} %bitcast.127, f32[3072]{0:T(1024)S(1)} %bitcast.129, ...), kind=kLoop, calls=%fused_computation.10 | loop fusion | flops 116391936 | bytes 17141760 | tf_op jit(solution)/shard_map/convert_element_type | solution.py:184
  (305 shorter events, 17.5 us)
Async XLA Ops:
  0.6 33.7 %copy-start = (bf16[2,4,32,3072]{3,2,1,0:T(8,128)(2,1)S(1)}, bf16[2,4,32,3072]{3,2,1,0:T(8,128)(2,1)}, u32[]{:S(2)}) copy-start(bf16[2,4,32,3072]{3,2,1,0:T(8,128)(2,1)} %param.11) | copy-start | bytes 4718596
  4.0 30.4 %collective-permute-start = (bf16[2,3,32,3072]{3,2,1,0:T(8,128)(2,1)}, bf16[2,3,32,3072]{3,2,1,0:T(8,128)(2,1)S(1)}, u32[]{:S(2)}, u32[]{:S(2)}) collective-permute-start(bf16[2,3,32,3072]{3,2,1,0:T(8,128)(2,1)} %get-tuple-element.29), channel_id=1, source_target_pairs={{0,1},{1,2},{2,3},{3,4},{4,5},{5,6},{6,7},{8,9},{9,10},{10,11},{11... | collective-permute-start | bytes 3538952 | tf_op jit(solution)/shard_map/ppermute | solution.py:23
  5.9 28.4 %collective-permute-start.1 = (bf16[2,3,32,3072]{3,2,1,0:T(8,128)(2,1)}, bf16[2,3,32,3072]{3,2,1,0:T(8,128)(2,1)}, u32[]{:S(2)}, u32[]{:S(2)}) collective-permute-start(bf16[2,3,32,3072]{3,2,1,0:T(8,128)(2,1)} %get-tuple-element.30), channel_id=1, source_target_pairs={{1,0},{2,1},{3,2},{4,3},{5,4},{6,5},{7,6},{9,8},{10,9},{11,10},{12... | collective-permute-start | bytes 3538952 | tf_op jit(solution)/shard_map/ppermute | solution.py:24
  67.7 3.1 %collective-permute-start.2 = (f32[2,3072]{1,0:T(2,128)S(1)}, f32[2,3072]{1,0:T(2,128)S(1)}, u32[]{:S(2)}, u32[]{:S(2)}) collective-permute-start(f32[2,3072]{1,0:T(2,128)S(1)} %broadcast_multiply_fusion.1), channel_id=1, source_target_pairs={{0,1},{1,0},{2,3},{3,2},{4,5},{5,4},{6,7},{7,6},{8,9},{9,8},{10,11... | collective-permute-start | bytes 73736 | tf_op jit(solution)/shard_map/ppermute | solution.py:33
  70.9 5.7 %collective-permute-start.3 = (f32[2,3072]{1,0:T(2,128)S(1)}, f32[2,3072]{1,0:T(2,128)S(1)}, u32[]{:S(2)}, u32[]{:S(2)}) collective-permute-start(f32[2,3072]{1,0:T(2,128)S(1)} %fusion.28), channel_id=1, source_target_pairs={{0,2},{1,3},{2,0},{3,1},{4,6},{5,7},{6,4},{7,5},{8,10},{9,11},{10,... | collective-permute-start | bytes 73736 | tf_op jit(solution)/shard_map/ppermute | solution.py:33
  76.6 5.7 %collective-permute-start.4 = (f32[2,3072]{1,0:T(2,128)S(1)}, f32[2,3072]{1,0:T(2,128)S(1)}, u32[]{:S(2)}, u32[]{:S(2)}) collective-permute-start(f32[2,3072]{1,0:T(2,128)S(1)} %add.565), channel_id=1, source_target_pairs={{0,4},{1,5},{2,6},{3,7},{4,0},{5,1},{6,2},{7,3},{8,12},{9,13},{10,... | collective-permute-start | bytes 73736 | tf_op jit(solution)/shard_map/ppermute | solution.py:33
  87.1 28.6 %copy-start.11 = (f32[2,1024]{1,0:T(2,128)}, f32[2,1024]{1,0:T(2,128)S(1)}, u32[]{:S(2)}) copy-start(f32[2,1024]{1,0:T(2,128)S(1)} %get-tuple-element.93) | copy-start | bytes 24580
  87.8 16.8 %collective-permute-start.5 = (bf16[4,1024]{1,0:T(4,128)(2,1)S(1)}, bf16[4,1024]{1,0:T(4,128)(2,1)S(1)}, u32[]{:S(2)}, u32[]{:S(2)}) collective-permute-start(bf16[4,1024]{1,0:T(4,128)(2,1)S(1)} %pad_maximum_fusion.6), channel_id=1, source_target_pairs={{0,24},{8,32},{16,40},{24,0},{32,8},{40,16},{1,25},{9,33},{17,41},... | collective-permute-start | bytes 24584 | tf_op jit(solution)/shard_map/ppermute | solution.py:54
  104.6 10.5 %collective-permute-start.6 = (bf16[2,4,1024]{2,1,0:T(4,128)(2,1)S(1)}, bf16[2,4,1024]{2,1,0:T(4,128)(2,1)S(1)}, u32[]{:S(2)}, u32[]{:S(2)}) collective-permute-start(bf16[2,4,1024]{2,1,0:T(4,128)(2,1)S(1)} %get-tuple-element.83), channel_id=1, source_target_pairs={{0,8},{8,16},{16,0},{24,32},{32,40},{40,24},{1,9},{9,17},{17,1},{2... | collective-permute-start | bytes 49160 | tf_op jit(solution)/shard_map/ppermute | solution.py:54
  108.3 7.5 %collective-permute-start.7 = (bf16[2,4,1024]{2,1,0:T(4,128)(2,1)S(1)}, bf16[2,4,1024]{2,1,0:T(4,128)(2,1)S(1)}, u32[]{:S(2)}, u32[]{:S(2)}) collective-permute-start(bf16[2,4,1024]{2,1,0:T(4,128)(2,1)S(1)} %get-tuple-element.83), channel_id=1, source_target_pairs={{0,16},{8,0},{16,8},{24,40},{32,24},{40,32},{1,17},{9,1},{17,9},{2... | collective-permute-start | bytes 49160 | tf_op jit(solution)/shard_map/ppermute | solution.py:54
  116.5 14.7 %collective-permute-start.10 = (bf16[6,4,1024]{2,1,0:T(4,128)(2,1)S(1)}, bf16[6,4,1024]{2,1,0:T(4,128)(2,1)S(1)}, u32[]{:S(2)}, u32[]{:S(2)}) collective-permute-start(bf16[6,4,1024]{2,1,0:T(4,128)(2,1)S(1)} %bitcast_select_fusion.2), channel_id=1, source_target_pairs={{0,576},{48,624},{96,672},{144,720},{192,0},{240,48},{288,96},{336... | collective-permute-start | bytes 147464 | tf_op jit(solution)/shard_map/ppermute | solution.py:54
  125.1 7.5 %collective-permute-start.9 = (bf16[6,4,1024]{2,1,0:T(4,128)(2,1)S(1)}, bf16[6,4,1024]{2,1,0:T(4,128)(2,1)S(1)}, u32[]{:S(2)}, u32[]{:S(2)}) collective-permute-start(bf16[6,4,1024]{2,1,0:T(4,128)(2,1)S(1)} %bitcast_select_fusion.2), channel_id=1, source_target_pairs={{0,384},{48,432},{96,480},{144,528},{192,576},{240,624},{288,672},... | collective-permute-start | bytes 147464 | tf_op jit(solution)/shard_map/ppermute | solution.py:54
  129.1 12.5 %collective-permute-start.8 = (bf16[6,4,1024]{2,1,0:T(4,128)(2,1)S(1)}, bf16[6,4,1024]{2,1,0:T(4,128)(2,1)S(1)}, u32[]{:S(2)}, u32[]{:S(2)}) collective-permute-start(bf16[6,4,1024]{2,1,0:T(4,128)(2,1)S(1)} %bitcast_select_fusion.2), channel_id=1, source_target_pairs={{0,192},{48,240},{96,288},{144,336},{192,384},{240,432},{288,480},... | collective-permute-start | bytes 147464 | tf_op jit(solution)/shard_map/ppermute | solution.py:54
  143.5 10.5 %collective-permute-start.13 = (bf16[4,6,4,1024]{3,2,1,0:T(4,128)(2,1)S(1)}, bf16[4,6,4,1024]{3,2,1,0:T(4,128)(2,1)S(1)}, u32[]{:S(2)}, u32[]{:S(2)}) collective-permute-start(bf16[4,6,4,1024]{3,2,1,0:T(4,128)(2,1)S(1)} %broadcast_select_fusion), channel_id=1, source_target_pairs={{0,144},{48,0},{96,48},{144,96},{192,336},{240,192},{288,240},{336... | collective-permute-start | bytes 589832 | tf_op jit(solution)/shard_map/ppermute | solution.py:54
  146.3 14.0 %collective-permute-start.12 = (bf16[4,6,4,1024]{3,2,1,0:T(4,128)(2,1)S(1)}, bf16[4,6,4,1024]{3,2,1,0:T(4,128)(2,1)S(1)}, u32[]{:S(2)}, u32[]{:S(2)}) collective-permute-start(bf16[4,6,4,1024]{3,2,1,0:T(4,128)(2,1)S(1)} %broadcast_select_fusion), channel_id=1, source_target_pairs={{0,96},{48,144},{96,0},{144,48},{192,288},{240,336},{288,192},{336... | collective-permute-start | bytes 589832 | tf_op jit(solution)/shard_map/ppermute | solution.py:54
  150.0 10.3 %collective-permute-start.11 = (bf16[4,6,4,1024]{3,2,1,0:T(4,128)(2,1)S(1)}, bf16[4,6,4,1024]{3,2,1,0:T(4,128)(2,1)S(1)}, u32[]{:S(2)}, u32[]{:S(2)}) collective-permute-start(bf16[4,6,4,1024]{3,2,1,0:T(4,128)(2,1)S(1)} %broadcast_select_fusion), channel_id=1, source_target_pairs={{0,48},{48,96},{96,144},{144,0},{192,240},{240,288},{288,336},{336... | collective-permute-start | bytes 589832 | tf_op jit(solution)/shard_map/ppermute | solution.py:54
  184.9 30.4 %collective-permute-start.14 = (bf16[2,3,32,3072]{3,2,1,0:T(8,128)(2,1)}, bf16[2,3,32,3072]{3,2,1,0:T(8,128)(2,1)S(1)}, u32[]{:S(2)}, u32[]{:S(2)}) collective-permute-start(bf16[2,3,32,3072]{3,2,1,0:T(8,128)(2,1)} %get-tuple-element.27), channel_id=1, source_target_pairs={{0,1},{1,2},{2,3},{3,4},{4,5},{5,6},{6,7},{8,9},{9,10},{10,11},{11... | collective-permute-start | bytes 3538952 | tf_op jit(solution)/shard_map/ppermute | solution.py:23
  186.8 28.4 %collective-permute-start.15 = (bf16[2,3,32,3072]{3,2,1,0:T(8,128)(2,1)S(1)}, bf16[2,3,32,3072]{3,2,1,0:T(8,128)(2,1)}, u32[]{:S(2)}, u32[]{:S(2)}) collective-permute-start(bf16[2,3,32,3072]{3,2,1,0:T(8,128)(2,1)S(1)} %get-tuple-element.28), channel_id=1, source_target_pairs={{1,0},{2,1},{3,2},{4,3},{5,4},{6,5},{7,6},{9,8},{10,9},{11,10},{12... | collective-permute-start | bytes 3538952 | tf_op jit(solution)/shard_map/ppermute | solution.py:24
  192.5 24.8 %copy-start.22 = (f32[1,1,3072]{2,1,0:T(1,128)S(1)}, f32[1,1,3072]{2,1,0:T(1,128)}, u32[]{:S(2)}) copy-start(f32[1,1,3072]{2,1,0:T(1,128)} %copy-done.21) | copy-start | bytes 36868
  192.5 24.8 %copy-start.24 = (f32[1,1,3072]{2,1,0:T(1,128)S(1)}, f32[1,1,3072]{2,1,0:T(1,128)}, u32[]{:S(2)}) copy-start(f32[1,1,3072]{2,1,0:T(1,128)} %copy-done.23) | copy-start | bytes 36868
  192.5 24.8 %copy-start.26 = (f32[1,1,3072]{2,1,0:T(1,128)S(1)}, f32[1,1,3072]{2,1,0:T(1,128)}, u32[]{:S(2)}) copy-start(f32[1,1,3072]{2,1,0:T(1,128)} %copy-done.25) | copy-start | bytes 36868
  192.5 24.8 %copy-start.28 = (f32[1,1,3072]{2,1,0:T(1,128)S(1)}, f32[1,1,3072]{2,1,0:T(1,128)}, u32[]{:S(2)}) copy-start(f32[1,1,3072]{2,1,0:T(1,128)} %copy-done.27) | copy-start | bytes 36868
  192.5 24.8 %copy-start.30 = (f32[1,1,3072]{2,1,0:T(1,128)S(1)}, f32[1,1,3072]{2,1,0:T(1,128)}, u32[]{:S(2)}) copy-start(f32[1,1,3072]{2,1,0:T(1,128)} %copy-done.29) | copy-start | bytes 36868
  192.5 24.8 %copy-start.32 = (f32[1,1,3072]{2,1,0:T(1,128)S(1)}, f32[1,1,3072]{2,1,0:T(1,128)}, u32[]{:S(2)}) copy-start(f32[1,1,3072]{2,1,0:T(1,128)} %copy-done.31) | copy-start | bytes 36868
  192.5 24.8 %copy-start.34 = (f32[1,1,3072]{2,1,0:T(1,128)S(1)}, f32[1,1,3072]{2,1,0:T(1,128)}, u32[]{:S(2)}) copy-start(f32[1,1,3072]{2,1,0:T(1,128)} %copy-done.33) | copy-start | bytes 36868
  192.5 24.8 %copy-start.36 = (f32[1,1,3072]{2,1,0:T(1,128)S(1)}, f32[1,1,3072]{2,1,0:T(1,128)}, u32[]{:S(2)}) copy-start(f32[1,1,3072]{2,1,0:T(1,128)} %copy-done.35) | copy-start | bytes 36868
  192.6 24.8 %copy-start.38 = (f32[1,1,3072]{2,1,0:T(1,128)S(1)}, f32[1,1,3072]{2,1,0:T(1,128)}, u32[]{:S(2)}) copy-start(f32[1,1,3072]{2,1,0:T(1,128)} %copy-done.37) | copy-start | bytes 36868
  192.6 24.8 %copy-start.40 = (f32[1,1,3072]{2,1,0:T(1,128)S(1)}, f32[1,1,3072]{2,1,0:T(1,128)}, u32[]{:S(2)}) copy-start(f32[1,1,3072]{2,1,0:T(1,128)} %copy-done.39) | copy-start | bytes 36868
  192.6 24.8 %copy-start.42 = (f32[1,1,3072]{2,1,0:T(1,128)S(1)}, f32[1,1,3072]{2,1,0:T(1,128)}, u32[]{:S(2)}) copy-start(f32[1,1,3072]{2,1,0:T(1,128)} %copy-done.41) | copy-start | bytes 36868
  192.6 24.8 %copy-start.44 = (f32[1,1,3072]{2,1,0:T(1,128)S(1)}, f32[1,1,3072]{2,1,0:T(1,128)}, u32[]{:S(2)}) copy-start(f32[1,1,3072]{2,1,0:T(1,128)} %copy-done.43) | copy-start | bytes 36868
  192.6 24.8 %copy-start.46 = (f32[1,1,3072]{2,1,0:T(1,128)S(1)}, f32[1,1,3072]{2,1,0:T(1,128)}, u32[]{:S(2)}) copy-start(f32[1,1,3072]{2,1,0:T(1,128)} %copy-done.45) | copy-start | bytes 36868
  192.6 24.8 %copy-start.48 = (f32[1,1,3072]{2,1,0:T(1,128)S(1)}, f32[1,1,3072]{2,1,0:T(1,128)}, u32[]{:S(2)}) copy-start(f32[1,1,3072]{2,1,0:T(1,128)} %copy-done.47) | copy-start | bytes 36868
  192.6 24.8 %copy-start.50 = (f32[1,1,3072]{2,1,0:T(1,128)S(1)}, f32[1,1,3072]{2,1,0:T(1,128)}, u32[]{:S(2)}) copy-start(f32[1,1,3072]{2,1,0:T(1,128)} %copy-done.49) | copy-start | bytes 36868
  192.6 24.8 %copy-start.52 = (f32[1,1,3072]{2,1,0:T(1,128)S(1)}, f32[1,1,3072]{2,1,0:T(1,128)}, u32[]{:S(2)}) copy-start(f32[1,1,3072]{2,1,0:T(1,128)} %copy-done.51) | copy-start | bytes 36868
  192.6 24.8 %copy-start.54 = (f32[1,1,3072]{2,1,0:T(1,128)S(1)}, f32[1,1,3072]{2,1,0:T(1,128)}, u32[]{:S(2)}) copy-start(f32[1,1,3072]{2,1,0:T(1,128)} %copy-done.53) | copy-start | bytes 36868
  192.6 24.8 %copy-start.56 = (f32[1,1,3072]{2,1,0:T(1,128)S(1)}, f32[1,1,3072]{2,1,0:T(1,128)}, u32[]{:S(2)}) copy-start(f32[1,1,3072]{2,1,0:T(1,128)} %copy-done.55) | copy-start | bytes 36868
  192.7 24.8 %copy-start.58 = (f32[1,1,3072]{2,1,0:T(1,128)S(1)}, f32[1,1,3072]{2,1,0:T(1,128)}, u32[]{:S(2)}) copy-start(f32[1,1,3072]{2,1,0:T(1,128)} %copy-done.57) | copy-start | bytes 36868
  192.7 24.8 %copy-start.60 = (f32[1,1,3072]{2,1,0:T(1,128)S(1)}, f32[1,1,3072]{2,1,0:T(1,128)}, u32[]{:S(2)}) copy-start(f32[1,1,3072]{2,1,0:T(1,128)} %copy-done.59) | copy-start | bytes 36868
  192.7 24.8 %copy-start.62 = (f32[1,1,3072]{2,1,0:T(1,128)S(1)}, f32[1,1,3072]{2,1,0:T(1,128)}, u32[]{:S(2)}) copy-start(f32[1,1,3072]{2,1,0:T(1,128)} %copy-done.61) | copy-start | bytes 36868
  192.7 24.8 %copy-start.64 = (f32[1,1,3072]{2,1,0:T(1,128)S(1)}, f32[1,1,3072]{2,1,0:T(1,128)}, u32[]{:S(2)}) copy-start(f32[1,1,3072]{2,1,0:T(1,128)} %copy-done.63) | copy-start | bytes 36868
  192.7 24.8 %copy-start.66 = (f32[1,1,3072]{2,1,0:T(1,128)S(1)}, f32[1,1,3072]{2,1,0:T(1,128)}, u32[]{:S(2)}) copy-start(f32[1,1,3072]{2,1,0:T(1,128)} %copy-done.65) | copy-start | bytes 36868
  192.7 24.8 %copy-start.68 = (f32[1,1,3072]{2,1,0:T(1,128)S(1)}, f32[1,1,3072]{2,1,0:T(1,128)}, u32[]{:S(2)}) copy-start(f32[1,1,3072]{2,1,0:T(1,128)} %copy-done.67) | copy-start | bytes 36868
  192.7 24.8 %copy-start.70 = (f32[1,1,3072]{2,1,0:T(1,128)S(1)}, f32[1,1,3072]{2,1,0:T(1,128)}, u32[]{:S(2)}) copy-start(f32[1,1,3072]{2,1,0:T(1,128)} %copy-done.69) | copy-start | bytes 36868
  192.7 24.8 %copy-start.72 = (f32[1,1,3072]{2,1,0:T(1,128)S(1)}, f32[1,1,3072]{2,1,0:T(1,128)}, u32[]{:S(2)}) copy-start(f32[1,1,3072]{2,1,0:T(1,128)} %copy-done.71) | copy-start | bytes 36868
  192.7 24.8 %copy-start.74 = (f32[1,1,3072]{2,1,0:T(1,128)S(1)}, f32[1,1,3072]{2,1,0:T(1,128)}, u32[]{:S(2)}) copy-start(f32[1,1,3072]{2,1,0:T(1,128)} %copy-done.73) | copy-start | bytes 36868
  192.7 24.8 %copy-start.76 = (f32[1,1,3072]{2,1,0:T(1,128)S(1)}, f32[1,1,3072]{2,1,0:T(1,128)}, u32[]{:S(2)}) copy-start(f32[1,1,3072]{2,1,0:T(1,128)} %copy-done.75) | copy-start | bytes 36868
  192.8 24.8 %copy-start.78 = (f32[1,1,3072]{2,1,0:T(1,128)S(1)}, f32[1,1,3072]{2,1,0:T(1,128)}, u32[]{:S(2)}) copy-start(f32[1,1,3072]{2,1,0:T(1,128)} %copy-done.77) | copy-start | bytes 36868
  192.8 24.8 %copy-start.80 = (f32[1,1,3072]{2,1,0:T(1,128)S(1)}, f32[1,1,3072]{2,1,0:T(1,128)}, u32[]{:S(2)}) copy-start(f32[1,1,3072]{2,1,0:T(1,128)} %copy-done.79) | copy-start | bytes 36868
  (84 other events, 1299.1 us)
